TPU v7x, 256 devices: a whole 4x4x8 slice. The times are simulated.
256 devices in a mesh: row: 16 (over y, x), col: 16 (over z, core).
Axes of the slice: x: 4, y: 4, z: 8, core: 2. Of those that a mesh axis runs over, the one named last changes fastest.
Arguments:
- intensity: int32 [512, 4096], P('row', 'col'), may hold values from 0 to 255
- agreement: int32 [4, 512, 4096], P(None, 'row', 'col'), may hold values from 0 to 8
- basis_block: float32 [128, 512, 4096], P(None, 'row', 'col'), may hold values from -2000 to 2000
Outputs:
- ortho_block: float32 [128, 512, 4096], P(None, 'row', 'col')
- upper_factor: float32 [128, 128], replicated
All inputs are finite; a program needn't handle non-finite values.
Results may differ from a plain program's by a relative error of at most 0.00014.
Values sent between devices are 32-bit elements; how exact they have to be, the bound alone decides.
No kernel may reach another device: no remote copies, remote signals or barrier semaphores. Data moves between devices by JAX's collectives and lax.ppermute only.
A program may use at most 64 MiB of HBM per device.

v0:
```python
import jax
import jax.numpy as jnp
from jax import lax
from jax.sharding import PartitionSpec as P

INV_SIGMA = 1.0 / 40.0
NEIGHBOURS = (
    (0, 1, 0, 1, 1.0 / 9.0),
    (0, -1, 0, 0, 1.0 / 9.0),
    (1, 0, 1, 1, 1.0 / 9.0),
    (-1, 0, 1, 0, 1.0 / 9.0),
    (1, 1, 2, 1, 1.0 / 18.0),
    (-1, -1, 2, 0, 1.0 / 18.0),
    (1, -1, 3, 1, 1.0 / 18.0),
    (-1, 1, 3, 0, 1.0 / 18.0),
)


def padded(cells, sides, width):
    for axis, dim in sides:
        count = lax.axis_size(axis)
        ends = count - 1
        head = lax.slice_in_dim(cells, 0, width, axis=dim)
        tail = lax.slice_in_dim(cells, cells.shape[dim] - width, cells.shape[dim], axis=dim)
        cells = jnp.concatenate(
            [
                lax.ppermute(tail, axis, [(i, (i + 1) % count) for i in range(ends)]),
                cells,
                lax.ppermute(head, axis, [((i + 1) % count, i) for i in range(ends)]),
            ],
            axis=dim,
        )
    return cells


def from_partner(block, axis, stride):
    count = lax.axis_size(axis)
    route = []
    for low in range(count):
        high = low | 1 << stride
        if high != low and high < count:
            route += [(low, high), (high, low)]
    return lax.ppermute(block, axis, route)


def shifted(array, step_row, step_col):
    height = array.shape[-2]
    width = array.shape[-1]
    return array[..., 1 + step_row : height - 1 + step_row, 1 + step_col : width - 1 + step_col]


def cropped(array, cycle):
    return array[..., cycle:-cycle, cycle:-cycle]


def neighbour_weights(levels, counts, inside):
    center = shifted(levels, 0, 0)
    center_in = shifted(inside, 0, 0)
    result = []
    for step_row, step_col, channel, at_center, factor in NEIGHBOURS:
        other = shifted(levels, step_row, step_col)
        if at_center == 1:
            source = shifted(counts[channel], 0, 0)
        else:
            source = shifted(counts[channel], step_row, step_col)
        gap = (center - other) * INV_SIGMA
        result.append(
            (1.0 + source)
            * factor
            * jnp.exp(-gap * gap)
            * center_in
            * shifted(inside, step_row, step_col)
        )
    return result


def degree_scales(weights):
    degree = weights[0]
    for weight in weights[1:]:
        degree = degree + weight
    return lax.rsqrt(1.0 + degree)


def apply_once(values_in, weights, scales):
    lifted = values_in * scales
    summed = None
    for weight, entry in zip(weights, NEIGHBOURS):
        term = weight * shifted(lifted, entry[0], entry[1])
        summed = term if summed is None else summed + term
    return shifted(values_in, 0, 0) - shifted(scales, 0, 0) * summed


def inner_products(first_mat, second_mat):
    return jnp.dot(
        first_mat, second_mat.T, precision=lax.Precision.HIGHEST, preferred_element_type=jnp.float32
    )


def per_device(intensity, agreement, basis_block):
    vectors, tile_rows, tile_cols = basis_block.shape
    row_count = lax.axis_size("row")
    col_count = lax.axis_size("col")
    total_rows = tile_rows * row_count
    total_cols = tile_cols * col_count
    labels = jnp.concatenate((intensity[None], agreement), axis=0)
    labels_wide = padded(labels, (("row", 1), ("col", 2)), 3)
    row_ids = lax.axis_index("row") * tile_rows + jnp.arange(-3, tile_rows + 3, dtype=jnp.int32)
    col_ids = lax.axis_index("col") * tile_cols + jnp.arange(-3, tile_cols + 3, dtype=jnp.int32)
    row_in = ((row_ids >= 0) & (row_ids < total_rows)).astype(jnp.float32)
    col_in = ((col_ids >= 0) & (col_ids < total_cols)).astype(jnp.float32)
    inside = row_in[:, None] * col_in[None, :]
    levels = labels_wide[0].astype(jnp.float32)
    counts = labels_wide[1:].astype(jnp.float32)
    weights = neighbour_weights(levels, counts, inside)
    scales = degree_scales(weights)
    cycle_zero = [cropped(weight, 2) for weight in weights]
    filtered = basis_block
    for repeat in range(2):
        extended = padded(filtered, (("row", 1), ("col", 2)), 1)
        filtered = apply_once(extended, cycle_zero, cropped(scales, 1))
    flat = filtered.reshape(vectors, tile_rows * tile_cols)
    pixel_total = float(total_rows * total_cols)
    gram_local = inner_products(flat, flat) / pixel_total
    factor = jnp.linalg.cholesky(gram_local)
    for bit_no in range(row_count.bit_length() - 1):
        partner = from_partner(factor, "row", bit_no)
        factor = jnp.linalg.cholesky(
            inner_products(factor, factor) + inner_products(partner, partner)
        )
    for bit_no in range(col_count.bit_length() - 1):
        partner = from_partner(factor, "col", bit_no)
        factor = jnp.linalg.cholesky(
            inner_products(factor, factor) + inner_products(partner, partner)
        )
    ortho = jax.scipy.linalg.solve_triangular(factor, flat, lower=True)
    return (ortho.reshape(vectors, tile_rows, tile_cols), factor.T)


def solution(mesh):
    return jax.shard_map(
        per_device,
        mesh=mesh,
        in_specs=(P("row", "col"), P(None, "row", "col"), P(None, "row", "col")),
        out_specs=(P(None, "row", "col"), P()),
        check_vma=False,
    )
```

profile of v0, /device:TPU:24, one launch (start us, length us, event | category | flops | bytes accessed | tf_op | source)
XLA Modules:
  0.0 286.8 jit_solution(13862747417356549333)
XLA Ops:
  0.6 0.8 pad_add_fusion.3
  1.4 3.4 %collective-permute-start = (s32[5,3,256]{2,1,0:T(4,128)S(1)}, s32[5,3,256]{2,1,0:T(4,128)S(1)}, u32[]{:S(2)}, u32[]{:S(2)}) collective-permute-start(s32[5,3,256]{2,1,0:T(4,128)S(1)} %get-tuple-element.32), channel_id=1, source_target_pairs={{0,16},{16,32},{32,48},{48,64},{64,80},{80,96},{96,112},{112,128},... | collective-permute-start | bytes 46088 | tf_op jit(solution)/shard_map/ppermute | solution.py:27
  4.8 4.6 %collective-permute-start.1 = (s32[5,3,256]{2,1,0:T(4,128)S(1)}, s32[5,3,256]{2,1,0:T(4,128)S(1)}, u32[]{:S(2)}, u32[]{:S(2)}) collective-permute-start(s32[5,3,256]{2,1,0:T(4,128)S(1)} %get-tuple-element.33), channel_id=1, source_target_pairs={{16,0},{32,16},{48,32},{64,48},{80,64},{96,80},{112,96},{128,112},... | collective-permute-start | bytes 46088 | tf_op jit(solution)/shard_map/ppermute | solution.py:29
  9.4 1.7 fusion.110
  11.1 2.7 collective-permute-start.5
  13.9 3.1 %collective-permute-start.4 = (f32[128,1,256]{2,0,1:T(8,128)S(1)}, f32[128,1,256]{2,0,1:T(8,128)S(1)}, u32[]{:S(2)}, u32[]{:S(2)}) collective-permute-start(f32[128,1,256]{2,0,1:T(8,128)S(1)} %copy.159), channel_id=1, source_target_pairs={{0,16},{16,32},{32,48},{48,64},{64,80},{80,96},{96,112},{112,128},... | collective-permute-start | bytes 393224 | tf_op jit(solution)/shard_map/ppermute | solution.py:27
  17.1 0.9 pad_add_fusion.1
  18.1 1.3 collective-permute-start.2
  19.4 1.3 collective-permute-start.3
  20.8 5.3 %copy.97 = f32[128,32,256]{0,2,1:T(8,128)} copy(f32[128,32,256]{2,1,0:T(8,128)} %param.6) | data formatting | bytes 8388608 | tf_op args[2]
  26.7 1.1 pad_maximum_fusion.5
  27.9 1.4 collective-permute-start.7
  29.4 5.8 %collective-permute-start.6 = (f32[128,34,1]{0,1,2:T(8,128)S(1)}, f32[128,34,1]{0,1,2:T(8,128)S(1)}, u32[]{:S(2)}, u32[]{:S(2)}) collective-permute-start(f32[128,34,1]{0,1,2:T(8,128)S(1)} %copy.93), channel_id=1, source_target_pairs={{0,1},{1,2},{2,3},{3,4},{4,5},{5,6},{6,7},{7,8},{8,9},{9,10},{10,1... | collective-permute-start | bytes 52232 | tf_op jit(solution)/shard_map/ppermute | solution.py:27
  36.4 2.2 maximum_multiply_fusion
  38.6 11.1 %fusion.11 = f32[128,32,256]{0,2,1:T(8,128)S(1)} fusion(f32[128,32,256]{0,2,1:T(8,128)S(1)} %copy-done.2, f32[128,34,258]{0,2,1:T(8,128)S(1)} %maximum_multiply_fusion, f32[32,256]{1,0:T(8,128)S(1)} %slice.346, f32[32,256]{1,0:T(8,128)S(1)} %slice.344, f32[32,256]{1,0:T(8,128)S(1)} %slice.342, f32[32,256]{1,0:T(8,128)S(1)} %slice.340, ...), kind=kLoop, calls=%fused_computation.22 | loop fusion | flops 17825792 | bytes 42237952 | tf_op jit(solution)/shard_map/sub | solution.py:90
  49.8 2.0 copy-done
  51.9 4.8 %collective-permute-start.9 = (f32[128,1,256]{2,0,1:T(8,128)S(1)}, f32[128,1,256]{2,0,1:T(8,128)S(1)}, u32[]{:S(2)}, u32[]{:S(2)}) collective-permute-start(f32[128,1,256]{2,0,1:T(8,128)S(1)} %copy.99), channel_id=1, source_target_pairs={{16,0},{32,16},{48,32},{64,48},{80,64},{96,80},{112,96},{128,112},... | collective-permute-start | bytes 393224 | tf_op jit(solution)/shard_map/ppermute | solution.py:29
  56.9 1.9 collective-permute-start.8
  58.8 1.1 collective-permute-done.9
  60.0 6.8 %collective-permute-done.8 = f32[128,1,256]{2,0,1:T(8,128)S(1)} collective-permute-done((f32[128,1,256]{2,0,1:T(8,128)S(1)}, f32[128,1,256]{2,0,1:T(8,128)S(1)}, u32[]{:S(2)}, u32[]{:S(2)}) %collective-permute-start.8) | collective-permute-done | bytes 131104 | tf_op jit(solution)/shard_map/ppermute | solution.py:27
  66.9 1.1 pad_maximum_fusion.2
  68.0 1.4 collective-permute-start.11
  69.5 3.0 %collective-permute-start.10 = (f32[128,34,1]{0,1,2:T(8,128)S(1)}, f32[128,34,1]{0,1,2:T(8,128)S(1)}, u32[]{:S(2)}, u32[]{:S(2)}) collective-permute-start(f32[128,34,1]{0,1,2:T(8,128)S(1)} %copy.102), channel_id=1, source_target_pairs={{0,1},{1,2},{2,3},{3,4},{4,5},{5,6},{6,7},{7,8},{8,9},{9,10},{10,1... | collective-permute-start | bytes 52232 | tf_op jit(solution)/shard_map/ppermute | solution.py:27
  72.5 0.8 collective-permute-done.10
  73.4 2.2 maximum_multiply_fusion.1
  75.6 11.3 %fusion.2 = f32[128,32,256]{0,2,1:T(8,128)S(1)} fusion(f32[128,32,256]{0,2,1:T(8,128)S(1)} %copy-done.1, f32[128,34,258]{0,2,1:T(8,128)S(1)} %maximum_multiply_fusion.1, f32[32,256]{1,0:T(8,128)S(1)} %slice.346, f32[32,256]{1,0:T(8,128)S(1)} %slice.344, f32[32,256]{1,0:T(8,128)S(1)} %slice.342, f32[32,256]{1,0:T(8,128)S(1)} %slice.340, ...), kind=kLoop, calls=%fused_computation.5 | loop fusion | flops 17825792 | bytes 42237952 | tf_op jit(solution)/shard_map/sub | solution.py:90
  86.9 2.0 copy-done.3
  88.9 6.9 %fusion.20 = f32[128,128]{0,1:T(8,128)S(1)} fusion(f32[128,32,256]{0,2,1:T(8,128)S(1)} %fusion.2), kind=kOutput, calls=%fused_computation.47 | convolution fusion | flops 1610629120 | bytes 4259840 | tf_op jit(solution)/shard_map/dot_general | solution.py:94
  95.9 11.7 %cholesky.149 = f32[128,128]{1,0:T(8,128)S(1)} custom-call(f32[128,128]{1,0:T(8,128)S(1)} %fusion.30), custom_call_target="Cholesky" | custom-call | tf_op jit(solution)/shard_map/jit(cholesky)/cholesky | solution.py:124
  107.6 0.6 compare_reduce_fusion.8
  108.3 0.7 select_select_fusion.8
  109.5 4.0 %collective-permute-done.12 = f32[128,128]{1,0:T(8,128)S(1)} collective-permute-done((f32[128,128]{1,0:T(8,128)S(1)}, f32[128,128]{1,0:T(8,128)S(1)}, u32[]{:S(2)}, u32[]{:S(2)}) %collective-permute-start.12) | collective-permute-done | bytes 65568 | tf_op jit(solution)/shard_map/ppermute | solution.py:43
  113.9 11.7 %cholesky.160 = f32[128,128]{1,0:T(8,128)S(1)} custom-call(f32[128,128]{1,0:T(8,128)S(1)} %fusion.29), custom_call_target="Cholesky" | custom-call | tf_op jit(solution)/shard_map/jit(cholesky)/cholesky | solution.py:127
  126.3 0.7 select_select_fusion.7
  127.3 5.7 %collective-permute-done.13 = f32[128,128]{1,0:T(8,128)S(1)} collective-permute-done((f32[128,128]{1,0:T(8,128)S(1)}, f32[128,128]{1,0:T(8,128)S(1)}, u32[]{:S(2)}, u32[]{:S(2)}) %collective-permute-start.13) | collective-permute-done | bytes 65568 | tf_op jit(solution)/shard_map/ppermute | solution.py:43
  133.4 11.7 %cholesky.171 = f32[128,128]{1,0:T(8,128)S(1)} custom-call(f32[128,128]{1,0:T(8,128)S(1)} %fusion.28), custom_call_target="Cholesky" | custom-call | tf_op jit(solution)/shard_map/jit(cholesky)/cholesky | solution.py:127
  145.8 0.7 select_select_fusion.6
  146.5 0.9 collective-permute-start.14
  147.7 3.6 %collective-permute-done.14 = f32[128,128]{1,0:T(8,128)S(1)} collective-permute-done((f32[128,128]{1,0:T(8,128)S(1)}, f32[128,128]{1,0:T(8,128)S(1)}, u32[]{:S(2)}, u32[]{:S(2)}) %collective-permute-start.14) | collective-permute-done | bytes 65568 | tf_op jit(solution)/shard_map/ppermute | solution.py:43
  151.6 11.7 %cholesky.182 = f32[128,128]{1,0:T(8,128)S(1)} custom-call(f32[128,128]{1,0:T(8,128)S(1)} %fusion.27), custom_call_target="Cholesky" | custom-call | tf_op jit(solution)/shard_map/jit(cholesky)/cholesky | solution.py:127
  164.0 0.7 select_select_fusion.5
  164.7 1.0 collective-permute-start.15
  166.0 4.6 %collective-permute-done.15 = f32[128,128]{1,0:T(8,128)S(1)} collective-permute-done((f32[128,128]{1,0:T(8,128)S(1)}, f32[128,128]{1,0:T(8,128)S(1)}, u32[]{:S(2)}, u32[]{:S(2)}) %collective-permute-start.15) | collective-permute-done | bytes 65568 | tf_op jit(solution)/shard_map/ppermute | solution.py:43
  170.9 11.7 %cholesky.193 = f32[128,128]{1,0:T(8,128)S(1)} custom-call(f32[128,128]{1,0:T(8,128)S(1)} %fusion.26), custom_call_target="Cholesky" | custom-call | tf_op jit(solution)/shard_map/jit(cholesky)/cholesky | solution.py:127
  183.3 0.7 select_select_fusion.4
  184.5 1.0 collective-permute-done.16
  185.9 11.7 %cholesky.204 = f32[128,128]{1,0:T(8,128)S(1)} custom-call(f32[128,128]{1,0:T(8,128)S(1)} %fusion.25), custom_call_target="Cholesky" | custom-call | tf_op jit(solution)/shard_map/jit(cholesky)/cholesky | solution.py:132
  198.3 0.7 select_select_fusion.3
  198.9 4.6 %collective-permute-start.17 = (f32[128,128]{1,0:T(8,128)S(1)}, f32[128,128]{1,0:T(8,128)S(1)}, u32[]{:S(2)}, u32[]{:S(2)}) collective-permute-start(f32[128,128]{1,0:T(8,128)S(1)} %select_select_fusion.3), channel_id=1, source_target_pairs={{0,2},{2,0},{1,3},{3,1},{4,6},{6,4},{5,7},{7,5},{8,10},{10,8},{9,1... | collective-permute-start | bytes 196616 | tf_op jit(solution)/shard_map/ppermute | solution.py:43
  203.8 2.2 collective-permute-done.17
  206.3 11.7 %cholesky.215 = f32[128,128]{1,0:T(8,128)S(1)} custom-call(f32[128,128]{1,0:T(8,128)S(1)} %fusion.24), custom_call_target="Cholesky" | custom-call | tf_op jit(solution)/shard_map/jit(cholesky)/cholesky | solution.py:132
  218.7 0.7 select_select_fusion.2
  219.4 3.9 %collective-permute-start.18 = (f32[128,128]{1,0:T(8,128)S(1)}, f32[128,128]{1,0:T(8,128)S(1)}, u32[]{:S(2)}, u32[]{:S(2)}) collective-permute-start(f32[128,128]{1,0:T(8,128)S(1)} %select_select_fusion.2), channel_id=1, source_target_pairs={{0,4},{4,0},{1,5},{5,1},{2,6},{6,2},{3,7},{7,3},{8,12},{12,8},{9,1... | collective-permute-start | bytes 196616 | tf_op jit(solution)/shard_map/ppermute | solution.py:43
  223.6 2.3 collective-permute-done.18
  226.3 11.7 %cholesky.226 = f32[128,128]{1,0:T(8,128)S(1)} custom-call(f32[128,128]{1,0:T(8,128)S(1)} %fusion.23), custom_call_target="Cholesky" | custom-call | tf_op jit(solution)/shard_map/jit(cholesky)/cholesky | solution.py:132
  238.6 0.7 select_select_fusion.1
  239.3 9.9 %collective-permute-start.19 = (f32[128,128]{1,0:T(8,128)S(1)}, f32[128,128]{1,0:T(8,128)S(1)}, u32[]{:S(2)}, u32[]{:S(2)}) collective-permute-start(f32[128,128]{1,0:T(8,128)S(1)} %select_select_fusion.1), channel_id=1, source_target_pairs={{0,8},{8,0},{1,9},{9,1},{2,10},{10,2},{3,11},{11,3},{4,12},{12,4},... | collective-permute-start | bytes 196616 | tf_op jit(solution)/shard_map/ppermute | solution.py:43
  249.5 2.7 collective-permute-done.19
  252.6 11.7 %cholesky.237 = f32[128,128]{1,0:T(8,128)S(1)} custom-call(f32[128,128]{1,0:T(8,128)S(1)} %fusion.22), custom_call_target="Cholesky" | custom-call | tf_op jit(solution)/shard_map/jit(cholesky)/cholesky | solution.py:132
  264.9 0.7 fusion.96
  265.6 0.7 copy.136
  266.3 9.8 %custom-call.6 = f32[1,128,128]{1,2,0:T(8,128)S(1)} custom-call(f32[1,128,128]{2,1,0:T(8,128)S(1)} %get-tuple-element.35), custom_call_target="InvertDiagBlocksLowerTriangular" | custom-call | tf_op jit(solution)/shard_map/jit(_solve_triangular)/triangular_solve | solution.py:135
  276.2 6.0 %fusion.18 = f32[128,32,256]{2,0,1:T(8,128)S(1)} fusion(f32[128,32,256]{0,2,1:T(8,128)} %copy-done.3, f32[1,128,128]{1,2,0:T(8,128)S(1)} %custom-call.6), kind=kOutput, calls=%fused_computation.36 | convolution fusion | flops 1610612736 | bytes 8454144 | tf_op jit(solution)/shard_map/jit(_solve_triangular)/triangular_solve | solution.py:135
  282.1 4.4 %copy.135 = f32[128,32,256]{2,1,0:T(8,128)} copy(f32[128,32,256]{2,0,1:T(8,128)S(1)} %fusion.18) | data formatting | bytes 8388608
  (109 shorter events, 13.7 us)
Async XLA Ops:
  1.4 15.6 %collective-permute-start = (s32[5,3,256]{2,1,0:T(4,128)S(1)}, s32[5,3,256]{2,1,0:T(4,128)S(1)}, u32[]{:S(2)}, u32[]{:S(2)}) collective-permute-start(s32[5,3,256]{2,1,0:T(4,128)S(1)} %get-tuple-element.32), channel_id=1, source_target_pairs={{0,16},{16,32},{32,48},{48,64},{64,80},{80,96},{96,112},{112,128},... | collective-permute-start | bytes 46088 | tf_op jit(solution)/shard_map/ppermute | solution.py:27
  4.8 12.2 %collective-permute-start.1 = (s32[5,3,256]{2,1,0:T(4,128)S(1)}, s32[5,3,256]{2,1,0:T(4,128)S(1)}, u32[]{:S(2)}, u32[]{:S(2)}) collective-permute-start(s32[5,3,256]{2,1,0:T(4,128)S(1)} %get-tuple-element.33), channel_id=1, source_target_pairs={{16,0},{32,16},{48,32},{64,48},{80,64},{96,80},{112,96},{128,112},... | collective-permute-start | bytes 46088 | tf_op jit(solution)/shard_map/ppermute | solution.py:29
  11.1 15.4 %collective-permute-start.5 = (f32[128,1,256]{2,0,1:T(8,128)S(1)}, f32[128,1,256]{2,0,1:T(8,128)S(1)}, u32[]{:S(2)}, u32[]{:S(2)}) collective-permute-start(f32[128,1,256]{2,0,1:T(8,128)S(1)} %copy.160), channel_id=1, source_target_pairs={{16,0},{32,16},{48,32},{64,48},{80,64},{96,80},{112,96},{128,112},... | collective-permute-start | bytes 393224 | tf_op jit(solution)/shard_map/ppermute | solution.py:29
  13.9 12.7 %collective-permute-start.4 = (f32[128,1,256]{2,0,1:T(8,128)S(1)}, f32[128,1,256]{2,0,1:T(8,128)S(1)}, u32[]{:S(2)}, u32[]{:S(2)}) collective-permute-start(f32[128,1,256]{2,0,1:T(8,128)S(1)} %copy.159), channel_id=1, source_target_pairs={{0,16},{16,32},{32,48},{48,64},{64,80},{80,96},{96,112},{112,128},... | collective-permute-start | bytes 393224 | tf_op jit(solution)/shard_map/ppermute | solution.py:27
  18.1 8.0 %collective-permute-start.2 = (s32[5,38,3]{2,1,0:T(8,128)S(1)}, s32[5,38,3]{2,1,0:T(8,128)S(1)}, u32[]{:S(2)}, u32[]{:S(2)}) collective-permute-start(s32[5,38,3]{2,1,0:T(8,128)S(1)} %get-tuple-element.30), channel_id=1, source_target_pairs={{0,1},{1,2},{2,3},{3,4},{4,5},{5,6},{6,7},{7,8},{8,9},{9,10},{10,1... | collective-permute-start | bytes 6848 | tf_op jit(solution)/shard_map/ppermute | solution.py:27
  19.4 6.7 %collective-permute-start.3 = (s32[5,38,3]{2,1,0:T(8,128)S(1)}, s32[5,38,3]{2,1,0:T(8,128)S(1)}, u32[]{:S(2)}, u32[]{:S(2)}) collective-permute-start(s32[5,38,3]{2,1,0:T(8,128)S(1)} %get-tuple-element.31), channel_id=1, source_target_pairs={{1,0},{2,1},{3,2},{4,3},{5,4},{6,5},{7,6},{8,7},{9,8},{10,9},{11,1... | collective-permute-start | bytes 6848 | tf_op jit(solution)/shard_map/ppermute | solution.py:29
  20.8 5.3 %copy-start.4 = (s32[4,32,256]{2,1,0:T(8,128)S(1)}, s32[4,32,256]{2,1,0:T(8,128)}, u32[]{:S(2)}) copy-start(s32[4,32,256]{2,1,0:T(8,128)} %param.5) | copy-start | bytes 393220
  20.8 5.4 %copy-start.5 = (s32[32,256]{1,0:T(8,128)S(1)}, s32[32,256]{1,0:T(8,128)}, u32[]{:S(2)}) copy-start(s32[32,256]{1,0:T(8,128)} %param.4) | copy-start | bytes 98308
  26.7 9.7 %copy-start.2 = (f32[128,32,256]{0,2,1:T(8,128)S(1)}, f32[128,32,256]{0,2,1:T(8,128)}, u32[]{:S(2)}) copy-start(f32[128,32,256]{0,2,1:T(8,128)} %copy.97) | copy-start | bytes 12582916
  27.9 8.4 %collective-permute-start.7 = (f32[128,34,1]{0,1,2:T(8,128)S(1)}, f32[128,34,1]{0,1,2:T(8,128)S(1)}, u32[]{:S(2)}, u32[]{:S(2)}) collective-permute-start(f32[128,34,1]{0,1,2:T(8,128)S(1)} %copy.94), channel_id=1, source_target_pairs={{1,0},{2,1},{3,2},{4,3},{5,4},{6,5},{7,6},{8,7},{9,8},{10,9},{11,1... | collective-permute-start | bytes 52232 | tf_op jit(solution)/shard_map/ppermute | solution.py:29
  29.4 7.0 %collective-permute-start.6 = (f32[128,34,1]{0,1,2:T(8,128)S(1)}, f32[128,34,1]{0,1,2:T(8,128)S(1)}, u32[]{:S(2)}, u32[]{:S(2)}) collective-permute-start(f32[128,34,1]{0,1,2:T(8,128)S(1)} %copy.93), channel_id=1, source_target_pairs={{0,1},{1,2},{2,3},{3,4},{4,5},{5,6},{6,7},{7,8},{8,9},{9,10},{10,1... | collective-permute-start | bytes 52232 | tf_op jit(solution)/shard_map/ppermute | solution.py:27
  49.8 2.0 copy-start
  51.9 8.0 %collective-permute-start.9 = (f32[128,1,256]{2,0,1:T(8,128)S(1)}, f32[128,1,256]{2,0,1:T(8,128)S(1)}, u32[]{:S(2)}, u32[]{:S(2)}) collective-permute-start(f32[128,1,256]{2,0,1:T(8,128)S(1)} %copy.99), channel_id=1, source_target_pairs={{16,0},{32,16},{48,32},{64,48},{80,64},{96,80},{112,96},{128,112},... | collective-permute-start | bytes 393224 | tf_op jit(solution)/shard_map/ppermute | solution.py:29
  56.9 9.9 %collective-permute-start.8 = (f32[128,1,256]{2,0,1:T(8,128)S(1)}, f32[128,1,256]{2,0,1:T(8,128)S(1)}, u32[]{:S(2)}, u32[]{:S(2)}) collective-permute-start(f32[128,1,256]{2,0,1:T(8,128)S(1)} %copy.98), channel_id=1, source_target_pairs={{0,16},{16,32},{32,48},{48,64},{64,80},{80,96},{96,112},{112,128},... | collective-permute-start | bytes 393224 | tf_op jit(solution)/shard_map/ppermute | solution.py:27
  66.8 6.5 %copy-start.1 = (f32[128,32,256]{0,2,1:T(8,128)S(1)}, f32[128,32,256]{0,2,1:T(8,128)}, u32[]{:S(2)}) copy-start(f32[128,32,256]{0,2,1:T(8,128)} %copy-done) | copy-start | bytes 12582916
  68.0 4.5 %collective-permute-start.11 = (f32[128,34,1]{0,1,2:T(8,128)S(1)}, f32[128,34,1]{0,1,2:T(8,128)S(1)}, u32[]{:S(2)}, u32[]{:S(2)}) collective-permute-start(f32[128,34,1]{0,1,2:T(8,128)S(1)} %copy.103), channel_id=1, source_target_pairs={{1,0},{2,1},{3,2},{4,3},{5,4},{6,5},{7,6},{8,7},{9,8},{10,9},{11,1... | collective-permute-start | bytes 52232 | tf_op jit(solution)/shard_map/ppermute | solution.py:29
  69.5 3.9 %collective-permute-start.10 = (f32[128,34,1]{0,1,2:T(8,128)S(1)}, f32[128,34,1]{0,1,2:T(8,128)S(1)}, u32[]{:S(2)}, u32[]{:S(2)}) collective-permute-start(f32[128,34,1]{0,1,2:T(8,128)S(1)} %copy.102), channel_id=1, source_target_pairs={{0,1},{1,2},{2,3},{3,4},{4,5},{5,6},{6,7},{7,8},{8,9},{9,10},{10,1... | collective-permute-start | bytes 52232 | tf_op jit(solution)/shard_map/ppermute | solution.py:27
  86.9 2.0 copy-start.3
  108.9 4.6 %collective-permute-start.12 = (f32[128,128]{1,0:T(8,128)S(1)}, f32[128,128]{1,0:T(8,128)S(1)}, u32[]{:S(2)}, u32[]{:S(2)}) collective-permute-start(f32[128,128]{1,0:T(8,128)S(1)} %select_select_fusion.8), channel_id=1, source_target_pairs={{0,16},{16,0},{32,48},{48,32},{64,80},{80,64},{96,112},{112,96},{1... | collective-permute-start | bytes 196616 | tf_op jit(solution)/shard_map/ppermute | solution.py:43
  126.9 6.1 %collective-permute-start.13 = (f32[128,128]{1,0:T(8,128)S(1)}, f32[128,128]{1,0:T(8,128)S(1)}, u32[]{:S(2)}, u32[]{:S(2)}) collective-permute-start(f32[128,128]{1,0:T(8,128)S(1)} %select_select_fusion.7), channel_id=1, source_target_pairs={{0,32},{32,0},{16,48},{48,16},{64,96},{96,64},{80,112},{112,80},{1... | collective-permute-start | bytes 196616 | tf_op jit(solution)/shard_map/ppermute | solution.py:43
  146.5 4.8 %collective-permute-start.14 = (f32[128,128]{1,0:T(8,128)S(1)}, f32[128,128]{1,0:T(8,128)S(1)}, u32[]{:S(2)}, u32[]{:S(2)}) collective-permute-start(f32[128,128]{1,0:T(8,128)S(1)} %select_select_fusion.6), channel_id=1, source_target_pairs={{0,64},{64,0},{16,80},{80,16},{32,96},{96,32},{48,112},{112,48},{1... | collective-permute-start | bytes 196616 | tf_op jit(solution)/shard_map/ppermute | solution.py:43
  164.7 5.9 %collective-permute-start.15 = (f32[128,128]{1,0:T(8,128)S(1)}, f32[128,128]{1,0:T(8,128)S(1)}, u32[]{:S(2)}, u32[]{:S(2)}) collective-permute-start(f32[128,128]{1,0:T(8,128)S(1)} %select_select_fusion.5), channel_id=1, source_target_pairs={{0,128},{128,0},{16,144},{144,16},{32,160},{160,32},{48,176},{176,... | collective-permute-start | bytes 196616 | tf_op jit(solution)/shard_map/ppermute | solution.py:43
  184.0 1.5 collective-permute-start.16
  198.9 7.0 %collective-permute-start.17 = (f32[128,128]{1,0:T(8,128)S(1)}, f32[128,128]{1,0:T(8,128)S(1)}, u32[]{:S(2)}, u32[]{:S(2)}) collective-permute-start(f32[128,128]{1,0:T(8,128)S(1)} %select_select_fusion.3), channel_id=1, source_target_pairs={{0,2},{2,0},{1,3},{3,1},{4,6},{6,4},{5,7},{7,5},{8,10},{10,8},{9,1... | collective-permute-start | bytes 196616 | tf_op jit(solution)/shard_map/ppermute | solution.py:43
  219.4 6.5 %collective-permute-start.18 = (f32[128,128]{1,0:T(8,128)S(1)}, f32[128,128]{1,0:T(8,128)S(1)}, u32[]{:S(2)}, u32[]{:S(2)}) collective-permute-start(f32[128,128]{1,0:T(8,128)S(1)} %select_select_fusion.2), channel_id=1, source_target_pairs={{0,4},{4,0},{1,5},{5,1},{2,6},{6,2},{3,7},{7,3},{8,12},{12,8},{9,1... | collective-permute-start | bytes 196616 | tf_op jit(solution)/shard_map/ppermute | solution.py:43
  239.3 12.9 %collective-permute-start.19 = (f32[128,128]{1,0:T(8,128)S(1)}, f32[128,128]{1,0:T(8,128)S(1)}, u32[]{:S(2)}, u32[]{:S(2)}) collective-permute-start(f32[128,128]{1,0:T(8,128)S(1)} %select_select_fusion.1), channel_id=1, source_target_pairs={{0,8},{8,0},{1,9},{9,1},{2,10},{10,2},{3,11},{11,3},{4,12},{12,4},... | collective-permute-start | bytes 196616 | tf_op jit(solution)/shard_map/ppermute | solution.py:43
where the time goes:
time: 292 us; the launch traced here: 287 us
  other arithmetic  159 us (54%)
  starting transfers between devices  55.9 us (19%)
  waiting for transfers between devices  34.6 us (12%)
  local copies, waits for them, and re-layouts  18.7 us (6%)
  matrix products  17.1 us (6%)
    another operation x24, other arithmetic, per_device(): jnp.linalg.cholesky(inner_products(factor, factor) + inner_products(partn...  99.1 us
    ppermute x8, waiting for transfers between devices, from_partner(): return lax.ppermute(block, axis, route)  26 us
    sub x2, other arithmetic, apply_once(): return shifted(values_in, 0, 0) - shifted(scales, 0, 0) * summed  22.5 us
    ppermute x8, starting transfers between devices, from_partner(): return lax.ppermute(block, axis, route)  21.1 us
    ppermute x6, starting transfers between devices, padded(): lax.ppermute(tail, axis, [(i, (i + 1) % count) for i in range(ends)])  18.6 us
    ppermute x6, starting transfers between devices, padded(): lax.ppermute(head, axis, [((i + 1) % count, i) for i in range(ends)])  16.3 us
    unnamed x17, local copies, waits for them, and re-layouts  14.6 us
    another operation x3, other arithmetic, per_device(): factor = jnp.linalg.cholesky(gram_local)  12.4 us
  transfers between devices with their start and end apart: 20, of which 11 were waited for; matrix products, arithmetic and copies ran while one was open for 4% of the time, Pallas kernels for 0%

commit v1 on v0

v1 whole, which is shorter than its diff:
```python
import jax
import jax.numpy as jnp
from jax import lax
from jax.sharding import PartitionSpec as P

INV_SIGMA = 1.0 / 40.0
NEIGHBOURS = (
    (0, 1, 0, 1, 1.0 / 9.0),
    (0, -1, 0, 0, 1.0 / 9.0),
    (1, 0, 1, 1, 1.0 / 9.0),
    (-1, 0, 1, 0, 1.0 / 9.0),
    (1, 1, 2, 1, 1.0 / 18.0),
    (-1, -1, 2, 0, 1.0 / 18.0),
    (1, -1, 3, 1, 1.0 / 18.0),
    (-1, 1, 3, 0, 1.0 / 18.0),
)
AXES = ("row", "col")


def from_neighbour(block, step_row, step_col):
    rows = lax.axis_size("row")
    cols = lax.axis_size("col")
    route = []
    for r in range(rows):
        for c in range(cols):
            tr, tc = r + step_row, c + step_col
            if 0 <= tr < rows and 0 <= tc < cols:
                route.append((r * cols + c, tr * cols + tc))
    return lax.ppermute(block, AXES, route)


def padded(cells, width):
    height = cells.shape[-2]
    span = cells.shape[-1]
    top = cells[..., :width, :]
    bottom = cells[..., height - width :, :]
    left = cells[..., :, :width]
    right = cells[..., :, span - width :]
    top_left = cells[..., :width, :width]
    top_right = cells[..., :width, span - width :]
    bottom_left = cells[..., height - width :, :width]
    bottom_right = cells[..., height - width :, span - width :]
    north = jnp.concatenate(
        [
            from_neighbour(bottom_right, 1, 1),
            from_neighbour(bottom, 1, 0),
            from_neighbour(bottom_left, 1, -1),
        ],
        axis=-1,
    )
    middle = jnp.concatenate(
        [from_neighbour(right, 0, 1), cells, from_neighbour(left, 0, -1)], axis=-1
    )
    south = jnp.concatenate(
        [
            from_neighbour(top_right, -1, 1),
            from_neighbour(top, -1, 0),
            from_neighbour(top_left, -1, -1),
        ],
        axis=-1,
    )
    return jnp.concatenate([north, middle, south], axis=-2)


def shifted(array, step_row, step_col):
    height = array.shape[-2]
    width = array.shape[-1]
    return array[..., 1 + step_row : height - 1 + step_row, 1 + step_col : width - 1 + step_col]


def cropped(array, cycle):
    return array[..., cycle:-cycle, cycle:-cycle]


def neighbour_weights(levels, counts, inside):
    center = shifted(levels, 0, 0)
    center_in = shifted(inside, 0, 0)
    result = []
    for step_row, step_col, channel, at_center, factor in NEIGHBOURS:
        other = shifted(levels, step_row, step_col)
        if at_center == 1:
            source = shifted(counts[channel], 0, 0)
        else:
            source = shifted(counts[channel], step_row, step_col)
        gap = (center - other) * INV_SIGMA
        result.append(
            (1.0 + source)
            * factor
            * jnp.exp(-gap * gap)
            * center_in
            * shifted(inside, step_row, step_col)
        )
    return result


def degree_scales(weights):
    degree = weights[0]
    for weight in weights[1:]:
        degree = degree + weight
    return lax.rsqrt(1.0 + degree)


def apply_once(values_in, weights, scales):
    lifted = values_in * scales
    summed = None
    for weight, entry in zip(weights, NEIGHBOURS):
        term = weight * shifted(lifted, entry[0], entry[1])
        summed = term if summed is None else summed + term
    return shifted(values_in, 0, 0) - shifted(scales, 0, 0) * summed


def per_device(intensity, agreement, basis_block):
    vectors, tile_rows, tile_cols = basis_block.shape
    row_count = lax.axis_size("row")
    col_count = lax.axis_size("col")
    total_rows = tile_rows * row_count
    total_cols = tile_cols * col_count
    labels = jnp.concatenate((intensity[None], agreement), axis=0)
    labels_wide = padded(labels, 3)
    extended = padded(basis_block, 2)
    row_ids = lax.axis_index("row") * tile_rows + jnp.arange(-3, tile_rows + 3, dtype=jnp.int32)
    col_ids = lax.axis_index("col") * tile_cols + jnp.arange(-3, tile_cols + 3, dtype=jnp.int32)
    row_in = ((row_ids >= 0) & (row_ids < total_rows)).astype(jnp.float32)
    col_in = ((col_ids >= 0) & (col_ids < total_cols)).astype(jnp.float32)
    inside = row_in[:, None] * col_in[None, :]
    levels = labels_wide[0].astype(jnp.float32)
    counts = labels_wide[1:].astype(jnp.float32)
    weights = neighbour_weights(levels, counts, inside)
    scales = degree_scales(weights)
    first = apply_once(extended, [cropped(w, 1) for w in weights], scales)
    filtered = apply_once(first, [cropped(w, 2) for w in weights], cropped(scales, 1))
    flat = filtered.reshape(vectors, tile_rows * tile_cols)
    pixel_total = float(total_rows * total_cols)
    gram_local = jnp.dot(
        flat, flat.T, precision=lax.Precision.HIGHEST, preferred_element_type=jnp.float32
    )
    gram = lax.psum(gram_local, AXES) / pixel_total
    factor = jnp.linalg.cholesky(gram)
    ortho = jax.scipy.linalg.solve_triangular(factor, flat, lower=True)
    return (ortho.reshape(vectors, tile_rows, tile_cols), factor.T)


def solution(mesh):
    return jax.shard_map(
        per_device,
        mesh=mesh,
        in_specs=(P("row", "col"), P(None, "row", "col"), P(None, "row", "col")),
        out_specs=(P(None, "row", "col"), P()),
        check_vma=False,
    )
```

time: 292 us -> 486 us (1.66)
  the two profiles are of different devices: /device:TPU:24 before, /device:TPU:1 now
where the time goes in v1:
time: 486 us; the launch traced here: 478 us
  waiting for transfers between devices  248 us (51%)
  other arithmetic  104 us (21%)
  local copies, waits for them, and re-layouts  50.2 us (10%)
  starting transfers between devices  46.2 us (10%)
  between operations  15 us (3%)
  matrix products  14.5 us (3%)
    psum x1, waiting for transfers between devices, per_device(): gram = lax.psum(gram_local, AXES) / pixel_total  239 us
    mul x2, other arithmetic, apply_once(): lifted = values_in * scales  46.7 us
    ppermute x16, starting transfers between devices, from_neighbour(): return lax.ppermute(block, AXES, route)  46.2 us
    unnamed x45, local copies, waits for them, and re-layouts  23.3 us
    sub x1, other arithmetic, apply_once(): return shifted(values_in, 0, 0) - shifted(scales, 0, 0) * summed  22.3 us
    another operation x3, other arithmetic, per_device(): factor = jnp.linalg.cholesky(gram)  12.4 us
    another operation x1, other arithmetic, per_device(): ortho = jax.scipy.linalg.solve_triangular(factor, flat, lower=True)  9.81 us
  transfers between devices with their start and end apart: 17, of which 4 were waited for; matrix products, arithmetic and copies ran while one was open for 10% of the time, Pallas kernels for 0%

profile of v1, /device:TPU:1, one launch (start us, length us, event | category | flops | bytes accessed | tf_op | source)
XLA Modules:
  0.0 478.2 jit_solution(1800400520753228515)
XLA Ops:
  7.2 1.5 pad_add_fusion.3
  8.7 6.4 %collective-permute-start.8 = (s32[5,3,3]{2,1,0:T(4,128)}, s32[5,3,3]{2,1,0:T(4,128)}, u32[]{:S(2)}, u32[]{:S(2)}) collective-permute-start(s32[5,3,3]{2,1,0:T(4,128)} %get-tuple-element.33), channel_id=1, source_target_pairs={{0,17},{1,18},{2,19},{3,20},{4,21},{5,22},{6,23},{7,24},{8,25},{9,... | collective-permute-start | bytes 548 | tf_op jit(solution)/shard_map/ppermute | solution.py:29
  15.1 1.4 pad_add_fusion
  16.5 2.5 collective-permute-start.9
  19.1 1.3 collective-permute-start.14
  20.4 1.6 fusion.23
  22.0 2.2 collective-permute-start.11
  24.2 2.1 collective-permute-start.12
  26.3 1.9 fusion.93
  28.2 1.7 fusion.94
  30.0 4.2 fusion.95
  34.7 0.7 broadcast_multiply_fusion.3
  35.4 0.7 copy.59
  36.1 0.7 copy.64
  36.8 1.3 collective-permute-start.13
  38.1 0.7 copy.61
  38.7 0.7 copy.66
  39.4 2.6 collective-permute-done.13
  42.0 1.3 collective-permute-start.15
  43.3 0.7 copy.65
  44.0 5.9 %collective-permute-done.15 = s32[5,3,3]{2,1,0:T(4,128)S(1)} collective-permute-done((s32[5,3,3]{2,1,0:T(4,128)}, s32[5,3,3]{2,1,0:T(4,128)S(1)}, u32[]{:S(2)}, u32[]{:S(2)}) %collective-permute-start.15) | collective-permute-done | bytes 212 | tf_op jit(solution)/shard_map/ppermute | solution.py:29
  49.9 1.3 collective-permute-start.10
  51.2 3.3 copy.62
  54.5 1.9 copy.63
  56.4 1.3 collective-permute-start.7
  57.7 1.3 collective-permute-start.5
  59.0 1.3 collective-permute-start.6
  60.3 7.3 %collective-permute-start.1 = (f32[128,2,256]{2,0,1:T(8,128)S(1)}, f32[128,2,256]{2,0,1:T(8,128)S(1)}, u32[]{:S(2)}, u32[]{:S(2)}) collective-permute-start(f32[128,2,256]{2,0,1:T(8,128)S(1)} %copy.60), channel_id=1, source_target_pairs={{0,16},{1,17},{2,18},{3,19},{4,20},{5,21},{6,22},{7,23},{8,24},{9,... | collective-permute-start | bytes 786440 | tf_op jit(solution)/shard_map/ppermute | solution.py:29
  67.7 5.0 %collective-permute-start.3 = (f32[128,32,2]{0,1,2:T(8,128)}, f32[128,32,2]{0,1,2:T(8,128)S(1)}, u32[]{:S(2)}, u32[]{:S(2)}) collective-permute-start(f32[128,32,2]{0,1,2:T(8,128)} %copy.62), channel_id=1, source_target_pairs={{0,1},{1,2},{2,3},{3,4},{4,5},{5,6},{6,7},{7,8},{8,9},{9,10},{10,1... | collective-permute-start | bytes 98312 | tf_op jit(solution)/shard_map/ppermute | solution.py:29
  72.7 1.0 add_add_fusion
  73.7 0.8 fusion.75
  74.6 1.9 collective-permute-start.4
  77.1 0.7 slice.413
  77.8 0.7 slice.417
  78.6 0.7 slice.419
  79.4 0.7 slice.421
  80.2 0.7 slice.423
  81.0 0.7 slice.425
  81.7 0.7 slice.427
  82.5 0.7 slice.412
  83.3 2.6 copy.40
  85.9 3.2 collective-permute-start.2
  89.1 3.6 copy.41
  92.7 6.5 %collective-permute-start = (f32[128,2,2]{2,0,1:T(8,128)}, f32[128,2,2]{2,0,1:T(8,128)S(1)}, u32[]{:S(2)}, u32[]{:S(2)}) collective-permute-start(f32[128,2,2]{2,0,1:T(8,128)} %copy.59), channel_id=1, source_target_pairs={{0,17},{1,18},{2,19},{3,20},{4,21},{5,22},{6,23},{7,24},{8,25},{9,... | collective-permute-start | bytes 6152 | tf_op jit(solution)/shard_map/ppermute | solution.py:29
  99.2 1.2 pad_maximum_fusion.2
  100.7 0.6 collective-permute-done
  101.3 1.1 pad_maximum_fusion.1
  102.7 9.1 %broadcast_multiply_fusion = (f32[128,36,260]{2,1,0:T(8,128)}, f32[128,36,260]{2,1,0:T(8,128)}) fusion(f32[36,260]{1,0:T(8,128)S(1)} %get-tuple-element.12, f32[128,2,260]{2,1,0:T(2,128)S(1)} %copy.46, f32[128,32,2]{2,1,0:T(8,128)S(1)} %copy-done.1, f32[128,32,256]{2,1,0:T(8,128)} %param.5, f32[128,32,2]{2,1,0:T(8,128)S(1)} %copy.40, f32[128,2,260]{2,1,0:T(2,128)S(1)} %copy.45), kind=kLoop, calls=%fused_computation.37 | loop fusion | flops 5990400 | bytes 14414400 | tf_op jit(solution)/shard_map/mul | solution.py:104
  111.9 37.6 %broadcast_multiply_fusion.1 = (f32[128,34,258]{2,1,0:T(8,128)}, f32[128,34,258]{2,1,0:T(8,128)}) fusion(f32[34,258]{1,0:T(8,128)S(1)} %slice.394, f32[128,36,260]{2,1,0:T(8,128)} %get-tuple-element.10, f32[34,258]{1,0:T(8,128)S(1)} %slice.409, f32[34,258]{1,0:T(8,128)S(1)} %slice.407, f32[34,258]{1,0:T(8,128)S(1)} %slice.405, f32[34,258]{1,0:T(8,128)S(1)} %slice.403, ...), kind=kLoop, calls=%fused_computation.38 | loop fusion | flops 20210688 | bytes 49719696 | tf_op jit(solution)/shard_map/mul | solution.py:104
  149.6 22.3 %fusion.11 = f32[128,32,256]{2,1,0:T(8,128)S(1)} fusion(f32[128,34,258]{2,1,0:T(8,128)} %get-tuple-element.8, f32[128,34,258]{2,1,0:T(8,128)} %get-tuple-element.9, f32[32,256]{1,0:T(8,128)S(1)} %copy-done.10, f32[32,256]{1,0:T(8,128)S(1)} %copy-done.9, f32[32,256]{1,0:T(8,128)S(1)} %copy-done.8, f32[32,256]{1,0:T(8,128)S(1)} %copy-done.7, ...), kind=kLoop, calls=%fused_computation.21 | loop fusion | flops 17825792 | bytes 42237952 | tf_op jit(solution)/shard_map/sub | solution.py:109
  171.9 2.0 copy-done
  173.9 8.6 %fusion.20 = f32[128,128]{0,1:T(8,128)} fusion(f32[128,32,256]{2,1,0:T(8,128)S(1)} %fusion.11), kind=kOutput, calls=%fused_computation.39 | convolution fusion | flops 1610612736 | bytes 4259840 | tf_op jit(solution)/shard_map/dot_general | solution.py:134
  182.5 7.5 %copy.67 = f32[16,8,32,256]{3,1,2,0:T(8,128)} copy(f32[16,8,32,256]{3,2,1,0:T(8,128)} %bitcast.32) | data formatting | bytes 8388608
  190.0 5.8 %copy.51 = f32[8192,128]{1,0:T(8,128)} copy(f32[8192,128]{0,1:T(8,128)} %bitcast.34) | data formatting | bytes 8388608 | tf_op jit(solution)/shard_map/jit(_solve_triangular)/triangular_solve | solution.py:139
  195.8 239.3 %all-reduce.2.cloned.1.call-done = f32[128,128]{0,1:T(8,128)} async-done(((f32[128,128]{0,1:T(8,128)}), f32[128,128]{0,1:T(8,128)}) %all-reduce.2.cloned.1.call-update) | async-done | bytes 65552 | tf_op jit(solution)/shard_map/psum | solution.py:137
  435.1 0.8 broadcast_multiply_fusion.2
  436.1 0.9 fusion.27
  436.9 11.7 %cholesky.16 = f32[128,128]{1,0:T(8,128)S(1)} custom-call(f32[128,128]{1,0:T(8,128)S(1)} %fusion.27), custom_call_target="Cholesky" | custom-call | tf_op jit(solution)/shard_map/jit(cholesky)/cholesky | solution.py:138
  448.7 0.6 compare_reduce_fusion
  449.3 0.7 fusion.77
  450.0 0.7 copy.54
  450.7 9.8 %custom-call.7 = f32[1,128,128]{1,2,0:T(8,128)S(1)} custom-call(f32[1,128,128]{2,1,0:T(8,128)S(1)} %get-tuple-element.42), custom_call_target="InvertDiagBlocksLowerTriangular" | custom-call | tf_op jit(solution)/shard_map/jit(_solve_triangular)/triangular_solve | solution.py:139
  460.5 6.0 %fusion.25 = f32[128,32,256]{2,0,1:T(8,128)S(1)} fusion(f32[32,256,128]{2,1,0:T(8,128)} %bitcast.33, f32[1,128,128]{1,2,0:T(8,128)S(1)} %custom-call.7), kind=kOutput, calls=%fused_computation.62 | convolution fusion | flops 1610612736 | bytes 8454144 | tf_op jit(solution)/shard_map/jit(_solve_triangular)/triangular_solve | solution.py:139
  466.5 4.4 copy.53
  (68 shorter events, 2.7 us)
Async XLA Ops:
  7.2 428.0 %all-reduce.2.cloned.1.call-start = ((), (), s32[]{:S(2)}) async-start(), calls=%async_computation | async-start | bytes 131072 | tf_op jit(solution)/shard_map/psum | solution.py:137
  8.7 28.1 %collective-permute-start.8 = (s32[5,3,3]{2,1,0:T(4,128)}, s32[5,3,3]{2,1,0:T(4,128)}, u32[]{:S(2)}, u32[]{:S(2)}) collective-permute-start(s32[5,3,3]{2,1,0:T(4,128)} %get-tuple-element.33), channel_id=1, source_target_pairs={{0,17},{1,18},{2,19},{3,20},{4,21},{5,22},{6,23},{7,24},{8,25},{9,... | collective-permute-start | bytes 548 | tf_op jit(solution)/shard_map/ppermute | solution.py:29
  16.5 43.8 %collective-permute-start.9 = (s32[5,3,256]{2,1,0:T(4,128)}, s32[5,3,256]{2,1,0:T(4,128)S(1)}, u32[]{:S(2)}, u32[]{:S(2)}) collective-permute-start(s32[5,3,256]{2,1,0:T(4,128)} %get-tuple-element.37), channel_id=1, source_target_pairs={{0,16},{1,17},{2,18},{3,19},{4,20},{5,21},{6,22},{7,23},{8,24},{9,... | collective-permute-start | bytes 46088 | tf_op jit(solution)/shard_map/ppermute | solution.py:29
  19.1 48.6 %collective-permute-start.14 = (s32[5,3,256]{2,1,0:T(4,128)}, s32[5,3,256]{2,1,0:T(4,128)}, u32[]{:S(2)}, u32[]{:S(2)}) collective-permute-start(s32[5,3,256]{2,1,0:T(4,128)} %get-tuple-element.38), channel_id=1, source_target_pairs={{16,0},{17,1},{18,2},{19,3},{20,4},{21,5},{22,6},{23,7},{24,8},{25... | collective-permute-start | bytes 46088 | tf_op jit(solution)/shard_map/ppermute | solution.py:29
  22.0 35.7 %collective-permute-start.11 = (s32[5,32,3]{2,1,0:T(8,128)}, s32[5,32,3]{2,1,0:T(8,128)S(1)}, u32[]{:S(2)}, u32[]{:S(2)}) collective-permute-start(s32[5,32,3]{2,1,0:T(8,128)} %get-tuple-element.39), channel_id=1, source_target_pairs={{0,1},{1,2},{2,3},{3,4},{4,5},{5,6},{6,7},{7,8},{8,9},{9,10},{10,1... | collective-permute-start | bytes 5768 | tf_op jit(solution)/shard_map/ppermute | solution.py:29
  24.2 34.9 %collective-permute-start.12 = (s32[5,32,3]{2,1,0:T(8,128)}, s32[5,32,3]{2,1,0:T(8,128)S(1)}, u32[]{:S(2)}, u32[]{:S(2)}) collective-permute-start(s32[5,32,3]{2,1,0:T(8,128)} %get-tuple-element.40), channel_id=1, source_target_pairs={{1,0},{2,1},{3,2},{4,3},{5,4},{6,5},{7,6},{8,7},{9,8},{10,9},{11,1... | collective-permute-start | bytes 5768 | tf_op jit(solution)/shard_map/ppermute | solution.py:29
  34.2 38.5 %copy-start.2 = (s32[4,32,256]{2,1,0:T(8,128)S(1)}, s32[4,32,256]{2,1,0:T(8,128)}, u32[]{:S(2)}) copy-start(s32[4,32,256]{2,1,0:T(8,128)} %param.4) | copy-start | bytes 393220
  34.2 38.5 %copy-start.3 = (s32[32,256]{1,0:T(8,128)S(1)}, s32[32,256]{1,0:T(8,128)}, u32[]{:S(2)}) copy-start(s32[32,256]{1,0:T(8,128)} %param.3) | copy-start | bytes 98308
  36.8 5.2 %collective-permute-start.13 = (s32[5,3,3]{2,1,0:T(4,128)}, s32[5,3,3]{2,1,0:T(4,128)S(1)}, u32[]{:S(2)}, u32[]{:S(2)}) collective-permute-start(s32[5,3,3]{2,1,0:T(4,128)} %get-tuple-element.34), channel_id=1, source_target_pairs={{16,1},{17,2},{18,3},{19,4},{20,5},{21,6},{22,7},{23,8},{24,9},{25... | collective-permute-start | bytes 548 | tf_op jit(solution)/shard_map/ppermute | solution.py:29
  42.0 1.3 copy-start.12
  42.0 8.0 %collective-permute-start.15 = (s32[5,3,3]{2,1,0:T(4,128)}, s32[5,3,3]{2,1,0:T(4,128)S(1)}, u32[]{:S(2)}, u32[]{:S(2)}) collective-permute-start(s32[5,3,3]{2,1,0:T(4,128)} %get-tuple-element.35), channel_id=1, source_target_pairs={{17,0},{18,1},{19,2},{20,3},{21,4},{22,5},{23,6},{24,7},{25,8},{26... | collective-permute-start | bytes 548 | tf_op jit(solution)/shard_map/ppermute | solution.py:29
  43.3 29.4 %copy-start.13 = (s32[5,3,3]{2,1,0:T(4,128)S(1)}, s32[5,3,3]{2,1,0:T(4,128)}, u32[]{:S(2)}) copy-start(s32[5,3,3]{2,1,0:T(4,128)} %copy-done.12) | copy-start | bytes 544
  49.9 9.1 %copy-start.14 = (s32[5,3,3]{2,1,0:T(4,128)}, s32[5,3,3]{2,1,0:T(4,128)S(1)}, u32[]{:S(2)}) copy-start(s32[5,3,3]{2,1,0:T(4,128)S(1)} %collective-permute-done.15) | copy-start | bytes 544
  49.9 6.5 %collective-permute-start.10 = (s32[5,3,3]{2,1,0:T(4,128)}, s32[5,3,3]{2,1,0:T(4,128)S(1)}, u32[]{:S(2)}, u32[]{:S(2)}) collective-permute-start(s32[5,3,3]{2,1,0:T(4,128)} %get-tuple-element.36), channel_id=1, source_target_pairs={{1,16},{2,17},{3,18},{4,19},{5,20},{6,21},{7,22},{8,23},{9,24},{10... | collective-permute-start | bytes 548 | tf_op jit(solution)/shard_map/ppermute | solution.py:29
  56.4 17.3 %copy-start.15 = (s32[5,3,3]{2,1,0:T(4,128)}, s32[5,3,3]{2,1,0:T(4,128)S(1)}, u32[]{:S(2)}) copy-start(s32[5,3,3]{2,1,0:T(4,128)S(1)} %collective-permute-done.10) | copy-start | bytes 544
  56.4 36.3 %collective-permute-start.7 = (f32[128,2,2]{2,0,1:T(8,128)}, f32[128,2,2]{2,0,1:T(8,128)}, u32[]{:S(2)}, u32[]{:S(2)}) collective-permute-start(f32[128,2,2]{2,0,1:T(8,128)} %copy.66), channel_id=1, source_target_pairs={{17,0},{18,1},{19,2},{20,3},{21,4},{22,5},{23,6},{24,7},{25,8},{26... | collective-permute-start | bytes 6152 | tf_op jit(solution)/shard_map/ppermute | solution.py:29
  57.7 41.5 %collective-permute-start.5 = (f32[128,2,2]{2,0,1:T(8,128)}, f32[128,2,2]{2,0,1:T(8,128)}, u32[]{:S(2)}, u32[]{:S(2)}) collective-permute-start(f32[128,2,2]{2,0,1:T(8,128)} %copy.64), channel_id=1, source_target_pairs={{16,1},{17,2},{18,3},{19,4},{20,5},{21,6},{22,7},{23,8},{24,9},{25... | collective-permute-start | bytes 6152 | tf_op jit(solution)/shard_map/ppermute | solution.py:29
  59.0 40.2 %collective-permute-start.6 = (f32[128,2,256]{2,0,1:T(8,128)}, f32[128,2,256]{2,0,1:T(8,128)S(1)}, u32[]{:S(2)}, u32[]{:S(2)}) collective-permute-start(f32[128,2,256]{2,0,1:T(8,128)} %copy.65), channel_id=1, source_target_pairs={{16,0},{17,1},{18,2},{19,3},{20,4},{21,5},{22,6},{23,7},{24,8},{25... | collective-permute-start | bytes 786440 | tf_op jit(solution)/shard_map/ppermute | solution.py:29
  60.3 41.0 %collective-permute-start.1 = (f32[128,2,256]{2,0,1:T(8,128)S(1)}, f32[128,2,256]{2,0,1:T(8,128)S(1)}, u32[]{:S(2)}, u32[]{:S(2)}) collective-permute-start(f32[128,2,256]{2,0,1:T(8,128)S(1)} %copy.60), channel_id=1, source_target_pairs={{0,16},{1,17},{2,18},{3,19},{4,20},{5,21},{6,22},{7,23},{8,24},{9,... | collective-permute-start | bytes 786440 | tf_op jit(solution)/shard_map/ppermute | solution.py:29
  67.7 6.9 %collective-permute-start.3 = (f32[128,32,2]{0,1,2:T(8,128)}, f32[128,32,2]{0,1,2:T(8,128)S(1)}, u32[]{:S(2)}, u32[]{:S(2)}) collective-permute-start(f32[128,32,2]{0,1,2:T(8,128)} %copy.62), channel_id=1, source_target_pairs={{0,1},{1,2},{2,3},{3,4},{4,5},{5,6},{6,7},{7,8},{8,9},{9,10},{10,1... | collective-permute-start | bytes 98312 | tf_op jit(solution)/shard_map/ppermute | solution.py:29
  74.6 1.9 copy-start.16
  74.6 11.3 %collective-permute-start.4 = (f32[128,32,2]{0,1,2:T(8,128)}, f32[128,32,2]{0,1,2:T(8,128)}, u32[]{:S(2)}, u32[]{:S(2)}) collective-permute-start(f32[128,32,2]{0,1,2:T(8,128)} %copy.63), channel_id=1, source_target_pairs={{1,0},{2,1},{3,2},{4,3},{5,4},{6,5},{7,6},{8,7},{9,8},{10,9},{11,1... | collective-permute-start | bytes 98312 | tf_op jit(solution)/shard_map/ppermute | solution.py:29
  85.9 14.8 %collective-permute-start.2 = (f32[128,2,2]{2,0,1:T(8,128)}, f32[128,2,2]{2,0,1:T(8,128)}, u32[]{:S(2)}, u32[]{:S(2)}) collective-permute-start(f32[128,2,2]{2,0,1:T(8,128)} %copy.61), channel_id=1, source_target_pairs={{1,16},{2,17},{3,18},{4,19},{5,20},{6,21},{7,22},{8,23},{9,24},{10... | collective-permute-start | bytes 6152 | tf_op jit(solution)/shard_map/ppermute | solution.py:29
  92.7 10.0 %copy-start.1 = (f32[128,32,2]{2,1,0:T(8,128)S(1)}, f32[128,32,2]{2,1,0:T(8,128)}, u32[]{:S(2)}) copy-start(f32[128,32,2]{2,1,0:T(8,128)} %copy.41) | copy-start | bytes 98308
  92.7 8.6 %collective-permute-start = (f32[128,2,2]{2,0,1:T(8,128)}, f32[128,2,2]{2,0,1:T(8,128)S(1)}, u32[]{:S(2)}, u32[]{:S(2)}) collective-permute-start(f32[128,2,2]{2,0,1:T(8,128)} %copy.59), channel_id=1, source_target_pairs={{0,17},{1,18},{2,19},{3,20},{4,21},{5,22},{6,23},{7,24},{8,25},{9,... | collective-permute-start | bytes 6152 | tf_op jit(solution)/shard_map/ppermute | solution.py:29
  111.9 37.7 %copy-start.4 = (f32[32,256]{1,0:T(8,128)S(1)}, f32[32,256]{1,0:T(8,128)}, u32[]{:S(2)}) copy-start(f32[32,256]{1,0:T(8,128)} %slice.413) | copy-start | bytes 98308
  111.9 37.7 %copy-start.5 = (f32[32,256]{1,0:T(8,128)S(1)}, f32[32,256]{1,0:T(8,128)}, u32[]{:S(2)}) copy-start(f32[32,256]{1,0:T(8,128)} %slice.417) | copy-start | bytes 98308
  111.9 37.7 %copy-start.6 = (f32[32,256]{1,0:T(8,128)S(1)}, f32[32,256]{1,0:T(8,128)}, u32[]{:S(2)}) copy-start(f32[32,256]{1,0:T(8,128)} %slice.419) | copy-start | bytes 98308
  111.9 37.7 %copy-start.7 = (f32[32,256]{1,0:T(8,128)S(1)}, f32[32,256]{1,0:T(8,128)}, u32[]{:S(2)}) copy-start(f32[32,256]{1,0:T(8,128)} %slice.421) | copy-start | bytes 98308
  111.9 37.7 %copy-start.8 = (f32[32,256]{1,0:T(8,128)S(1)}, f32[32,256]{1,0:T(8,128)}, u32[]{:S(2)}) copy-start(f32[32,256]{1,0:T(8,128)} %slice.423) | copy-start | bytes 98308
  111.9 37.7 %copy-start.9 = (f32[32,256]{1,0:T(8,128)S(1)}, f32[32,256]{1,0:T(8,128)}, u32[]{:S(2)}) copy-start(f32[32,256]{1,0:T(8,128)} %slice.425) | copy-start | bytes 98308
  111.9 37.7 %copy-start.10 = (f32[32,256]{1,0:T(8,128)S(1)}, f32[32,256]{1,0:T(8,128)}, u32[]{:S(2)}) copy-start(f32[32,256]{1,0:T(8,128)} %slice.427) | copy-start | bytes 98308
  111.9 37.7 %copy-start.11 = (f32[32,256]{1,0:T(8,128)S(1)}, f32[32,256]{1,0:T(8,128)}, u32[]{:S(2)}) copy-start(f32[32,256]{1,0:T(8,128)} %slice.412) | copy-start | bytes 98308
  171.9 2.0 copy-start
Sparse Core Ops, SparseCore 0:
  182.7 252.4 all-reduce.1

commit v2 on v0

--- a/solution.py
+++ b/solution.py
@@ -31,16 +31,6 @@
             axis=dim,
         )
     return cells
-
-
-def from_partner(block, axis, stride):
-    count = lax.axis_size(axis)
-    route = []
-    for low in range(count):
-        high = low | 1 << stride
-        if high != low and high < count:
-            route += [(low, high), (high, low)]
-    return lax.ppermute(block, axis, route)
 
 
 def shifted(array, step_row, step_col):
@@ -90,10 +80,29 @@
     return shifted(values_in, 0, 0) - shifted(scales, 0, 0) * summed
 
 
-def inner_products(first_mat, second_mat):
-    return jnp.dot(
-        first_mat, second_mat.T, precision=lax.Precision.HIGHEST, preferred_element_type=jnp.float32
-    )
+def exchange_sum(block, axis, low_bit, bits):
+    count = lax.axis_size(axis)
+    received = [block]
+    for offset in range(1, 1 << bits):
+        flip = offset << low_bit
+        route = [(i, i ^ flip) for i in range(count)]
+        received.append(lax.ppermute(block, axis, route))
+    while len(received) > 1:
+        received = [received[i] + received[i + 1] for i in range(0, len(received), 2)]
+    return received[0]
+
+
+def all_sum(block, axis):
+    count = lax.axis_size(axis)
+    levels = count.bit_length() - 1
+    if (1 << levels) != count:
+        return lax.psum(block, axis)
+    low_bit = 0
+    while low_bit < levels:
+        bits = min(2, levels - low_bit)
+        block = exchange_sum(block, axis, low_bit, bits)
+        low_bit += bits
+    return block
 
 
 def per_device(intensity, agreement, basis_block):
@@ -118,22 +127,21 @@
     for repeat in range(2):
         extended = padded(filtered, (("row", 1), ("col", 2)), 1)
         filtered = apply_once(extended, cycle_zero, cropped(scales, 1))
-    flat = filtered.reshape(vectors, tile_rows * tile_cols)
     pixel_total = float(total_rows * total_cols)
-    gram_local = inner_products(flat, flat) / pixel_total
-    factor = jnp.linalg.cholesky(gram_local)
-    for bit_no in range(row_count.bit_length() - 1):
-        partner = from_partner(factor, "row", bit_no)
-        factor = jnp.linalg.cholesky(
-            inner_products(factor, factor) + inner_products(partner, partner)
-        )
-    for bit_no in range(col_count.bit_length() - 1):
-        partner = from_partner(factor, "col", bit_no)
-        factor = jnp.linalg.cholesky(
-            inner_products(factor, factor) + inner_products(partner, partner)
-        )
-    ortho = jax.scipy.linalg.solve_triangular(factor, flat, lower=True)
-    return (ortho.reshape(vectors, tile_rows, tile_cols), factor.T)
+    gram_local = jnp.einsum(
+        "krc,jrc->kj", filtered, filtered,
+        precision=lax.Precision.HIGHEST, preferred_element_type=jnp.float32,
+    )
+    gram = all_sum(all_sum(gram_local, "col"), "row") / pixel_total
+    factor = jnp.linalg.cholesky(gram)
+    inverse = jax.scipy.linalg.solve_triangular(
+        factor, jnp.eye(vectors, dtype=jnp.float32), lower=True
+    )
+    ortho = jnp.einsum(
+        "kj,jrc->krc", inverse, filtered,
+        precision=lax.Precision.HIGHEST, preferred_element_type=jnp.float32,
+    )
+    return (ortho, factor.T)
 
 
 def solution(mesh):

time: 292 us -> 181 us (0.62)
  the two profiles are of different devices: /device:TPU:24 before, /device:TPU:2 now
where the time goes in v2:
time: 181 us; the launch traced here: 180 us
  starting transfers between devices  61.4 us (34%)
  other arithmetic  58.4 us (32%)
  waiting for transfers between devices  26.1 us (14%)
  local copies, waits for them, and re-layouts  17.6 us (10%)
  matrix products  15.2 us (8%)
    ppermute x12, starting transfers between devices, exchange_sum(): received.append(lax.ppermute(block, axis, route))  30 us
    sub x2, other arithmetic, apply_once(): return shifted(values_in, 0, 0) - shifted(scales, 0, 0) * summed  23.2 us
    ppermute x6, starting transfers between devices, padded(): lax.ppermute(tail, axis, [(i, (i + 1) % count) for i in range(ends)])  21 us
    ppermute x12, waiting for transfers between devices, exchange_sum(): received.append(lax.ppermute(block, axis, route))  18.5 us
    unnamed x17, local copies, waits for them, and re-layouts  13.2 us
    another operation x3, other arithmetic, per_device(): factor = jnp.linalg.cholesky(gram)  12.4 us
    ppermute x6, starting transfers between devices, padded(): lax.ppermute(head, axis, [((i + 1) % count, i) for i in range(ends)])  10.3 us
    another operation x1, other arithmetic, per_device(): jax.scipy.linalg.solve_triangular(factor, jnp.eye(vectors, dtype=jnp.floa...  9.81 us
  transfers between devices with their start and end apart: 24, of which 13 were waited for; matrix products, arithmetic and copies ran while one was open for 6% of the time, Pallas kernels for 0%

profile of v2, /device:TPU:2, one launch (start us, length us, event | category | flops | bytes accessed | tf_op | source)
XLA Modules:
  0.0 180.0 jit_solution(12117555303939043483)
XLA Ops:
  0.6 0.8 pad_add_fusion.3
  1.4 3.4 %collective-permute-start = (s32[5,3,256]{2,1,0:T(4,128)S(1)}, s32[5,3,256]{2,1,0:T(4,128)S(1)}, u32[]{:S(2)}, u32[]{:S(2)}) collective-permute-start(s32[5,3,256]{2,1,0:T(4,128)S(1)} %get-tuple-element.29), channel_id=1, source_target_pairs={{0,16},{16,32},{32,48},{48,64},{64,80},{80,96},{96,112},{112,128},... | collective-permute-start | bytes 46088 | tf_op jit(solution)/shard_map/ppermute | solution.py:27
  4.8 2.4 %collective-permute-start.1 = (s32[5,3,256]{2,1,0:T(4,128)S(1)}, s32[5,3,256]{2,1,0:T(4,128)S(1)}, u32[]{:S(2)}, u32[]{:S(2)}) collective-permute-start(s32[5,3,256]{2,1,0:T(4,128)S(1)} %get-tuple-element.30), channel_id=1, source_target_pairs={{16,0},{32,16},{48,32},{64,48},{80,64},{96,80},{112,96},{128,112},... | collective-permute-start | bytes 46088 | tf_op jit(solution)/shard_map/ppermute | solution.py:29
  7.3 1.7 fusion.85
  9.0 1.9 %collective-permute-start.5 = (f32[128,1,256]{2,0,1:T(8,128)S(1)}, f32[128,1,256]{2,0,1:T(8,128)S(1)}, u32[]{:S(2)}, u32[]{:S(2)}) collective-permute-start(f32[128,1,256]{2,0,1:T(8,128)S(1)} %copy.53), channel_id=1, source_target_pairs={{16,0},{32,16},{48,32},{64,48},{80,64},{96,80},{112,96},{128,112},... | collective-permute-start | bytes 393224 | tf_op jit(solution)/shard_map/ppermute | solution.py:29
  11.0 3.9 %collective-permute-start.4 = (f32[128,1,256]{2,0,1:T(8,128)S(1)}, f32[128,1,256]{2,0,1:T(8,128)S(1)}, u32[]{:S(2)}, u32[]{:S(2)}) collective-permute-start(f32[128,1,256]{2,0,1:T(8,128)S(1)} %copy.52), channel_id=1, source_target_pairs={{0,16},{16,32},{32,48},{48,64},{64,80},{80,96},{96,112},{112,128},... | collective-permute-start | bytes 393224 | tf_op jit(solution)/shard_map/ppermute | solution.py:27
  15.0 0.9 pad_add_fusion.1
  16.0 1.3 collective-permute-start.2
  17.3 1.3 collective-permute-start.3
  18.7 5.9 %copy.30 = f32[128,32,256]{0,1,2:T(8,128)} copy(f32[128,32,256]{2,1,0:T(8,128)} %param.5) | data formatting | bytes 8388608 | tf_op args[2]
  24.6 0.2 pad_add_fusion
  25.2 0.8 pad_maximum_fusion.5
  26.0 5.2 %collective-permute-start.6 = (f32[128,34,1]{0,1,2:T(8,128)S(1)}, f32[128,34,1]{0,1,2:T(8,128)S(1)}, u32[]{:S(2)}, u32[]{:S(2)}) collective-permute-start(f32[128,34,1]{0,1,2:T(8,128)S(1)} %get-tuple-element.17), channel_id=1, source_target_pairs={{0,1},{1,2},{2,3},{3,4},{4,5},{5,6},{6,7},{7,8},{8,9},{9,10},{10,1... | collective-permute-start | bytes 52232 | tf_op jit(solution)/shard_map/ppermute | solution.py:27
  31.2 1.3 collective-permute-start.7
  32.5 0.4 add_rsqrt_fusion
  33.6 0.1 copy.22
  33.7 0.1 copy.15
  33.8 0.1 copy.29
  33.9 0.1 copy.28
  34.2 0.1 copy.25
  34.5 0.1 copy.23
  34.7 0.8 collective-permute-done.7
  35.5 5.5 %maximum_multiply_fusion = f32[128,34,258]{0,1,2:T(8,128)S(1)} fusion(f32[128,34,1]{0,1,2:T(8,128)S(1)} %collective-permute-done.7, f32[128,1,256]{0,1,2:T(1,128)S(1)} %copy.21, f32[128,32,256]{0,1,2:T(8,128)} %copy.30, f32[128,1,256]{0,1,2:T(1,128)S(1)} %copy.19, f32[128,34,1]{0,1,2:T(8,128)S(1)} %collective-permute-done.6, f32[34,258]{0,1:T(8,128)S(1)} %copy.22), kind=kLoop, calls=%fused_computation | loop fusion | flops 5614080 | bytes 9017616 | tf_op jit(solution)/shard_map/mul | solution.py:75
  41.0 11.6 %fusion.11 = f32[128,32,256]{0,1,2:T(8,128)S(1)} fusion(f32[128,32,256]{0,1,2:T(8,128)S(1)} %copy-done.3, f32[128,34,258]{0,1,2:T(8,128)S(1)} %maximum_multiply_fusion, f32[32,256]{0,1:T(8,128)S(1)} %copy.29, f32[32,256]{0,1:T(8,128)S(1)} %copy.28, f32[32,256]{0,1:T(8,128)S(1)} %copy.27, f32[32,256]{0,1:T(8,128)S(1)} %copy.26, f32[32,256]{0,1:T(8,128)S(1)} %copy.25, ...), kind=kLoop, calls=%fused_computation.22 | loop fusion | flops 17825792 | bytes 42237952 | tf_op jit(solution)/shard_map/sub | solution.py:80
  52.6 2.0 %copy-done = f32[128,32,256]{0,1,2:T(8,128)} copy-done((f32[128,32,256]{0,1,2:T(8,128)}, f32[128,32,256]{0,1,2:T(8,128)S(1)}, u32[]{:S(2)}) %copy-start) | copy-done | bytes 4194328
  54.6 0.2 fusion.84
  54.9 1.9 %collective-permute-start.9 = (f32[128,1,256]{2,0,1:T(8,128)S(1)}, f32[128,1,256]{2,0,1:T(8,128)S(1)}, u32[]{:S(2)}, u32[]{:S(2)}) collective-permute-start(f32[128,1,256]{2,0,1:T(8,128)S(1)} %copy.32), channel_id=1, source_target_pairs={{16,0},{32,16},{48,32},{64,48},{80,64},{96,80},{112,96},{128,112},... | collective-permute-start | bytes 393224 | tf_op jit(solution)/shard_map/ppermute | solution.py:29
  57.0 3.9 %collective-permute-start.8 = (f32[128,1,256]{2,0,1:T(8,128)S(1)}, f32[128,1,256]{2,0,1:T(8,128)S(1)}, u32[]{:S(2)}, u32[]{:S(2)}) collective-permute-start(f32[128,1,256]{2,0,1:T(8,128)S(1)} %copy.31), channel_id=1, source_target_pairs={{0,16},{16,32},{32,48},{48,64},{64,80},{80,96},{96,112},{112,128},... | collective-permute-start | bytes 393224 | tf_op jit(solution)/shard_map/ppermute | solution.py:27
  60.9 0.9 collective-permute-done.9
  61.9 1.9 %collective-permute-done.8 = f32[128,1,256]{2,0,1:T(8,128)S(1)} collective-permute-done((f32[128,1,256]{2,0,1:T(8,128)S(1)}, f32[128,1,256]{2,0,1:T(8,128)S(1)}, u32[]{:S(2)}, u32[]{:S(2)}) %collective-permute-start.8) | collective-permute-done | bytes 131104 | tf_op jit(solution)/shard_map/ppermute | solution.py:27
  63.9 0.9 pad_maximum_fusion.2
  64.8 3.3 %collective-permute-start.10 = (f32[128,34,1]{0,1,2:T(8,128)S(1)}, f32[128,34,1]{0,1,2:T(8,128)S(1)}, u32[]{:S(2)}, u32[]{:S(2)}) collective-permute-start(f32[128,34,1]{0,1,2:T(8,128)S(1)} %get-tuple-element.15), channel_id=1, source_target_pairs={{0,1},{1,2},{2,3},{3,4},{4,5},{5,6},{6,7},{7,8},{8,9},{9,10},{10,1... | collective-permute-start | bytes 52232 | tf_op jit(solution)/shard_map/ppermute | solution.py:27
  68.1 1.5 collective-permute-start.11
  69.6 3.9 %collective-permute-done.11 = f32[128,34,1]{0,1,2:T(8,128)S(1)} collective-permute-done((f32[128,34,1]{0,1,2:T(8,128)S(1)}, f32[128,34,1]{0,1,2:T(8,128)S(1)}, u32[]{:S(2)}, u32[]{:S(2)}) %collective-permute-start.11) | collective-permute-done | bytes 17440 | tf_op jit(solution)/shard_map/ppermute | solution.py:29
  73.5 2.5 %maximum_multiply_fusion.1 = f32[128,34,258]{0,1,2:T(8,128)S(1)} fusion(f32[128,34,1]{0,1,2:T(8,128)S(1)} %collective-permute-done.11, f32[128,1,256]{0,1,2:T(1,128)S(1)} %copy.34, f32[128,32,256]{0,1,2:T(8,128)S(1)} %copy-done.1, f32[128,1,256]{0,1,2:T(1,128)S(1)} %copy.33, f32[128,34,1]{0,1,2:T(8,128)S(1)} %collective-permute-done.10, f32[34,258]{0,1:T(8,128)S(1)} %copy.22), kind=kLoop, calls=%fused_computation.1 | loop fusion | flops 5614080 | bytes 9017616 | tf_op jit(solution)/shard_map/mul | solution.py:75
  76.1 11.6 %fusion.2 = f32[128,32,256]{0,1,2:T(8,128)S(1)} fusion(f32[128,32,256]{0,1,2:T(8,128)S(1)} %copy-done.1, f32[128,34,258]{0,1,2:T(8,128)S(1)} %maximum_multiply_fusion.1, f32[32,256]{0,1:T(8,128)S(1)} %copy.29, f32[32,256]{0,1:T(8,128)S(1)} %copy.28, f32[32,256]{0,1:T(8,128)S(1)} %copy.27, f32[32,256]{0,1:T(8,128)S(1)} %copy.26, f32[32,256]{0,1:T(8,128)S(1)} %copy.25, ...), kind=kLoop, calls=%fused_computation.5 | loop fusion | flops 17825792 | bytes 42237952 | tf_op jit(solution)/shard_map/sub | solution.py:80
  87.7 7.0 %convolution_bitcast_fusion.1 = f32[128,128]{0,1:T(8,128)S(1)} fusion(f32[128,32,256]{0,1,2:T(8,128)S(1)} %fusion.2), kind=kOutput, calls=%fused_computation.39 | convolution fusion | flops 1610612736 | bytes 4259840 | tf_op jit(solution)/shard_map/krc,jrc->kj/dot_general | solution.py:131
  94.7 2.5 %collective-permute-start.13 = (f32[128,128]{0,1:T(8,128)S(1)}, f32[128,128]{0,1:T(8,128)S(1)}, u32[]{:S(2)}, u32[]{:S(2)}) collective-permute-start(f32[128,128]{0,1:T(8,128)S(1)} %convolution_bitcast_fusion.1), channel_id=1, source_target_pairs={{0,2},{1,3},{2,0},{3,1},{4,6},{5,7},{6,4},{7,5},{8,10},{9,11},{10,... | collective-permute-start | bytes 196616 | tf_op jit(solution)/shard_map/ppermute | solution.py:89
  97.2 1.7 collective-permute-start.12
  99.0 0.4 collective-permute-done.13
  99.5 0.4 collective-permute-done.12
  99.8 3.3 %collective-permute-done.14 = f32[128,128]{0,1:T(8,128)S(1)} collective-permute-done((f32[128,128]{0,1:T(8,128)S(1)}, f32[128,128]{0,1:T(8,128)S(1)}, u32[]{:S(2)}, u32[]{:S(2)}) %collective-permute-start.14) | collective-permute-done | bytes 65568 | tf_op jit(solution)/shard_map/ppermute | solution.py:89
  103.2 3.3 %collective-permute-start.17 = (f32[128,128]{0,1:T(8,128)S(1)}, f32[128,128]{0,1:T(8,128)S(1)}, u32[]{:S(2)}, u32[]{:S(2)}) collective-permute-start(f32[128,128]{0,1:T(8,128)S(1)} %add_add_fusion.2), channel_id=1, source_target_pairs={{0,12},{1,13},{2,14},{3,15},{4,8},{5,9},{6,10},{7,11},{8,4},{9,5},... | collective-permute-start | bytes 196616 | tf_op jit(solution)/shard_map/ppermute | solution.py:89
  106.5 7.4 %collective-permute-start.16 = (f32[128,128]{0,1:T(8,128)S(1)}, f32[128,128]{0,1:T(8,128)S(1)}, u32[]{:S(2)}, u32[]{:S(2)}) collective-permute-start(f32[128,128]{0,1:T(8,128)S(1)} %add_add_fusion.2), channel_id=1, source_target_pairs={{0,8},{1,9},{2,10},{3,11},{4,12},{5,13},{6,14},{7,15},{8,0},{9,1},... | collective-permute-start | bytes 196616 | tf_op jit(solution)/shard_map/ppermute | solution.py:89
  113.9 3.5 %collective-permute-done.16 = f32[128,128]{0,1:T(8,128)S(1)} collective-permute-done((f32[128,128]{0,1:T(8,128)S(1)}, f32[128,128]{0,1:T(8,128)S(1)}, u32[]{:S(2)}, u32[]{:S(2)}) %collective-permute-start.16) | collective-permute-done | bytes 65568 | tf_op jit(solution)/shard_map/ppermute | solution.py:89
  117.4 2.9 %collective-permute-done.15 = f32[128,128]{0,1:T(8,128)S(1)} collective-permute-done((f32[128,128]{0,1:T(8,128)S(1)}, f32[128,128]{0,1:T(8,128)S(1)}, u32[]{:S(2)}, u32[]{:S(2)}) %collective-permute-start.15) | collective-permute-done | bytes 65568 | tf_op jit(solution)/shard_map/ppermute | solution.py:89
  120.3 2.4 %collective-permute-start.20 = (f32[128,128]{0,1:T(8,128)S(1)}, f32[128,128]{0,1:T(8,128)S(1)}, u32[]{:S(2)}, u32[]{:S(2)}) collective-permute-start(f32[128,128]{0,1:T(8,128)S(1)} %add_add_fusion.1), channel_id=1, source_target_pairs={{0,48},{16,32},{32,16},{48,0},{64,112},{80,96},{96,80},{112,64},{1... | collective-permute-start | bytes 196616 | tf_op jit(solution)/shard_map/ppermute | solution.py:89
  122.8 3.7 %collective-permute-start.19 = (f32[128,128]{0,1:T(8,128)S(1)}, f32[128,128]{0,1:T(8,128)S(1)}, u32[]{:S(2)}, u32[]{:S(2)}) collective-permute-start(f32[128,128]{0,1:T(8,128)S(1)} %add_add_fusion.1), channel_id=1, source_target_pairs={{0,32},{16,48},{32,0},{48,16},{64,96},{80,112},{96,64},{112,80},{1... | collective-permute-start | bytes 196616 | tf_op jit(solution)/shard_map/ppermute | solution.py:89
  126.4 1.1 collective-permute-start.18
  127.5 1.2 collective-permute-done.19
  128.7 2.0 %collective-permute-done.18 = f32[128,128]{0,1:T(8,128)S(1)} collective-permute-done((f32[128,128]{0,1:T(8,128)S(1)}, f32[128,128]{0,1:T(8,128)S(1)}, u32[]{:S(2)}, u32[]{:S(2)}) %collective-permute-start.18) | collective-permute-done | bytes 65568 | tf_op jit(solution)/shard_map/ppermute | solution.py:89
  130.7 6.8 %collective-permute-start.23 = (f32[128,128]{0,1:T(8,128)S(1)}, f32[128,128]{0,1:T(8,128)S(1)}, u32[]{:S(2)}, u32[]{:S(2)}) collective-permute-start(f32[128,128]{0,1:T(8,128)S(1)} %add_add_fusion), channel_id=1, source_target_pairs={{0,192},{16,208},{32,224},{48,240},{64,128},{80,144},{96,160},{112... | collective-permute-start | bytes 196616 | tf_op jit(solution)/shard_map/ppermute | solution.py:89
  137.6 0.3 collective-permute-start.22
  137.9 0.6 collective-permute-start.21
  138.5 2.0 %collective-permute-done.23 = f32[128,128]{0,1:T(8,128)S(1)} collective-permute-done((f32[128,128]{0,1:T(8,128)S(1)}, f32[128,128]{0,1:T(8,128)S(1)}, u32[]{:S(2)}, u32[]{:S(2)}) %collective-permute-start.23) | collective-permute-done | bytes 65568 | tf_op jit(solution)/shard_map/ppermute | solution.py:89
  140.5 2.8 %collective-permute-done.22 = f32[128,128]{0,1:T(8,128)S(1)} collective-permute-done((f32[128,128]{0,1:T(8,128)S(1)}, f32[128,128]{0,1:T(8,128)S(1)}, u32[]{:S(2)}, u32[]{:S(2)}) %collective-permute-start.22) | collective-permute-done | bytes 65568 | tf_op jit(solution)/shard_map/ppermute | solution.py:89
  143.5 11.7 %cholesky.17 = f32[128,128]{1,0:T(8,128)S(1)} custom-call(f32[128,128]{1,0:T(8,128)S(1)} %fusion.21), custom_call_target="Cholesky" | custom-call | tf_op jit(solution)/shard_map/jit(cholesky)/cholesky | solution.py:136
  155.2 0.6 compare_reduce_fusion
  155.9 0.7 fusion.71
  156.5 0.7 copy.44
  157.3 9.8 %custom-call.7 = f32[1,128,128]{1,2,0:T(8,128)S(1)} custom-call(f32[1,128,128]{2,1,0:T(8,128)S(1)} %get-tuple-element.32), custom_call_target="InvertDiagBlocksLowerTriangular" | custom-call | tf_op jit(solution)/shard_map/jit(_solve_triangular)/triangular_solve | solution.py:137
  167.1 0.2 convolution_bitcast_fusion
  167.3 8.0 %fusion.18 = f32[128,32,256]{2,0,1:T(8,128)S(1)} fusion(f32[128,128,1]{1,0,2:T(8,128)S(1)} %convolution_bitcast_fusion, f32[128,32,256]{0,1,2:T(8,128)} %copy-done.2), kind=kOutput, calls=%fused_computation.36 | convolution fusion | flops 1610612736 | bytes 8454144 | tf_op jit(solution)/shard_map/kj,jrc->krc/dot_general | solution.py:140
  175.5 4.4 %copy.43 = f32[128,32,256]{2,1,0:T(8,128)} copy(f32[128,32,256]{2,0,1:T(8,128)S(1)} %fusion.18) | data formatting | bytes 8388608
  (60 shorter events, 2.4 us)
Async XLA Ops:
  1.4 13.5 %collective-permute-start = (s32[5,3,256]{2,1,0:T(4,128)S(1)}, s32[5,3,256]{2,1,0:T(4,128)S(1)}, u32[]{:S(2)}, u32[]{:S(2)}) collective-permute-start(s32[5,3,256]{2,1,0:T(4,128)S(1)} %get-tuple-element.29), channel_id=1, source_target_pairs={{0,16},{16,32},{32,48},{48,64},{64,80},{80,96},{96,112},{112,128},... | collective-permute-start | bytes 46088 | tf_op jit(solution)/shard_map/ppermute | solution.py:27
  4.8 10.1 %collective-permute-start.1 = (s32[5,3,256]{2,1,0:T(4,128)S(1)}, s32[5,3,256]{2,1,0:T(4,128)S(1)}, u32[]{:S(2)}, u32[]{:S(2)}) collective-permute-start(s32[5,3,256]{2,1,0:T(4,128)S(1)} %get-tuple-element.30), channel_id=1, source_target_pairs={{16,0},{32,16},{48,32},{64,48},{80,64},{96,80},{112,96},{128,112},... | collective-permute-start | bytes 46088 | tf_op jit(solution)/shard_map/ppermute | solution.py:29
  9.0 16.0 %collective-permute-start.5 = (f32[128,1,256]{2,0,1:T(8,128)S(1)}, f32[128,1,256]{2,0,1:T(8,128)S(1)}, u32[]{:S(2)}, u32[]{:S(2)}) collective-permute-start(f32[128,1,256]{2,0,1:T(8,128)S(1)} %copy.53), channel_id=1, source_target_pairs={{16,0},{32,16},{48,32},{64,48},{80,64},{96,80},{112,96},{128,112},... | collective-permute-start | bytes 393224 | tf_op jit(solution)/shard_map/ppermute | solution.py:29
  11.0 14.1 %collective-permute-start.4 = (f32[128,1,256]{2,0,1:T(8,128)S(1)}, f32[128,1,256]{2,0,1:T(8,128)S(1)}, u32[]{:S(2)}, u32[]{:S(2)}) collective-permute-start(f32[128,1,256]{2,0,1:T(8,128)S(1)} %copy.52), channel_id=1, source_target_pairs={{0,16},{16,32},{32,48},{48,64},{64,80},{80,96},{96,112},{112,128},... | collective-permute-start | bytes 393224 | tf_op jit(solution)/shard_map/ppermute | solution.py:27
  16.0 8.6 %collective-permute-start.2 = (s32[5,38,3]{2,1,0:T(8,128)S(1)}, s32[5,38,3]{2,1,0:T(8,128)S(1)}, u32[]{:S(2)}, u32[]{:S(2)}) collective-permute-start(s32[5,38,3]{2,1,0:T(8,128)S(1)} %get-tuple-element.27), channel_id=1, source_target_pairs={{0,1},{1,2},{2,3},{3,4},{4,5},{5,6},{6,7},{7,8},{8,9},{9,10},{10,1... | collective-permute-start | bytes 6848 | tf_op jit(solution)/shard_map/ppermute | solution.py:27
  17.3 7.3 %collective-permute-start.3 = (s32[5,38,3]{2,1,0:T(8,128)S(1)}, s32[5,38,3]{2,1,0:T(8,128)S(1)}, u32[]{:S(2)}, u32[]{:S(2)}) collective-permute-start(s32[5,38,3]{2,1,0:T(8,128)S(1)} %get-tuple-element.28), channel_id=1, source_target_pairs={{1,0},{2,1},{3,2},{4,3},{5,4},{6,5},{7,6},{8,7},{9,8},{10,9},{11,1... | collective-permute-start | bytes 6848 | tf_op jit(solution)/shard_map/ppermute | solution.py:29
  18.7 6.0 %copy-start.4 = (s32[4,32,256]{2,1,0:T(8,128)S(1)}, s32[4,32,256]{2,1,0:T(8,128)}, u32[]{:S(2)}) copy-start(s32[4,32,256]{2,1,0:T(8,128)} %param.4) | copy-start | bytes 393220
  18.7 6.0 %copy-start.5 = (s32[32,256]{1,0:T(8,128)S(1)}, s32[32,256]{1,0:T(8,128)}, u32[]{:S(2)}) copy-start(s32[32,256]{1,0:T(8,128)} %param.3) | copy-start | bytes 98308
  26.0 8.7 %collective-permute-start.6 = (f32[128,34,1]{0,1,2:T(8,128)S(1)}, f32[128,34,1]{0,1,2:T(8,128)S(1)}, u32[]{:S(2)}, u32[]{:S(2)}) collective-permute-start(f32[128,34,1]{0,1,2:T(8,128)S(1)} %get-tuple-element.17), channel_id=1, source_target_pairs={{0,1},{1,2},{2,3},{3,4},{4,5},{5,6},{6,7},{7,8},{8,9},{9,10},{10,1... | collective-permute-start | bytes 52232 | tf_op jit(solution)/shard_map/ppermute | solution.py:27
  31.2 4.3 %collective-permute-start.7 = (f32[128,34,1]{0,1,2:T(8,128)S(1)}, f32[128,34,1]{0,1,2:T(8,128)S(1)}, u32[]{:S(2)}, u32[]{:S(2)}) collective-permute-start(f32[128,34,1]{0,1,2:T(8,128)S(1)} %get-tuple-element.18), channel_id=1, source_target_pairs={{1,0},{2,1},{3,2},{4,3},{5,4},{6,5},{7,6},{8,7},{9,8},{10,9},{11,1... | collective-permute-start | bytes 52232 | tf_op jit(solution)/shard_map/ppermute | solution.py:29
  34.7 6.3 %copy-start.3 = (f32[128,32,256]{0,1,2:T(8,128)S(1)}, f32[128,32,256]{0,1,2:T(8,128)}, u32[]{:S(2)}) copy-start(f32[128,32,256]{0,1,2:T(8,128)} %copy.30) | copy-start | bytes 12582916
  52.6 2.0 %copy-start = (f32[128,32,256]{0,1,2:T(8,128)}, f32[128,32,256]{0,1,2:T(8,128)S(1)}, u32[]{:S(2)}) copy-start(f32[128,32,256]{0,1,2:T(8,128)S(1)} %fusion.11) | copy-start | bytes 12582916
  54.9 6.9 %collective-permute-start.9 = (f32[128,1,256]{2,0,1:T(8,128)S(1)}, f32[128,1,256]{2,0,1:T(8,128)S(1)}, u32[]{:S(2)}, u32[]{:S(2)}) collective-permute-start(f32[128,1,256]{2,0,1:T(8,128)S(1)} %copy.32), channel_id=1, source_target_pairs={{16,0},{32,16},{48,32},{64,48},{80,64},{96,80},{112,96},{128,112},... | collective-permute-start | bytes 393224 | tf_op jit(solution)/shard_map/ppermute | solution.py:29
  57.0 6.9 %collective-permute-start.8 = (f32[128,1,256]{2,0,1:T(8,128)S(1)}, f32[128,1,256]{2,0,1:T(8,128)S(1)}, u32[]{:S(2)}, u32[]{:S(2)}) collective-permute-start(f32[128,1,256]{2,0,1:T(8,128)S(1)} %copy.31), channel_id=1, source_target_pairs={{0,16},{16,32},{32,48},{48,64},{64,80},{80,96},{96,112},{112,128},... | collective-permute-start | bytes 393224 | tf_op jit(solution)/shard_map/ppermute | solution.py:27
  63.9 9.6 %copy-start.1 = (f32[128,32,256]{0,1,2:T(8,128)S(1)}, f32[128,32,256]{0,1,2:T(8,128)}, u32[]{:S(2)}) copy-start(f32[128,32,256]{0,1,2:T(8,128)} %copy-done) | copy-start | bytes 12582916
  64.8 4.8 %collective-permute-start.10 = (f32[128,34,1]{0,1,2:T(8,128)S(1)}, f32[128,34,1]{0,1,2:T(8,128)S(1)}, u32[]{:S(2)}, u32[]{:S(2)}) collective-permute-start(f32[128,34,1]{0,1,2:T(8,128)S(1)} %get-tuple-element.15), channel_id=1, source_target_pairs={{0,1},{1,2},{2,3},{3,4},{4,5},{5,6},{6,7},{7,8},{8,9},{9,10},{10,1... | collective-permute-start | bytes 52232 | tf_op jit(solution)/shard_map/ppermute | solution.py:27
  68.1 5.4 %collective-permute-start.11 = (f32[128,34,1]{0,1,2:T(8,128)S(1)}, f32[128,34,1]{0,1,2:T(8,128)S(1)}, u32[]{:S(2)}, u32[]{:S(2)}) collective-permute-start(f32[128,34,1]{0,1,2:T(8,128)S(1)} %get-tuple-element.16), channel_id=1, source_target_pairs={{1,0},{2,1},{3,2},{4,3},{5,4},{6,5},{7,6},{8,7},{9,8},{10,9},{11,1... | collective-permute-start | bytes 52232 | tf_op jit(solution)/shard_map/ppermute | solution.py:29
  87.7 7.0 %copy-start.2 = (f32[128,32,256]{0,1,2:T(8,128)}, f32[128,32,256]{0,1,2:T(8,128)S(1)}, u32[]{:S(2)}) copy-start(f32[128,32,256]{0,1,2:T(8,128)S(1)} %fusion.2) | copy-start | bytes 12582916
  94.7 4.8 %collective-permute-start.13 = (f32[128,128]{0,1:T(8,128)S(1)}, f32[128,128]{0,1:T(8,128)S(1)}, u32[]{:S(2)}, u32[]{:S(2)}) collective-permute-start(f32[128,128]{0,1:T(8,128)S(1)} %convolution_bitcast_fusion.1), channel_id=1, source_target_pairs={{0,2},{1,3},{2,0},{3,1},{4,6},{5,7},{6,4},{7,5},{8,10},{9,11},{10,... | collective-permute-start | bytes 196616 | tf_op jit(solution)/shard_map/ppermute | solution.py:89
  97.2 2.6 %collective-permute-start.12 = (f32[128,128]{0,1:T(8,128)S(1)}, f32[128,128]{0,1:T(8,128)S(1)}, u32[]{:S(2)}, u32[]{:S(2)}) collective-permute-start(f32[128,128]{0,1:T(8,128)S(1)} %convolution_bitcast_fusion.1), channel_id=1, source_target_pairs={{0,1},{1,0},{2,3},{3,2},{4,5},{5,4},{6,7},{7,6},{8,9},{9,8},{10,11... | collective-permute-start | bytes 196616 | tf_op jit(solution)/shard_map/ppermute | solution.py:89
  98.9 4.2 %collective-permute-start.14 = (f32[128,128]{0,1:T(8,128)S(1)}, f32[128,128]{0,1:T(8,128)S(1)}, u32[]{:S(2)}, u32[]{:S(2)}) collective-permute-start(f32[128,128]{0,1:T(8,128)S(1)} %convolution_bitcast_fusion.1), channel_id=1, source_target_pairs={{0,3},{1,2},{2,1},{3,0},{4,7},{5,6},{6,5},{7,4},{8,11},{9,10},{10,... | collective-permute-start | bytes 196616 | tf_op jit(solution)/shard_map/ppermute | solution.py:89
  103.2 10.8 %collective-permute-start.17 = (f32[128,128]{0,1:T(8,128)S(1)}, f32[128,128]{0,1:T(8,128)S(1)}, u32[]{:S(2)}, u32[]{:S(2)}) collective-permute-start(f32[128,128]{0,1:T(8,128)S(1)} %add_add_fusion.2), channel_id=1, source_target_pairs={{0,12},{1,13},{2,14},{3,15},{4,8},{5,9},{6,10},{7,11},{8,4},{9,5},... | collective-permute-start | bytes 196616 | tf_op jit(solution)/shard_map/ppermute | solution.py:89
  106.5 10.9 %collective-permute-start.16 = (f32[128,128]{0,1:T(8,128)S(1)}, f32[128,128]{0,1:T(8,128)S(1)}, u32[]{:S(2)}, u32[]{:S(2)}) collective-permute-start(f32[128,128]{0,1:T(8,128)S(1)} %add_add_fusion.2), channel_id=1, source_target_pairs={{0,8},{1,9},{2,10},{3,11},{4,12},{5,13},{6,14},{7,15},{8,0},{9,1},... | collective-permute-start | bytes 196616 | tf_op jit(solution)/shard_map/ppermute | solution.py:89
  113.9 6.4 %collective-permute-start.15 = (f32[128,128]{0,1:T(8,128)S(1)}, f32[128,128]{0,1:T(8,128)S(1)}, u32[]{:S(2)}, u32[]{:S(2)}) collective-permute-start(f32[128,128]{0,1:T(8,128)S(1)} %add_add_fusion.2), channel_id=1, source_target_pairs={{0,4},{1,5},{2,6},{3,7},{4,0},{5,1},{6,2},{7,3},{8,12},{9,13},{10,... | collective-permute-start | bytes 196616 | tf_op jit(solution)/shard_map/ppermute | solution.py:89
  120.3 7.2 %collective-permute-start.20 = (f32[128,128]{0,1:T(8,128)S(1)}, f32[128,128]{0,1:T(8,128)S(1)}, u32[]{:S(2)}, u32[]{:S(2)}) collective-permute-start(f32[128,128]{0,1:T(8,128)S(1)} %add_add_fusion.1), channel_id=1, source_target_pairs={{0,48},{16,32},{32,16},{48,0},{64,112},{80,96},{96,80},{112,64},{1... | collective-permute-start | bytes 196616 | tf_op jit(solution)/shard_map/ppermute | solution.py:89
  122.8 5.9 %collective-permute-start.19 = (f32[128,128]{0,1:T(8,128)S(1)}, f32[128,128]{0,1:T(8,128)S(1)}, u32[]{:S(2)}, u32[]{:S(2)}) collective-permute-start(f32[128,128]{0,1:T(8,128)S(1)} %add_add_fusion.1), channel_id=1, source_target_pairs={{0,32},{16,48},{32,0},{48,16},{64,96},{80,112},{96,64},{112,80},{1... | collective-permute-start | bytes 196616 | tf_op jit(solution)/shard_map/ppermute | solution.py:89
  126.4 4.3 %collective-permute-start.18 = (f32[128,128]{0,1:T(8,128)S(1)}, f32[128,128]{0,1:T(8,128)S(1)}, u32[]{:S(2)}, u32[]{:S(2)}) collective-permute-start(f32[128,128]{0,1:T(8,128)S(1)} %add_add_fusion.1), channel_id=1, source_target_pairs={{0,16},{16,0},{32,48},{48,32},{64,80},{80,64},{96,112},{112,96},{1... | collective-permute-start | bytes 196616 | tf_op jit(solution)/shard_map/ppermute | solution.py:89
  130.7 9.8 %collective-permute-start.23 = (f32[128,128]{0,1:T(8,128)S(1)}, f32[128,128]{0,1:T(8,128)S(1)}, u32[]{:S(2)}, u32[]{:S(2)}) collective-permute-start(f32[128,128]{0,1:T(8,128)S(1)} %add_add_fusion), channel_id=1, source_target_pairs={{0,192},{16,208},{32,224},{48,240},{64,128},{80,144},{96,160},{112... | collective-permute-start | bytes 196616 | tf_op jit(solution)/shard_map/ppermute | solution.py:89
  137.6 5.8 %collective-permute-start.22 = (f32[128,128]{0,1:T(8,128)S(1)}, f32[128,128]{0,1:T(8,128)S(1)}, u32[]{:S(2)}, u32[]{:S(2)}) collective-permute-start(f32[128,128]{0,1:T(8,128)S(1)} %add_add_fusion), channel_id=1, source_target_pairs={{0,128},{16,144},{32,160},{48,176},{64,192},{80,208},{96,224},{112... | collective-permute-start | bytes 196616 | tf_op jit(solution)/shard_map/ppermute | solution.py:89
  137.9 5.4 %collective-permute-start.21 = (f32[128,128]{0,1:T(8,128)S(1)}, f32[128,128]{0,1:T(8,128)S(1)}, u32[]{:S(2)}, u32[]{:S(2)}) collective-permute-start(f32[128,128]{0,1:T(8,128)S(1)} %add_add_fusion), channel_id=1, source_target_pairs={{0,64},{16,80},{32,96},{48,112},{64,0},{80,16},{96,32},{112,48},{1... | collective-permute-start | bytes 196616 | tf_op jit(solution)/shard_map/ppermute | solution.py:89

commit v3 on v2

--- a/solution.py
+++ b/solution.py
@@ -80,6 +80,21 @@
     return shifted(values_in, 0, 0) - shifted(scales, 0, 0) * summed
 
 
+def shifted_pixels(array, step_row, step_col):
+    height = array.shape[0]
+    width = array.shape[1]
+    return array[1 + step_row : height - 1 + step_row, 1 + step_col : width - 1 + step_col]
+
+
+def apply_pixels(values_in, weights, scales):
+    lifted = values_in * scales[:, :, None]
+    summed = None
+    for weight, entry in zip(weights, NEIGHBOURS):
+        term = weight[:, :, None] * shifted_pixels(lifted, entry[0], entry[1])
+        summed = term if summed is None else summed + term
+    return shifted_pixels(values_in, 0, 0) - shifted(scales, 0, 0)[:, :, None] * summed
+
+
 def exchange_sum(block, axis, low_bit, bits):
     count = lax.axis_size(axis)
     received = [block]
@@ -122,14 +137,13 @@
     counts = labels_wide[1:].astype(jnp.float32)
     weights = neighbour_weights(levels, counts, inside)
     scales = degree_scales(weights)
-    cycle_zero = [cropped(weight, 2) for weight in weights]
-    filtered = basis_block
-    for repeat in range(2):
-        extended = padded(filtered, (("row", 1), ("col", 2)), 1)
-        filtered = apply_once(extended, cycle_zero, cropped(scales, 1))
+    pixels = jnp.transpose(basis_block, (1, 2, 0))
+    extended = padded(pixels, (("row", 0), ("col", 1)), 2)
+    first = apply_pixels(extended, [cropped(weight, 1) for weight in weights], scales)
+    filtered = apply_pixels(first, [cropped(weight, 2) for weight in weights], cropped(scales, 1))
     pixel_total = float(total_rows * total_cols)
     gram_local = jnp.einsum(
-        "krc,jrc->kj", filtered, filtered,
+        "rck,rcj->kj", filtered, filtered,
         precision=lax.Precision.HIGHEST, preferred_element_type=jnp.float32,
     )
     gram = all_sum(all_sum(gram_local, "col"), "row") / pixel_total
@@ -138,7 +152,7 @@
         factor, jnp.eye(vectors, dtype=jnp.float32), lower=True
     )
     ortho = jnp.einsum(
-        "kj,jrc->krc", inverse, filtered,
+        "kj,rcj->krc", inverse, filtered,
         precision=lax.Precision.HIGHEST, preferred_element_type=jnp.float32,
     )
     return (ortho, factor.T)

time: 181 us -> 156 us (0.86)
  starting transfers between devices: 61.4 us -> 45.5 us
  other arithmetic: 58.4 us -> 53.9 us
  waiting for transfers between devices: 26.1 us -> 22.9 us
  matrix products: 15.2 us -> 13.1 us
    sub x2 -> x1, other arithmetic: 23.2 us -> 12.9 us  [apply_pixels(): shifted_pixels(values_in, 0, 0) - shifted(scales, 0, 0)[:, :, None] * summed]
    ppermute x6 -> x4, starting transfers between devices: 21 us -> 13.4 us  [padded(): lax.ppermute(tail, axis, [(i, (i + 1) % count) for i in range(ends)])]
    ppermute x12, starting transfers between devices: 30 us -> 24.5 us  [exchange_sum(): received.append(lax.ppermute(block, axis, route))]
    mul x2 -> x1, other arithmetic: 8.05 us -> 13.4 us  [apply_pixels(): lifted = values_in * scales[:, :, None]]
    slice x18 -> x16, local copies, waits for them, and re-layouts: 1.59 us -> 6.1 us  [cropped(): return array[..., cycle:-cycle, cycle:-cycle]]
    ppermute x6 -> x4, starting transfers between devices: 10.3 us -> 7.61 us  [padded(): lax.ppermute(head, axis, [((i + 1) % count, i) for i in range(ends)])]
    unnamed x17 -> x11, local copies, waits for them, and re-layouts: 13.2 us -> 10.5 us
    dot_general x2, matrix products: 14.9 us -> 12.8 us  [the longest x1 6.94 us: per_device(): jnp.einsum('rck,rcj->kj', filtered, filtered, precision=lax.Precision.HIG...]
  transfers between devices with their start and end apart: 24 -> 20, of which waited for: 13 -> 9; matrix products, arithmetic and copies ran while one was open for 6% -> 9% of each run, Pallas kernels for 0% -> 0%
where the time goes in v3:
time: 156 us
  other arithmetic  53.9 us (35%)
  starting transfers between devices  45.5 us (29%)
  waiting for transfers between devices  22.9 us (15%)
  local copies, waits for them, and re-layouts  19.2 us (12%)
  matrix products  13.1 us (8%)
    ppermute x12, starting transfers between devices, exchange_sum(): received.append(lax.ppermute(block, axis, route))  24.5 us
    ppermute x12, waiting for transfers between devices, exchange_sum(): received.append(lax.ppermute(block, axis, route))  18.9 us
    ppermute x4, starting transfers between devices, padded(): lax.ppermute(tail, axis, [(i, (i + 1) % count) for i in range(ends)])  13.4 us
    mul x1, other arithmetic, apply_pixels(): lifted = values_in * scales[:, :, None]  13.4 us
    sub x1, other arithmetic, apply_pixels(): shifted_pixels(values_in, 0, 0) - shifted(scales, 0, 0)[:, :, None] * summed  12.9 us
    another operation x3, other arithmetic, per_device(): factor = jnp.linalg.cholesky(gram)  12.4 us
    unnamed x11, local copies, waits for them, and re-layouts  10.5 us
    another operation x1, other arithmetic, per_device(): jax.scipy.linalg.solve_triangular(factor, jnp.eye(vectors, dtype=jnp.floa...  9.81 us
  transfers between devices with their start and end apart: 20, of which 9 were waited for; matrix products, arithmetic and copies ran while one was open for 9% of the time, Pallas kernels for 0%

profile of v3, /device:TPU:2, one launch (start us, length us, event | category | flops | bytes accessed | tf_op | source)
XLA Modules:
  0.0 155.7 jit_solution(12851382274818013826)
XLA Ops:
  0.6 0.8 pad_add_fusion.3
  1.4 3.4 %collective-permute-start.4 = (s32[5,3,256]{2,1,0:T(4,128)S(1)}, s32[5,3,256]{2,1,0:T(4,128)S(1)}, u32[]{:S(2)}, u32[]{:S(2)}) collective-permute-start(s32[5,3,256]{2,1,0:T(4,128)S(1)} %get-tuple-element.29), channel_id=1, source_target_pairs={{0,16},{16,32},{32,48},{48,64},{64,80},{80,96},{96,112},{112,128},... | collective-permute-start | bytes 46088 | tf_op jit(solution)/shard_map/ppermute | solution.py:27
  4.9 2.6 %collective-permute-start.5 = (s32[5,3,256]{2,1,0:T(4,128)S(1)}, s32[5,3,256]{2,1,0:T(4,128)S(1)}, u32[]{:S(2)}, u32[]{:S(2)}) collective-permute-start(s32[5,3,256]{2,1,0:T(4,128)S(1)} %get-tuple-element.30), channel_id=1, source_target_pairs={{16,0},{32,16},{48,32},{64,48},{80,64},{96,80},{112,96},{128,112},... | collective-permute-start | bytes 46088 | tf_op jit(solution)/shard_map/ppermute | solution.py:29
  7.4 5.3 %copy.15 = f32[128,32,256]{0,2,1:T(8,128)} copy(f32[128,32,256]{2,1,0:T(8,128)} %param.5) | data formatting | bytes 8388608 | tf_op args[2]
  12.7 1.1 fusion.83
  13.8 3.4 %collective-permute-start = (f32[2,256,128]{2,1,0:T(8,128)S(1)}, f32[2,256,128]{2,1,0:T(8,128)S(1)}, u32[]{:S(2)}, u32[]{:S(2)}) collective-permute-start(f32[2,256,128]{2,1,0:T(8,128)S(1)} %get-tuple-element.21), channel_id=1, source_target_pairs={{0,16},{16,32},{32,48},{48,64},{64,80},{80,96},{96,112},{112,128},... | collective-permute-start | bytes 786440 | tf_op jit(solution)/shard_map/ppermute | solution.py:27
  17.2 2.5 %collective-permute-start.1 = (f32[2,256,128]{2,1,0:T(8,128)S(1)}, f32[2,256,128]{2,1,0:T(8,128)S(1)}, u32[]{:S(2)}, u32[]{:S(2)}) collective-permute-start(f32[2,256,128]{2,1,0:T(8,128)S(1)} %get-tuple-element.22), channel_id=1, source_target_pairs={{16,0},{32,16},{48,32},{64,48},{80,64},{96,80},{112,96},{128,112},... | collective-permute-start | bytes 786440 | tf_op jit(solution)/shard_map/ppermute | solution.py:29
  19.8 0.1 fusion.84
  19.9 1.3 collective-permute-start.6
  21.2 1.3 collective-permute-start.7
  22.6 4.0 %collective-permute-done.7 = s32[5,38,3]{2,1,0:T(8,128)S(1)} collective-permute-done((s32[5,38,3]{2,1,0:T(8,128)S(1)}, s32[5,38,3]{2,1,0:T(8,128)S(1)}, u32[]{:S(2)}, u32[]{:S(2)}) %collective-permute-start.7) | collective-permute-done | bytes 2312 | tf_op jit(solution)/shard_map/ppermute | solution.py:29
  26.5 0.2 pad_add_fusion
  26.8 0.1 fusion.67
  26.9 1.2 pad_maximum_fusion.3
  28.1 5.3 %collective-permute-start.2 = (f32[36,2,128]{2,1,0:T(2,128)S(1)}, f32[36,2,128]{2,1,0:T(2,128)S(1)}, u32[]{:S(2)}, u32[]{:S(2)}) collective-permute-start(f32[36,2,128]{2,1,0:T(2,128)S(1)} %get-tuple-element.19), channel_id=1, source_target_pairs={{0,1},{1,2},{2,3},{3,4},{4,5},{5,6},{6,7},{7,8},{8,9},{9,10},{10,1... | collective-permute-start | bytes 110600 | tf_op jit(solution)/shard_map/ppermute | solution.py:27
  33.4 1.3 collective-permute-start.3
  34.7 0.4 add_rsqrt_fusion
  35.1 0.7 slice.379
  35.8 0.1 slice.361
  35.8 0.7 slice.377
  36.5 0.1 slice.359
  36.6 0.7 slice.381
  37.3 0.1 slice.363
  37.4 0.7 slice.383
  38.1 0.1 slice.365
  38.2 0.7 slice.385
  38.8 0.1 slice.367
  38.9 0.7 slice.387
  39.7 0.7 slice.389
  40.5 0.7 slice.391
  41.2 0.7 slice.376
  41.9 0.7 slice.358
  42.6 2.0 %pad_maximum_fusion = (f32[36,260,128]{2,1,0:T(8,128)S(1)}, f32[36,260,128]{2,1,0:T(8,128)S(1)}) fusion(f32[36,2,128]{2,1,0:T(2,128)S(1)} %collective-permute-done.3, f32[2,256,128]{2,1,0:T(8,128)S(1)} %collective-permute-done.1, f32[32,256,128]{2,1,0:T(8,128)S(1)} %bitcast.37, f32[2,256,128]{2,1,0:T(8,128)S(1)} %collective-permute-done, ...), kind=kLoop, calls=%fused_computation | loop fusion | flops 5990400 | bytes 14414400 | tf_op jit(solution)/shard_map/concatenate | solution.py:25
  44.6 13.4 %broadcast_multiply_fusion.1 = (f32[34,258,128]{2,1,0:T(8,128)S(1)}, f32[34,258,128]{2,1,0:T(8,128)S(1)}) fusion(f32[34,258]{1,0:T(8,128)} %slice.358, f32[36,260,128]{2,1,0:T(8,128)S(1)} %get-tuple-element.18, f32[34,258]{1,0:T(8,128)S(1)} %slice.373, f32[34,258]{1,0:T(8,128)S(1)} %slice.371, f32[34,258]{1,0:T(8,128)S(1)} %slice.369, ...), kind=kLoop, calls=%fused_computation.36 | loop fusion | flops 20210688 | bytes 49719696 | tf_op jit(solution)/shard_map/mul | solution.py:90
  58.0 12.9 %fusion.11 = f32[32,256,128]{2,1,0:T(8,128)S(1)} fusion(f32[34,258,128]{2,1,0:T(8,128)S(1)} %get-tuple-element.6, f32[34,258,128]{2,1,0:T(8,128)S(1)} %get-tuple-element.7, f32[32,256]{1,0:T(8,128)} %slice.391, f32[32,256]{1,0:T(8,128)} %slice.389, f32[32,256]{1,0:T(8,128)} %slice.387, f32[32,256]{1,0:T(8,128)} %slice.385, f32[32,256]{1,0:T(8,128)} %slice.383, ...), kind=kLoop, calls=%fused_computation.21 | loop fusion | flops 17825792 | bytes 42237952 | tf_op jit(solution)/shard_map/sub | solution.py:95
  70.9 6.9 %convolution_bitcast_fusion.1 = f32[128,128]{0,1:T(8,128)S(1)} fusion(f32[32,256,128]{2,1,0:T(8,128)S(1)} %fusion.11), kind=kOutput, calls=%fused_computation.38 | convolution fusion | flops 1610612736 | bytes 4259840 | tf_op jit(solution)/shard_map/rck,rcj->kj/dot_general | solution.py:145
  77.9 2.6 %collective-permute-start.9 = (f32[128,128]{0,1:T(8,128)S(1)}, f32[128,128]{0,1:T(8,128)S(1)}, u32[]{:S(2)}, u32[]{:S(2)}) collective-permute-start(f32[128,128]{0,1:T(8,128)S(1)} %convolution_bitcast_fusion.1), channel_id=1, source_target_pairs={{0,2},{1,3},{2,0},{3,1},{4,6},{5,7},{6,4},{7,5},{8,10},{9,11},{10,... | collective-permute-start | bytes 196616 | tf_op jit(solution)/shard_map/ppermute | solution.py:104
  80.5 0.2 collective-permute-start.8
  80.7 0.3 collective-permute-start.10
  81.0 2.3 %collective-permute-done.9 = f32[128,128]{0,1:T(8,128)S(1)} collective-permute-done((f32[128,128]{0,1:T(8,128)S(1)}, f32[128,128]{0,1:T(8,128)S(1)}, u32[]{:S(2)}, u32[]{:S(2)}) %collective-permute-start.9) | collective-permute-done | bytes 65568 | tf_op jit(solution)/shard_map/ppermute | solution.py:104
  83.2 1.4 collective-permute-done.10
  84.7 5.3 %collective-permute-start.13 = (f32[128,128]{0,1:T(8,128)S(1)}, f32[128,128]{0,1:T(8,128)S(1)}, u32[]{:S(2)}, u32[]{:S(2)}) collective-permute-start(f32[128,128]{0,1:T(8,128)S(1)} %add_add_fusion.2), channel_id=1, source_target_pairs={{0,12},{1,13},{2,14},{3,15},{4,8},{5,9},{6,10},{7,11},{8,4},{9,5},... | collective-permute-start | bytes 196616 | tf_op jit(solution)/shard_map/ppermute | solution.py:104
  89.9 4.1 %collective-permute-start.12 = (f32[128,128]{0,1:T(8,128)S(1)}, f32[128,128]{0,1:T(8,128)S(1)}, u32[]{:S(2)}, u32[]{:S(2)}) collective-permute-start(f32[128,128]{0,1:T(8,128)S(1)} %add_add_fusion.2), channel_id=1, source_target_pairs={{0,8},{1,9},{2,10},{3,11},{4,12},{5,13},{6,14},{7,15},{8,0},{9,1},... | collective-permute-start | bytes 196616 | tf_op jit(solution)/shard_map/ppermute | solution.py:104
  94.0 4.5 %collective-permute-done.12 = f32[128,128]{0,1:T(8,128)S(1)} collective-permute-done((f32[128,128]{0,1:T(8,128)S(1)}, f32[128,128]{0,1:T(8,128)S(1)}, u32[]{:S(2)}, u32[]{:S(2)}) %collective-permute-start.12) | collective-permute-done | bytes 65568 | tf_op jit(solution)/shard_map/ppermute | solution.py:104
  98.5 2.8 %collective-permute-done.11 = f32[128,128]{0,1:T(8,128)S(1)} collective-permute-done((f32[128,128]{0,1:T(8,128)S(1)}, f32[128,128]{0,1:T(8,128)S(1)}, u32[]{:S(2)}, u32[]{:S(2)}) %collective-permute-start.11) | collective-permute-done | bytes 65568 | tf_op jit(solution)/shard_map/ppermute | solution.py:104
  101.3 1.6 %collective-permute-start.16 = (f32[128,128]{0,1:T(8,128)S(1)}, f32[128,128]{0,1:T(8,128)S(1)}, u32[]{:S(2)}, u32[]{:S(2)}) collective-permute-start(f32[128,128]{0,1:T(8,128)S(1)} %add_add_fusion.1), channel_id=1, source_target_pairs={{0,48},{16,32},{32,16},{48,0},{64,112},{80,96},{96,80},{112,64},{1... | collective-permute-start | bytes 196616 | tf_op jit(solution)/shard_map/ppermute | solution.py:104
  102.9 2.5 %collective-permute-start.15 = (f32[128,128]{0,1:T(8,128)S(1)}, f32[128,128]{0,1:T(8,128)S(1)}, u32[]{:S(2)}, u32[]{:S(2)}) collective-permute-start(f32[128,128]{0,1:T(8,128)S(1)} %add_add_fusion.1), channel_id=1, source_target_pairs={{0,32},{16,48},{32,0},{48,16},{64,96},{80,112},{96,64},{112,80},{1... | collective-permute-start | bytes 196616 | tf_op jit(solution)/shard_map/ppermute | solution.py:104
  105.3 1.1 collective-permute-start.14
  106.4 2.2 %collective-permute-done.15 = f32[128,128]{0,1:T(8,128)S(1)} collective-permute-done((f32[128,128]{0,1:T(8,128)S(1)}, f32[128,128]{0,1:T(8,128)S(1)}, u32[]{:S(2)}, u32[]{:S(2)}) %collective-permute-start.15) | collective-permute-done | bytes 65568 | tf_op jit(solution)/shard_map/ppermute | solution.py:104
  108.6 1.0 collective-permute-done.14
  109.6 6.0 %collective-permute-start.19 = (f32[128,128]{0,1:T(8,128)S(1)}, f32[128,128]{0,1:T(8,128)S(1)}, u32[]{:S(2)}, u32[]{:S(2)}) collective-permute-start(f32[128,128]{0,1:T(8,128)S(1)} %add_add_fusion), channel_id=1, source_target_pairs={{0,192},{16,208},{32,224},{48,240},{64,128},{80,144},{96,160},{112... | collective-permute-start | bytes 196616 | tf_op jit(solution)/shard_map/ppermute | solution.py:104
  115.6 0.6 collective-permute-start.18
  116.2 0.3 collective-permute-start.17
  116.6 1.6 %collective-permute-done.19 = f32[128,128]{0,1:T(8,128)S(1)} collective-permute-done((f32[128,128]{0,1:T(8,128)S(1)}, f32[128,128]{0,1:T(8,128)S(1)}, u32[]{:S(2)}, u32[]{:S(2)}) %collective-permute-start.19) | collective-permute-done | bytes 65568 | tf_op jit(solution)/shard_map/ppermute | solution.py:104
  118.1 3.3 %collective-permute-done.18 = f32[128,128]{0,1:T(8,128)S(1)} collective-permute-done((f32[128,128]{0,1:T(8,128)S(1)}, f32[128,128]{0,1:T(8,128)S(1)}, u32[]{:S(2)}, u32[]{:S(2)}) %collective-permute-start.18) | collective-permute-done | bytes 65568 | tf_op jit(solution)/shard_map/ppermute | solution.py:104
  121.4 0.1 copy.21
  121.5 11.7 %cholesky.17 = f32[128,128]{1,0:T(8,128)S(1)} custom-call(f32[128,128]{1,0:T(8,128)S(1)} %fusion.19), custom_call_target="Cholesky" | custom-call | tf_op jit(solution)/shard_map/jit(cholesky)/cholesky | solution.py:150
  133.3 0.6 compare_reduce_fusion
  133.9 0.7 fusion.69
  134.6 0.7 copy.23
  135.3 9.8 %custom-call.7 = f32[1,128,128]{1,2,0:T(8,128)S(1)} custom-call(f32[1,128,128]{2,1,0:T(8,128)S(1)} %get-tuple-element.32), custom_call_target="InvertDiagBlocksLowerTriangular" | custom-call | tf_op jit(solution)/shard_map/jit(_solve_triangular)/triangular_solve | solution.py:151
  145.1 0.2 convolution_bitcast_fusion
  145.4 5.9 %fusion.85 = f32[128,32,256]{2,0,1:T(8,128)S(1)} fusion(f32[128,128,1]{1,0,2:T(8,128)S(1)} %convolution_bitcast_fusion, f32[32,256,128]{2,1,0:T(8,128)} %copy-done), kind=kOutput, calls=%fused_computation.149 | convolution fusion | flops 1610612736 | bytes 8454144 | tf_op jit(solution)/shard_map/kj,rcj->krc/dot_general | solution.py:154
  151.2 4.4 %copy.22 = f32[128,32,256]{2,1,0:T(8,128)} copy(f32[128,32,256]{2,0,1:T(8,128)S(1)} %fusion.85) | data formatting | bytes 8388608
  (35 shorter events, 0.6 us)
Async XLA Ops:
  1.4 18.3 %collective-permute-start.4 = (s32[5,3,256]{2,1,0:T(4,128)S(1)}, s32[5,3,256]{2,1,0:T(4,128)S(1)}, u32[]{:S(2)}, u32[]{:S(2)}) collective-permute-start(s32[5,3,256]{2,1,0:T(4,128)S(1)} %get-tuple-element.29), channel_id=1, source_target_pairs={{0,16},{16,32},{32,48},{48,64},{64,80},{80,96},{96,112},{112,128},... | collective-permute-start | bytes 46088 | tf_op jit(solution)/shard_map/ppermute | solution.py:27
  4.8 14.9 %copy-start.2 = (s32[4,32,256]{2,1,0:T(8,128)S(1)}, s32[4,32,256]{2,1,0:T(8,128)}, u32[]{:S(2)}) copy-start(s32[4,32,256]{2,1,0:T(8,128)} %param.4) | copy-start | bytes 393220
  4.8 14.9 %copy-start.3 = (s32[32,256]{1,0:T(8,128)S(1)}, s32[32,256]{1,0:T(8,128)}, u32[]{:S(2)}) copy-start(s32[32,256]{1,0:T(8,128)} %param.3) | copy-start | bytes 98308
  4.9 14.9 %collective-permute-start.5 = (s32[5,3,256]{2,1,0:T(4,128)S(1)}, s32[5,3,256]{2,1,0:T(4,128)S(1)}, u32[]{:S(2)}, u32[]{:S(2)}) collective-permute-start(s32[5,3,256]{2,1,0:T(4,128)S(1)} %get-tuple-element.30), channel_id=1, source_target_pairs={{16,0},{32,16},{48,32},{64,48},{80,64},{96,80},{112,96},{128,112},... | collective-permute-start | bytes 46088 | tf_op jit(solution)/shard_map/ppermute | solution.py:29
  13.8 13.1 %collective-permute-start = (f32[2,256,128]{2,1,0:T(8,128)S(1)}, f32[2,256,128]{2,1,0:T(8,128)S(1)}, u32[]{:S(2)}, u32[]{:S(2)}) collective-permute-start(f32[2,256,128]{2,1,0:T(8,128)S(1)} %get-tuple-element.21), channel_id=1, source_target_pairs={{0,16},{16,32},{32,48},{48,64},{64,80},{80,96},{96,112},{112,128},... | collective-permute-start | bytes 786440 | tf_op jit(solution)/shard_map/ppermute | solution.py:27
  17.2 9.7 %collective-permute-start.1 = (f32[2,256,128]{2,1,0:T(8,128)S(1)}, f32[2,256,128]{2,1,0:T(8,128)S(1)}, u32[]{:S(2)}, u32[]{:S(2)}) collective-permute-start(f32[2,256,128]{2,1,0:T(8,128)S(1)} %get-tuple-element.22), channel_id=1, source_target_pairs={{16,0},{32,16},{48,32},{64,48},{80,64},{96,80},{112,96},{128,112},... | collective-permute-start | bytes 786440 | tf_op jit(solution)/shard_map/ppermute | solution.py:29
  19.9 2.7 %collective-permute-start.6 = (s32[5,38,3]{2,1,0:T(8,128)S(1)}, s32[5,38,3]{2,1,0:T(8,128)S(1)}, u32[]{:S(2)}, u32[]{:S(2)}) collective-permute-start(s32[5,38,3]{2,1,0:T(8,128)S(1)} %get-tuple-element.27), channel_id=1, source_target_pairs={{0,1},{1,2},{2,3},{3,4},{4,5},{5,6},{6,7},{7,8},{8,9},{9,10},{10,1... | collective-permute-start | bytes 6848 | tf_op jit(solution)/shard_map/ppermute | solution.py:27
  21.2 5.3 %collective-permute-start.7 = (s32[5,38,3]{2,1,0:T(8,128)S(1)}, s32[5,38,3]{2,1,0:T(8,128)S(1)}, u32[]{:S(2)}, u32[]{:S(2)}) collective-permute-start(s32[5,38,3]{2,1,0:T(8,128)S(1)} %get-tuple-element.28), channel_id=1, source_target_pairs={{1,0},{2,1},{3,2},{4,3},{5,4},{6,5},{7,6},{8,7},{9,8},{10,9},{11,1... | collective-permute-start | bytes 6848 | tf_op jit(solution)/shard_map/ppermute | solution.py:29
  26.9 15.8 %copy-start.1 = (f32[128,32,256]{0,2,1:T(8,128)S(1)}, f32[128,32,256]{0,2,1:T(8,128)}, u32[]{:S(2)}) copy-start(f32[128,32,256]{0,2,1:T(8,128)} %copy.15) | copy-start | bytes 12582916
  28.1 14.5 %collective-permute-start.2 = (f32[36,2,128]{2,1,0:T(2,128)S(1)}, f32[36,2,128]{2,1,0:T(2,128)S(1)}, u32[]{:S(2)}, u32[]{:S(2)}) collective-permute-start(f32[36,2,128]{2,1,0:T(2,128)S(1)} %get-tuple-element.19), channel_id=1, source_target_pairs={{0,1},{1,2},{2,3},{3,4},{4,5},{5,6},{6,7},{7,8},{8,9},{9,10},{10,1... | collective-permute-start | bytes 110600 | tf_op jit(solution)/shard_map/ppermute | solution.py:27
  33.4 9.2 %collective-permute-start.3 = (f32[36,2,128]{2,1,0:T(2,128)S(1)}, f32[36,2,128]{2,1,0:T(2,128)S(1)}, u32[]{:S(2)}, u32[]{:S(2)}) collective-permute-start(f32[36,2,128]{2,1,0:T(2,128)S(1)} %get-tuple-element.20), channel_id=1, source_target_pairs={{1,0},{2,1},{3,2},{4,3},{5,4},{6,5},{7,6},{8,7},{9,8},{10,9},{11,1... | collective-permute-start | bytes 110600 | tf_op jit(solution)/shard_map/ppermute | solution.py:29
  70.9 38.7 %copy-start = (f32[32,256,128]{2,1,0:T(8,128)}, f32[32,256,128]{2,1,0:T(8,128)S(1)}, u32[]{:S(2)}) copy-start(f32[32,256,128]{2,1,0:T(8,128)S(1)} %fusion.11) | copy-start | bytes 12582916
  77.9 5.4 %collective-permute-start.9 = (f32[128,128]{0,1:T(8,128)S(1)}, f32[128,128]{0,1:T(8,128)S(1)}, u32[]{:S(2)}, u32[]{:S(2)}) collective-permute-start(f32[128,128]{0,1:T(8,128)S(1)} %convolution_bitcast_fusion.1), channel_id=1, source_target_pairs={{0,2},{1,3},{2,0},{3,1},{4,6},{5,7},{6,4},{7,5},{8,10},{9,11},{10,... | collective-permute-start | bytes 196616 | tf_op jit(solution)/shard_map/ppermute | solution.py:104
  80.5 2.8 %collective-permute-start.8 = (f32[128,128]{0,1:T(8,128)S(1)}, f32[128,128]{0,1:T(8,128)S(1)}, u32[]{:S(2)}, u32[]{:S(2)}) collective-permute-start(f32[128,128]{0,1:T(8,128)S(1)} %convolution_bitcast_fusion.1), channel_id=1, source_target_pairs={{0,1},{1,0},{2,3},{3,2},{4,5},{5,4},{6,7},{7,6},{8,9},{9,8},{10,11... | collective-permute-start | bytes 196616 | tf_op jit(solution)/shard_map/ppermute | solution.py:104
  80.7 3.9 %collective-permute-start.10 = (f32[128,128]{0,1:T(8,128)S(1)}, f32[128,128]{0,1:T(8,128)S(1)}, u32[]{:S(2)}, u32[]{:S(2)}) collective-permute-start(f32[128,128]{0,1:T(8,128)S(1)} %convolution_bitcast_fusion.1), channel_id=1, source_target_pairs={{0,3},{1,2},{2,1},{3,0},{4,7},{5,6},{6,5},{7,4},{8,11},{9,10},{10,... | collective-permute-start | bytes 196616 | tf_op jit(solution)/shard_map/ppermute | solution.py:104
  84.7 9.4 %collective-permute-start.13 = (f32[128,128]{0,1:T(8,128)S(1)}, f32[128,128]{0,1:T(8,128)S(1)}, u32[]{:S(2)}, u32[]{:S(2)}) collective-permute-start(f32[128,128]{0,1:T(8,128)S(1)} %add_add_fusion.2), channel_id=1, source_target_pairs={{0,12},{1,13},{2,14},{3,15},{4,8},{5,9},{6,10},{7,11},{8,4},{9,5},... | collective-permute-start | bytes 196616 | tf_op jit(solution)/shard_map/ppermute | solution.py:104
  89.9 8.6 %collective-permute-start.12 = (f32[128,128]{0,1:T(8,128)S(1)}, f32[128,128]{0,1:T(8,128)S(1)}, u32[]{:S(2)}, u32[]{:S(2)}) collective-permute-start(f32[128,128]{0,1:T(8,128)S(1)} %add_add_fusion.2), channel_id=1, source_target_pairs={{0,8},{1,9},{2,10},{3,11},{4,12},{5,13},{6,14},{7,15},{8,0},{9,1},... | collective-permute-start | bytes 196616 | tf_op jit(solution)/shard_map/ppermute | solution.py:104
  94.0 7.3 %collective-permute-start.11 = (f32[128,128]{0,1:T(8,128)S(1)}, f32[128,128]{0,1:T(8,128)S(1)}, u32[]{:S(2)}, u32[]{:S(2)}) collective-permute-start(f32[128,128]{0,1:T(8,128)S(1)} %add_add_fusion.2), channel_id=1, source_target_pairs={{0,4},{1,5},{2,6},{3,7},{4,0},{5,1},{6,2},{7,3},{8,12},{9,13},{10,... | collective-permute-start | bytes 196616 | tf_op jit(solution)/shard_map/ppermute | solution.py:104
  101.3 5.1 %collective-permute-start.16 = (f32[128,128]{0,1:T(8,128)S(1)}, f32[128,128]{0,1:T(8,128)S(1)}, u32[]{:S(2)}, u32[]{:S(2)}) collective-permute-start(f32[128,128]{0,1:T(8,128)S(1)} %add_add_fusion.1), channel_id=1, source_target_pairs={{0,48},{16,32},{32,16},{48,0},{64,112},{80,96},{96,80},{112,64},{1... | collective-permute-start | bytes 196616 | tf_op jit(solution)/shard_map/ppermute | solution.py:104
  102.9 5.8 %collective-permute-start.15 = (f32[128,128]{0,1:T(8,128)S(1)}, f32[128,128]{0,1:T(8,128)S(1)}, u32[]{:S(2)}, u32[]{:S(2)}) collective-permute-start(f32[128,128]{0,1:T(8,128)S(1)} %add_add_fusion.1), channel_id=1, source_target_pairs={{0,32},{16,48},{32,0},{48,16},{64,96},{80,112},{96,64},{112,80},{1... | collective-permute-start | bytes 196616 | tf_op jit(solution)/shard_map/ppermute | solution.py:104
  105.3 4.3 %collective-permute-start.14 = (f32[128,128]{0,1:T(8,128)S(1)}, f32[128,128]{0,1:T(8,128)S(1)}, u32[]{:S(2)}, u32[]{:S(2)}) collective-permute-start(f32[128,128]{0,1:T(8,128)S(1)} %add_add_fusion.1), channel_id=1, source_target_pairs={{0,16},{16,0},{32,48},{48,32},{64,80},{80,64},{96,112},{112,96},{1... | collective-permute-start | bytes 196616 | tf_op jit(solution)/shard_map/ppermute | solution.py:104
  109.6 8.5 %collective-permute-start.19 = (f32[128,128]{0,1:T(8,128)S(1)}, f32[128,128]{0,1:T(8,128)S(1)}, u32[]{:S(2)}, u32[]{:S(2)}) collective-permute-start(f32[128,128]{0,1:T(8,128)S(1)} %add_add_fusion), channel_id=1, source_target_pairs={{0,192},{16,208},{32,224},{48,240},{64,128},{80,144},{96,160},{112... | collective-permute-start | bytes 196616 | tf_op jit(solution)/shard_map/ppermute | solution.py:104
  115.6 5.8 %collective-permute-start.18 = (f32[128,128]{0,1:T(8,128)S(1)}, f32[128,128]{0,1:T(8,128)S(1)}, u32[]{:S(2)}, u32[]{:S(2)}) collective-permute-start(f32[128,128]{0,1:T(8,128)S(1)} %add_add_fusion), channel_id=1, source_target_pairs={{0,128},{16,144},{32,160},{48,176},{64,192},{80,208},{96,224},{112... | collective-permute-start | bytes 196616 | tf_op jit(solution)/shard_map/ppermute | solution.py:104
  116.2 5.1 %collective-permute-start.17 = (f32[128,128]{0,1:T(8,128)S(1)}, f32[128,128]{0,1:T(8,128)S(1)}, u32[]{:S(2)}, u32[]{:S(2)}) collective-permute-start(f32[128,128]{0,1:T(8,128)S(1)} %add_add_fusion), channel_id=1, source_target_pairs={{0,64},{16,80},{32,96},{48,112},{64,0},{80,16},{96,32},{112,48},{1... | collective-permute-start | bytes 196616 | tf_op jit(solution)/shard_map/ppermute | solution.py:104

commit v4 on v3

--- a/solution.py
+++ b/solution.py
@@ -139,8 +139,11 @@
     scales = degree_scales(weights)
     pixels = jnp.transpose(basis_block, (1, 2, 0))
     extended = padded(pixels, (("row", 0), ("col", 1)), 2)
-    first = apply_pixels(extended, [cropped(weight, 1) for weight in weights], scales)
-    filtered = apply_pixels(first, [cropped(weight, 2) for weight in weights], cropped(scales, 1))
+    stacked = jnp.stack(weights)
+    ring_weights = cropped(stacked, 1)
+    tile_weights = cropped(stacked, 2)
+    first = apply_pixels(extended, [ring_weights[i] for i in range(len(weights))], scales)
+    filtered = apply_pixels(first, [tile_weights[i] for i in range(len(weights))], cropped(scales, 1))
     pixel_total = float(total_rows * total_cols)
     gram_local = jnp.einsum(
         "rck,rcj->kj", filtered, filtered,

time: 156 us -> 154 us (0.987)
  local copies, waits for them, and re-layouts: 19.2 us -> 16.3 us
  starting transfers between devices: 45.5 us -> 47.9 us
    slice x16 -> x0, local copies, waits for them, and re-layouts: 6.1 us -> none  [cropped(): return array[..., cycle:-cycle, cycle:-cycle]]
    mul x0 -> x8, local copies, waits for them, and re-layouts: none -> 3.82 us  [apply_pixels(): term = weight[:, :, None] * shifted_pixels(lifted, entry[0], entry[1])]
    ppermute x12, starting transfers between devices: 24.5 us -> 26.8 us  [exchange_sum(): received.append(lax.ppermute(block, axis, route))]
  transfers between devices with their start and end apart: 20 -> 20, of which waited for: 9 -> 11; matrix products, arithmetic and copies ran while one was open for 9% -> 8% of each run, Pallas kernels for 0% -> 0%
where the time goes in v4:
time: 154 us
  other arithmetic  52.8 us (34%)
  starting transfers between devices  47.9 us (31%)
  waiting for transfers between devices  22.5 us (15%)
  local copies, waits for them, and re-layouts  16.3 us (11%)
  matrix products  13.1 us (9%)
    ppermute x12, starting transfers between devices, exchange_sum(): received.append(lax.ppermute(block, axis, route))  26.8 us
    ppermute x12, waiting for transfers between devices, exchange_sum(): received.append(lax.ppermute(block, axis, route))  18.2 us
    ppermute x4, starting transfers between devices, padded(): lax.ppermute(tail, axis, [(i, (i + 1) % count) for i in range(ends)])  13.5 us
    mul x1, other arithmetic, apply_pixels(): lifted = values_in * scales[:, :, None]  13.4 us
    sub x1, other arithmetic, apply_pixels(): shifted_pixels(values_in, 0, 0) - shifted(scales, 0, 0)[:, :, None] * summed  12.9 us
    another operation x3, other arithmetic, per_device(): factor = jnp.linalg.cholesky(gram)  12.4 us
    unnamed x11, local copies, waits for them, and re-layouts  10.5 us
    another operation x1, other arithmetic, per_device(): jax.scipy.linalg.solve_triangular(factor, jnp.eye(vectors, dtype=jnp.floa...  9.81 us
  transfers between devices with their start and end apart: 20, of which 11 were waited for; matrix products, arithmetic and copies ran while one was open for 8% of the time, Pallas kernels for 0%

profile of v4, /device:TPU:2, one launch (start us, length us, event | category | flops | bytes accessed | tf_op | source)
XLA Modules:
  0.0 153.6 jit_solution(12708867696504394445)
XLA Ops:
  0.6 0.8 pad_add_fusion.3
  1.4 3.4 %collective-permute-start.4 = (s32[5,3,256]{2,1,0:T(4,128)S(1)}, s32[5,3,256]{2,1,0:T(4,128)S(1)}, u32[]{:S(2)}, u32[]{:S(2)}) collective-permute-start(s32[5,3,256]{2,1,0:T(4,128)S(1)} %get-tuple-element.29), channel_id=1, source_target_pairs={{0,16},{16,32},{32,48},{48,64},{64,80},{80,96},{96,112},{112,128},... | collective-permute-start | bytes 46088 | tf_op jit(solution)/shard_map/ppermute | solution.py:27
  4.8 0.0 copy-start.2
  4.8 0.0 copy-start.3
  4.9 2.6 %collective-permute-start.5 = (s32[5,3,256]{2,1,0:T(4,128)S(1)}, s32[5,3,256]{2,1,0:T(4,128)S(1)}, u32[]{:S(2)}, u32[]{:S(2)}) collective-permute-start(s32[5,3,256]{2,1,0:T(4,128)S(1)} %get-tuple-element.30), channel_id=1, source_target_pairs={{16,0},{32,16},{48,32},{64,48},{80,64},{96,80},{112,96},{128,112},... | collective-permute-start | bytes 46088 | tf_op jit(solution)/shard_map/ppermute | solution.py:29
  7.4 5.3 %copy.15 = f32[128,32,256]{0,2,1:T(8,128)} copy(f32[128,32,256]{2,1,0:T(8,128)} %param.5) | data formatting | bytes 8388608 | tf_op args[2]
  12.7 1.1 fusion.83
  13.8 3.4 %collective-permute-start = (f32[2,256,128]{2,1,0:T(8,128)S(1)}, f32[2,256,128]{2,1,0:T(8,128)S(1)}, u32[]{:S(2)}, u32[]{:S(2)}) collective-permute-start(f32[2,256,128]{2,1,0:T(8,128)S(1)} %get-tuple-element.21), channel_id=1, source_target_pairs={{0,16},{16,32},{32,48},{48,64},{64,80},{80,96},{96,112},{112,128},... | collective-permute-start | bytes 786440 | tf_op jit(solution)/shard_map/ppermute | solution.py:27
  17.2 2.5 %collective-permute-start.1 = (f32[2,256,128]{2,1,0:T(8,128)S(1)}, f32[2,256,128]{2,1,0:T(8,128)S(1)}, u32[]{:S(2)}, u32[]{:S(2)}) collective-permute-start(f32[2,256,128]{2,1,0:T(8,128)S(1)} %get-tuple-element.22), channel_id=1, source_target_pairs={{16,0},{32,16},{48,32},{64,48},{80,64},{96,80},{112,96},{128,112},... | collective-permute-start | bytes 786440 | tf_op jit(solution)/shard_map/ppermute | solution.py:29
  19.8 0.1 fusion.84
  19.9 1.6 %collective-permute-start.6 = (s32[5,38,3]{2,1,0:T(8,128)S(1)}, s32[5,38,3]{2,1,0:T(8,128)S(1)}, u32[]{:S(2)}, u32[]{:S(2)}) collective-permute-start(s32[5,38,3]{2,1,0:T(8,128)S(1)} %get-tuple-element.27), channel_id=1, source_target_pairs={{0,1},{1,2},{2,3},{3,4},{4,5},{5,6},{6,7},{7,8},{8,9},{9,10},{10,1... | collective-permute-start | bytes 6848 | tf_op jit(solution)/shard_map/ppermute | solution.py:27
  21.5 1.3 collective-permute-start.7
  22.8 0.1 broadcast_multiply_fusion.2
  22.8 4.0 %collective-permute-done.7 = s32[5,38,3]{2,1,0:T(8,128)S(1)} collective-permute-done((s32[5,38,3]{2,1,0:T(8,128)S(1)}, s32[5,38,3]{2,1,0:T(8,128)S(1)}, u32[]{:S(2)}, u32[]{:S(2)}) %collective-permute-start.7) | collective-permute-done | bytes 2312 | tf_op jit(solution)/shard_map/ppermute | solution.py:29
  26.8 0.2 pad_add_fusion
  27.1 0.1 fusion.67
  27.2 0.4 add_rsqrt_fusion
  27.5 0.7 slice_bitcast_fusion.18
  28.2 0.1 slice_bitcast_fusion.6
  28.3 0.7 slice_bitcast_fusion.16
  29.1 0.1 slice_bitcast_fusion.4
  29.1 0.1 slice_bitcast_fusion.2
  29.3 0.7 slice_bitcast_fusion.14
  30.0 0.7 slice_bitcast_fusion
  30.7 5.2 %collective-permute-start.2 = (f32[36,2,128]{2,1,0:T(2,128)S(1)}, f32[36,2,128]{2,1,0:T(2,128)S(1)}, u32[]{:S(2)}, u32[]{:S(2)}) collective-permute-start(f32[36,2,128]{2,1,0:T(2,128)S(1)} %get-tuple-element.19), channel_id=1, source_target_pairs={{0,1},{1,2},{2,3},{3,4},{4,5},{5,6},{6,7},{7,8},{8,9},{9,10},{10,1... | collective-permute-start | bytes 110600 | tf_op jit(solution)/shard_map/ppermute | solution.py:27
  35.9 1.3 collective-permute-start.3
  37.2 0.7 slice_bitcast_fusion.12
  37.9 0.7 slice.410
  38.6 0.1 slice.392
  38.7 0.3 collective-permute-done.3
  39.0 1.9 %pad_maximum_fusion = (f32[36,260,128]{2,1,0:T(8,128)S(1)}, f32[36,260,128]{2,1,0:T(8,128)S(1)}) fusion(f32[36,2,128]{2,1,0:T(2,128)S(1)} %collective-permute-done.3, f32[2,256,128]{2,1,0:T(8,128)S(1)} %collective-permute-done.1, f32[32,256,128]{2,1,0:T(8,128)S(1)} %bitcast.77, f32[2,256,128]{2,1,0:T(8,128)S(1)} %collective-permute-done, ...), kind=kLoop, calls=%fused_computation | loop fusion | flops 5990400 | bytes 14414400 | tf_op jit(solution)/shard_map/concatenate | solution.py:25
  41.0 13.4 %broadcast_multiply_fusion.1 = (f32[34,258,128]{2,1,0:T(8,128)S(1)}, f32[34,258,128]{2,1,0:T(8,128)S(1)}) fusion(f32[34,258]{1,0:T(8,128)S(1)} %slice.392, f32[36,260,128]{2,1,0:T(8,128)S(1)} %get-tuple-element.18, f32[34,258]{1,0:T(8,128)S(1)} %get-tuple-element.33, f32[34,258]{1,0:T(8,128)} %get-tuple-element.34, f32[34,258]{1,0:T(8,128)S(1)} %get-tuple-element.35, ...), kind=kLoop, calls=%fused_computation.36 | loop fusion | flops 20210688 | bytes 49719696 | tf_op jit(solution)/shard_map/mul | solution.py:90
  54.4 12.9 %fusion.11 = f32[32,256,128]{2,1,0:T(8,128)S(1)} fusion(f32[34,258,128]{2,1,0:T(8,128)S(1)} %get-tuple-element.6, f32[34,258,128]{2,1,0:T(8,128)S(1)} %get-tuple-element.7, f32[32,256]{1,0:T(8,128)} %get-tuple-element.41, f32[32,256]{1,0:T(8,128)} %get-tuple-element.42, f32[32,256]{1,0:T(8,128)} %get-tuple-element.43, f32[32,256]{1,0:T(8,128)} %get-tuple-element.44, ...), kind=kLoop, calls=%fused_computation.21 | loop fusion | flops 17825792 | bytes 42237952 | tf_op jit(solution)/shard_map/sub | solution.py:95
  67.3 0.0 copy-start
  67.3 6.9 %convolution_bitcast_fusion.1 = f32[128,128]{0,1:T(8,128)S(1)} fusion(f32[32,256,128]{2,1,0:T(8,128)S(1)} %fusion.11), kind=kOutput, calls=%fused_computation.38 | convolution fusion | flops 1610612736 | bytes 4259840 | tf_op jit(solution)/shard_map/rck,rcj->kj/dot_general | solution.py:148
  74.2 2.4 %collective-permute-start.9 = (f32[128,128]{0,1:T(8,128)S(1)}, f32[128,128]{0,1:T(8,128)S(1)}, u32[]{:S(2)}, u32[]{:S(2)}) collective-permute-start(f32[128,128]{0,1:T(8,128)S(1)} %convolution_bitcast_fusion.1), channel_id=1, source_target_pairs={{0,2},{1,3},{2,0},{3,1},{4,6},{5,7},{6,4},{7,5},{8,10},{9,11},{10,... | collective-permute-start | bytes 196616 | tf_op jit(solution)/shard_map/ppermute | solution.py:104
  76.7 1.8 %collective-permute-start.8 = (f32[128,128]{0,1:T(8,128)S(1)}, f32[128,128]{0,1:T(8,128)S(1)}, u32[]{:S(2)}, u32[]{:S(2)}) collective-permute-start(f32[128,128]{0,1:T(8,128)S(1)} %convolution_bitcast_fusion.1), channel_id=1, source_target_pairs={{0,1},{1,0},{2,3},{3,2},{4,5},{5,4},{6,7},{7,6},{8,9},{9,8},{10,11... | collective-permute-start | bytes 196616 | tf_op jit(solution)/shard_map/ppermute | solution.py:104
  78.4 0.3 collective-permute-start.10
  78.7 0.2 collective-permute-done.9
  78.9 0.4 collective-permute-done.8
  79.3 3.3 %collective-permute-done.10 = f32[128,128]{0,1:T(8,128)S(1)} collective-permute-done((f32[128,128]{0,1:T(8,128)S(1)}, f32[128,128]{0,1:T(8,128)S(1)}, u32[]{:S(2)}, u32[]{:S(2)}) %collective-permute-start.10) | collective-permute-done | bytes 65568 | tf_op jit(solution)/shard_map/ppermute | solution.py:104
  82.7 4.6 %collective-permute-start.13 = (f32[128,128]{0,1:T(8,128)S(1)}, f32[128,128]{0,1:T(8,128)S(1)}, u32[]{:S(2)}, u32[]{:S(2)}) collective-permute-start(f32[128,128]{0,1:T(8,128)S(1)} %add_add_fusion.2), channel_id=1, source_target_pairs={{0,12},{1,13},{2,14},{3,15},{4,8},{5,9},{6,10},{7,11},{8,4},{9,5},... | collective-permute-start | bytes 196616 | tf_op jit(solution)/shard_map/ppermute | solution.py:104
  87.3 5.7 %collective-permute-start.12 = (f32[128,128]{0,1:T(8,128)S(1)}, f32[128,128]{0,1:T(8,128)S(1)}, u32[]{:S(2)}, u32[]{:S(2)}) collective-permute-start(f32[128,128]{0,1:T(8,128)S(1)} %add_add_fusion.2), channel_id=1, source_target_pairs={{0,8},{1,9},{2,10},{3,11},{4,12},{5,13},{6,14},{7,15},{8,0},{9,1},... | collective-permute-start | bytes 196616 | tf_op jit(solution)/shard_map/ppermute | solution.py:104
  92.9 4.9 %collective-permute-done.12 = f32[128,128]{0,1:T(8,128)S(1)} collective-permute-done((f32[128,128]{0,1:T(8,128)S(1)}, f32[128,128]{0,1:T(8,128)S(1)}, u32[]{:S(2)}, u32[]{:S(2)}) %collective-permute-start.12) | collective-permute-done | bytes 65568 | tf_op jit(solution)/shard_map/ppermute | solution.py:104
  97.8 1.4 collective-permute-done.11
  99.2 1.6 %collective-permute-start.16 = (f32[128,128]{0,1:T(8,128)S(1)}, f32[128,128]{0,1:T(8,128)S(1)}, u32[]{:S(2)}, u32[]{:S(2)}) collective-permute-start(f32[128,128]{0,1:T(8,128)S(1)} %add_add_fusion.1), channel_id=1, source_target_pairs={{0,48},{16,32},{32,16},{48,0},{64,112},{80,96},{96,80},{112,64},{1... | collective-permute-start | bytes 196616 | tf_op jit(solution)/shard_map/ppermute | solution.py:104
  100.8 2.3 %collective-permute-start.15 = (f32[128,128]{0,1:T(8,128)S(1)}, f32[128,128]{0,1:T(8,128)S(1)}, u32[]{:S(2)}, u32[]{:S(2)}) collective-permute-start(f32[128,128]{0,1:T(8,128)S(1)} %add_add_fusion.1), channel_id=1, source_target_pairs={{0,32},{16,48},{32,0},{48,16},{64,96},{80,112},{96,64},{112,80},{1... | collective-permute-start | bytes 196616 | tf_op jit(solution)/shard_map/ppermute | solution.py:104
  103.1 1.1 collective-permute-start.14
  104.2 2.4 %collective-permute-done.15 = f32[128,128]{0,1:T(8,128)S(1)} collective-permute-done((f32[128,128]{0,1:T(8,128)S(1)}, f32[128,128]{0,1:T(8,128)S(1)}, u32[]{:S(2)}, u32[]{:S(2)}) %collective-permute-start.15) | collective-permute-done | bytes 65568 | tf_op jit(solution)/shard_map/ppermute | solution.py:104
  106.6 0.8 collective-permute-done.14
  107.4 6.1 %collective-permute-start.19 = (f32[128,128]{0,1:T(8,128)S(1)}, f32[128,128]{0,1:T(8,128)S(1)}, u32[]{:S(2)}, u32[]{:S(2)}) collective-permute-start(f32[128,128]{0,1:T(8,128)S(1)} %add_add_fusion), channel_id=1, source_target_pairs={{0,192},{16,208},{32,224},{48,240},{64,128},{80,144},{96,160},{112... | collective-permute-start | bytes 196616 | tf_op jit(solution)/shard_map/ppermute | solution.py:104
  113.5 0.6 collective-permute-start.18
  114.1 0.3 collective-permute-start.17
  114.5 2.0 %collective-permute-done.19 = f32[128,128]{0,1:T(8,128)S(1)} collective-permute-done((f32[128,128]{0,1:T(8,128)S(1)}, f32[128,128]{0,1:T(8,128)S(1)}, u32[]{:S(2)}, u32[]{:S(2)}) %collective-permute-start.19) | collective-permute-done | bytes 65568 | tf_op jit(solution)/shard_map/ppermute | solution.py:104
  116.5 2.8 %collective-permute-done.18 = f32[128,128]{0,1:T(8,128)S(1)} collective-permute-done((f32[128,128]{0,1:T(8,128)S(1)}, f32[128,128]{0,1:T(8,128)S(1)}, u32[]{:S(2)}, u32[]{:S(2)}) %collective-permute-start.18) | collective-permute-done | bytes 65568 | tf_op jit(solution)/shard_map/ppermute | solution.py:104
  119.3 0.1 copy.21
  119.4 11.7 %cholesky.17 = f32[128,128]{1,0:T(8,128)S(1)} custom-call(f32[128,128]{1,0:T(8,128)S(1)} %fusion.19), custom_call_target="Cholesky" | custom-call | tf_op jit(solution)/shard_map/jit(cholesky)/cholesky | solution.py:153
  131.2 0.6 compare_reduce_fusion
  131.8 0.7 fusion.69
  132.5 0.7 copy.23
  133.2 9.8 %custom-call.7 = f32[1,128,128]{1,2,0:T(8,128)S(1)} custom-call(f32[1,128,128]{2,1,0:T(8,128)S(1)} %get-tuple-element.32), custom_call_target="InvertDiagBlocksLowerTriangular" | custom-call | tf_op jit(solution)/shard_map/jit(_solve_triangular)/triangular_solve | solution.py:154
  143.0 0.2 convolution_bitcast_fusion
  143.3 5.9 %fusion.85 = f32[128,32,256]{2,0,1:T(8,128)S(1)} fusion(f32[128,128,1]{1,0,2:T(8,128)S(1)} %convolution_bitcast_fusion, f32[32,256,128]{2,1,0:T(8,128)} %copy-done), kind=kOutput, calls=%fused_computation.165 | convolution fusion | flops 1610612736 | bytes 8454144 | tf_op jit(solution)/shard_map/kj,rcj->krc/dot_general | solution.py:157
  149.2 4.4 %copy.22 = f32[128,32,256]{2,1,0:T(8,128)} copy(f32[128,32,256]{2,0,1:T(8,128)S(1)} %fusion.85) | data formatting | bytes 8388608
  (27 shorter events, 0.3 us)
Async XLA Ops:
  1.4 18.3 %collective-permute-start.4 = (s32[5,3,256]{2,1,0:T(4,128)S(1)}, s32[5,3,256]{2,1,0:T(4,128)S(1)}, u32[]{:S(2)}, u32[]{:S(2)}) collective-permute-start(s32[5,3,256]{2,1,0:T(4,128)S(1)} %get-tuple-element.29), channel_id=1, source_target_pairs={{0,16},{16,32},{32,48},{48,64},{64,80},{80,96},{96,112},{112,128},... | collective-permute-start | bytes 46088 | tf_op jit(solution)/shard_map/ppermute | solution.py:27
  4.8 14.9 %copy-start.2 = (s32[4,32,256]{2,1,0:T(8,128)S(1)}, s32[4,32,256]{2,1,0:T(8,128)}, u32[]{:S(2)}) copy-start(s32[4,32,256]{2,1,0:T(8,128)} %param.4) | copy-start | bytes 393220
  4.8 14.9 %copy-start.3 = (s32[32,256]{1,0:T(8,128)S(1)}, s32[32,256]{1,0:T(8,128)}, u32[]{:S(2)}) copy-start(s32[32,256]{1,0:T(8,128)} %param.3) | copy-start | bytes 98308
  4.9 14.9 %collective-permute-start.5 = (s32[5,3,256]{2,1,0:T(4,128)S(1)}, s32[5,3,256]{2,1,0:T(4,128)S(1)}, u32[]{:S(2)}, u32[]{:S(2)}) collective-permute-start(s32[5,3,256]{2,1,0:T(4,128)S(1)} %get-tuple-element.30), channel_id=1, source_target_pairs={{16,0},{32,16},{48,32},{64,48},{80,64},{96,80},{112,96},{128,112},... | collective-permute-start | bytes 46088 | tf_op jit(solution)/shard_map/ppermute | solution.py:29
  13.8 16.9 %collective-permute-start = (f32[2,256,128]{2,1,0:T(8,128)S(1)}, f32[2,256,128]{2,1,0:T(8,128)S(1)}, u32[]{:S(2)}, u32[]{:S(2)}) collective-permute-start(f32[2,256,128]{2,1,0:T(8,128)S(1)} %get-tuple-element.21), channel_id=1, source_target_pairs={{0,16},{16,32},{32,48},{48,64},{64,80},{80,96},{96,112},{112,128},... | collective-permute-start | bytes 786440 | tf_op jit(solution)/shard_map/ppermute | solution.py:27
  17.2 13.5 %collective-permute-start.1 = (f32[2,256,128]{2,1,0:T(8,128)S(1)}, f32[2,256,128]{2,1,0:T(8,128)S(1)}, u32[]{:S(2)}, u32[]{:S(2)}) collective-permute-start(f32[2,256,128]{2,1,0:T(8,128)S(1)} %get-tuple-element.22), channel_id=1, source_target_pairs={{16,0},{32,16},{48,32},{64,48},{80,64},{96,80},{112,96},{128,112},... | collective-permute-start | bytes 786440 | tf_op jit(solution)/shard_map/ppermute | solution.py:29
  19.7 11.0 %copy-start.1 = (f32[128,32,256]{0,2,1:T(8,128)S(1)}, f32[128,32,256]{0,2,1:T(8,128)}, u32[]{:S(2)}) copy-start(f32[128,32,256]{0,2,1:T(8,128)} %copy.15) | copy-start | bytes 12582916
  19.9 2.9 %collective-permute-start.6 = (s32[5,38,3]{2,1,0:T(8,128)S(1)}, s32[5,38,3]{2,1,0:T(8,128)S(1)}, u32[]{:S(2)}, u32[]{:S(2)}) collective-permute-start(s32[5,38,3]{2,1,0:T(8,128)S(1)} %get-tuple-element.27), channel_id=1, source_target_pairs={{0,1},{1,2},{2,3},{3,4},{4,5},{5,6},{6,7},{7,8},{8,9},{9,10},{10,1... | collective-permute-start | bytes 6848 | tf_op jit(solution)/shard_map/ppermute | solution.py:27
  21.5 5.3 %collective-permute-start.7 = (s32[5,38,3]{2,1,0:T(8,128)S(1)}, s32[5,38,3]{2,1,0:T(8,128)S(1)}, u32[]{:S(2)}, u32[]{:S(2)}) collective-permute-start(s32[5,38,3]{2,1,0:T(8,128)S(1)} %get-tuple-element.28), channel_id=1, source_target_pairs={{1,0},{2,1},{3,2},{4,3},{5,4},{6,5},{7,6},{8,7},{9,8},{10,9},{11,1... | collective-permute-start | bytes 6848 | tf_op jit(solution)/shard_map/ppermute | solution.py:29
  30.7 8.0 %collective-permute-start.2 = (f32[36,2,128]{2,1,0:T(2,128)S(1)}, f32[36,2,128]{2,1,0:T(2,128)S(1)}, u32[]{:S(2)}, u32[]{:S(2)}) collective-permute-start(f32[36,2,128]{2,1,0:T(2,128)S(1)} %get-tuple-element.19), channel_id=1, source_target_pairs={{0,1},{1,2},{2,3},{3,4},{4,5},{5,6},{6,7},{7,8},{8,9},{9,10},{10,1... | collective-permute-start | bytes 110600 | tf_op jit(solution)/shard_map/ppermute | solution.py:27
  35.9 3.1 %collective-permute-start.3 = (f32[36,2,128]{2,1,0:T(2,128)S(1)}, f32[36,2,128]{2,1,0:T(2,128)S(1)}, u32[]{:S(2)}, u32[]{:S(2)}) collective-permute-start(f32[36,2,128]{2,1,0:T(2,128)S(1)} %get-tuple-element.20), channel_id=1, source_target_pairs={{1,0},{2,1},{3,2},{4,3},{5,4},{6,5},{7,6},{8,7},{9,8},{10,9},{11,1... | collective-permute-start | bytes 110600 | tf_op jit(solution)/shard_map/ppermute | solution.py:29
  67.3 40.1 %copy-start = (f32[32,256,128]{2,1,0:T(8,128)}, f32[32,256,128]{2,1,0:T(8,128)S(1)}, u32[]{:S(2)}) copy-start(f32[32,256,128]{2,1,0:T(8,128)S(1)} %fusion.11) | copy-start | bytes 12582916
  74.2 4.7 %collective-permute-start.9 = (f32[128,128]{0,1:T(8,128)S(1)}, f32[128,128]{0,1:T(8,128)S(1)}, u32[]{:S(2)}, u32[]{:S(2)}) collective-permute-start(f32[128,128]{0,1:T(8,128)S(1)} %convolution_bitcast_fusion.1), channel_id=1, source_target_pairs={{0,2},{1,3},{2,0},{3,1},{4,6},{5,7},{6,4},{7,5},{8,10},{9,11},{10,... | collective-permute-start | bytes 196616 | tf_op jit(solution)/shard_map/ppermute | solution.py:104
  76.7 2.7 %collective-permute-start.8 = (f32[128,128]{0,1:T(8,128)S(1)}, f32[128,128]{0,1:T(8,128)S(1)}, u32[]{:S(2)}, u32[]{:S(2)}) collective-permute-start(f32[128,128]{0,1:T(8,128)S(1)} %convolution_bitcast_fusion.1), channel_id=1, source_target_pairs={{0,1},{1,0},{2,3},{3,2},{4,5},{5,4},{6,7},{7,6},{8,9},{9,8},{10,11... | collective-permute-start | bytes 196616 | tf_op jit(solution)/shard_map/ppermute | solution.py:104
  78.4 4.2 %collective-permute-start.10 = (f32[128,128]{0,1:T(8,128)S(1)}, f32[128,128]{0,1:T(8,128)S(1)}, u32[]{:S(2)}, u32[]{:S(2)}) collective-permute-start(f32[128,128]{0,1:T(8,128)S(1)} %convolution_bitcast_fusion.1), channel_id=1, source_target_pairs={{0,3},{1,2},{2,1},{3,0},{4,7},{5,6},{6,5},{7,4},{8,11},{9,10},{10,... | collective-permute-start | bytes 196616 | tf_op jit(solution)/shard_map/ppermute | solution.py:104
  82.7 10.3 %collective-permute-start.13 = (f32[128,128]{0,1:T(8,128)S(1)}, f32[128,128]{0,1:T(8,128)S(1)}, u32[]{:S(2)}, u32[]{:S(2)}) collective-permute-start(f32[128,128]{0,1:T(8,128)S(1)} %add_add_fusion.2), channel_id=1, source_target_pairs={{0,12},{1,13},{2,14},{3,15},{4,8},{5,9},{6,10},{7,11},{8,4},{9,5},... | collective-permute-start | bytes 196616 | tf_op jit(solution)/shard_map/ppermute | solution.py:104
  87.3 10.6 %collective-permute-start.12 = (f32[128,128]{0,1:T(8,128)S(1)}, f32[128,128]{0,1:T(8,128)S(1)}, u32[]{:S(2)}, u32[]{:S(2)}) collective-permute-start(f32[128,128]{0,1:T(8,128)S(1)} %add_add_fusion.2), channel_id=1, source_target_pairs={{0,8},{1,9},{2,10},{3,11},{4,12},{5,13},{6,14},{7,15},{8,0},{9,1},... | collective-permute-start | bytes 196616 | tf_op jit(solution)/shard_map/ppermute | solution.py:104
  92.9 6.3 %collective-permute-start.11 = (f32[128,128]{0,1:T(8,128)S(1)}, f32[128,128]{0,1:T(8,128)S(1)}, u32[]{:S(2)}, u32[]{:S(2)}) collective-permute-start(f32[128,128]{0,1:T(8,128)S(1)} %add_add_fusion.2), channel_id=1, source_target_pairs={{0,4},{1,5},{2,6},{3,7},{4,0},{5,1},{6,2},{7,3},{8,12},{9,13},{10,... | collective-permute-start | bytes 196616 | tf_op jit(solution)/shard_map/ppermute | solution.py:104
  99.2 5.0 %collective-permute-start.16 = (f32[128,128]{0,1:T(8,128)S(1)}, f32[128,128]{0,1:T(8,128)S(1)}, u32[]{:S(2)}, u32[]{:S(2)}) collective-permute-start(f32[128,128]{0,1:T(8,128)S(1)} %add_add_fusion.1), channel_id=1, source_target_pairs={{0,48},{16,32},{32,16},{48,0},{64,112},{80,96},{96,80},{112,64},{1... | collective-permute-start | bytes 196616 | tf_op jit(solution)/shard_map/ppermute | solution.py:104
  100.8 5.8 %collective-permute-start.15 = (f32[128,128]{0,1:T(8,128)S(1)}, f32[128,128]{0,1:T(8,128)S(1)}, u32[]{:S(2)}, u32[]{:S(2)}) collective-permute-start(f32[128,128]{0,1:T(8,128)S(1)} %add_add_fusion.1), channel_id=1, source_target_pairs={{0,32},{16,48},{32,0},{48,16},{64,96},{80,112},{96,64},{112,80},{1... | collective-permute-start | bytes 196616 | tf_op jit(solution)/shard_map/ppermute | solution.py:104
  103.1 4.3 %collective-permute-start.14 = (f32[128,128]{0,1:T(8,128)S(1)}, f32[128,128]{0,1:T(8,128)S(1)}, u32[]{:S(2)}, u32[]{:S(2)}) collective-permute-start(f32[128,128]{0,1:T(8,128)S(1)} %add_add_fusion.1), channel_id=1, source_target_pairs={{0,16},{16,0},{32,48},{48,32},{64,80},{80,64},{96,112},{112,96},{1... | collective-permute-start | bytes 196616 | tf_op jit(solution)/shard_map/ppermute | solution.py:104
  107.4 9.1 %collective-permute-start.19 = (f32[128,128]{0,1:T(8,128)S(1)}, f32[128,128]{0,1:T(8,128)S(1)}, u32[]{:S(2)}, u32[]{:S(2)}) collective-permute-start(f32[128,128]{0,1:T(8,128)S(1)} %add_add_fusion), channel_id=1, source_target_pairs={{0,192},{16,208},{32,224},{48,240},{64,128},{80,144},{96,160},{112... | collective-permute-start | bytes 196616 | tf_op jit(solution)/shard_map/ppermute | solution.py:104
  113.5 5.8 %collective-permute-start.18 = (f32[128,128]{0,1:T(8,128)S(1)}, f32[128,128]{0,1:T(8,128)S(1)}, u32[]{:S(2)}, u32[]{:S(2)}) collective-permute-start(f32[128,128]{0,1:T(8,128)S(1)} %add_add_fusion), channel_id=1, source_target_pairs={{0,128},{16,144},{32,160},{48,176},{64,192},{80,208},{96,224},{112... | collective-permute-start | bytes 196616 | tf_op jit(solution)/shard_map/ppermute | solution.py:104
  114.1 5.1 %collective-permute-start.17 = (f32[128,128]{0,1:T(8,128)S(1)}, f32[128,128]{0,1:T(8,128)S(1)}, u32[]{:S(2)}, u32[]{:S(2)}) collective-permute-start(f32[128,128]{0,1:T(8,128)S(1)} %add_add_fusion), channel_id=1, source_target_pairs={{0,64},{16,80},{32,96},{48,112},{64,0},{80,16},{96,32},{112,48},{1... | collective-permute-start | bytes 196616 | tf_op jit(solution)/shard_map/ppermute | solution.py:104

commit v5 on v4

--- a/solution.py
+++ b/solution.py
@@ -1,6 +1,8 @@
 import jax
 import jax.numpy as jnp
 from jax import lax
+from jax.experimental import pallas as pl
+from jax.experimental.pallas import tpu as pltpu
 from jax.sharding import PartitionSpec as P
 
 INV_SIGMA = 1.0 / 40.0
@@ -118,6 +120,43 @@
         block = exchange_sum(block, axis, low_bit, bits)
         low_bit += bits
     return block
+
+
+def factor_kernel(gram_ref, upper_ref, inverse_ref, work_ref):
+    size = gram_ref.shape[0]
+    work_ref[...] = gram_ref[...]
+    sub = lax.broadcasted_iota(jnp.int32, (size, size), 0)
+    lane = lax.broadcasted_iota(jnp.int32, (size, size), 1)
+    upper_ref[...] = jnp.zeros((size, size), jnp.float32)
+    inverse_ref[...] = jnp.where(sub == lane, 1.0, 0.0).astype(jnp.float32)
+    lane_row = lax.broadcasted_iota(jnp.int32, (1, size), 1)
+    sub_col = lax.broadcasted_iota(jnp.int32, (size, 1), 0)
+
+    def step(j, carry):
+        row = work_ref[pl.ds(j, 1), :]
+        pivot = jnp.sum(jnp.where(lane_row == j, row, 0.0), axis=1, keepdims=True)
+        root = jnp.sqrt(pivot)
+        urow = jnp.where(lane_row >= j, row / root, 0.0)
+        column = jnp.transpose(jnp.broadcast_to(row, (8, size)))[:, :1]
+        lcol = jnp.where(sub_col >= j, column / root, 0.0)
+        work_ref[...] = work_ref[...] - lcol * urow
+        upper_ref[pl.ds(j, 1), :] = urow
+        brow = inverse_ref[pl.ds(j, 1), :] / root
+        below = jnp.where(sub_col > j, lcol, 0.0)
+        inverse_ref[...] = inverse_ref[...] - below * brow
+        inverse_ref[pl.ds(j, 1), :] = brow
+        return carry
+
+    lax.fori_loop(0, size, step, 0)
+
+
+def factor_and_inverse(gram):
+    size = gram.shape[0]
+    return pl.pallas_call(
+        factor_kernel,
+        out_shape=(jax.ShapeDtypeStruct((size, size), jnp.float32),) * 2,
+        scratch_shapes=[pltpu.VMEM((size, size), jnp.float32)],
+    )(gram)
 
 
 def per_device(intensity, agreement, basis_block):
@@ -150,15 +189,12 @@
         precision=lax.Precision.HIGHEST, preferred_element_type=jnp.float32,
     )
     gram = all_sum(all_sum(gram_local, "col"), "row") / pixel_total
-    factor = jnp.linalg.cholesky(gram)
-    inverse = jax.scipy.linalg.solve_triangular(
-        factor, jnp.eye(vectors, dtype=jnp.float32), lower=True
-    )
+    upper, inverse = factor_and_inverse(gram)
     ortho = jnp.einsum(
         "kj,rcj->krc", inverse, filtered,
         precision=lax.Precision.HIGHEST, preferred_element_type=jnp.float32,
     )
-    return (ortho, factor.T)
+    return (ortho, upper)
 
 
 def solution(mesh):

time: 154 us -> 162 us (1.052)
  Pallas kernels: 0 us -> 31.4 us
  other arithmetic: 52.8 us -> 30.5 us
    pallas_call x0 -> x1, Pallas kernels: none -> 31.4 us  [factor_and_inverse(): pl.pallas_call(factor_kernel, out_shape=(jax.ShapeDtypeStruct((size, size...]
    another operation x4 -> x0, other arithmetic: 22.2 us -> none  [the longest x3 12.4 us: per_device(): factor = jnp.linalg.cholesky(gram)]
    unnamed x11 -> x10, local copies, waits for them, and re-layouts: 10.5 us -> 9.76 us
  transfers between devices with their start and end apart: 20 -> 20, of which waited for: 11 -> 10; matrix products, arithmetic and copies ran while one was open for 8% -> 7% of each run, Pallas kernels for 0% -> 0%
where the time goes in v5:
time: 162 us; the launch traced here: 161 us
  starting transfers between devices  47.9 us (30%)
  Pallas kernels  31.4 us (19%)
  other arithmetic  30.5 us (19%)
  waiting for transfers between devices  22.2 us (14%)
  local copies, waits for them, and re-layouts  15.5 us (10%)
  matrix products  12.8 us (8%)
    pallas_call x1, Pallas kernels, factor_and_inverse(): pl.pallas_call(factor_kernel, out_shape=(jax.ShapeDtypeStruct((size, size...  31.4 us
    ppermute x12, starting transfers between devices, exchange_sum(): received.append(lax.ppermute(block, axis, route))  26.8 us
    ppermute x12, waiting for transfers between devices, exchange_sum(): received.append(lax.ppermute(block, axis, route))  18 us
    ppermute x4, starting transfers between devices, padded(): lax.ppermute(tail, axis, [(i, (i + 1) % count) for i in range(ends)])  13.5 us
    mul x1, other arithmetic, apply_pixels(): lifted = values_in * scales[:, :, None]  13.4 us
    sub x1, other arithmetic, apply_pixels(): shifted_pixels(values_in, 0, 0) - shifted(scales, 0, 0)[:, :, None] * summed  12.9 us
    unnamed x10, local copies, waits for them, and re-layouts  9.76 us
    ppermute x4, starting transfers between devices, padded(): lax.ppermute(head, axis, [((i + 1) % count, i) for i in range(ends)])  7.61 us
  transfers between devices with their start and end apart: 20, of which 10 were waited for; matrix products, arithmetic and copies ran while one was open for 7% of the time, Pallas kernels for 0%

profile of v5, /device:TPU:2, one launch (start us, length us, event | category | flops | bytes accessed | tf_op | source)
XLA Modules:
  0.0 161.4 jit_solution(12642184319125539276)
XLA Ops:
  0.6 0.8 pad_add_fusion.3
  1.4 3.4 %collective-permute-start.4 = (s32[5,3,256]{2,1,0:T(4,128)S(1)}, s32[5,3,256]{2,1,0:T(4,128)S(1)}, u32[]{:S(2)}, u32[]{:S(2)}) collective-permute-start(s32[5,3,256]{2,1,0:T(4,128)S(1)} %get-tuple-element.33), channel_id=1, source_target_pairs={{0,16},{16,32},{32,48},{48,64},{64,80},{80,96},{96,112},{112,128},... | collective-permute-start | bytes 46088 | tf_op jit(solution)/shard_map/ppermute | solution.py:29
  4.8 0.0 copy-start.2
  4.8 0.0 copy-start.3
  4.9 2.6 %collective-permute-start.5 = (s32[5,3,256]{2,1,0:T(4,128)S(1)}, s32[5,3,256]{2,1,0:T(4,128)S(1)}, u32[]{:S(2)}, u32[]{:S(2)}) collective-permute-start(s32[5,3,256]{2,1,0:T(4,128)S(1)} %get-tuple-element.34), channel_id=1, source_target_pairs={{16,0},{32,16},{48,32},{64,48},{80,64},{96,80},{112,96},{128,112},... | collective-permute-start | bytes 46088 | tf_op jit(solution)/shard_map/ppermute | solution.py:31
  7.4 5.3 %copy.9 = f32[128,32,256]{0,2,1:T(8,128)} copy(f32[128,32,256]{2,1,0:T(8,128)} %param.5) | data formatting | bytes 8388608 | tf_op args[2]
  12.7 1.1 fusion.82
  13.8 3.4 %collective-permute-start = (f32[2,256,128]{2,1,0:T(8,128)S(1)}, f32[2,256,128]{2,1,0:T(8,128)S(1)}, u32[]{:S(2)}, u32[]{:S(2)}) collective-permute-start(f32[2,256,128]{2,1,0:T(8,128)S(1)} %get-tuple-element.25), channel_id=1, source_target_pairs={{0,16},{16,32},{32,48},{48,64},{64,80},{80,96},{96,112},{112,128},... | collective-permute-start | bytes 786440 | tf_op jit(solution)/shard_map/ppermute | solution.py:29
  17.2 2.5 %collective-permute-start.1 = (f32[2,256,128]{2,1,0:T(8,128)S(1)}, f32[2,256,128]{2,1,0:T(8,128)S(1)}, u32[]{:S(2)}, u32[]{:S(2)}) collective-permute-start(f32[2,256,128]{2,1,0:T(8,128)S(1)} %get-tuple-element.26), channel_id=1, source_target_pairs={{16,0},{32,16},{48,32},{64,48},{80,64},{96,80},{112,96},{128,112},... | collective-permute-start | bytes 786440 | tf_op jit(solution)/shard_map/ppermute | solution.py:31
  19.7 0.0 copy-start.1
  19.7 0.0 collective-permute-done.5
  19.8 0.1 fusion.83
  19.9 1.6 collective-permute-start.6
  21.5 1.3 collective-permute-start.7
  22.8 0.1 broadcast_multiply_fusion.2
  22.8 0.0 collective-permute-done.6
  22.8 4.0 %collective-permute-done.7 = s32[5,38,3]{2,1,0:T(8,128)S(1)} collective-permute-done((s32[5,38,3]{2,1,0:T(8,128)S(1)}, s32[5,38,3]{2,1,0:T(8,128)S(1)}, u32[]{:S(2)}, u32[]{:S(2)}) %collective-permute-start.7) | collective-permute-done | bytes 2312 | tf_op jit(solution)/shard_map/ppermute | solution.py:31
  26.8 0.2 pad_add_fusion
  27.1 0.1 fusion.67
  27.2 0.4 add_rsqrt_fusion
  27.5 0.7 slice_bitcast_fusion.18
  28.3 0.1 slice_bitcast_fusion.6
  28.4 0.7 slice_bitcast_fusion.16
  29.1 0.1 slice_bitcast_fusion.4
  29.2 0.1 slice_bitcast_fusion.2
  29.3 0.7 slice_bitcast_fusion.14
  30.0 0.7 slice_bitcast_fusion
  30.7 5.2 %collective-permute-start.2 = (f32[36,2,128]{2,1,0:T(2,128)S(1)}, f32[36,2,128]{2,1,0:T(2,128)S(1)}, u32[]{:S(2)}, u32[]{:S(2)}) collective-permute-start(f32[36,2,128]{2,1,0:T(2,128)S(1)} %get-tuple-element.23), channel_id=1, source_target_pairs={{0,1},{1,2},{2,3},{3,4},{4,5},{5,6},{6,7},{7,8},{8,9},{9,10},{10,1... | collective-permute-start | bytes 110600 | tf_op jit(solution)/shard_map/ppermute | solution.py:29
  35.9 1.3 collective-permute-start.3
  37.2 0.7 slice_bitcast_fusion.12
  37.9 0.7 slice.398
  38.6 0.1 slice.380
  38.7 0.0 collective-permute-done.2
  38.7 0.3 collective-permute-done.3
  39.0 1.9 %pad_maximum_fusion = (f32[36,260,128]{2,1,0:T(8,128)S(1)}, f32[36,260,128]{2,1,0:T(8,128)S(1)}) fusion(f32[36,2,128]{2,1,0:T(2,128)S(1)} %collective-permute-done.3, f32[2,256,128]{2,1,0:T(8,128)S(1)} %collective-permute-done.1, f32[32,256,128]{2,1,0:T(8,128)S(1)} %bitcast.62, f32[2,256,128]{2,1,0:T(8,128)S(1)} %collective-permute-done, ...), kind=kLoop, calls=%fused_computation | loop fusion | flops 5990400 | bytes 14414400 | tf_op jit(solution)/shard_map/concatenate | solution.py:27
  41.0 13.4 %broadcast_multiply_fusion.1 = (f32[34,258,128]{2,1,0:T(8,128)S(1)}, f32[34,258,128]{2,1,0:T(8,128)S(1)}) fusion(f32[34,258]{1,0:T(8,128)S(1)} %slice.380, f32[36,260,128]{2,1,0:T(8,128)S(1)} %get-tuple-element.22, f32[34,258]{1,0:T(8,128)S(1)} %get-tuple-element.35, f32[34,258]{1,0:T(8,128)} %get-tuple-element.36, f32[34,258]{1,0:T(8,128)S(1)} %get-tuple-element.37, ...), kind=kLoop, calls=%fused_computation.36 | loop fusion | flops 20210688 | bytes 49719696 | tf_op jit(solution)/shard_map/mul | solution.py:92
  54.4 12.9 %fusion.11 = f32[32,256,128]{2,1,0:T(8,128)S(1)} fusion(f32[34,258,128]{2,1,0:T(8,128)S(1)} %get-tuple-element.10, f32[34,258,128]{2,1,0:T(8,128)S(1)} %get-tuple-element.11, f32[32,256]{1,0:T(8,128)} %get-tuple-element.43, f32[32,256]{1,0:T(8,128)} %get-tuple-element.44, f32[32,256]{1,0:T(8,128)} %get-tuple-element.45, f32[32,256]{1,0:T(8,128)} %get-tuple-element.46, ...), kind=kLoop, calls=%fused_computation.21 | loop fusion | flops 17825792 | bytes 42237952 | tf_op jit(solution)/shard_map/sub | solution.py:97
  67.3 0.0 copy-start
  67.3 6.9 %convolution_bitcast_fusion = f32[128,128]{1,0:T(8,128)S(1)} fusion(f32[32,256,128]{2,1,0:T(8,128)S(1)} %fusion.11), kind=kOutput, calls=%fused_computation.37 | convolution fusion | flops 1610612736 | bytes 4259840 | tf_op jit(solution)/shard_map/rck,rcj->kj/dot_general | solution.py:187
  74.2 4.1 %collective-permute-start.10 = (f32[128,128]{1,0:T(8,128)S(1)}, f32[128,128]{1,0:T(8,128)S(1)}, u32[]{:S(2)}, u32[]{:S(2)}) collective-permute-start(f32[128,128]{1,0:T(8,128)S(1)} %convolution_bitcast_fusion), channel_id=1, source_target_pairs={{0,3},{1,2},{2,1},{3,0},{4,7},{5,6},{6,5},{7,4},{8,11},{9,10},{10,... | collective-permute-start | bytes 196616 | tf_op jit(solution)/shard_map/ppermute | solution.py:106
  78.3 0.1 collective-permute-start.9
  78.4 0.3 collective-permute-start.8
  78.7 1.9 %collective-permute-done.10 = f32[128,128]{1,0:T(8,128)S(1)} collective-permute-done((f32[128,128]{1,0:T(8,128)S(1)}, f32[128,128]{1,0:T(8,128)S(1)}, u32[]{:S(2)}, u32[]{:S(2)}) %collective-permute-start.10) | collective-permute-done | bytes 65568 | tf_op jit(solution)/shard_map/ppermute | solution.py:106
  80.5 2.0 %collective-permute-done.9 = f32[128,128]{1,0:T(8,128)S(1)} collective-permute-done((f32[128,128]{1,0:T(8,128)S(1)}, f32[128,128]{1,0:T(8,128)S(1)}, u32[]{:S(2)}, u32[]{:S(2)}) %collective-permute-start.9) | collective-permute-done | bytes 65568 | tf_op jit(solution)/shard_map/ppermute | solution.py:106
  82.6 0.0 collective-permute-done.8
  82.6 4.4 %collective-permute-start.13 = (f32[128,128]{1,0:T(8,128)S(1)}, f32[128,128]{1,0:T(8,128)S(1)}, u32[]{:S(2)}, u32[]{:S(2)}) collective-permute-start(f32[128,128]{1,0:T(8,128)S(1)} %add_add_fusion.2), channel_id=1, source_target_pairs={{0,12},{1,13},{2,14},{3,15},{4,8},{5,9},{6,10},{7,11},{8,4},{9,5},... | collective-permute-start | bytes 196616 | tf_op jit(solution)/shard_map/ppermute | solution.py:106
  87.0 5.9 %collective-permute-start.12 = (f32[128,128]{1,0:T(8,128)S(1)}, f32[128,128]{1,0:T(8,128)S(1)}, u32[]{:S(2)}, u32[]{:S(2)}) collective-permute-start(f32[128,128]{1,0:T(8,128)S(1)} %add_add_fusion.2), channel_id=1, source_target_pairs={{0,8},{1,9},{2,10},{3,11},{4,12},{5,13},{6,14},{7,15},{8,0},{9,1},... | collective-permute-start | bytes 196616 | tf_op jit(solution)/shard_map/ppermute | solution.py:106
  92.9 0.0 collective-permute-start.11
  92.9 2.8 %collective-permute-done.12 = f32[128,128]{1,0:T(8,128)S(1)} collective-permute-done((f32[128,128]{1,0:T(8,128)S(1)}, f32[128,128]{1,0:T(8,128)S(1)}, u32[]{:S(2)}, u32[]{:S(2)}) %collective-permute-start.12) | collective-permute-done | bytes 65568 | tf_op jit(solution)/shard_map/ppermute | solution.py:106
  95.7 3.2 %collective-permute-done.11 = f32[128,128]{1,0:T(8,128)S(1)} collective-permute-done((f32[128,128]{1,0:T(8,128)S(1)}, f32[128,128]{1,0:T(8,128)S(1)}, u32[]{:S(2)}, u32[]{:S(2)}) %collective-permute-start.11) | collective-permute-done | bytes 65568 | tf_op jit(solution)/shard_map/ppermute | solution.py:106
  99.0 1.6 collective-permute-start.16
  100.5 2.3 %collective-permute-start.15 = (f32[128,128]{1,0:T(8,128)S(1)}, f32[128,128]{1,0:T(8,128)S(1)}, u32[]{:S(2)}, u32[]{:S(2)}) collective-permute-start(f32[128,128]{1,0:T(8,128)S(1)} %add_add_fusion.1), channel_id=1, source_target_pairs={{0,32},{16,48},{32,0},{48,16},{64,96},{80,112},{96,64},{112,80},{1... | collective-permute-start | bytes 196616 | tf_op jit(solution)/shard_map/ppermute | solution.py:106
  102.9 1.1 collective-permute-start.14
  103.9 2.4 %collective-permute-done.15 = f32[128,128]{1,0:T(8,128)S(1)} collective-permute-done((f32[128,128]{1,0:T(8,128)S(1)}, f32[128,128]{1,0:T(8,128)S(1)}, u32[]{:S(2)}, u32[]{:S(2)}) %collective-permute-start.15) | collective-permute-done | bytes 65568 | tf_op jit(solution)/shard_map/ppermute | solution.py:106
  106.3 0.8 collective-permute-done.14
  107.1 6.1 %collective-permute-start.19 = (f32[128,128]{1,0:T(8,128)S(1)}, f32[128,128]{1,0:T(8,128)S(1)}, u32[]{:S(2)}, u32[]{:S(2)}) collective-permute-start(f32[128,128]{1,0:T(8,128)S(1)} %add_add_fusion), channel_id=1, source_target_pairs={{0,192},{16,208},{32,224},{48,240},{64,128},{80,144},{96,160},{112... | collective-permute-start | bytes 196616 | tf_op jit(solution)/shard_map/ppermute | solution.py:106
  113.3 0.6 collective-permute-start.18
  113.9 0.3 collective-permute-start.17
  114.2 1.6 collective-permute-done.19
  115.8 3.3 %collective-permute-done.18 = f32[128,128]{1,0:T(8,128)S(1)} collective-permute-done((f32[128,128]{1,0:T(8,128)S(1)}, f32[128,128]{1,0:T(8,128)S(1)}, u32[]{:S(2)}, u32[]{:S(2)}) %collective-permute-start.18) | collective-permute-done | bytes 65568 | tf_op jit(solution)/shard_map/ppermute | solution.py:106
  119.0 0.6 add_multiply_fusion.gram_ref
  119.7 31.4 %shard_map.50 = (f32[128,128]{1,0:T(8,128)}, f32[128,128]{1,0:T(8,128)}) custom-call(f32[128,128]{1,0:T(8,128)} %add_multiply_fusion.gram_ref), custom_call_target="tpu_custom_call" | custom-call | tf_op jit(solution)/shard_map/pallas_call | solution.py:155
  151.1 5.9 %fusion.18 = f32[128,32,256]{2,0,1:T(8,128)S(1)} fusion(f32[32,256,128]{2,1,0:T(8,128)} %copy-done, f32[128,128]{1,0:T(8,128)} %get-tuple-element.4), kind=kOutput, calls=%fused_computation.49 | convolution fusion | flops 1610612736 | bytes 8454144 | tf_op jit(solution)/shard_map/kj,rcj->krc/dot_general | solution.py:193
  157.0 4.4 %copy.11 = f32[128,32,256]{2,1,0:T(8,128)} copy(f32[128,32,256]{2,0,1:T(8,128)S(1)} %fusion.18) | data formatting | bytes 8388608
  (19 shorter events, 0.2 us)
Async XLA Ops:
  1.4 18.3 %collective-permute-start.4 = (s32[5,3,256]{2,1,0:T(4,128)S(1)}, s32[5,3,256]{2,1,0:T(4,128)S(1)}, u32[]{:S(2)}, u32[]{:S(2)}) collective-permute-start(s32[5,3,256]{2,1,0:T(4,128)S(1)} %get-tuple-element.33), channel_id=1, source_target_pairs={{0,16},{16,32},{32,48},{48,64},{64,80},{80,96},{96,112},{112,128},... | collective-permute-start | bytes 46088 | tf_op jit(solution)/shard_map/ppermute | solution.py:29
  4.8 14.9 %copy-start.2 = (s32[4,32,256]{2,1,0:T(8,128)S(1)}, s32[4,32,256]{2,1,0:T(8,128)}, u32[]{:S(2)}) copy-start(s32[4,32,256]{2,1,0:T(8,128)} %param.4) | copy-start | bytes 393220
  4.8 14.9 %copy-start.3 = (s32[32,256]{1,0:T(8,128)S(1)}, s32[32,256]{1,0:T(8,128)}, u32[]{:S(2)}) copy-start(s32[32,256]{1,0:T(8,128)} %param.3) | copy-start | bytes 98308
  4.9 14.9 %collective-permute-start.5 = (s32[5,3,256]{2,1,0:T(4,128)S(1)}, s32[5,3,256]{2,1,0:T(4,128)S(1)}, u32[]{:S(2)}, u32[]{:S(2)}) collective-permute-start(s32[5,3,256]{2,1,0:T(4,128)S(1)} %get-tuple-element.34), channel_id=1, source_target_pairs={{16,0},{32,16},{48,32},{64,48},{80,64},{96,80},{112,96},{128,112},... | collective-permute-start | bytes 46088 | tf_op jit(solution)/shard_map/ppermute | solution.py:31
  13.8 16.9 %collective-permute-start = (f32[2,256,128]{2,1,0:T(8,128)S(1)}, f32[2,256,128]{2,1,0:T(8,128)S(1)}, u32[]{:S(2)}, u32[]{:S(2)}) collective-permute-start(f32[2,256,128]{2,1,0:T(8,128)S(1)} %get-tuple-element.25), channel_id=1, source_target_pairs={{0,16},{16,32},{32,48},{48,64},{64,80},{80,96},{96,112},{112,128},... | collective-permute-start | bytes 786440 | tf_op jit(solution)/shard_map/ppermute | solution.py:29
  17.2 13.5 %collective-permute-start.1 = (f32[2,256,128]{2,1,0:T(8,128)S(1)}, f32[2,256,128]{2,1,0:T(8,128)S(1)}, u32[]{:S(2)}, u32[]{:S(2)}) collective-permute-start(f32[2,256,128]{2,1,0:T(8,128)S(1)} %get-tuple-element.26), channel_id=1, source_target_pairs={{16,0},{32,16},{48,32},{64,48},{80,64},{96,80},{112,96},{128,112},... | collective-permute-start | bytes 786440 | tf_op jit(solution)/shard_map/ppermute | solution.py:31
  19.7 11.0 %copy-start.1 = (f32[128,32,256]{0,2,1:T(8,128)S(1)}, f32[128,32,256]{0,2,1:T(8,128)}, u32[]{:S(2)}) copy-start(f32[128,32,256]{0,2,1:T(8,128)} %copy.9) | copy-start | bytes 12582916
  19.9 2.9 %collective-permute-start.6 = (s32[5,38,3]{2,1,0:T(8,128)S(1)}, s32[5,38,3]{2,1,0:T(8,128)S(1)}, u32[]{:S(2)}, u32[]{:S(2)}) collective-permute-start(s32[5,38,3]{2,1,0:T(8,128)S(1)} %get-tuple-element.31), channel_id=1, source_target_pairs={{0,1},{1,2},{2,3},{3,4},{4,5},{5,6},{6,7},{7,8},{8,9},{9,10},{10,1... | collective-permute-start | bytes 6848 | tf_op jit(solution)/shard_map/ppermute | solution.py:29
  21.5 5.3 %collective-permute-start.7 = (s32[5,38,3]{2,1,0:T(8,128)S(1)}, s32[5,38,3]{2,1,0:T(8,128)S(1)}, u32[]{:S(2)}, u32[]{:S(2)}) collective-permute-start(s32[5,38,3]{2,1,0:T(8,128)S(1)} %get-tuple-element.32), channel_id=1, source_target_pairs={{1,0},{2,1},{3,2},{4,3},{5,4},{6,5},{7,6},{8,7},{9,8},{10,9},{11,1... | collective-permute-start | bytes 6848 | tf_op jit(solution)/shard_map/ppermute | solution.py:31
  30.7 8.0 %collective-permute-start.2 = (f32[36,2,128]{2,1,0:T(2,128)S(1)}, f32[36,2,128]{2,1,0:T(2,128)S(1)}, u32[]{:S(2)}, u32[]{:S(2)}) collective-permute-start(f32[36,2,128]{2,1,0:T(2,128)S(1)} %get-tuple-element.23), channel_id=1, source_target_pairs={{0,1},{1,2},{2,3},{3,4},{4,5},{5,6},{6,7},{7,8},{8,9},{9,10},{10,1... | collective-permute-start | bytes 110600 | tf_op jit(solution)/shard_map/ppermute | solution.py:29
  35.9 3.1 %collective-permute-start.3 = (f32[36,2,128]{2,1,0:T(2,128)S(1)}, f32[36,2,128]{2,1,0:T(2,128)S(1)}, u32[]{:S(2)}, u32[]{:S(2)}) collective-permute-start(f32[36,2,128]{2,1,0:T(2,128)S(1)} %get-tuple-element.24), channel_id=1, source_target_pairs={{1,0},{2,1},{3,2},{4,3},{5,4},{6,5},{7,6},{8,7},{9,8},{10,9},{11,1... | collective-permute-start | bytes 110600 | tf_op jit(solution)/shard_map/ppermute | solution.py:31
  67.3 39.8 %copy-start = (f32[32,256,128]{2,1,0:T(8,128)}, f32[32,256,128]{2,1,0:T(8,128)S(1)}, u32[]{:S(2)}) copy-start(f32[32,256,128]{2,1,0:T(8,128)S(1)} %fusion.11) | copy-start | bytes 12582916
  74.2 6.3 %collective-permute-start.10 = (f32[128,128]{1,0:T(8,128)S(1)}, f32[128,128]{1,0:T(8,128)S(1)}, u32[]{:S(2)}, u32[]{:S(2)}) collective-permute-start(f32[128,128]{1,0:T(8,128)S(1)} %convolution_bitcast_fusion), channel_id=1, source_target_pairs={{0,3},{1,2},{2,1},{3,0},{4,7},{5,6},{6,5},{7,4},{8,11},{9,10},{10,... | collective-permute-start | bytes 196616 | tf_op jit(solution)/shard_map/ppermute | solution.py:106
  78.3 4.3 %collective-permute-start.9 = (f32[128,128]{1,0:T(8,128)S(1)}, f32[128,128]{1,0:T(8,128)S(1)}, u32[]{:S(2)}, u32[]{:S(2)}) collective-permute-start(f32[128,128]{1,0:T(8,128)S(1)} %convolution_bitcast_fusion), channel_id=1, source_target_pairs={{0,2},{1,3},{2,0},{3,1},{4,6},{5,7},{6,4},{7,5},{8,10},{9,11},{10,... | collective-permute-start | bytes 196616 | tf_op jit(solution)/shard_map/ppermute | solution.py:106
  78.4 4.2 %collective-permute-start.8 = (f32[128,128]{1,0:T(8,128)S(1)}, f32[128,128]{1,0:T(8,128)S(1)}, u32[]{:S(2)}, u32[]{:S(2)}) collective-permute-start(f32[128,128]{1,0:T(8,128)S(1)} %convolution_bitcast_fusion), channel_id=1, source_target_pairs={{0,1},{1,0},{2,3},{3,2},{4,5},{5,4},{6,7},{7,6},{8,9},{9,8},{10,11... | collective-permute-start | bytes 196616 | tf_op jit(solution)/shard_map/ppermute | solution.py:106
  82.6 10.3 %collective-permute-start.13 = (f32[128,128]{1,0:T(8,128)S(1)}, f32[128,128]{1,0:T(8,128)S(1)}, u32[]{:S(2)}, u32[]{:S(2)}) collective-permute-start(f32[128,128]{1,0:T(8,128)S(1)} %add_add_fusion.2), channel_id=1, source_target_pairs={{0,12},{1,13},{2,14},{3,15},{4,8},{5,9},{6,10},{7,11},{8,4},{9,5},... | collective-permute-start | bytes 196616 | tf_op jit(solution)/shard_map/ppermute | solution.py:106
  87.0 8.7 %collective-permute-start.12 = (f32[128,128]{1,0:T(8,128)S(1)}, f32[128,128]{1,0:T(8,128)S(1)}, u32[]{:S(2)}, u32[]{:S(2)}) collective-permute-start(f32[128,128]{1,0:T(8,128)S(1)} %add_add_fusion.2), channel_id=1, source_target_pairs={{0,8},{1,9},{2,10},{3,11},{4,12},{5,13},{6,14},{7,15},{8,0},{9,1},... | collective-permute-start | bytes 196616 | tf_op jit(solution)/shard_map/ppermute | solution.py:106
  92.9 6.1 %collective-permute-start.11 = (f32[128,128]{1,0:T(8,128)S(1)}, f32[128,128]{1,0:T(8,128)S(1)}, u32[]{:S(2)}, u32[]{:S(2)}) collective-permute-start(f32[128,128]{1,0:T(8,128)S(1)} %add_add_fusion.2), channel_id=1, source_target_pairs={{0,4},{1,5},{2,6},{3,7},{4,0},{5,1},{6,2},{7,3},{8,12},{9,13},{10,... | collective-permute-start | bytes 196616 | tf_op jit(solution)/shard_map/ppermute | solution.py:106
  99.0 5.0 %collective-permute-start.16 = (f32[128,128]{1,0:T(8,128)S(1)}, f32[128,128]{1,0:T(8,128)S(1)}, u32[]{:S(2)}, u32[]{:S(2)}) collective-permute-start(f32[128,128]{1,0:T(8,128)S(1)} %add_add_fusion.1), channel_id=1, source_target_pairs={{0,48},{16,32},{32,16},{48,0},{64,112},{80,96},{96,80},{112,64},{1... | collective-permute-start | bytes 196616 | tf_op jit(solution)/shard_map/ppermute | solution.py:106
  100.5 5.8 %collective-permute-start.15 = (f32[128,128]{1,0:T(8,128)S(1)}, f32[128,128]{1,0:T(8,128)S(1)}, u32[]{:S(2)}, u32[]{:S(2)}) collective-permute-start(f32[128,128]{1,0:T(8,128)S(1)} %add_add_fusion.1), channel_id=1, source_target_pairs={{0,32},{16,48},{32,0},{48,16},{64,96},{80,112},{96,64},{112,80},{1... | collective-permute-start | bytes 196616 | tf_op jit(solution)/shard_map/ppermute | solution.py:106
  102.9 4.3 %collective-permute-start.14 = (f32[128,128]{1,0:T(8,128)S(1)}, f32[128,128]{1,0:T(8,128)S(1)}, u32[]{:S(2)}, u32[]{:S(2)}) collective-permute-start(f32[128,128]{1,0:T(8,128)S(1)} %add_add_fusion.1), channel_id=1, source_target_pairs={{0,16},{16,0},{32,48},{48,32},{64,80},{80,64},{96,112},{112,96},{1... | collective-permute-start | bytes 196616 | tf_op jit(solution)/shard_map/ppermute | solution.py:106
  107.1 8.6 %collective-permute-start.19 = (f32[128,128]{1,0:T(8,128)S(1)}, f32[128,128]{1,0:T(8,128)S(1)}, u32[]{:S(2)}, u32[]{:S(2)}) collective-permute-start(f32[128,128]{1,0:T(8,128)S(1)} %add_add_fusion), channel_id=1, source_target_pairs={{0,192},{16,208},{32,224},{48,240},{64,128},{80,144},{96,160},{112... | collective-permute-start | bytes 196616 | tf_op jit(solution)/shard_map/ppermute | solution.py:106
  113.3 5.8 %collective-permute-start.18 = (f32[128,128]{1,0:T(8,128)S(1)}, f32[128,128]{1,0:T(8,128)S(1)}, u32[]{:S(2)}, u32[]{:S(2)}) collective-permute-start(f32[128,128]{1,0:T(8,128)S(1)} %add_add_fusion), channel_id=1, source_target_pairs={{0,128},{16,144},{32,160},{48,176},{64,192},{80,208},{96,224},{112... | collective-permute-start | bytes 196616 | tf_op jit(solution)/shard_map/ppermute | solution.py:106
  113.9 5.1 %collective-permute-start.17 = (f32[128,128]{1,0:T(8,128)S(1)}, f32[128,128]{1,0:T(8,128)S(1)}, u32[]{:S(2)}, u32[]{:S(2)}) collective-permute-start(f32[128,128]{1,0:T(8,128)S(1)} %add_add_fusion), channel_id=1, source_target_pairs={{0,64},{16,80},{32,96},{48,112},{64,0},{80,16},{96,32},{112,48},{1... | collective-permute-start | bytes 196616 | tf_op jit(solution)/shard_map/ppermute | solution.py:106

commit v6 on v4

--- a/solution.py
+++ b/solution.py
@@ -147,7 +147,7 @@
     pixel_total = float(total_rows * total_cols)
     gram_local = jnp.einsum(
         "rck,rcj->kj", filtered, filtered,
-        precision=lax.Precision.HIGHEST, preferred_element_type=jnp.float32,
+        precision=lax.Precision.HIGH, preferred_element_type=jnp.float32,
     )
     gram = all_sum(all_sum(gram_local, "col"), "row") / pixel_total
     factor = jnp.linalg.cholesky(gram)
@@ -156,7 +156,7 @@
     )
     ortho = jnp.einsum(
         "kj,rcj->krc", inverse, filtered,
-        precision=lax.Precision.HIGHEST, preferred_element_type=jnp.float32,
+        precision=lax.Precision.HIGH, preferred_element_type=jnp.float32,
     )
     return (ortho, factor.T)
 

time: 154 us -> 149 us (0.968)
  matrix products: 13.1 us -> 7.8 us
    dot_general x1, matrix products: 6.94 us -> 3.49 us  [per_device(): jnp.einsum('rck,rcj->kj', filtered, filtered, precision=lax.Precision.HIG...]
    dot_general x1, matrix products: 5.86 us -> 4.05 us  [per_device(): jnp.einsum('kj,rcj->krc', inverse, filtered, precision=lax.Precision.HIGH...]
where the time goes in v6:
time: 149 us; the launch traced here: 148 us
  other arithmetic  52.8 us (35%)
  starting transfers between devices  47.6 us (32%)
  waiting for transfers between devices  23 us (15%)
  local copies, waits for them, and re-layouts  16.3 us (11%)
  matrix products  7.8 us (5%)
    ppermute x12, starting transfers between devices, exchange_sum(): received.append(lax.ppermute(block, axis, route))  26.4 us
    ppermute x12, waiting for transfers between devices, exchange_sum(): received.append(lax.ppermute(block, axis, route))  18.7 us
    ppermute x4, starting transfers between devices, padded(): lax.ppermute(tail, axis, [(i, (i + 1) % count) for i in range(ends)])  13.5 us
    mul x1, other arithmetic, apply_pixels(): lifted = values_in * scales[:, :, None]  13.4 us
    sub x1, other arithmetic, apply_pixels(): shifted_pixels(values_in, 0, 0) - shifted(scales, 0, 0)[:, :, None] * summed  12.9 us
    another operation x3, other arithmetic, per_device(): factor = jnp.linalg.cholesky(gram)  12.4 us
    unnamed x11, local copies, waits for them, and re-layouts  10.5 us
    another operation x1, other arithmetic, per_device(): jax.scipy.linalg.solve_triangular(factor, jnp.eye(vectors, dtype=jnp.floa...  9.81 us
  transfers between devices with their start and end apart: 20, of which 11 were waited for; matrix products, arithmetic and copies ran while one was open for 8% of the time, Pallas kernels for 0%

profile of v6, /device:TPU:2, one launch (start us, length us, event | category | flops | bytes accessed | tf_op | source)
XLA Modules:
  0.0 148.5 jit_solution(12848607862263202093)
XLA Ops:
  0.6 0.8 pad_add_fusion.3
  1.4 3.4 %collective-permute-start.4 = (s32[5,3,256]{2,1,0:T(4,128)S(1)}, s32[5,3,256]{2,1,0:T(4,128)S(1)}, u32[]{:S(2)}, u32[]{:S(2)}) collective-permute-start(s32[5,3,256]{2,1,0:T(4,128)S(1)} %get-tuple-element.29), channel_id=1, source_target_pairs={{0,16},{16,32},{32,48},{48,64},{64,80},{80,96},{96,112},{112,128},... | collective-permute-start | bytes 46088 | tf_op jit(solution)/shard_map/ppermute | solution.py:27
  4.8 0.0 copy-start.3
  4.9 2.6 %collective-permute-start.5 = (s32[5,3,256]{2,1,0:T(4,128)S(1)}, s32[5,3,256]{2,1,0:T(4,128)S(1)}, u32[]{:S(2)}, u32[]{:S(2)}) collective-permute-start(s32[5,3,256]{2,1,0:T(4,128)S(1)} %get-tuple-element.30), channel_id=1, source_target_pairs={{16,0},{32,16},{48,32},{64,48},{80,64},{96,80},{112,96},{128,112},... | collective-permute-start | bytes 46088 | tf_op jit(solution)/shard_map/ppermute | solution.py:29
  7.4 5.3 %copy.15 = f32[128,32,256]{0,2,1:T(8,128)} copy(f32[128,32,256]{2,1,0:T(8,128)} %param.5) | data formatting | bytes 8388608 | tf_op args[2]
  12.7 1.1 fusion.83
  13.8 3.4 %collective-permute-start = (f32[2,256,128]{2,1,0:T(8,128)S(1)}, f32[2,256,128]{2,1,0:T(8,128)S(1)}, u32[]{:S(2)}, u32[]{:S(2)}) collective-permute-start(f32[2,256,128]{2,1,0:T(8,128)S(1)} %get-tuple-element.21), channel_id=1, source_target_pairs={{0,16},{16,32},{32,48},{48,64},{64,80},{80,96},{96,112},{112,128},... | collective-permute-start | bytes 786440 | tf_op jit(solution)/shard_map/ppermute | solution.py:27
  17.2 2.5 %collective-permute-start.1 = (f32[2,256,128]{2,1,0:T(8,128)S(1)}, f32[2,256,128]{2,1,0:T(8,128)S(1)}, u32[]{:S(2)}, u32[]{:S(2)}) collective-permute-start(f32[2,256,128]{2,1,0:T(8,128)S(1)} %get-tuple-element.22), channel_id=1, source_target_pairs={{16,0},{32,16},{48,32},{64,48},{80,64},{96,80},{112,96},{128,112},... | collective-permute-start | bytes 786440 | tf_op jit(solution)/shard_map/ppermute | solution.py:29
  19.7 0.0 copy-start.1
  19.8 0.1 fusion.84
  19.9 1.6 %collective-permute-start.6 = (s32[5,38,3]{2,1,0:T(8,128)S(1)}, s32[5,38,3]{2,1,0:T(8,128)S(1)}, u32[]{:S(2)}, u32[]{:S(2)}) collective-permute-start(s32[5,38,3]{2,1,0:T(8,128)S(1)} %get-tuple-element.27), channel_id=1, source_target_pairs={{0,1},{1,2},{2,3},{3,4},{4,5},{5,6},{6,7},{7,8},{8,9},{9,10},{10,1... | collective-permute-start | bytes 6848 | tf_op jit(solution)/shard_map/ppermute | solution.py:27
  21.5 1.3 collective-permute-start.7
  22.8 0.1 broadcast_multiply_fusion.2
  22.8 4.0 %collective-permute-done.7 = s32[5,38,3]{2,1,0:T(8,128)S(1)} collective-permute-done((s32[5,38,3]{2,1,0:T(8,128)S(1)}, s32[5,38,3]{2,1,0:T(8,128)S(1)}, u32[]{:S(2)}, u32[]{:S(2)}) %collective-permute-start.7) | collective-permute-done | bytes 2312 | tf_op jit(solution)/shard_map/ppermute | solution.py:29
  26.8 0.2 pad_add_fusion
  27.1 0.1 fusion.67
  27.2 0.4 add_rsqrt_fusion
  27.5 0.7 slice_bitcast_fusion.18
  28.2 0.1 slice_bitcast_fusion.6
  28.3 0.7 slice_bitcast_fusion.16
  29.1 0.1 slice_bitcast_fusion.4
  29.1 0.1 slice_bitcast_fusion.2
  29.3 0.7 slice_bitcast_fusion.14
  30.0 0.7 slice_bitcast_fusion
  30.7 5.2 %collective-permute-start.2 = (f32[36,2,128]{2,1,0:T(2,128)S(1)}, f32[36,2,128]{2,1,0:T(2,128)S(1)}, u32[]{:S(2)}, u32[]{:S(2)}) collective-permute-start(f32[36,2,128]{2,1,0:T(2,128)S(1)} %get-tuple-element.19), channel_id=1, source_target_pairs={{0,1},{1,2},{2,3},{3,4},{4,5},{5,6},{6,7},{7,8},{8,9},{9,10},{10,1... | collective-permute-start | bytes 110600 | tf_op jit(solution)/shard_map/ppermute | solution.py:27
  35.9 1.3 collective-permute-start.3
  37.2 0.7 slice_bitcast_fusion.12
  37.9 0.7 slice.410
  38.6 0.1 slice.392
  38.7 0.3 collective-permute-done.3
  39.0 1.9 %pad_maximum_fusion = (f32[36,260,128]{2,1,0:T(8,128)S(1)}, f32[36,260,128]{2,1,0:T(8,128)S(1)}) fusion(f32[36,2,128]{2,1,0:T(2,128)S(1)} %collective-permute-done.3, f32[2,256,128]{2,1,0:T(8,128)S(1)} %collective-permute-done.1, f32[32,256,128]{2,1,0:T(8,128)S(1)} %bitcast.77, f32[2,256,128]{2,1,0:T(8,128)S(1)} %collective-permute-done, ...), kind=kLoop, calls=%fused_computation | loop fusion | flops 5990400 | bytes 14414400 | tf_op jit(solution)/shard_map/concatenate | solution.py:25
  41.0 13.4 %broadcast_multiply_fusion.1 = (f32[34,258,128]{2,1,0:T(8,128)S(1)}, f32[34,258,128]{2,1,0:T(8,128)S(1)}) fusion(f32[34,258]{1,0:T(8,128)S(1)} %slice.392, f32[36,260,128]{2,1,0:T(8,128)S(1)} %get-tuple-element.18, f32[34,258]{1,0:T(8,128)S(1)} %get-tuple-element.33, f32[34,258]{1,0:T(8,128)} %get-tuple-element.34, f32[34,258]{1,0:T(8,128)S(1)} %get-tuple-element.35, ...), kind=kLoop, calls=%fused_computation.36 | loop fusion | flops 20210688 | bytes 49719696 | tf_op jit(solution)/shard_map/mul | solution.py:90
  54.4 12.9 %fusion.11 = f32[32,256,128]{2,1,0:T(8,128)S(1)} fusion(f32[34,258,128]{2,1,0:T(8,128)S(1)} %get-tuple-element.6, f32[34,258,128]{2,1,0:T(8,128)S(1)} %get-tuple-element.7, f32[32,256]{1,0:T(8,128)} %get-tuple-element.41, f32[32,256]{1,0:T(8,128)} %get-tuple-element.42, f32[32,256]{1,0:T(8,128)} %get-tuple-element.43, f32[32,256]{1,0:T(8,128)} %get-tuple-element.44, ...), kind=kLoop, calls=%fused_computation.21 | loop fusion | flops 17825792 | bytes 42237952 | tf_op jit(solution)/shard_map/sub | solution.py:95
  67.3 0.0 copy-start
  67.3 3.5 %convolution_bitcast_fusion.1 = f32[128,128]{0,1:T(8,128)S(1)} fusion(f32[32,256,128]{2,1,0:T(8,128)S(1)} %fusion.11), kind=kOutput, calls=%fused_computation.38 | convolution fusion | flops 805306368 | bytes 4259840 | tf_op jit(solution)/shard_map/rck,rcj->kj/dot_general | solution.py:148
  70.8 2.4 %collective-permute-start.9 = (f32[128,128]{0,1:T(8,128)S(1)}, f32[128,128]{0,1:T(8,128)S(1)}, u32[]{:S(2)}, u32[]{:S(2)}) collective-permute-start(f32[128,128]{0,1:T(8,128)S(1)} %convolution_bitcast_fusion.1), channel_id=1, source_target_pairs={{0,2},{1,3},{2,0},{3,1},{4,6},{5,7},{6,4},{7,5},{8,10},{9,11},{10,... | collective-permute-start | bytes 196616 | tf_op jit(solution)/shard_map/ppermute | solution.py:104
  73.2 1.8 %collective-permute-start.8 = (f32[128,128]{0,1:T(8,128)S(1)}, f32[128,128]{0,1:T(8,128)S(1)}, u32[]{:S(2)}, u32[]{:S(2)}) collective-permute-start(f32[128,128]{0,1:T(8,128)S(1)} %convolution_bitcast_fusion.1), channel_id=1, source_target_pairs={{0,1},{1,0},{2,3},{3,2},{4,5},{5,4},{6,7},{7,6},{8,9},{9,8},{10,11... | collective-permute-start | bytes 196616 | tf_op jit(solution)/shard_map/ppermute | solution.py:104
  75.0 0.1 collective-permute-start.10
  75.1 0.4 collective-permute-done.9
  75.5 0.4 collective-permute-done.8
  75.9 3.3 %collective-permute-done.10 = f32[128,128]{0,1:T(8,128)S(1)} collective-permute-done((f32[128,128]{0,1:T(8,128)S(1)}, f32[128,128]{0,1:T(8,128)S(1)}, u32[]{:S(2)}, u32[]{:S(2)}) %collective-permute-start.10) | collective-permute-done | bytes 65568 | tf_op jit(solution)/shard_map/ppermute | solution.py:104
  79.2 4.6 %collective-permute-start.13 = (f32[128,128]{0,1:T(8,128)S(1)}, f32[128,128]{0,1:T(8,128)S(1)}, u32[]{:S(2)}, u32[]{:S(2)}) collective-permute-start(f32[128,128]{0,1:T(8,128)S(1)} %add_add_fusion.2), channel_id=1, source_target_pairs={{0,12},{1,13},{2,14},{3,15},{4,8},{5,9},{6,10},{7,11},{8,4},{9,5},... | collective-permute-start | bytes 196616 | tf_op jit(solution)/shard_map/ppermute | solution.py:104
  83.8 5.7 %collective-permute-start.12 = (f32[128,128]{0,1:T(8,128)S(1)}, f32[128,128]{0,1:T(8,128)S(1)}, u32[]{:S(2)}, u32[]{:S(2)}) collective-permute-start(f32[128,128]{0,1:T(8,128)S(1)} %add_add_fusion.2), channel_id=1, source_target_pairs={{0,8},{1,9},{2,10},{3,11},{4,12},{5,13},{6,14},{7,15},{8,0},{9,1},... | collective-permute-start | bytes 196616 | tf_op jit(solution)/shard_map/ppermute | solution.py:104
  89.5 4.9 %collective-permute-done.12 = f32[128,128]{0,1:T(8,128)S(1)} collective-permute-done((f32[128,128]{0,1:T(8,128)S(1)}, f32[128,128]{0,1:T(8,128)S(1)}, u32[]{:S(2)}, u32[]{:S(2)}) %collective-permute-start.12) | collective-permute-done | bytes 65568 | tf_op jit(solution)/shard_map/ppermute | solution.py:104
  94.4 1.5 %collective-permute-done.11 = f32[128,128]{0,1:T(8,128)S(1)} collective-permute-done((f32[128,128]{0,1:T(8,128)S(1)}, f32[128,128]{0,1:T(8,128)S(1)}, u32[]{:S(2)}, u32[]{:S(2)}) %collective-permute-start.11) | collective-permute-done | bytes 65568 | tf_op jit(solution)/shard_map/ppermute | solution.py:104
  95.9 1.6 %collective-permute-start.16 = (f32[128,128]{0,1:T(8,128)S(1)}, f32[128,128]{0,1:T(8,128)S(1)}, u32[]{:S(2)}, u32[]{:S(2)}) collective-permute-start(f32[128,128]{0,1:T(8,128)S(1)} %add_add_fusion.1), channel_id=1, source_target_pairs={{0,48},{16,32},{32,16},{48,0},{64,112},{80,96},{96,80},{112,64},{1... | collective-permute-start | bytes 196616 | tf_op jit(solution)/shard_map/ppermute | solution.py:104
  97.5 2.5 %collective-permute-start.15 = (f32[128,128]{0,1:T(8,128)S(1)}, f32[128,128]{0,1:T(8,128)S(1)}, u32[]{:S(2)}, u32[]{:S(2)}) collective-permute-start(f32[128,128]{0,1:T(8,128)S(1)} %add_add_fusion.1), channel_id=1, source_target_pairs={{0,32},{16,48},{32,0},{48,16},{64,96},{80,112},{96,64},{112,80},{1... | collective-permute-start | bytes 196616 | tf_op jit(solution)/shard_map/ppermute | solution.py:104
  100.0 0.9 collective-permute-start.14
  100.9 2.4 %collective-permute-done.15 = f32[128,128]{0,1:T(8,128)S(1)} collective-permute-done((f32[128,128]{0,1:T(8,128)S(1)}, f32[128,128]{0,1:T(8,128)S(1)}, u32[]{:S(2)}, u32[]{:S(2)}) %collective-permute-start.15) | collective-permute-done | bytes 65568 | tf_op jit(solution)/shard_map/ppermute | solution.py:104
  103.2 1.0 collective-permute-done.14
  104.3 5.9 %collective-permute-start.19 = (f32[128,128]{0,1:T(8,128)S(1)}, f32[128,128]{0,1:T(8,128)S(1)}, u32[]{:S(2)}, u32[]{:S(2)}) collective-permute-start(f32[128,128]{0,1:T(8,128)S(1)} %add_add_fusion), channel_id=1, source_target_pairs={{0,192},{16,208},{32,224},{48,240},{64,128},{80,144},{96,160},{112... | collective-permute-start | bytes 196616 | tf_op jit(solution)/shard_map/ppermute | solution.py:104
  110.2 0.6 collective-permute-start.18
  110.8 0.3 collective-permute-start.17
  111.2 2.0 %collective-permute-done.19 = f32[128,128]{0,1:T(8,128)S(1)} collective-permute-done((f32[128,128]{0,1:T(8,128)S(1)}, f32[128,128]{0,1:T(8,128)S(1)}, u32[]{:S(2)}, u32[]{:S(2)}) %collective-permute-start.19) | collective-permute-done | bytes 65568 | tf_op jit(solution)/shard_map/ppermute | solution.py:104
  113.2 2.8 %collective-permute-done.18 = f32[128,128]{0,1:T(8,128)S(1)} collective-permute-done((f32[128,128]{0,1:T(8,128)S(1)}, f32[128,128]{0,1:T(8,128)S(1)}, u32[]{:S(2)}, u32[]{:S(2)}) %collective-permute-start.18) | collective-permute-done | bytes 65568 | tf_op jit(solution)/shard_map/ppermute | solution.py:104
  116.0 0.1 copy.21
  116.1 11.7 %cholesky.17 = f32[128,128]{1,0:T(8,128)S(1)} custom-call(f32[128,128]{1,0:T(8,128)S(1)} %fusion.19), custom_call_target="Cholesky" | custom-call | tf_op jit(solution)/shard_map/jit(cholesky)/cholesky | solution.py:153
  127.9 0.6 compare_reduce_fusion
  128.5 0.7 fusion.69
  129.2 0.7 copy.23
  129.9 9.8 %custom-call.7 = f32[1,128,128]{1,2,0:T(8,128)S(1)} custom-call(f32[1,128,128]{2,1,0:T(8,128)S(1)} %get-tuple-element.32), custom_call_target="InvertDiagBlocksLowerTriangular" | custom-call | tf_op jit(solution)/shard_map/jit(_solve_triangular)/triangular_solve | solution.py:154
  139.7 0.2 convolution_bitcast_fusion
  140.0 4.1 %fusion.85 = f32[128,32,256]{2,0,1:T(8,128)S(1)} fusion(f32[128,128,1]{1,0,2:T(8,128)S(1)} %convolution_bitcast_fusion, f32[32,256,128]{2,1,0:T(8,128)} %copy-done), kind=kOutput, calls=%fused_computation.165 | convolution fusion | flops 805306368 | bytes 8454144 | tf_op jit(solution)/shard_map/kj,rcj->krc/dot_general | solution.py:157
  144.0 4.4 %copy.22 = f32[128,32,256]{2,1,0:T(8,128)} copy(f32[128,32,256]{2,0,1:T(8,128)S(1)} %fusion.85) | data formatting | bytes 8388608
  (27 shorter events, 0.3 us)
Async XLA Ops:
  1.4 18.3 %collective-permute-start.4 = (s32[5,3,256]{2,1,0:T(4,128)S(1)}, s32[5,3,256]{2,1,0:T(4,128)S(1)}, u32[]{:S(2)}, u32[]{:S(2)}) collective-permute-start(s32[5,3,256]{2,1,0:T(4,128)S(1)} %get-tuple-element.29), channel_id=1, source_target_pairs={{0,16},{16,32},{32,48},{48,64},{64,80},{80,96},{96,112},{112,128},... | collective-permute-start | bytes 46088 | tf_op jit(solution)/shard_map/ppermute | solution.py:27
  4.8 14.9 %copy-start.2 = (s32[4,32,256]{2,1,0:T(8,128)S(1)}, s32[4,32,256]{2,1,0:T(8,128)}, u32[]{:S(2)}) copy-start(s32[4,32,256]{2,1,0:T(8,128)} %param.4) | copy-start | bytes 393220
  4.8 14.9 %copy-start.3 = (s32[32,256]{1,0:T(8,128)S(1)}, s32[32,256]{1,0:T(8,128)}, u32[]{:S(2)}) copy-start(s32[32,256]{1,0:T(8,128)} %param.3) | copy-start | bytes 98308
  4.9 14.9 %collective-permute-start.5 = (s32[5,3,256]{2,1,0:T(4,128)S(1)}, s32[5,3,256]{2,1,0:T(4,128)S(1)}, u32[]{:S(2)}, u32[]{:S(2)}) collective-permute-start(s32[5,3,256]{2,1,0:T(4,128)S(1)} %get-tuple-element.30), channel_id=1, source_target_pairs={{16,0},{32,16},{48,32},{64,48},{80,64},{96,80},{112,96},{128,112},... | collective-permute-start | bytes 46088 | tf_op jit(solution)/shard_map/ppermute | solution.py:29
  13.8 16.9 %collective-permute-start = (f32[2,256,128]{2,1,0:T(8,128)S(1)}, f32[2,256,128]{2,1,0:T(8,128)S(1)}, u32[]{:S(2)}, u32[]{:S(2)}) collective-permute-start(f32[2,256,128]{2,1,0:T(8,128)S(1)} %get-tuple-element.21), channel_id=1, source_target_pairs={{0,16},{16,32},{32,48},{48,64},{64,80},{80,96},{96,112},{112,128},... | collective-permute-start | bytes 786440 | tf_op jit(solution)/shard_map/ppermute | solution.py:27
  17.2 13.5 %collective-permute-start.1 = (f32[2,256,128]{2,1,0:T(8,128)S(1)}, f32[2,256,128]{2,1,0:T(8,128)S(1)}, u32[]{:S(2)}, u32[]{:S(2)}) collective-permute-start(f32[2,256,128]{2,1,0:T(8,128)S(1)} %get-tuple-element.22), channel_id=1, source_target_pairs={{16,0},{32,16},{48,32},{64,48},{80,64},{96,80},{112,96},{128,112},... | collective-permute-start | bytes 786440 | tf_op jit(solution)/shard_map/ppermute | solution.py:29
  19.7 11.0 %copy-start.1 = (f32[128,32,256]{0,2,1:T(8,128)S(1)}, f32[128,32,256]{0,2,1:T(8,128)}, u32[]{:S(2)}) copy-start(f32[128,32,256]{0,2,1:T(8,128)} %copy.15) | copy-start | bytes 12582916
  19.9 2.9 %collective-permute-start.6 = (s32[5,38,3]{2,1,0:T(8,128)S(1)}, s32[5,38,3]{2,1,0:T(8,128)S(1)}, u32[]{:S(2)}, u32[]{:S(2)}) collective-permute-start(s32[5,38,3]{2,1,0:T(8,128)S(1)} %get-tuple-element.27), channel_id=1, source_target_pairs={{0,1},{1,2},{2,3},{3,4},{4,5},{5,6},{6,7},{7,8},{8,9},{9,10},{10,1... | collective-permute-start | bytes 6848 | tf_op jit(solution)/shard_map/ppermute | solution.py:27
  21.5 5.3 %collective-permute-start.7 = (s32[5,38,3]{2,1,0:T(8,128)S(1)}, s32[5,38,3]{2,1,0:T(8,128)S(1)}, u32[]{:S(2)}, u32[]{:S(2)}) collective-permute-start(s32[5,38,3]{2,1,0:T(8,128)S(1)} %get-tuple-element.28), channel_id=1, source_target_pairs={{1,0},{2,1},{3,2},{4,3},{5,4},{6,5},{7,6},{8,7},{9,8},{10,9},{11,1... | collective-permute-start | bytes 6848 | tf_op jit(solution)/shard_map/ppermute | solution.py:29
  30.7 8.0 %collective-permute-start.2 = (f32[36,2,128]{2,1,0:T(2,128)S(1)}, f32[36,2,128]{2,1,0:T(2,128)S(1)}, u32[]{:S(2)}, u32[]{:S(2)}) collective-permute-start(f32[36,2,128]{2,1,0:T(2,128)S(1)} %get-tuple-element.19), channel_id=1, source_target_pairs={{0,1},{1,2},{2,3},{3,4},{4,5},{5,6},{6,7},{7,8},{8,9},{9,10},{10,1... | collective-permute-start | bytes 110600 | tf_op jit(solution)/shard_map/ppermute | solution.py:27
  35.9 3.1 %collective-permute-start.3 = (f32[36,2,128]{2,1,0:T(2,128)S(1)}, f32[36,2,128]{2,1,0:T(2,128)S(1)}, u32[]{:S(2)}, u32[]{:S(2)}) collective-permute-start(f32[36,2,128]{2,1,0:T(2,128)S(1)} %get-tuple-element.20), channel_id=1, source_target_pairs={{1,0},{2,1},{3,2},{4,3},{5,4},{6,5},{7,6},{8,7},{9,8},{10,9},{11,1... | collective-permute-start | bytes 110600 | tf_op jit(solution)/shard_map/ppermute | solution.py:29
  67.3 37.0 %copy-start = (f32[32,256,128]{2,1,0:T(8,128)}, f32[32,256,128]{2,1,0:T(8,128)S(1)}, u32[]{:S(2)}) copy-start(f32[32,256,128]{2,1,0:T(8,128)S(1)} %fusion.11) | copy-start | bytes 12582916
  70.8 4.7 %collective-permute-start.9 = (f32[128,128]{0,1:T(8,128)S(1)}, f32[128,128]{0,1:T(8,128)S(1)}, u32[]{:S(2)}, u32[]{:S(2)}) collective-permute-start(f32[128,128]{0,1:T(8,128)S(1)} %convolution_bitcast_fusion.1), channel_id=1, source_target_pairs={{0,2},{1,3},{2,0},{3,1},{4,6},{5,7},{6,4},{7,5},{8,10},{9,11},{10,... | collective-permute-start | bytes 196616 | tf_op jit(solution)/shard_map/ppermute | solution.py:104
  73.2 2.7 %collective-permute-start.8 = (f32[128,128]{0,1:T(8,128)S(1)}, f32[128,128]{0,1:T(8,128)S(1)}, u32[]{:S(2)}, u32[]{:S(2)}) collective-permute-start(f32[128,128]{0,1:T(8,128)S(1)} %convolution_bitcast_fusion.1), channel_id=1, source_target_pairs={{0,1},{1,0},{2,3},{3,2},{4,5},{5,4},{6,7},{7,6},{8,9},{9,8},{10,11... | collective-permute-start | bytes 196616 | tf_op jit(solution)/shard_map/ppermute | solution.py:104
  75.0 4.2 %collective-permute-start.10 = (f32[128,128]{0,1:T(8,128)S(1)}, f32[128,128]{0,1:T(8,128)S(1)}, u32[]{:S(2)}, u32[]{:S(2)}) collective-permute-start(f32[128,128]{0,1:T(8,128)S(1)} %convolution_bitcast_fusion.1), channel_id=1, source_target_pairs={{0,3},{1,2},{2,1},{3,0},{4,7},{5,6},{6,5},{7,4},{8,11},{9,10},{10,... | collective-permute-start | bytes 196616 | tf_op jit(solution)/shard_map/ppermute | solution.py:104
  79.2 10.3 %collective-permute-start.13 = (f32[128,128]{0,1:T(8,128)S(1)}, f32[128,128]{0,1:T(8,128)S(1)}, u32[]{:S(2)}, u32[]{:S(2)}) collective-permute-start(f32[128,128]{0,1:T(8,128)S(1)} %add_add_fusion.2), channel_id=1, source_target_pairs={{0,12},{1,13},{2,14},{3,15},{4,8},{5,9},{6,10},{7,11},{8,4},{9,5},... | collective-permute-start | bytes 196616 | tf_op jit(solution)/shard_map/ppermute | solution.py:104
  83.8 10.6 %collective-permute-start.12 = (f32[128,128]{0,1:T(8,128)S(1)}, f32[128,128]{0,1:T(8,128)S(1)}, u32[]{:S(2)}, u32[]{:S(2)}) collective-permute-start(f32[128,128]{0,1:T(8,128)S(1)} %add_add_fusion.2), channel_id=1, source_target_pairs={{0,8},{1,9},{2,10},{3,11},{4,12},{5,13},{6,14},{7,15},{8,0},{9,1},... | collective-permute-start | bytes 196616 | tf_op jit(solution)/shard_map/ppermute | solution.py:104
  89.5 6.4 %collective-permute-start.11 = (f32[128,128]{0,1:T(8,128)S(1)}, f32[128,128]{0,1:T(8,128)S(1)}, u32[]{:S(2)}, u32[]{:S(2)}) collective-permute-start(f32[128,128]{0,1:T(8,128)S(1)} %add_add_fusion.2), channel_id=1, source_target_pairs={{0,4},{1,5},{2,6},{3,7},{4,0},{5,1},{6,2},{7,3},{8,12},{9,13},{10,... | collective-permute-start | bytes 196616 | tf_op jit(solution)/shard_map/ppermute | solution.py:104
  95.9 5.0 %collective-permute-start.16 = (f32[128,128]{0,1:T(8,128)S(1)}, f32[128,128]{0,1:T(8,128)S(1)}, u32[]{:S(2)}, u32[]{:S(2)}) collective-permute-start(f32[128,128]{0,1:T(8,128)S(1)} %add_add_fusion.1), channel_id=1, source_target_pairs={{0,48},{16,32},{32,16},{48,0},{64,112},{80,96},{96,80},{112,64},{1... | collective-permute-start | bytes 196616 | tf_op jit(solution)/shard_map/ppermute | solution.py:104
  97.5 5.8 %collective-permute-start.15 = (f32[128,128]{0,1:T(8,128)S(1)}, f32[128,128]{0,1:T(8,128)S(1)}, u32[]{:S(2)}, u32[]{:S(2)}) collective-permute-start(f32[128,128]{0,1:T(8,128)S(1)} %add_add_fusion.1), channel_id=1, source_target_pairs={{0,32},{16,48},{32,0},{48,16},{64,96},{80,112},{96,64},{112,80},{1... | collective-permute-start | bytes 196616 | tf_op jit(solution)/shard_map/ppermute | solution.py:104
  100.0 4.3 %collective-permute-start.14 = (f32[128,128]{0,1:T(8,128)S(1)}, f32[128,128]{0,1:T(8,128)S(1)}, u32[]{:S(2)}, u32[]{:S(2)}) collective-permute-start(f32[128,128]{0,1:T(8,128)S(1)} %add_add_fusion.1), channel_id=1, source_target_pairs={{0,16},{16,0},{32,48},{48,32},{64,80},{80,64},{96,112},{112,96},{1... | collective-permute-start | bytes 196616 | tf_op jit(solution)/shard_map/ppermute | solution.py:104
  104.3 8.9 %collective-permute-start.19 = (f32[128,128]{0,1:T(8,128)S(1)}, f32[128,128]{0,1:T(8,128)S(1)}, u32[]{:S(2)}, u32[]{:S(2)}) collective-permute-start(f32[128,128]{0,1:T(8,128)S(1)} %add_add_fusion), channel_id=1, source_target_pairs={{0,192},{16,208},{32,224},{48,240},{64,128},{80,144},{96,160},{112... | collective-permute-start | bytes 196616 | tf_op jit(solution)/shard_map/ppermute | solution.py:104
  110.2 5.8 %collective-permute-start.18 = (f32[128,128]{0,1:T(8,128)S(1)}, f32[128,128]{0,1:T(8,128)S(1)}, u32[]{:S(2)}, u32[]{:S(2)}) collective-permute-start(f32[128,128]{0,1:T(8,128)S(1)} %add_add_fusion), channel_id=1, source_target_pairs={{0,128},{16,144},{32,160},{48,176},{64,192},{80,208},{96,224},{112... | collective-permute-start | bytes 196616 | tf_op jit(solution)/shard_map/ppermute | solution.py:104
  110.8 5.1 %collective-permute-start.17 = (f32[128,128]{0,1:T(8,128)S(1)}, f32[128,128]{0,1:T(8,128)S(1)}, u32[]{:S(2)}, u32[]{:S(2)}) collective-permute-start(f32[128,128]{0,1:T(8,128)S(1)} %add_add_fusion), channel_id=1, source_target_pairs={{0,64},{16,80},{32,96},{48,112},{64,0},{80,16},{96,32},{112,48},{1... | collective-permute-start | bytes 196616 | tf_op jit(solution)/shard_map/ppermute | solution.py:104

commit v7 on v6

--- a/solution.py
+++ b/solution.py
@@ -86,13 +86,19 @@
     return array[1 + step_row : height - 1 + step_row, 1 + step_col : width - 1 + step_col]
 
 
-def apply_pixels(values_in, weights, scales):
-    lifted = values_in * scales[:, :, None]
+def pass_coefficients(weights, scales):
+    center = shifted(scales, 0, 0)
+    return jnp.stack(
+        [center * weight * shifted(scales, entry[0], entry[1]) for weight, entry in zip(weights, NEIGHBOURS)]
+    )
+
+
+def apply_pixels(values_in, coefficients):
     summed = None
-    for weight, entry in zip(weights, NEIGHBOURS):
-        term = weight[:, :, None] * shifted_pixels(lifted, entry[0], entry[1])
+    for index, entry in enumerate(NEIGHBOURS):
+        term = coefficients[index][:, :, None] * shifted_pixels(values_in, entry[0], entry[1])
         summed = term if summed is None else summed + term
-    return shifted_pixels(values_in, 0, 0) - shifted(scales, 0, 0)[:, :, None] * summed
+    return shifted_pixels(values_in, 0, 0) - summed
 
 
 def exchange_sum(block, axis, low_bit, bits):
@@ -139,11 +145,9 @@
     scales = degree_scales(weights)
     pixels = jnp.transpose(basis_block, (1, 2, 0))
     extended = padded(pixels, (("row", 0), ("col", 1)), 2)
-    stacked = jnp.stack(weights)
-    ring_weights = cropped(stacked, 1)
-    tile_weights = cropped(stacked, 2)
-    first = apply_pixels(extended, [ring_weights[i] for i in range(len(weights))], scales)
-    filtered = apply_pixels(first, [tile_weights[i] for i in range(len(weights))], cropped(scales, 1))
+    first = apply_pixels(extended, pass_coefficients([cropped(w, 1) for w in weights], scales))
+    tile_scales = cropped(scales, 1)
+    filtered = apply_pixels(first, pass_coefficients([cropped(w, 2) for w in weights], tile_scales))
     pixel_total = float(total_rows * total_cols)
     gram_local = jnp.einsum(
         "rck,rcj->kj", filtered, filtered,

time: 149 us -> 145 us (0.973)
  local copies, waits for them, and re-layouts: 16.3 us -> 11.7 us
  other arithmetic: 52.8 us -> 50.8 us
  waiting for transfers between devices: 23 us -> 24.6 us
    mul x1 -> x4, other arithmetic: 13.4 us -> 0.69 us  [pass_coefficients(): center * weight * shifted(scales, entry[0], entry[1])]
    sub x1 -> x2, other arithmetic: 12.9 us -> 21.6 us  [apply_pixels(): return shifted_pixels(values_in, 0, 0) - summed]
    mul x8 -> x0, local copies, waits for them, and re-layouts: 3.82 us -> none  [apply_pixels(): term = weight[:, :, None] * shifted_pixels(lifted, entry[0], entry[1])]
    concatenate x3 -> x4, other arithmetic: 2.18 us -> 4.12 us  [padded(): jnp.concatenate([lax.ppermute(tail, axis, [(i, (i + 1) % count) for i in...]
  transfers between devices with their start and end apart: 20 -> 20, of which waited for: 11 -> 11; matrix products, arithmetic and copies ran while one was open for 8% -> 6% of each run, Pallas kernels for 0% -> 0%
where the time goes in v7:
time: 145 us; the launch traced here: 144 us
  other arithmetic  50.8 us (35%)
  starting transfers between devices  47.6 us (33%)
  waiting for transfers between devices  24.6 us (17%)
  local copies, waits for them, and re-layouts  11.7 us (8%)
  matrix products  7.8 us (5%)
    ppermute x12, starting transfers between devices, exchange_sum(): received.append(lax.ppermute(block, axis, route))  26.5 us
    sub x2, other arithmetic, apply_pixels(): return shifted_pixels(values_in, 0, 0) - summed  21.6 us
    ppermute x12, waiting for transfers between devices, exchange_sum(): received.append(lax.ppermute(block, axis, route))  18.9 us
    ppermute x4, starting transfers between devices, padded(): lax.ppermute(tail, axis, [(i, (i + 1) % count) for i in range(ends)])  13.5 us
    another operation x3, other arithmetic, per_device(): factor = jnp.linalg.cholesky(gram)  12.4 us
    unnamed x11, local copies, waits for them, and re-layouts  10.5 us
    another operation x1, other arithmetic, per_device(): jax.scipy.linalg.solve_triangular(factor, jnp.eye(vectors, dtype=jnp.floa...  9.81 us
    ppermute x4, starting transfers between devices, padded(): lax.ppermute(head, axis, [((i + 1) % count, i) for i in range(ends)])  7.61 us
  transfers between devices with their start and end apart: 20, of which 11 were waited for; matrix products, arithmetic and copies ran while one was open for 6% of the time, Pallas kernels for 0%

profile of v7, /device:TPU:2, one launch (start us, length us, event | category | flops | bytes accessed | tf_op | source)
XLA Modules:
  0.0 143.6 jit_solution(1093673671178491318)
XLA Ops:
  0.6 0.8 pad_add_fusion.3
  1.4 3.4 %collective-permute-start.4 = (s32[5,3,256]{2,1,0:T(4,128)S(1)}, s32[5,3,256]{2,1,0:T(4,128)S(1)}, u32[]{:S(2)}, u32[]{:S(2)}) collective-permute-start(s32[5,3,256]{2,1,0:T(4,128)S(1)} %get-tuple-element.27), channel_id=1, source_target_pairs={{0,16},{16,32},{32,48},{48,64},{64,80},{80,96},{96,112},{112,128},... | collective-permute-start | bytes 46088 | tf_op jit(solution)/shard_map/ppermute | solution.py:27
  4.8 0.0 copy-start.2
  4.8 0.0 copy-start.3
  4.9 2.6 %collective-permute-start.5 = (s32[5,3,256]{2,1,0:T(4,128)S(1)}, s32[5,3,256]{2,1,0:T(4,128)S(1)}, u32[]{:S(2)}, u32[]{:S(2)}) collective-permute-start(s32[5,3,256]{2,1,0:T(4,128)S(1)} %get-tuple-element.28), channel_id=1, source_target_pairs={{16,0},{32,16},{48,32},{64,48},{80,64},{96,80},{112,96},{128,112},... | collective-permute-start | bytes 46088 | tf_op jit(solution)/shard_map/ppermute | solution.py:29
  7.4 5.3 %copy.15 = f32[128,32,256]{0,2,1:T(8,128)} copy(f32[128,32,256]{2,1,0:T(8,128)} %param.5) | data formatting | bytes 8388608 | tf_op args[2]
  12.7 1.1 fusion.80
  13.8 3.4 %collective-permute-start = (f32[2,256,128]{2,1,0:T(8,128)S(1)}, f32[2,256,128]{2,1,0:T(8,128)S(1)}, u32[]{:S(2)}, u32[]{:S(2)}) collective-permute-start(f32[2,256,128]{2,1,0:T(8,128)S(1)} %get-tuple-element.19), channel_id=1, source_target_pairs={{0,16},{16,32},{32,48},{48,64},{64,80},{80,96},{96,112},{112,128},... | collective-permute-start | bytes 786440 | tf_op jit(solution)/shard_map/ppermute | solution.py:27
  17.2 2.5 %collective-permute-start.1 = (f32[2,256,128]{2,1,0:T(8,128)S(1)}, f32[2,256,128]{2,1,0:T(8,128)S(1)}, u32[]{:S(2)}, u32[]{:S(2)}) collective-permute-start(f32[2,256,128]{2,1,0:T(8,128)S(1)} %get-tuple-element.20), channel_id=1, source_target_pairs={{16,0},{32,16},{48,32},{64,48},{80,64},{96,80},{112,96},{128,112},... | collective-permute-start | bytes 786440 | tf_op jit(solution)/shard_map/ppermute | solution.py:29
  19.7 0.0 copy-start
  19.7 0.0 collective-permute-done.4
  19.8 0.1 fusion.81
  19.9 1.6 %collective-permute-start.6 = (s32[5,38,3]{2,1,0:T(8,128)S(1)}, s32[5,38,3]{2,1,0:T(8,128)S(1)}, u32[]{:S(2)}, u32[]{:S(2)}) collective-permute-start(s32[5,38,3]{2,1,0:T(8,128)S(1)} %get-tuple-element.25), channel_id=1, source_target_pairs={{0,1},{1,2},{2,3},{3,4},{4,5},{5,6},{6,7},{7,8},{8,9},{9,10},{10,1... | collective-permute-start | bytes 6848 | tf_op jit(solution)/shard_map/ppermute | solution.py:27
  21.5 1.3 collective-permute-start.7
  22.8 0.1 broadcast_multiply_fusion
  22.8 4.0 %collective-permute-done.7 = s32[5,38,3]{2,1,0:T(8,128)S(1)} collective-permute-done((s32[5,38,3]{2,1,0:T(8,128)S(1)}, s32[5,38,3]{2,1,0:T(8,128)S(1)}, u32[]{:S(2)}, u32[]{:S(2)}) %collective-permute-start.7) | collective-permute-done | bytes 2312 | tf_op jit(solution)/shard_map/ppermute | solution.py:29
  26.8 0.2 pad_add_fusion
  27.1 0.1 fusion.65
  27.2 0.4 add_rsqrt_fusion
  27.5 0.2 slice_multiply_fusion.46
  27.7 0.1 slice_multiply_fusion.28
  27.9 0.3 slice_multiply_fusion.30
  28.1 0.0 collective-permute-done
  28.2 0.0 collective-permute-done.1
  28.2 5.2 %collective-permute-start.2 = (f32[36,2,128]{2,1,0:T(2,128)S(1)}, f32[36,2,128]{2,1,0:T(2,128)S(1)}, u32[]{:S(2)}, u32[]{:S(2)}) collective-permute-start(f32[36,2,128]{2,1,0:T(2,128)S(1)} %get-tuple-element.17), channel_id=1, source_target_pairs={{0,1},{1,2},{2,3},{3,4},{4,5},{5,6},{6,7},{7,8},{8,9},{9,10},{10,1... | collective-permute-start | bytes 110600 | tf_op jit(solution)/shard_map/ppermute | solution.py:27
  33.4 1.3 collective-permute-start.3
  34.7 0.1 slice_multiply_fusion.34
  34.8 0.0 collective-permute-done.2
  34.8 1.7 %collective-permute-done.3 = f32[36,2,128]{2,1,0:T(2,128)S(1)} collective-permute-done((f32[36,2,128]{2,1,0:T(2,128)S(1)}, f32[36,2,128]{2,1,0:T(2,128)S(1)}, u32[]{:S(2)}, u32[]{:S(2)}) %collective-permute-start.3) | collective-permute-done | bytes 36896 | tf_op jit(solution)/shard_map/ppermute | solution.py:29
  36.5 2.3 %maximum_maximum_fusion = (f32[36,258,128]{2,1,0:T(8,128)S(1)}, f32[36,258,128]{2,1,0:T(8,128)S(1)}) fusion(f32[2,256,128]{2,1,0:T(8,128)S(1)} %collective-permute-done.1, f32[32,256,128]{2,1,0:T(8,128)S(1)} %bitcast.37, f32[2,256,128]{2,1,0:T(8,128)S(1)} %collective-permute-done, f32[36,2,128]{2,1,0:T(2,128)S(1)} %collective-permute-done.2, ...), kind=kLoop, calls=%fused_computation.2 | loop fusion | flops 7133184 | bytes 14303232 | tf_op jit(solution)/shard_map/concatenate | solution.py:25
  38.8 1.6 %pad_maximum_fusion = f32[36,260,128]{2,1,0:T(8,128)S(1)} fusion(f32[36,2,128]{2,1,0:T(2,128)S(1)} %collective-permute-done.3, f32[2,256,128]{2,1,0:T(8,128)S(1)} %collective-permute-done.1, f32[32,256,128]{2,1,0:T(8,128)S(1)} %bitcast.38, f32[2,256,128]{2,1,0:T(8,128)S(1)} %collective-permute-done, f32[36,2,128]{2,1,0:T(2,128)S(1)} %collective-permute-done.2), kind=kLoop, calls=%fused_computation | loop fusion | flops 4792320 | bytes 9584640 | tf_op jit(solution)/shard_map/concatenate | solution.py:25
  40.4 11.6 %fusion.1 = f32[34,258,128]{2,1,0:T(8,128)S(1)} fusion(f32[36,258,128]{2,1,0:T(8,128)S(1)} %get-tuple-element.16, f32[36,258,128]{2,1,0:T(8,128)S(1)} %get-tuple-element.15, f32[36,260,128]{2,1,0:T(8,128)S(1)} %pad_maximum_fusion, f32[34,258]{1,0:T(8,128)S(1)} %get-tuple-element.40, f32[34,258]{1,0:T(8,128)S(1)} %get-tuple-element.41, ...), kind=kLoop, calls=%fused_computation.5 | loop fusion | flops 17965056 | bytes 45193344 | tf_op jit(solution)/shard_map/sub | solution.py:101
  52.0 10.1 %fusion.9 = f32[32,256,128]{2,1,0:T(8,128)S(1)} fusion(f32[34,258,128]{2,1,0:T(8,128)S(1)} %fusion.1, f32[32,256]{1,0:T(8,128)S(1)} %get-tuple-element.38, f32[32,256]{1,0:T(8,128)S(1)} %get-tuple-element.37, f32[32,256]{1,0:T(8,128)S(1)} %get-tuple-element.32, f32[32,256]{1,0:T(8,128)S(1)} %get-tuple-element.33, f32[32,256]{1,0:T(8,128)S(1)} %get-tuple-element.34, ...), kind=kLoop, calls=%fused_computation.21 | loop fusion | flops 16777216 | bytes 42205184 | tf_op jit(solution)/shard_map/sub | solution.py:101
  62.1 0.0 copy-start.1
  62.1 3.5 %convolution_bitcast_fusion.1 = f32[128,128]{0,1:T(8,128)S(1)} fusion(f32[32,256,128]{2,1,0:T(8,128)S(1)} %fusion.9), kind=kOutput, calls=%fused_computation.36 | convolution fusion | flops 805306368 | bytes 4259840 | tf_op jit(solution)/shard_map/rck,rcj->kj/dot_general | solution.py:152
  65.6 4.1 %collective-permute-start.10 = (f32[128,128]{0,1:T(8,128)S(1)}, f32[128,128]{0,1:T(8,128)S(1)}, u32[]{:S(2)}, u32[]{:S(2)}) collective-permute-start(f32[128,128]{0,1:T(8,128)S(1)} %convolution_bitcast_fusion.1), channel_id=1, source_target_pairs={{0,3},{1,2},{2,1},{3,0},{4,7},{5,6},{6,5},{7,4},{8,11},{9,10},{10,... | collective-permute-start | bytes 196616 | tf_op jit(solution)/shard_map/ppermute | solution.py:110
  69.7 0.5 collective-permute-start.9
  70.1 1.8 %collective-permute-done.10 = f32[128,128]{0,1:T(8,128)S(1)} collective-permute-done((f32[128,128]{0,1:T(8,128)S(1)}, f32[128,128]{0,1:T(8,128)S(1)}, u32[]{:S(2)}, u32[]{:S(2)}) %collective-permute-start.10) | collective-permute-done | bytes 65568 | tf_op jit(solution)/shard_map/ppermute | solution.py:110
  72.0 2.2 %collective-permute-done.9 = f32[128,128]{0,1:T(8,128)S(1)} collective-permute-done((f32[128,128]{0,1:T(8,128)S(1)}, f32[128,128]{0,1:T(8,128)S(1)}, u32[]{:S(2)}, u32[]{:S(2)}) %collective-permute-start.9) | collective-permute-done | bytes 65568 | tf_op jit(solution)/shard_map/ppermute | solution.py:110
  74.2 6.7 %collective-permute-start.11 = (f32[128,128]{0,1:T(8,128)S(1)}, f32[128,128]{0,1:T(8,128)S(1)}, u32[]{:S(2)}, u32[]{:S(2)}) collective-permute-start(f32[128,128]{0,1:T(8,128)S(1)} %add_add_fusion.2), channel_id=1, source_target_pairs={{0,4},{1,5},{2,6},{3,7},{4,0},{5,1},{6,2},{7,3},{8,12},{9,13},{10,... | collective-permute-start | bytes 196616 | tf_op jit(solution)/shard_map/ppermute | solution.py:110
  80.9 0.0 collective-permute-start.12
  80.9 3.8 %collective-permute-start.13 = (f32[128,128]{0,1:T(8,128)S(1)}, f32[128,128]{0,1:T(8,128)S(1)}, u32[]{:S(2)}, u32[]{:S(2)}) collective-permute-start(f32[128,128]{0,1:T(8,128)S(1)} %add_add_fusion.2), channel_id=1, source_target_pairs={{0,12},{1,13},{2,14},{3,15},{4,8},{5,9},{6,10},{7,11},{8,4},{9,5},... | collective-permute-start | bytes 196616 | tf_op jit(solution)/shard_map/ppermute | solution.py:110
  84.7 0.2 collective-permute-done.11
  84.9 5.5 %collective-permute-done.12 = f32[128,128]{0,1:T(8,128)S(1)} collective-permute-done((f32[128,128]{0,1:T(8,128)S(1)}, f32[128,128]{0,1:T(8,128)S(1)}, u32[]{:S(2)}, u32[]{:S(2)}) %collective-permute-start.12) | collective-permute-done | bytes 65568 | tf_op jit(solution)/shard_map/ppermute | solution.py:110
  90.4 0.1 collective-permute-start.14
  90.5 3.8 %collective-permute-start.15 = (f32[128,128]{0,1:T(8,128)S(1)}, f32[128,128]{0,1:T(8,128)S(1)}, u32[]{:S(2)}, u32[]{:S(2)}) collective-permute-start(f32[128,128]{0,1:T(8,128)S(1)} %add_add_fusion.1), channel_id=1, source_target_pairs={{0,32},{16,48},{32,0},{48,16},{64,96},{80,112},{96,64},{112,80},{1... | collective-permute-start | bytes 196616 | tf_op jit(solution)/shard_map/ppermute | solution.py:110
  94.3 0.5 collective-permute-start.16
  94.8 0.2 collective-permute-done.14
  95.0 2.2 %collective-permute-done.15 = f32[128,128]{0,1:T(8,128)S(1)} collective-permute-done((f32[128,128]{0,1:T(8,128)S(1)}, f32[128,128]{0,1:T(8,128)S(1)}, u32[]{:S(2)}, u32[]{:S(2)}) %collective-permute-start.15) | collective-permute-done | bytes 65568 | tf_op jit(solution)/shard_map/ppermute | solution.py:110
  97.2 1.4 collective-permute-done.16
  98.6 4.1 %collective-permute-start.17 = (f32[128,128]{0,1:T(8,128)S(1)}, f32[128,128]{0,1:T(8,128)S(1)}, u32[]{:S(2)}, u32[]{:S(2)}) collective-permute-start(f32[128,128]{0,1:T(8,128)S(1)} %add_add_fusion), channel_id=1, source_target_pairs={{0,64},{16,80},{32,96},{48,112},{64,0},{80,16},{96,32},{112,48},{1... | collective-permute-start | bytes 196616 | tf_op jit(solution)/shard_map/ppermute | solution.py:110
  102.7 2.9 %collective-permute-start.18 = (f32[128,128]{0,1:T(8,128)S(1)}, f32[128,128]{0,1:T(8,128)S(1)}, u32[]{:S(2)}, u32[]{:S(2)}) collective-permute-start(f32[128,128]{0,1:T(8,128)S(1)} %add_add_fusion), channel_id=1, source_target_pairs={{0,128},{16,144},{32,160},{48,176},{64,192},{80,208},{96,224},{112... | collective-permute-start | bytes 196616 | tf_op jit(solution)/shard_map/ppermute | solution.py:110
  105.6 0.0 collective-permute-start.19
  105.6 2.9 %collective-permute-done.18 = f32[128,128]{0,1:T(8,128)S(1)} collective-permute-done((f32[128,128]{0,1:T(8,128)S(1)}, f32[128,128]{0,1:T(8,128)S(1)}, u32[]{:S(2)}, u32[]{:S(2)}) %collective-permute-start.18) | collective-permute-done | bytes 65568 | tf_op jit(solution)/shard_map/ppermute | solution.py:110
  108.6 2.5 %collective-permute-done.19 = f32[128,128]{0,1:T(8,128)S(1)} collective-permute-done((f32[128,128]{0,1:T(8,128)S(1)}, f32[128,128]{0,1:T(8,128)S(1)}, u32[]{:S(2)}, u32[]{:S(2)}) %collective-permute-start.19) | collective-permute-done | bytes 65568 | tf_op jit(solution)/shard_map/ppermute | solution.py:110
  111.1 0.1 copy.21
  111.2 11.7 %cholesky.17 = f32[128,128]{1,0:T(8,128)S(1)} custom-call(f32[128,128]{1,0:T(8,128)S(1)} %fusion.17), custom_call_target="Cholesky" | custom-call | tf_op jit(solution)/shard_map/jit(cholesky)/cholesky | solution.py:157
  123.0 0.6 compare_reduce_fusion
  123.6 0.7 fusion.67
  124.3 9.8 %custom-call.7 = f32[1,128,128]{1,2,0:T(8,128)S(1)} custom-call(f32[1,128,128]{2,1,0:T(8,128)S(1)} %get-tuple-element.30), custom_call_target="InvertDiagBlocksLowerTriangular" | custom-call | tf_op jit(solution)/shard_map/jit(_solve_triangular)/triangular_solve | solution.py:158
  134.1 0.2 convolution_bitcast_fusion
  134.4 4.1 %fusion.82 = f32[128,32,256]{2,0,1:T(8,128)S(1)} fusion(f32[128,128,1]{1,0,2:T(8,128)S(1)} %convolution_bitcast_fusion, f32[32,256,128]{2,1,0:T(8,128)} %copy-done.1), kind=kOutput, calls=%fused_computation.179 | convolution fusion | flops 805306368 | bytes 8454144 | tf_op jit(solution)/shard_map/kj,rcj->krc/dot_general | solution.py:161
  138.4 4.4 %copy.22 = f32[128,32,256]{2,1,0:T(8,128)} copy(f32[128,32,256]{2,0,1:T(8,128)S(1)} %fusion.82) | data formatting | bytes 8388608
  142.9 0.7 copy.23
  (22 shorter events, 0.2 us)
Async XLA Ops:
  1.4 18.3 %collective-permute-start.4 = (s32[5,3,256]{2,1,0:T(4,128)S(1)}, s32[5,3,256]{2,1,0:T(4,128)S(1)}, u32[]{:S(2)}, u32[]{:S(2)}) collective-permute-start(s32[5,3,256]{2,1,0:T(4,128)S(1)} %get-tuple-element.27), channel_id=1, source_target_pairs={{0,16},{16,32},{32,48},{48,64},{64,80},{80,96},{96,112},{112,128},... | collective-permute-start | bytes 46088 | tf_op jit(solution)/shard_map/ppermute | solution.py:27
  4.8 14.9 %copy-start.2 = (s32[4,32,256]{2,1,0:T(8,128)S(1)}, s32[4,32,256]{2,1,0:T(8,128)}, u32[]{:S(2)}) copy-start(s32[4,32,256]{2,1,0:T(8,128)} %param.4) | copy-start | bytes 393220
  4.8 14.9 %copy-start.3 = (s32[32,256]{1,0:T(8,128)S(1)}, s32[32,256]{1,0:T(8,128)}, u32[]{:S(2)}) copy-start(s32[32,256]{1,0:T(8,128)} %param.3) | copy-start | bytes 98308
  4.9 14.9 %collective-permute-start.5 = (s32[5,3,256]{2,1,0:T(4,128)S(1)}, s32[5,3,256]{2,1,0:T(4,128)S(1)}, u32[]{:S(2)}, u32[]{:S(2)}) collective-permute-start(s32[5,3,256]{2,1,0:T(4,128)S(1)} %get-tuple-element.28), channel_id=1, source_target_pairs={{16,0},{32,16},{48,32},{64,48},{80,64},{96,80},{112,96},{128,112},... | collective-permute-start | bytes 46088 | tf_op jit(solution)/shard_map/ppermute | solution.py:29
  13.8 14.3 %collective-permute-start = (f32[2,256,128]{2,1,0:T(8,128)S(1)}, f32[2,256,128]{2,1,0:T(8,128)S(1)}, u32[]{:S(2)}, u32[]{:S(2)}) collective-permute-start(f32[2,256,128]{2,1,0:T(8,128)S(1)} %get-tuple-element.19), channel_id=1, source_target_pairs={{0,16},{16,32},{32,48},{48,64},{64,80},{80,96},{96,112},{112,128},... | collective-permute-start | bytes 786440 | tf_op jit(solution)/shard_map/ppermute | solution.py:27
  17.2 10.9 %collective-permute-start.1 = (f32[2,256,128]{2,1,0:T(8,128)S(1)}, f32[2,256,128]{2,1,0:T(8,128)S(1)}, u32[]{:S(2)}, u32[]{:S(2)}) collective-permute-start(f32[2,256,128]{2,1,0:T(8,128)S(1)} %get-tuple-element.20), channel_id=1, source_target_pairs={{16,0},{32,16},{48,32},{64,48},{80,64},{96,80},{112,96},{128,112},... | collective-permute-start | bytes 786440 | tf_op jit(solution)/shard_map/ppermute | solution.py:29
  19.7 8.5 %copy-start = (f32[128,32,256]{0,2,1:T(8,128)S(1)}, f32[128,32,256]{0,2,1:T(8,128)}, u32[]{:S(2)}) copy-start(f32[128,32,256]{0,2,1:T(8,128)} %copy.15) | copy-start | bytes 12582916
  19.9 2.9 %collective-permute-start.6 = (s32[5,38,3]{2,1,0:T(8,128)S(1)}, s32[5,38,3]{2,1,0:T(8,128)S(1)}, u32[]{:S(2)}, u32[]{:S(2)}) collective-permute-start(s32[5,38,3]{2,1,0:T(8,128)S(1)} %get-tuple-element.25), channel_id=1, source_target_pairs={{0,1},{1,2},{2,3},{3,4},{4,5},{5,6},{6,7},{7,8},{8,9},{9,10},{10,1... | collective-permute-start | bytes 6848 | tf_op jit(solution)/shard_map/ppermute | solution.py:27
  21.5 5.3 %collective-permute-start.7 = (s32[5,38,3]{2,1,0:T(8,128)S(1)}, s32[5,38,3]{2,1,0:T(8,128)S(1)}, u32[]{:S(2)}, u32[]{:S(2)}) collective-permute-start(s32[5,38,3]{2,1,0:T(8,128)S(1)} %get-tuple-element.26), channel_id=1, source_target_pairs={{1,0},{2,1},{3,2},{4,3},{5,4},{6,5},{7,6},{8,7},{9,8},{10,9},{11,1... | collective-permute-start | bytes 6848 | tf_op jit(solution)/shard_map/ppermute | solution.py:29
  28.2 6.6 %collective-permute-start.2 = (f32[36,2,128]{2,1,0:T(2,128)S(1)}, f32[36,2,128]{2,1,0:T(2,128)S(1)}, u32[]{:S(2)}, u32[]{:S(2)}) collective-permute-start(f32[36,2,128]{2,1,0:T(2,128)S(1)} %get-tuple-element.17), channel_id=1, source_target_pairs={{0,1},{1,2},{2,3},{3,4},{4,5},{5,6},{6,7},{7,8},{8,9},{9,10},{10,1... | collective-permute-start | bytes 110600 | tf_op jit(solution)/shard_map/ppermute | solution.py:27
  33.4 3.1 %collective-permute-start.3 = (f32[36,2,128]{2,1,0:T(2,128)S(1)}, f32[36,2,128]{2,1,0:T(2,128)S(1)}, u32[]{:S(2)}, u32[]{:S(2)}) collective-permute-start(f32[36,2,128]{2,1,0:T(2,128)S(1)} %get-tuple-element.18), channel_id=1, source_target_pairs={{1,0},{2,1},{3,2},{4,3},{5,4},{6,5},{7,6},{8,7},{9,8},{10,9},{11,1... | collective-permute-start | bytes 110600 | tf_op jit(solution)/shard_map/ppermute | solution.py:29
  62.1 36.5 %copy-start.1 = (f32[32,256,128]{2,1,0:T(8,128)}, f32[32,256,128]{2,1,0:T(8,128)S(1)}, u32[]{:S(2)}) copy-start(f32[32,256,128]{2,1,0:T(8,128)S(1)} %fusion.9) | copy-start | bytes 12582916
  65.6 6.4 %collective-permute-start.10 = (f32[128,128]{0,1:T(8,128)S(1)}, f32[128,128]{0,1:T(8,128)S(1)}, u32[]{:S(2)}, u32[]{:S(2)}) collective-permute-start(f32[128,128]{0,1:T(8,128)S(1)} %convolution_bitcast_fusion.1), channel_id=1, source_target_pairs={{0,3},{1,2},{2,1},{3,0},{4,7},{5,6},{6,5},{7,4},{8,11},{9,10},{10,... | collective-permute-start | bytes 196616 | tf_op jit(solution)/shard_map/ppermute | solution.py:110
  69.7 2.3 %collective-permute-start.8 = (f32[128,128]{0,1:T(8,128)S(1)}, f32[128,128]{0,1:T(8,128)S(1)}, u32[]{:S(2)}, u32[]{:S(2)}) collective-permute-start(f32[128,128]{0,1:T(8,128)S(1)} %convolution_bitcast_fusion.1), channel_id=1, source_target_pairs={{0,1},{1,0},{2,3},{3,2},{4,5},{5,4},{6,7},{7,6},{8,9},{9,8},{10,11... | collective-permute-start | bytes 196616 | tf_op jit(solution)/shard_map/ppermute | solution.py:110
  69.7 4.5 %collective-permute-start.9 = (f32[128,128]{0,1:T(8,128)S(1)}, f32[128,128]{0,1:T(8,128)S(1)}, u32[]{:S(2)}, u32[]{:S(2)}) collective-permute-start(f32[128,128]{0,1:T(8,128)S(1)} %convolution_bitcast_fusion.1), channel_id=1, source_target_pairs={{0,2},{1,3},{2,0},{3,1},{4,6},{5,7},{6,4},{7,5},{8,10},{9,11},{10,... | collective-permute-start | bytes 196616 | tf_op jit(solution)/shard_map/ppermute | solution.py:110
  74.2 10.7 %collective-permute-start.11 = (f32[128,128]{0,1:T(8,128)S(1)}, f32[128,128]{0,1:T(8,128)S(1)}, u32[]{:S(2)}, u32[]{:S(2)}) collective-permute-start(f32[128,128]{0,1:T(8,128)S(1)} %add_add_fusion.2), channel_id=1, source_target_pairs={{0,4},{1,5},{2,6},{3,7},{4,0},{5,1},{6,2},{7,3},{8,12},{9,13},{10,... | collective-permute-start | bytes 196616 | tf_op jit(solution)/shard_map/ppermute | solution.py:110
  80.9 9.5 %collective-permute-start.12 = (f32[128,128]{0,1:T(8,128)S(1)}, f32[128,128]{0,1:T(8,128)S(1)}, u32[]{:S(2)}, u32[]{:S(2)}) collective-permute-start(f32[128,128]{0,1:T(8,128)S(1)} %add_add_fusion.2), channel_id=1, source_target_pairs={{0,8},{1,9},{2,10},{3,11},{4,12},{5,13},{6,14},{7,15},{8,0},{9,1},... | collective-permute-start | bytes 196616 | tf_op jit(solution)/shard_map/ppermute | solution.py:110
  80.9 9.5 %collective-permute-start.13 = (f32[128,128]{0,1:T(8,128)S(1)}, f32[128,128]{0,1:T(8,128)S(1)}, u32[]{:S(2)}, u32[]{:S(2)}) collective-permute-start(f32[128,128]{0,1:T(8,128)S(1)} %add_add_fusion.2), channel_id=1, source_target_pairs={{0,12},{1,13},{2,14},{3,15},{4,8},{5,9},{6,10},{7,11},{8,4},{9,5},... | collective-permute-start | bytes 196616 | tf_op jit(solution)/shard_map/ppermute | solution.py:110
  90.4 4.5 %collective-permute-start.14 = (f32[128,128]{0,1:T(8,128)S(1)}, f32[128,128]{0,1:T(8,128)S(1)}, u32[]{:S(2)}, u32[]{:S(2)}) collective-permute-start(f32[128,128]{0,1:T(8,128)S(1)} %add_add_fusion.1), channel_id=1, source_target_pairs={{0,16},{16,0},{32,48},{48,32},{64,80},{80,64},{96,112},{112,96},{1... | collective-permute-start | bytes 196616 | tf_op jit(solution)/shard_map/ppermute | solution.py:110
  90.5 6.6 %collective-permute-start.15 = (f32[128,128]{0,1:T(8,128)S(1)}, f32[128,128]{0,1:T(8,128)S(1)}, u32[]{:S(2)}, u32[]{:S(2)}) collective-permute-start(f32[128,128]{0,1:T(8,128)S(1)} %add_add_fusion.1), channel_id=1, source_target_pairs={{0,32},{16,48},{32,0},{48,16},{64,96},{80,112},{96,64},{112,80},{1... | collective-permute-start | bytes 196616 | tf_op jit(solution)/shard_map/ppermute | solution.py:110
  94.3 4.3 %collective-permute-start.16 = (f32[128,128]{0,1:T(8,128)S(1)}, f32[128,128]{0,1:T(8,128)S(1)}, u32[]{:S(2)}, u32[]{:S(2)}) collective-permute-start(f32[128,128]{0,1:T(8,128)S(1)} %add_add_fusion.1), channel_id=1, source_target_pairs={{0,48},{16,32},{32,16},{48,0},{64,112},{80,96},{96,80},{112,64},{1... | collective-permute-start | bytes 196616 | tf_op jit(solution)/shard_map/ppermute | solution.py:110
  98.6 7.0 %collective-permute-start.17 = (f32[128,128]{0,1:T(8,128)S(1)}, f32[128,128]{0,1:T(8,128)S(1)}, u32[]{:S(2)}, u32[]{:S(2)}) collective-permute-start(f32[128,128]{0,1:T(8,128)S(1)} %add_add_fusion), channel_id=1, source_target_pairs={{0,64},{16,80},{32,96},{48,112},{64,0},{80,16},{96,32},{112,48},{1... | collective-permute-start | bytes 196616 | tf_op jit(solution)/shard_map/ppermute | solution.py:110
  102.7 5.8 %collective-permute-start.18 = (f32[128,128]{0,1:T(8,128)S(1)}, f32[128,128]{0,1:T(8,128)S(1)}, u32[]{:S(2)}, u32[]{:S(2)}) collective-permute-start(f32[128,128]{0,1:T(8,128)S(1)} %add_add_fusion), channel_id=1, source_target_pairs={{0,128},{16,144},{32,160},{48,176},{64,192},{80,208},{96,224},{112... | collective-permute-start | bytes 196616 | tf_op jit(solution)/shard_map/ppermute | solution.py:110
  105.6 5.5 %collective-permute-start.19 = (f32[128,128]{0,1:T(8,128)S(1)}, f32[128,128]{0,1:T(8,128)S(1)}, u32[]{:S(2)}, u32[]{:S(2)}) collective-permute-start(f32[128,128]{0,1:T(8,128)S(1)} %add_add_fusion), channel_id=1, source_target_pairs={{0,192},{16,208},{32,224},{48,240},{64,128},{80,144},{96,160},{112... | collective-permute-start | bytes 196616 | tf_op jit(solution)/shard_map/ppermute | solution.py:110

commit v8 on v7

--- a/solution.py
+++ b/solution.py
@@ -143,8 +143,15 @@
     counts = labels_wide[1:].astype(jnp.float32)
     weights = neighbour_weights(levels, counts, inside)
     scales = degree_scales(weights)
-    pixels = jnp.transpose(basis_block, (1, 2, 0))
-    extended = padded(pixels, (("row", 0), ("col", 1)), 2)
+    row_ends = row_count - 1
+    head = basis_block[:, :2, :]
+    tail = basis_block[:, tile_rows - 2 :, :]
+    from_above = lax.ppermute(tail, "row", [(i, i + 1) for i in range(row_ends)])
+    from_below = lax.ppermute(head, "row", [(i + 1, i) for i in range(row_ends)])
+    pixels = jnp.concatenate(
+        [jnp.transpose(part, (1, 2, 0)) for part in (from_above, basis_block, from_below)], axis=0
+    )
+    extended = padded(pixels, (("col", 1),), 2)
     first = apply_pixels(extended, pass_coefficients([cropped(w, 1) for w in weights], scales))
     tile_scales = cropped(scales, 1)
     filtered = apply_pixels(first, pass_coefficients([cropped(w, 2) for w in weights], tile_scales))

time: 145 us -> 146 us (level)
  waiting for transfers between devices: 24.6 us -> 21.9 us
  other arithmetic: 50.8 us -> 52.8 us
    ppermute x0 -> x2, starting transfers between devices: none -> 5.85 us  [the longest x1 3.4 us: per_device(): lax.ppermute(tail, 'row', [(i, i + 1) for i in range(row_ends)])]
    ppermute x4 -> x3, starting transfers between devices: 13.5 us -> 10 us  [padded(): lax.ppermute(tail, axis, [(i, (i + 1) % count) for i in range(ends)])]
    ppermute x4 -> x3, waiting for transfers between devices: 5.66 us -> 2.92 us  [padded(): lax.ppermute(head, axis, [((i + 1) % count, i) for i in range(ends)])]
    ppermute x4 -> x3, starting transfers between devices: 7.61 us -> 5.02 us  [padded(): lax.ppermute(head, axis, [((i + 1) % count, i) for i in range(ends)])]
    slice x0 -> x1, local copies, waits for them, and re-layouts: none -> 1.74 us  [per_device(): tail = basis_block[:, tile_rows - 2:, :]]
    unnamed x11 -> x13, local copies, waits for them, and re-layouts: 10.5 us -> 10.5 us
  transfers between devices with their start and end apart: 20 -> 20, of which waited for: 11 -> 10; matrix products, arithmetic and copies ran while one was open for 6% -> 7% of each run, Pallas kernels for 0% -> 0%
where the time goes in v8:
time: 146 us; the launch traced here: 144 us
  other arithmetic  52.8 us (36%)
  starting transfers between devices  47.9 us (33%)
  waiting for transfers between devices  21.9 us (15%)
  local copies, waits for them, and re-layouts  12.7 us (9%)
  matrix products  7.8 us (5%)
    ppermute x12, starting transfers between devices, exchange_sum(): received.append(lax.ppermute(block, axis, route))  27 us
    sub x2, other arithmetic, apply_pixels(): return shifted_pixels(values_in, 0, 0) - summed  21.6 us
    ppermute x12, waiting for transfers between devices, exchange_sum(): received.append(lax.ppermute(block, axis, route))  18.9 us
    another operation x3, other arithmetic, per_device(): factor = jnp.linalg.cholesky(gram)  12.4 us
    unnamed x13, local copies, waits for them, and re-layouts  10.5 us
    ppermute x3, starting transfers between devices, padded(): lax.ppermute(tail, axis, [(i, (i + 1) % count) for i in range(ends)])  10 us
    another operation x1, other arithmetic, per_device(): jax.scipy.linalg.solve_triangular(factor, jnp.eye(vectors, dtype=jnp.floa...  9.81 us
    concatenate x4, other arithmetic, padded(): jnp.concatenate([lax.ppermute(tail, axis, [(i, (i + 1) % count) for i in...  5.09 us
  transfers between devices with their start and end apart: 20, of which 10 were waited for; matrix products, arithmetic and copies ran while one was open for 7% of the time, Pallas kernels for 0%

profile of v8, /device:TPU:2, one launch (start us, length us, event | category | flops | bytes accessed | tf_op | source)
XLA Modules:
  0.0 144.1 jit_solution(3901173327988056268)
XLA Ops:
  0.6 0.8 pad_add_fusion.3
  1.4 3.4 %collective-permute-start.4 = (s32[5,3,256]{2,1,0:T(4,128)S(1)}, s32[5,3,256]{2,1,0:T(4,128)S(1)}, u32[]{:S(2)}, u32[]{:S(2)}) collective-permute-start(s32[5,3,256]{2,1,0:T(4,128)S(1)} %get-tuple-element.27), channel_id=1, source_target_pairs={{0,16},{16,32},{32,48},{48,64},{64,80},{80,96},{96,112},{112,128},... | collective-permute-start | bytes 46088 | tf_op jit(solution)/shard_map/ppermute | solution.py:27
  4.8 2.4 %collective-permute-start.5 = (s32[5,3,256]{2,1,0:T(4,128)S(1)}, s32[5,3,256]{2,1,0:T(4,128)S(1)}, u32[]{:S(2)}, u32[]{:S(2)}) collective-permute-start(s32[5,3,256]{2,1,0:T(4,128)S(1)} %get-tuple-element.28), channel_id=1, source_target_pairs={{16,0},{32,16},{48,32},{64,48},{80,64},{96,80},{112,96},{128,112},... | collective-permute-start | bytes 46088 | tf_op jit(solution)/shard_map/ppermute | solution.py:29
  7.3 1.7 %fusion.80 = (f32[128,2,256]{2,1,0:T(2,128)S(1)}, f32[128,2,256]{2,1,0:T(2,128)S(1)}) fusion(f32[128,32,256]{2,1,0:T(8,128)} %param.5), kind=kLoop, calls=%fused_computation.177 | loop fusion | bytes 1048576 | tf_op jit(solution)/shard_map/slice | solution.py:148
  9.0 3.4 %collective-permute-start = (f32[128,2,256]{2,0,1:T(8,128)S(1)}, f32[128,2,256]{2,0,1:T(8,128)S(1)}, u32[]{:S(2)}, u32[]{:S(2)}) collective-permute-start(f32[128,2,256]{2,0,1:T(8,128)S(1)} %copy.34), channel_id=1, source_target_pairs={{0,16},{16,32},{32,48},{48,64},{64,80},{80,96},{96,112},{112,128},... | collective-permute-start | bytes 786440 | tf_op jit(solution)/shard_map/ppermute | solution.py:149
  12.5 2.5 %collective-permute-start.1 = (f32[128,2,256]{2,0,1:T(8,128)S(1)}, f32[128,2,256]{2,0,1:T(8,128)S(1)}, u32[]{:S(2)}, u32[]{:S(2)}) collective-permute-start(f32[128,2,256]{2,0,1:T(8,128)S(1)} %copy.35), channel_id=1, source_target_pairs={{16,0},{32,16},{48,32},{64,48},{80,64},{96,80},{112,96},{128,112},... | collective-permute-start | bytes 786440 | tf_op jit(solution)/shard_map/ppermute | solution.py:150
  15.0 0.0 copy-start.2
  15.0 0.0 copy-start.3
  15.0 0.0 collective-permute-done.4
  15.0 1.0 pad_add_fusion.1
  16.0 0.1 fusion.81
  16.1 1.3 collective-permute-start.6
  17.4 1.3 collective-permute-start.7
  18.7 0.1 broadcast_multiply_fusion
  18.8 5.3 %copy.16 = f32[128,32,256]{0,2,1:T(8,128)} copy(f32[128,32,256]{2,1,0:T(8,128)} %param.5) | data formatting | bytes 8388608 | tf_op args[2]
  24.1 0.2 pad_add_fusion
  24.3 0.1 fusion.65
  24.4 0.4 add_rsqrt_fusion
  24.8 0.2 slice_multiply_fusion.46
  25.0 0.1 slice_multiply_fusion.28
  25.2 0.3 slice_multiply_fusion.30
  25.4 0.1 copy.18
  25.6 0.1 copy.19
  25.7 0.0 copy-start.1
  25.7 1.1 pad_maximum_fusion.4
  26.9 5.3 %collective-permute-start.2 = (f32[36,2,128]{2,1,0:T(2,128)S(1)}, f32[36,2,128]{2,1,0:T(2,128)S(1)}, u32[]{:S(2)}, u32[]{:S(2)}) collective-permute-start(f32[36,2,128]{2,1,0:T(2,128)S(1)} %get-tuple-element.17), channel_id=1, source_target_pairs={{0,1},{1,2},{2,3},{3,4},{4,5},{5,6},{6,7},{7,8},{8,9},{9,10},{10,1... | collective-permute-start | bytes 110600 | tf_op jit(solution)/shard_map/ppermute | solution.py:27
  32.2 1.3 collective-permute-start.3
  33.5 0.1 slice_multiply_fusion.34
  33.6 2.9 %collective-permute-done.3 = f32[36,2,128]{2,1,0:T(2,128)S(1)} collective-permute-done((f32[36,2,128]{2,1,0:T(2,128)S(1)}, f32[36,2,128]{2,1,0:T(2,128)S(1)}, u32[]{:S(2)}, u32[]{:S(2)}) %collective-permute-start.3) | collective-permute-done | bytes 36896 | tf_op jit(solution)/shard_map/ppermute | solution.py:29
  36.5 2.3 %maximum_maximum_fusion = (f32[36,258,128]{2,1,0:T(8,128)S(1)}, f32[36,258,128]{2,1,0:T(8,128)S(1)}) fusion(f32[2,256,128]{2,1,0:T(8,128)S(1)} %copy.19, f32[32,256,128]{2,1,0:T(8,128)S(1)} %bitcast.38, f32[2,256,128]{2,1,0:T(8,128)S(1)} %copy.18, f32[36,2,128]{2,1,0:T(2,128)S(1)} %collective-permute-done.2, f32[36,2,128]{2,1,0:T(2,128)S(1)} %collective-permute-done.3), kind=kLoop, calls=%fused_computation.2 | loop fusion | flops 7133184 | bytes 14303232 | tf_op jit(solution)/shard_map/concatenate | solution.py:25
  38.8 1.6 %pad_maximum_fusion = f32[36,260,128]{2,1,0:T(8,128)S(1)} fusion(f32[36,2,128]{2,1,0:T(2,128)S(1)} %collective-permute-done.3, f32[2,256,128]{2,1,0:T(8,128)S(1)} %copy.19, f32[32,256,128]{2,1,0:T(8,128)S(1)} %bitcast.39, f32[2,256,128]{2,1,0:T(8,128)S(1)} %copy.18, f32[36,2,128]{2,1,0:T(2,128)S(1)} %collective-permute-done.2), kind=kLoop, calls=%fused_computation | loop fusion | flops 4792320 | bytes 9584640 | tf_op jit(solution)/shard_map/concatenate | solution.py:25
  40.5 11.6 %fusion.1 = f32[34,258,128]{2,1,0:T(8,128)S(1)} fusion(f32[36,258,128]{2,1,0:T(8,128)S(1)} %get-tuple-element.16, f32[36,258,128]{2,1,0:T(8,128)S(1)} %get-tuple-element.15, f32[36,260,128]{2,1,0:T(8,128)S(1)} %pad_maximum_fusion, f32[34,258]{1,0:T(8,128)S(1)} %get-tuple-element.40, f32[34,258]{1,0:T(8,128)S(1)} %get-tuple-element.41, ...), kind=kLoop, calls=%fused_computation.5 | loop fusion | flops 17965056 | bytes 45193344 | tf_op jit(solution)/shard_map/sub | solution.py:101
  52.0 10.1 %fusion.9 = f32[32,256,128]{2,1,0:T(8,128)S(1)} fusion(f32[34,258,128]{2,1,0:T(8,128)S(1)} %fusion.1, f32[32,256]{1,0:T(8,128)S(1)} %get-tuple-element.38, f32[32,256]{1,0:T(8,128)S(1)} %get-tuple-element.37, f32[32,256]{1,0:T(8,128)S(1)} %get-tuple-element.32, f32[32,256]{1,0:T(8,128)S(1)} %get-tuple-element.33, f32[32,256]{1,0:T(8,128)S(1)} %get-tuple-element.34, ...), kind=kLoop, calls=%fused_computation.21 | loop fusion | flops 16777216 | bytes 42205184 | tf_op jit(solution)/shard_map/sub | solution.py:101
  62.1 0.0 copy-start
  62.1 3.5 %convolution_bitcast_fusion.1 = f32[128,128]{0,1:T(8,128)S(1)} fusion(f32[32,256,128]{2,1,0:T(8,128)S(1)} %fusion.9), kind=kOutput, calls=%fused_computation.36 | convolution fusion | flops 805306368 | bytes 4259840 | tf_op jit(solution)/shard_map/rck,rcj->kj/dot_general | solution.py:159
  65.6 4.3 %collective-permute-start.10 = (f32[128,128]{0,1:T(8,128)S(1)}, f32[128,128]{0,1:T(8,128)S(1)}, u32[]{:S(2)}, u32[]{:S(2)}) collective-permute-start(f32[128,128]{0,1:T(8,128)S(1)} %convolution_bitcast_fusion.1), channel_id=1, source_target_pairs={{0,3},{1,2},{2,1},{3,0},{4,7},{5,6},{6,5},{7,4},{8,11},{9,10},{10,... | collective-permute-start | bytes 196616 | tf_op jit(solution)/shard_map/ppermute | solution.py:110
  69.9 0.5 collective-permute-start.9
  70.4 1.8 %collective-permute-done.10 = f32[128,128]{0,1:T(8,128)S(1)} collective-permute-done((f32[128,128]{0,1:T(8,128)S(1)}, f32[128,128]{0,1:T(8,128)S(1)}, u32[]{:S(2)}, u32[]{:S(2)}) %collective-permute-start.10) | collective-permute-done | bytes 65568 | tf_op jit(solution)/shard_map/ppermute | solution.py:110
  72.2 2.2 %collective-permute-done.9 = f32[128,128]{0,1:T(8,128)S(1)} collective-permute-done((f32[128,128]{0,1:T(8,128)S(1)}, f32[128,128]{0,1:T(8,128)S(1)}, u32[]{:S(2)}, u32[]{:S(2)}) %collective-permute-start.9) | collective-permute-done | bytes 65568 | tf_op jit(solution)/shard_map/ppermute | solution.py:110
  74.4 7.0 %collective-permute-start.11 = (f32[128,128]{0,1:T(8,128)S(1)}, f32[128,128]{0,1:T(8,128)S(1)}, u32[]{:S(2)}, u32[]{:S(2)}) collective-permute-start(f32[128,128]{0,1:T(8,128)S(1)} %add_add_fusion.2), channel_id=1, source_target_pairs={{0,4},{1,5},{2,6},{3,7},{4,0},{5,1},{6,2},{7,3},{8,12},{9,13},{10,... | collective-permute-start | bytes 196616 | tf_op jit(solution)/shard_map/ppermute | solution.py:110
  81.4 0.0 collective-permute-start.12
  81.4 3.8 %collective-permute-start.13 = (f32[128,128]{0,1:T(8,128)S(1)}, f32[128,128]{0,1:T(8,128)S(1)}, u32[]{:S(2)}, u32[]{:S(2)}) collective-permute-start(f32[128,128]{0,1:T(8,128)S(1)} %add_add_fusion.2), channel_id=1, source_target_pairs={{0,12},{1,13},{2,14},{3,15},{4,8},{5,9},{6,10},{7,11},{8,4},{9,5},... | collective-permute-start | bytes 196616 | tf_op jit(solution)/shard_map/ppermute | solution.py:110
  85.3 0.2 collective-permute-done.11
  85.4 5.5 %collective-permute-done.12 = f32[128,128]{0,1:T(8,128)S(1)} collective-permute-done((f32[128,128]{0,1:T(8,128)S(1)}, f32[128,128]{0,1:T(8,128)S(1)}, u32[]{:S(2)}, u32[]{:S(2)}) %collective-permute-start.12) | collective-permute-done | bytes 65568 | tf_op jit(solution)/shard_map/ppermute | solution.py:110
  90.9 0.1 collective-permute-start.14
  91.0 3.8 %collective-permute-start.15 = (f32[128,128]{0,1:T(8,128)S(1)}, f32[128,128]{0,1:T(8,128)S(1)}, u32[]{:S(2)}, u32[]{:S(2)}) collective-permute-start(f32[128,128]{0,1:T(8,128)S(1)} %add_add_fusion.1), channel_id=1, source_target_pairs={{0,32},{16,48},{32,0},{48,16},{64,96},{80,112},{96,64},{112,80},{1... | collective-permute-start | bytes 196616 | tf_op jit(solution)/shard_map/ppermute | solution.py:110
  94.8 0.5 collective-permute-start.16
  95.3 0.2 collective-permute-done.14
  95.5 2.2 %collective-permute-done.15 = f32[128,128]{0,1:T(8,128)S(1)} collective-permute-done((f32[128,128]{0,1:T(8,128)S(1)}, f32[128,128]{0,1:T(8,128)S(1)}, u32[]{:S(2)}, u32[]{:S(2)}) %collective-permute-start.15) | collective-permute-done | bytes 65568 | tf_op jit(solution)/shard_map/ppermute | solution.py:110
  97.7 1.4 collective-permute-done.16
  99.1 4.1 %collective-permute-start.17 = (f32[128,128]{0,1:T(8,128)S(1)}, f32[128,128]{0,1:T(8,128)S(1)}, u32[]{:S(2)}, u32[]{:S(2)}) collective-permute-start(f32[128,128]{0,1:T(8,128)S(1)} %add_add_fusion), channel_id=1, source_target_pairs={{0,64},{16,80},{32,96},{48,112},{64,0},{80,16},{96,32},{112,48},{1... | collective-permute-start | bytes 196616 | tf_op jit(solution)/shard_map/ppermute | solution.py:110
  103.2 2.9 %collective-permute-start.18 = (f32[128,128]{0,1:T(8,128)S(1)}, f32[128,128]{0,1:T(8,128)S(1)}, u32[]{:S(2)}, u32[]{:S(2)}) collective-permute-start(f32[128,128]{0,1:T(8,128)S(1)} %add_add_fusion), channel_id=1, source_target_pairs={{0,128},{16,144},{32,160},{48,176},{64,192},{80,208},{96,224},{112... | collective-permute-start | bytes 196616 | tf_op jit(solution)/shard_map/ppermute | solution.py:110
  106.1 0.0 collective-permute-start.19
  106.1 2.9 %collective-permute-done.18 = f32[128,128]{0,1:T(8,128)S(1)} collective-permute-done((f32[128,128]{0,1:T(8,128)S(1)}, f32[128,128]{0,1:T(8,128)S(1)}, u32[]{:S(2)}, u32[]{:S(2)}) %collective-permute-start.18) | collective-permute-done | bytes 65568 | tf_op jit(solution)/shard_map/ppermute | solution.py:110
  109.1 2.5 %collective-permute-done.19 = f32[128,128]{0,1:T(8,128)S(1)} collective-permute-done((f32[128,128]{0,1:T(8,128)S(1)}, f32[128,128]{0,1:T(8,128)S(1)}, u32[]{:S(2)}, u32[]{:S(2)}) %collective-permute-start.19) | collective-permute-done | bytes 65568 | tf_op jit(solution)/shard_map/ppermute | solution.py:110
  111.6 0.1 copy.25
  111.8 11.7 %cholesky.17 = f32[128,128]{1,0:T(8,128)S(1)} custom-call(f32[128,128]{1,0:T(8,128)S(1)} %fusion.17), custom_call_target="Cholesky" | custom-call | tf_op jit(solution)/shard_map/jit(cholesky)/cholesky | solution.py:164
  123.5 0.6 compare_reduce_fusion
  124.1 0.7 fusion.67
  124.8 9.8 %custom-call.7 = f32[1,128,128]{1,2,0:T(8,128)S(1)} custom-call(f32[1,128,128]{2,1,0:T(8,128)S(1)} %get-tuple-element.30), custom_call_target="InvertDiagBlocksLowerTriangular" | custom-call | tf_op jit(solution)/shard_map/jit(_solve_triangular)/triangular_solve | solution.py:165
  134.6 0.2 convolution_bitcast_fusion
  134.9 4.1 %fusion.82 = f32[128,32,256]{2,0,1:T(8,128)S(1)} fusion(f32[128,128,1]{1,0,2:T(8,128)S(1)} %convolution_bitcast_fusion, f32[32,256,128]{2,1,0:T(8,128)} %copy-done), kind=kOutput, calls=%fused_computation.179 | convolution fusion | flops 805306368 | bytes 8454144 | tf_op jit(solution)/shard_map/kj,rcj->krc/dot_general | solution.py:168
  138.9 4.4 %copy.26 = f32[128,32,256]{2,1,0:T(8,128)} copy(f32[128,32,256]{2,0,1:T(8,128)S(1)} %fusion.82) | data formatting | bytes 8388608
  143.4 0.7 copy.27
  (26 shorter events, 0.2 us)
Async XLA Ops:
  1.4 13.6 %collective-permute-start.4 = (s32[5,3,256]{2,1,0:T(4,128)S(1)}, s32[5,3,256]{2,1,0:T(4,128)S(1)}, u32[]{:S(2)}, u32[]{:S(2)}) collective-permute-start(s32[5,3,256]{2,1,0:T(4,128)S(1)} %get-tuple-element.27), channel_id=1, source_target_pairs={{0,16},{16,32},{32,48},{48,64},{64,80},{80,96},{96,112},{112,128},... | collective-permute-start | bytes 46088 | tf_op jit(solution)/shard_map/ppermute | solution.py:27
  4.8 10.2 %collective-permute-start.5 = (s32[5,3,256]{2,1,0:T(4,128)S(1)}, s32[5,3,256]{2,1,0:T(4,128)S(1)}, u32[]{:S(2)}, u32[]{:S(2)}) collective-permute-start(s32[5,3,256]{2,1,0:T(4,128)S(1)} %get-tuple-element.28), channel_id=1, source_target_pairs={{16,0},{32,16},{48,32},{64,48},{80,64},{96,80},{112,96},{128,112},... | collective-permute-start | bytes 46088 | tf_op jit(solution)/shard_map/ppermute | solution.py:29
  9.0 16.4 %collective-permute-start = (f32[128,2,256]{2,0,1:T(8,128)S(1)}, f32[128,2,256]{2,0,1:T(8,128)S(1)}, u32[]{:S(2)}, u32[]{:S(2)}) collective-permute-start(f32[128,2,256]{2,0,1:T(8,128)S(1)} %copy.34), channel_id=1, source_target_pairs={{0,16},{16,32},{32,48},{48,64},{64,80},{80,96},{96,112},{112,128},... | collective-permute-start | bytes 786440 | tf_op jit(solution)/shard_map/ppermute | solution.py:149
  12.5 13.1 %collective-permute-start.1 = (f32[128,2,256]{2,0,1:T(8,128)S(1)}, f32[128,2,256]{2,0,1:T(8,128)S(1)}, u32[]{:S(2)}, u32[]{:S(2)}) collective-permute-start(f32[128,2,256]{2,0,1:T(8,128)S(1)} %copy.35), channel_id=1, source_target_pairs={{16,0},{32,16},{48,32},{64,48},{80,64},{96,80},{112,96},{128,112},... | collective-permute-start | bytes 786440 | tf_op jit(solution)/shard_map/ppermute | solution.py:150
  15.0 9.1 %copy-start.2 = (s32[4,32,256]{2,1,0:T(8,128)S(1)}, s32[4,32,256]{2,1,0:T(8,128)}, u32[]{:S(2)}) copy-start(s32[4,32,256]{2,1,0:T(8,128)} %param.4) | copy-start | bytes 393220
  15.0 9.1 %copy-start.3 = (s32[32,256]{1,0:T(8,128)S(1)}, s32[32,256]{1,0:T(8,128)}, u32[]{:S(2)}) copy-start(s32[32,256]{1,0:T(8,128)} %param.3) | copy-start | bytes 98308
  16.1 8.0 %collective-permute-start.6 = (s32[5,38,3]{2,1,0:T(8,128)S(1)}, s32[5,38,3]{2,1,0:T(8,128)S(1)}, u32[]{:S(2)}, u32[]{:S(2)}) collective-permute-start(s32[5,38,3]{2,1,0:T(8,128)S(1)} %get-tuple-element.25), channel_id=1, source_target_pairs={{0,1},{1,2},{2,3},{3,4},{4,5},{5,6},{6,7},{7,8},{8,9},{9,10},{10,1... | collective-permute-start | bytes 6848 | tf_op jit(solution)/shard_map/ppermute | solution.py:27
  17.4 6.7 %collective-permute-start.7 = (s32[5,38,3]{2,1,0:T(8,128)S(1)}, s32[5,38,3]{2,1,0:T(8,128)S(1)}, u32[]{:S(2)}, u32[]{:S(2)}) collective-permute-start(s32[5,38,3]{2,1,0:T(8,128)S(1)} %get-tuple-element.26), channel_id=1, source_target_pairs={{1,0},{2,1},{3,2},{4,3},{5,4},{6,5},{7,6},{8,7},{9,8},{10,9},{11,1... | collective-permute-start | bytes 6848 | tf_op jit(solution)/shard_map/ppermute | solution.py:29
  25.7 10.8 %copy-start.1 = (f32[128,32,256]{0,2,1:T(8,128)S(1)}, f32[128,32,256]{0,2,1:T(8,128)}, u32[]{:S(2)}) copy-start(f32[128,32,256]{0,2,1:T(8,128)} %copy.16) | copy-start | bytes 12582916
  26.9 6.7 %collective-permute-start.2 = (f32[36,2,128]{2,1,0:T(2,128)S(1)}, f32[36,2,128]{2,1,0:T(2,128)S(1)}, u32[]{:S(2)}, u32[]{:S(2)}) collective-permute-start(f32[36,2,128]{2,1,0:T(2,128)S(1)} %get-tuple-element.17), channel_id=1, source_target_pairs={{0,1},{1,2},{2,3},{3,4},{4,5},{5,6},{6,7},{7,8},{8,9},{9,10},{10,1... | collective-permute-start | bytes 110600 | tf_op jit(solution)/shard_map/ppermute | solution.py:27
  32.2 4.3 %collective-permute-start.3 = (f32[36,2,128]{2,1,0:T(2,128)S(1)}, f32[36,2,128]{2,1,0:T(2,128)S(1)}, u32[]{:S(2)}, u32[]{:S(2)}) collective-permute-start(f32[36,2,128]{2,1,0:T(2,128)S(1)} %get-tuple-element.18), channel_id=1, source_target_pairs={{1,0},{2,1},{3,2},{4,3},{5,4},{6,5},{7,6},{8,7},{9,8},{10,9},{11,1... | collective-permute-start | bytes 110600 | tf_op jit(solution)/shard_map/ppermute | solution.py:29
  62.1 37.0 %copy-start = (f32[32,256,128]{2,1,0:T(8,128)}, f32[32,256,128]{2,1,0:T(8,128)S(1)}, u32[]{:S(2)}) copy-start(f32[32,256,128]{2,1,0:T(8,128)S(1)} %fusion.9) | copy-start | bytes 12582916
  65.6 6.6 %collective-permute-start.10 = (f32[128,128]{0,1:T(8,128)S(1)}, f32[128,128]{0,1:T(8,128)S(1)}, u32[]{:S(2)}, u32[]{:S(2)}) collective-permute-start(f32[128,128]{0,1:T(8,128)S(1)} %convolution_bitcast_fusion.1), channel_id=1, source_target_pairs={{0,3},{1,2},{2,1},{3,0},{4,7},{5,6},{6,5},{7,4},{8,11},{9,10},{10,... | collective-permute-start | bytes 196616 | tf_op jit(solution)/shard_map/ppermute | solution.py:110
  69.9 2.3 %collective-permute-start.8 = (f32[128,128]{0,1:T(8,128)S(1)}, f32[128,128]{0,1:T(8,128)S(1)}, u32[]{:S(2)}, u32[]{:S(2)}) collective-permute-start(f32[128,128]{0,1:T(8,128)S(1)} %convolution_bitcast_fusion.1), channel_id=1, source_target_pairs={{0,1},{1,0},{2,3},{3,2},{4,5},{5,4},{6,7},{7,6},{8,9},{9,8},{10,11... | collective-permute-start | bytes 196616 | tf_op jit(solution)/shard_map/ppermute | solution.py:110
  69.9 4.5 %collective-permute-start.9 = (f32[128,128]{0,1:T(8,128)S(1)}, f32[128,128]{0,1:T(8,128)S(1)}, u32[]{:S(2)}, u32[]{:S(2)}) collective-permute-start(f32[128,128]{0,1:T(8,128)S(1)} %convolution_bitcast_fusion.1), channel_id=1, source_target_pairs={{0,2},{1,3},{2,0},{3,1},{4,6},{5,7},{6,4},{7,5},{8,10},{9,11},{10,... | collective-permute-start | bytes 196616 | tf_op jit(solution)/shard_map/ppermute | solution.py:110
  74.4 11.0 %collective-permute-start.11 = (f32[128,128]{0,1:T(8,128)S(1)}, f32[128,128]{0,1:T(8,128)S(1)}, u32[]{:S(2)}, u32[]{:S(2)}) collective-permute-start(f32[128,128]{0,1:T(8,128)S(1)} %add_add_fusion.2), channel_id=1, source_target_pairs={{0,4},{1,5},{2,6},{3,7},{4,0},{5,1},{6,2},{7,3},{8,12},{9,13},{10,... | collective-permute-start | bytes 196616 | tf_op jit(solution)/shard_map/ppermute | solution.py:110
  81.4 9.5 %collective-permute-start.12 = (f32[128,128]{0,1:T(8,128)S(1)}, f32[128,128]{0,1:T(8,128)S(1)}, u32[]{:S(2)}, u32[]{:S(2)}) collective-permute-start(f32[128,128]{0,1:T(8,128)S(1)} %add_add_fusion.2), channel_id=1, source_target_pairs={{0,8},{1,9},{2,10},{3,11},{4,12},{5,13},{6,14},{7,15},{8,0},{9,1},... | collective-permute-start | bytes 196616 | tf_op jit(solution)/shard_map/ppermute | solution.py:110
  81.4 9.5 %collective-permute-start.13 = (f32[128,128]{0,1:T(8,128)S(1)}, f32[128,128]{0,1:T(8,128)S(1)}, u32[]{:S(2)}, u32[]{:S(2)}) collective-permute-start(f32[128,128]{0,1:T(8,128)S(1)} %add_add_fusion.2), channel_id=1, source_target_pairs={{0,12},{1,13},{2,14},{3,15},{4,8},{5,9},{6,10},{7,11},{8,4},{9,5},... | collective-permute-start | bytes 196616 | tf_op jit(solution)/shard_map/ppermute | solution.py:110
  90.9 4.5 %collective-permute-start.14 = (f32[128,128]{0,1:T(8,128)S(1)}, f32[128,128]{0,1:T(8,128)S(1)}, u32[]{:S(2)}, u32[]{:S(2)}) collective-permute-start(f32[128,128]{0,1:T(8,128)S(1)} %add_add_fusion.1), channel_id=1, source_target_pairs={{0,16},{16,0},{32,48},{48,32},{64,80},{80,64},{96,112},{112,96},{1... | collective-permute-start | bytes 196616 | tf_op jit(solution)/shard_map/ppermute | solution.py:110
  91.0 6.6 %collective-permute-start.15 = (f32[128,128]{0,1:T(8,128)S(1)}, f32[128,128]{0,1:T(8,128)S(1)}, u32[]{:S(2)}, u32[]{:S(2)}) collective-permute-start(f32[128,128]{0,1:T(8,128)S(1)} %add_add_fusion.1), channel_id=1, source_target_pairs={{0,32},{16,48},{32,0},{48,16},{64,96},{80,112},{96,64},{112,80},{1... | collective-permute-start | bytes 196616 | tf_op jit(solution)/shard_map/ppermute | solution.py:110
  94.8 4.3 %collective-permute-start.16 = (f32[128,128]{0,1:T(8,128)S(1)}, f32[128,128]{0,1:T(8,128)S(1)}, u32[]{:S(2)}, u32[]{:S(2)}) collective-permute-start(f32[128,128]{0,1:T(8,128)S(1)} %add_add_fusion.1), channel_id=1, source_target_pairs={{0,48},{16,32},{32,16},{48,0},{64,112},{80,96},{96,80},{112,64},{1... | collective-permute-start | bytes 196616 | tf_op jit(solution)/shard_map/ppermute | solution.py:110
  99.1 7.0 %collective-permute-start.17 = (f32[128,128]{0,1:T(8,128)S(1)}, f32[128,128]{0,1:T(8,128)S(1)}, u32[]{:S(2)}, u32[]{:S(2)}) collective-permute-start(f32[128,128]{0,1:T(8,128)S(1)} %add_add_fusion), channel_id=1, source_target_pairs={{0,64},{16,80},{32,96},{48,112},{64,0},{80,16},{96,32},{112,48},{1... | collective-permute-start | bytes 196616 | tf_op jit(solution)/shard_map/ppermute | solution.py:110
  103.2 5.8 %collective-permute-start.18 = (f32[128,128]{0,1:T(8,128)S(1)}, f32[128,128]{0,1:T(8,128)S(1)}, u32[]{:S(2)}, u32[]{:S(2)}) collective-permute-start(f32[128,128]{0,1:T(8,128)S(1)} %add_add_fusion), channel_id=1, source_target_pairs={{0,128},{16,144},{32,160},{48,176},{64,192},{80,208},{96,224},{112... | collective-permute-start | bytes 196616 | tf_op jit(solution)/shard_map/ppermute | solution.py:110
  106.1 5.5 %collective-permute-start.19 = (f32[128,128]{0,1:T(8,128)S(1)}, f32[128,128]{0,1:T(8,128)S(1)}, u32[]{:S(2)}, u32[]{:S(2)}) collective-permute-start(f32[128,128]{0,1:T(8,128)S(1)} %add_add_fusion), channel_id=1, source_target_pairs={{0,192},{16,208},{32,224},{48,240},{64,128},{80,144},{96,160},{112... | collective-permute-start | bytes 196616 | tf_op jit(solution)/shard_map/ppermute | solution.py:110

commit v9 on v8

--- a/solution.py
+++ b/solution.py
@@ -152,7 +152,11 @@
         [jnp.transpose(part, (1, 2, 0)) for part in (from_above, basis_block, from_below)], axis=0
     )
     extended = padded(pixels, (("col", 1),), 2)
-    first = apply_pixels(extended, pass_coefficients([cropped(w, 1) for w in weights], scales))
+    ring_coefficients = pass_coefficients([cropped(w, 1) for w in weights], scales)
+    core = apply_pixels(pixels, ring_coefficients[:, :, 2 : tile_cols])
+    left = apply_pixels(extended[:, :4], ring_coefficients[:, :, :2])
+    right = apply_pixels(extended[:, tile_cols:], ring_coefficients[:, :, tile_cols:])
+    first = jnp.concatenate([left, core, right], axis=1)
     tile_scales = cropped(scales, 1)
     filtered = apply_pixels(first, pass_coefficients([cropped(w, 2) for w in weights], tile_scales))
     pixel_total = float(total_rows * total_cols)

time: 146 us -> 147 us (level)
  local copies, waits for them, and re-layouts: 12.7 us -> 17.2 us
  waiting for transfers between devices: 21.9 us -> 18.9 us
  other arithmetic: 52.8 us -> 54.7 us
  starting transfers between devices: 47.9 us -> 46.1 us
    concatenate x4 -> x2, other arithmetic: 5.09 us -> 1.15 us  [padded(): jnp.concatenate([lax.ppermute(tail, axis, [(i, (i + 1) % count) for i in...]
    sub x2 -> x4, other arithmetic: 21.6 us -> 24.7 us  [apply_pixels(): return shifted_pixels(values_in, 0, 0) - summed]
    ppermute x3, waiting for transfers between devices: 2.92 us -> 0.01 us  [padded(): lax.ppermute(head, axis, [((i + 1) % count, i) for i in range(ends)])]
    mul x0 -> x8, local copies, waits for them, and re-layouts: none -> 2.91 us  [apply_pixels(): coefficients[index][:, :, None]]
    ppermute x12, starting transfers between devices: 27 us -> 24.7 us  [exchange_sum(): received.append(lax.ppermute(block, axis, route))]
    slice x0 -> x1, other arithmetic: none -> 1.77 us  [padded(): head = lax.slice_in_dim(cells, 0, width, axis=dim)]
    unnamed x13 -> x43, local copies, waits for them, and re-layouts: 10.5 us -> 12.2 us
  transfers between devices with their start and end apart: 20 -> 20, of which waited for: 10 -> 8; matrix products, arithmetic and copies ran while one was open for 7% -> 19% of each run, Pallas kernels for 0% -> 0%
where the time goes in v9:
time: 147 us; the launch traced here: 146 us
  other arithmetic  54.7 us (37%)
  starting transfers between devices  46.1 us (31%)
  waiting for transfers between devices  18.9 us (13%)
  local copies, waits for them, and re-layouts  17.2 us (12%)
  matrix products  7.8 us (5%)
    ppermute x12, starting transfers between devices, exchange_sum(): received.append(lax.ppermute(block, axis, route))  24.7 us
    sub x4, other arithmetic, apply_pixels(): return shifted_pixels(values_in, 0, 0) - summed  24.7 us
    ppermute x12, waiting for transfers between devices, exchange_sum(): received.append(lax.ppermute(block, axis, route))  18.9 us
    another operation x3, other arithmetic, per_device(): factor = jnp.linalg.cholesky(gram)  12.4 us
    unnamed x43, local copies, waits for them, and re-layouts  12.2 us
    ppermute x3, starting transfers between devices, padded(): lax.ppermute(tail, axis, [(i, (i + 1) % count) for i in range(ends)])  10.5 us
    another operation x1, other arithmetic, per_device(): jax.scipy.linalg.solve_triangular(factor, jnp.eye(vectors, dtype=jnp.floa...  9.81 us
    ppermute x3, starting transfers between devices, padded(): lax.ppermute(head, axis, [((i + 1) % count, i) for i in range(ends)])  5.02 us
  transfers between devices with their start and end apart: 20, of which 8 were waited for; matrix products, arithmetic and copies ran while one was open for 19% of the time, Pallas kernels for 0%

profile of v9, /device:TPU:2, one launch (start us, length us, event | category | flops | bytes accessed | tf_op | source)
XLA Modules:
  0.0 145.9 jit_solution(2175971314029749608)
XLA Ops:
  0.6 0.8 pad_add_fusion.3
  1.4 3.4 %collective-permute-start.3 = (s32[5,3,256]{2,1,0:T(4,128)S(1)}, s32[5,3,256]{2,1,0:T(4,128)S(1)}, u32[]{:S(2)}, u32[]{:S(2)}) collective-permute-start(s32[5,3,256]{2,1,0:T(4,128)S(1)} %get-tuple-element.25), channel_id=1, source_target_pairs={{0,16},{16,32},{32,48},{48,64},{64,80},{80,96},{96,112},{112,128},... | collective-permute-start | bytes 46088 | tf_op jit(solution)/shard_map/ppermute | solution.py:27
  4.8 2.4 %collective-permute-start.4 = (s32[5,3,256]{2,1,0:T(4,128)S(1)}, s32[5,3,256]{2,1,0:T(4,128)S(1)}, u32[]{:S(2)}, u32[]{:S(2)}) collective-permute-start(s32[5,3,256]{2,1,0:T(4,128)S(1)} %get-tuple-element.26), channel_id=1, source_target_pairs={{16,0},{32,16},{48,32},{64,48},{80,64},{96,80},{112,96},{128,112},... | collective-permute-start | bytes 46088 | tf_op jit(solution)/shard_map/ppermute | solution.py:29
  7.3 1.7 %fusion.130 = (f32[128,2,256]{2,1,0:T(2,128)S(1)}, f32[128,2,256]{2,1,0:T(2,128)S(1)}) fusion(f32[128,32,256]{2,1,0:T(8,128)} %param.5), kind=kLoop, calls=%fused_computation.269 | loop fusion | bytes 1048576 | tf_op jit(solution)/shard_map/slice | solution.py:147
  9.0 3.4 %collective-permute-start = (f32[128,2,256]{2,0,1:T(8,128)S(1)}, f32[128,2,256]{2,0,1:T(8,128)S(1)}, u32[]{:S(2)}, u32[]{:S(2)}) collective-permute-start(f32[128,2,256]{2,0,1:T(8,128)S(1)} %copy.116), channel_id=1, source_target_pairs={{0,16},{16,32},{32,48},{48,64},{64,80},{80,96},{96,112},{112,128},... | collective-permute-start | bytes 786440 | tf_op jit(solution)/shard_map/ppermute | solution.py:149
  12.5 2.5 %collective-permute-start.1 = (f32[128,2,256]{2,0,1:T(8,128)S(1)}, f32[128,2,256]{2,0,1:T(8,128)S(1)}, u32[]{:S(2)}, u32[]{:S(2)}) collective-permute-start(f32[128,2,256]{2,0,1:T(8,128)S(1)} %copy.117), channel_id=1, source_target_pairs={{16,0},{32,16},{48,32},{64,48},{80,64},{96,80},{112,96},{128,112},... | collective-permute-start | bytes 786440 | tf_op jit(solution)/shard_map/ppermute | solution.py:150
  15.0 0.9 pad_add_fusion.1
  16.0 0.1 fusion.131
  16.1 1.3 collective-permute-start.5
  17.4 1.3 collective-permute-start.6
  18.7 5.3 %copy.48 = f32[128,32,256]{0,2,1:T(8,128)} copy(f32[128,32,256]{2,1,0:T(8,128)} %param.5) | data formatting | bytes 8388608 | tf_op args[2]
  24.0 0.2 pad_add_fusion
  24.3 0.1 fusion.95
  24.4 0.4 add_rsqrt_fusion
  24.8 0.7 slice_multiply_fusion.28
  25.5 0.2 fusion.79
  25.8 0.6 slice_bitcast_fusion.16
  26.5 0.6 slice_bitcast_fusion.12
  27.2 0.6 slice_bitcast_fusion.14
  27.9 0.1 fusion.78
  28.2 0.7 slice_bitcast_fusion.17
  28.8 0.8 slice_multiply_fusion.40
  29.7 0.1 copy.50
  29.8 0.1 copy.51
  30.0 1.8 %pad_maximum_fusion.4 = (f32[36,2,128]{2,1,0:T(2,128)}, f32[36,2,128]{2,1,0:T(2,128)}) fusion(f32[2,256,128]{2,1,0:T(8,128)S(1)} %copy.51, f32[32,256,128]{2,1,0:T(8,128)} %bitcast.101, f32[2,256,128]{2,1,0:T(8,128)S(1)} %copy.50), kind=kLoop, calls=%fused_computation.185 | loop fusion | flops 36864 | bytes 4792320 | tf_op jit(solution)/shard_map/slice | solution.py:23
  31.7 0.6 copy-done
  32.3 0.5 pad_maximum_fusion
  32.8 1.3 collective-permute-start.7
  34.1 5.8 %collective-permute-start.2 = (f32[36,2,128]{2,1,0:T(2,128)}, f32[36,2,128]{2,1,0:T(2,128)S(1)}, u32[]{:S(2)}, u32[]{:S(2)}) collective-permute-start(f32[36,2,128]{2,1,0:T(2,128)} %get-tuple-element.16), channel_id=1, source_target_pairs={{0,1},{1,2},{2,3},{3,4},{4,5},{5,6},{6,7},{7,8},{8,9},{9,10},{10,1... | collective-permute-start | bytes 110600 | tf_op jit(solution)/shard_map/ppermute | solution.py:27
  39.9 12.5 %fusion.3 = f32[34,254,128]{2,1,0:T(8,128)} fusion(f32[2,256,128]{2,1,0:T(8,128)S(1)} %copy.50, f32[2,256,128]{2,1,0:T(8,128)S(1)} %copy.51, f32[36,256,128]{2,1,0:T(8,128)S(1)} %pad_maximum_fusion, f32[32,256,128]{2,1,0:T(8,128)S(1)} %bitcast.103, f32[34,254]{1,0:T(8,128)S(1)} %get-tuple-element.61, f32[34,254]{1,0:T(8,128)S(1)} %get-tuple-element.62, ...), kind=kLoop, calls=%fused_computation.15 | loop fusion | flops 24318976 | bytes 22681472 | tf_op jit(solution)/shard_map/sub | solution.py:101
  52.5 1.3 fusion.99
  53.9 0.4 fusion.110
  54.3 0.6 copy-done.2
  54.9 0.4 pad_maximum_fusion.1
  55.3 0.3 copy-done.5
  55.7 10.5 %fusion.25 = f32[32,256,128]{2,1,0:T(8,128)S(1)} fusion(f32[34,2,128]{2,1,0:T(2,128)S(1)} %fusion.110, f32[34,2,128]{2,1,0:T(2,128)S(1)} %fusion.99, f32[34,254,128]{2,1,0:T(8,128)S(1)} %copy-done.2, f32[34,258,128]{2,1,0:T(8,128)S(1)} %pad_maximum_fusion.1, f32[32,256]{1,0:T(8,128)S(1)} %copy-done.5, f32[32,256]{1,0:T(8,128)S(1)} %get-tuple-element.35, ...), kind=kLoop, calls=%fused_computation.39 | loop fusion | flops 23068672 | bytes 21530624 | tf_op jit(solution)/shard_map/sub | solution.py:101
  66.2 3.5 %convolution_bitcast_fusion.1 = f32[128,128]{0,1:T(8,128)S(1)} fusion(f32[32,256,128]{2,1,0:T(8,128)S(1)} %fusion.25), kind=kOutput, calls=%fused_computation.57 | convolution fusion | flops 805306368 | bytes 4259840 | tf_op jit(solution)/shard_map/rck,rcj->kj/dot_general | solution.py:163
  69.7 2.2 %collective-permute-start.9 = (f32[128,128]{0,1:T(8,128)S(1)}, f32[128,128]{0,1:T(8,128)S(1)}, u32[]{:S(2)}, u32[]{:S(2)}) collective-permute-start(f32[128,128]{0,1:T(8,128)S(1)} %convolution_bitcast_fusion.1), channel_id=1, source_target_pairs={{0,2},{1,3},{2,0},{3,1},{4,6},{5,7},{6,4},{7,5},{8,10},{9,11},{10,... | collective-permute-start | bytes 196616 | tf_op jit(solution)/shard_map/ppermute | solution.py:110
  71.9 1.3 collective-permute-start.8
  73.3 0.9 collective-permute-done.9
  74.2 3.2 %collective-permute-done.10 = f32[128,128]{0,1:T(8,128)S(1)} collective-permute-done((f32[128,128]{0,1:T(8,128)S(1)}, f32[128,128]{0,1:T(8,128)S(1)}, u32[]{:S(2)}, u32[]{:S(2)}) %collective-permute-start.10) | collective-permute-done | bytes 65568 | tf_op jit(solution)/shard_map/ppermute | solution.py:110
  77.4 4.7 %collective-permute-start.13 = (f32[128,128]{0,1:T(8,128)S(1)}, f32[128,128]{0,1:T(8,128)S(1)}, u32[]{:S(2)}, u32[]{:S(2)}) collective-permute-start(f32[128,128]{0,1:T(8,128)S(1)} %add_add_fusion.2), channel_id=1, source_target_pairs={{0,12},{1,13},{2,14},{3,15},{4,8},{5,9},{6,10},{7,11},{8,4},{9,5},... | collective-permute-start | bytes 196616 | tf_op jit(solution)/shard_map/ppermute | solution.py:110
  82.1 4.6 %collective-permute-start.12 = (f32[128,128]{0,1:T(8,128)S(1)}, f32[128,128]{0,1:T(8,128)S(1)}, u32[]{:S(2)}, u32[]{:S(2)}) collective-permute-start(f32[128,128]{0,1:T(8,128)S(1)} %add_add_fusion.2), channel_id=1, source_target_pairs={{0,8},{1,9},{2,10},{3,11},{4,12},{5,13},{6,14},{7,15},{8,0},{9,1},... | collective-permute-start | bytes 196616 | tf_op jit(solution)/shard_map/ppermute | solution.py:110
  86.8 5.9 %collective-permute-done.12 = f32[128,128]{0,1:T(8,128)S(1)} collective-permute-done((f32[128,128]{0,1:T(8,128)S(1)}, f32[128,128]{0,1:T(8,128)S(1)}, u32[]{:S(2)}, u32[]{:S(2)}) %collective-permute-start.12) | collective-permute-done | bytes 65568 | tf_op jit(solution)/shard_map/ppermute | solution.py:110
  92.7 0.6 collective-permute-done.11
  93.4 1.6 %collective-permute-start.16 = (f32[128,128]{0,1:T(8,128)S(1)}, f32[128,128]{0,1:T(8,128)S(1)}, u32[]{:S(2)}, u32[]{:S(2)}) collective-permute-start(f32[128,128]{0,1:T(8,128)S(1)} %add_add_fusion.1), channel_id=1, source_target_pairs={{0,48},{16,32},{32,16},{48,0},{64,112},{80,96},{96,80},{112,64},{1... | collective-permute-start | bytes 196616 | tf_op jit(solution)/shard_map/ppermute | solution.py:110
  95.0 2.3 %collective-permute-start.15 = (f32[128,128]{0,1:T(8,128)S(1)}, f32[128,128]{0,1:T(8,128)S(1)}, u32[]{:S(2)}, u32[]{:S(2)}) collective-permute-start(f32[128,128]{0,1:T(8,128)S(1)} %add_add_fusion.1), channel_id=1, source_target_pairs={{0,32},{16,48},{32,0},{48,16},{64,96},{80,112},{96,64},{112,80},{1... | collective-permute-start | bytes 196616 | tf_op jit(solution)/shard_map/ppermute | solution.py:110
  97.3 1.1 collective-permute-start.14
  98.4 2.4 %collective-permute-done.15 = f32[128,128]{0,1:T(8,128)S(1)} collective-permute-done((f32[128,128]{0,1:T(8,128)S(1)}, f32[128,128]{0,1:T(8,128)S(1)}, u32[]{:S(2)}, u32[]{:S(2)}) %collective-permute-start.15) | collective-permute-done | bytes 65568 | tf_op jit(solution)/shard_map/ppermute | solution.py:110
  100.7 1.0 collective-permute-done.14
  101.8 5.9 %collective-permute-start.19 = (f32[128,128]{0,1:T(8,128)S(1)}, f32[128,128]{0,1:T(8,128)S(1)}, u32[]{:S(2)}, u32[]{:S(2)}) collective-permute-start(f32[128,128]{0,1:T(8,128)S(1)} %add_add_fusion), channel_id=1, source_target_pairs={{0,192},{16,208},{32,224},{48,240},{64,128},{80,144},{96,160},{112... | collective-permute-start | bytes 196616 | tf_op jit(solution)/shard_map/ppermute | solution.py:110
  107.7 0.6 collective-permute-start.18
  108.3 0.3 collective-permute-start.17
  108.6 1.6 %collective-permute-done.19 = f32[128,128]{0,1:T(8,128)S(1)} collective-permute-done((f32[128,128]{0,1:T(8,128)S(1)}, f32[128,128]{0,1:T(8,128)S(1)}, u32[]{:S(2)}, u32[]{:S(2)}) %collective-permute-start.19) | collective-permute-done | bytes 65568 | tf_op jit(solution)/shard_map/ppermute | solution.py:110
  110.2 3.3 %collective-permute-done.18 = f32[128,128]{0,1:T(8,128)S(1)} collective-permute-done((f32[128,128]{0,1:T(8,128)S(1)}, f32[128,128]{0,1:T(8,128)S(1)}, u32[]{:S(2)}, u32[]{:S(2)}) %collective-permute-start.18) | collective-permute-done | bytes 65568 | tf_op jit(solution)/shard_map/ppermute | solution.py:110
  113.5 0.1 copy.91
  113.6 11.7 %cholesky.17 = f32[128,128]{1,0:T(8,128)S(1)} custom-call(f32[128,128]{1,0:T(8,128)S(1)} %fusion.39), custom_call_target="Cholesky" | custom-call | tf_op jit(solution)/shard_map/jit(cholesky)/cholesky | solution.py:168
  125.3 0.6 compare_reduce_fusion
  126.0 0.7 fusion.97
  126.6 0.7 copy.93
  127.4 9.8 %custom-call.7 = f32[1,128,128]{1,2,0:T(8,128)S(1)} custom-call(f32[1,128,128]{2,1,0:T(8,128)S(1)} %get-tuple-element.28), custom_call_target="InvertDiagBlocksLowerTriangular" | custom-call | tf_op jit(solution)/shard_map/jit(_solve_triangular)/triangular_solve | solution.py:169
  137.2 0.2 convolution_bitcast_fusion
  137.4 4.1 %fusion.132 = f32[128,32,256]{2,0,1:T(8,128)S(1)} fusion(f32[128,128,1]{1,0,2:T(8,128)S(1)} %convolution_bitcast_fusion, f32[32,256,128]{2,1,0:T(8,128)} %copy-done.1), kind=kOutput, calls=%fused_computation.271 | convolution fusion | flops 805306368 | bytes 8454144 | tf_op jit(solution)/shard_map/kj,rcj->krc/dot_general | solution.py:172
  141.5 4.4 %copy.92 = f32[128,32,256]{2,1,0:T(8,128)} copy(f32[128,32,256]{2,0,1:T(8,128)S(1)} %fusion.132) | data formatting | bytes 8388608
  (66 shorter events, 0.9 us)
Async XLA Ops:
  1.4 13.6 %collective-permute-start.3 = (s32[5,3,256]{2,1,0:T(4,128)S(1)}, s32[5,3,256]{2,1,0:T(4,128)S(1)}, u32[]{:S(2)}, u32[]{:S(2)}) collective-permute-start(s32[5,3,256]{2,1,0:T(4,128)S(1)} %get-tuple-element.25), channel_id=1, source_target_pairs={{0,16},{16,32},{32,48},{48,64},{64,80},{80,96},{96,112},{112,128},... | collective-permute-start | bytes 46088 | tf_op jit(solution)/shard_map/ppermute | solution.py:27
  4.8 10.2 %collective-permute-start.4 = (s32[5,3,256]{2,1,0:T(4,128)S(1)}, s32[5,3,256]{2,1,0:T(4,128)S(1)}, u32[]{:S(2)}, u32[]{:S(2)}) collective-permute-start(s32[5,3,256]{2,1,0:T(4,128)S(1)} %get-tuple-element.26), channel_id=1, source_target_pairs={{16,0},{32,16},{48,32},{64,48},{80,64},{96,80},{112,96},{128,112},... | collective-permute-start | bytes 46088 | tf_op jit(solution)/shard_map/ppermute | solution.py:29
  9.0 20.6 %collective-permute-start = (f32[128,2,256]{2,0,1:T(8,128)S(1)}, f32[128,2,256]{2,0,1:T(8,128)S(1)}, u32[]{:S(2)}, u32[]{:S(2)}) collective-permute-start(f32[128,2,256]{2,0,1:T(8,128)S(1)} %copy.116), channel_id=1, source_target_pairs={{0,16},{16,32},{32,48},{48,64},{64,80},{80,96},{96,112},{112,128},... | collective-permute-start | bytes 786440 | tf_op jit(solution)/shard_map/ppermute | solution.py:149
  12.5 17.3 %collective-permute-start.1 = (f32[128,2,256]{2,0,1:T(8,128)S(1)}, f32[128,2,256]{2,0,1:T(8,128)S(1)}, u32[]{:S(2)}, u32[]{:S(2)}) collective-permute-start(f32[128,2,256]{2,0,1:T(8,128)S(1)} %copy.117), channel_id=1, source_target_pairs={{16,0},{32,16},{48,32},{64,48},{80,64},{96,80},{112,96},{128,112},... | collective-permute-start | bytes 786440 | tf_op jit(solution)/shard_map/ppermute | solution.py:150
  15.9 8.1 %copy-start.3 = (s32[4,32,256]{2,1,0:T(8,128)S(1)}, s32[4,32,256]{2,1,0:T(8,128)}, u32[]{:S(2)}) copy-start(s32[4,32,256]{2,1,0:T(8,128)} %param.4) | copy-start | bytes 393220
  15.9 8.1 %copy-start.4 = (s32[32,256]{1,0:T(8,128)S(1)}, s32[32,256]{1,0:T(8,128)}, u32[]{:S(2)}) copy-start(s32[32,256]{1,0:T(8,128)} %param.3) | copy-start | bytes 98308
  16.1 8.0 %collective-permute-start.5 = (s32[5,38,3]{2,1,0:T(8,128)S(1)}, s32[5,38,3]{2,1,0:T(8,128)S(1)}, u32[]{:S(2)}, u32[]{:S(2)}) collective-permute-start(s32[5,38,3]{2,1,0:T(8,128)S(1)} %get-tuple-element.23), channel_id=1, source_target_pairs={{0,1},{1,2},{2,3},{3,4},{4,5},{5,6},{6,7},{7,8},{8,9},{9,10},{10,1... | collective-permute-start | bytes 6848 | tf_op jit(solution)/shard_map/ppermute | solution.py:27
  17.4 6.7 %collective-permute-start.6 = (s32[5,38,3]{2,1,0:T(8,128)S(1)}, s32[5,38,3]{2,1,0:T(8,128)S(1)}, u32[]{:S(2)}, u32[]{:S(2)}) collective-permute-start(s32[5,38,3]{2,1,0:T(8,128)S(1)} %get-tuple-element.24), channel_id=1, source_target_pairs={{1,0},{2,1},{3,2},{4,3},{5,4},{6,5},{7,6},{8,7},{9,8},{10,9},{11,1... | collective-permute-start | bytes 6848 | tf_op jit(solution)/shard_map/ppermute | solution.py:29
  29.9 2.4 %copy-start = (f32[128,32,256]{0,2,1:T(8,128)S(1)}, f32[128,32,256]{0,2,1:T(8,128)}, u32[]{:S(2)}) copy-start(f32[128,32,256]{0,2,1:T(8,128)} %copy.48) | copy-start | bytes 12582916
  32.8 19.7 %collective-permute-start.7 = (f32[36,2,128]{2,1,0:T(2,128)}, f32[36,2,128]{2,1,0:T(2,128)S(1)}, u32[]{:S(2)}, u32[]{:S(2)}) collective-permute-start(f32[36,2,128]{2,1,0:T(2,128)} %get-tuple-element.15), channel_id=1, source_target_pairs={{1,0},{2,1},{3,2},{4,3},{5,4},{6,5},{7,6},{8,7},{9,8},{10,9},{11,1... | collective-permute-start | bytes 110600 | tf_op jit(solution)/shard_map/ppermute | solution.py:29
  34.1 19.7 %collective-permute-start.2 = (f32[36,2,128]{2,1,0:T(2,128)}, f32[36,2,128]{2,1,0:T(2,128)S(1)}, u32[]{:S(2)}, u32[]{:S(2)}) collective-permute-start(f32[36,2,128]{2,1,0:T(2,128)} %get-tuple-element.16), channel_id=1, source_target_pairs={{0,1},{1,2},{2,3},{3,4},{4,5},{5,6},{6,7},{7,8},{8,9},{9,10},{10,1... | collective-permute-start | bytes 110600 | tf_op jit(solution)/shard_map/ppermute | solution.py:27
  52.4 1.4 copy-start.12
  52.4 1.4 copy-start.13
  52.4 1.4 copy-start.14
  52.4 1.4 copy-start.15
  52.4 1.4 copy-start.16
  52.4 1.4 copy-start.17
  52.4 1.4 copy-start.18
  52.5 2.4 %copy-start.2 = (f32[34,254,128]{2,1,0:T(8,128)S(1)}, f32[34,254,128]{2,1,0:T(8,128)}, u32[]{:S(2)}) copy-start(f32[34,254,128]{2,1,0:T(8,128)} %fusion.3) | copy-start | bytes 13264900
  54.9 0.8 copy-start.5
  54.9 0.8 copy-start.6
  54.9 0.8 copy-start.7
  54.9 0.8 copy-start.8
  54.9 0.8 copy-start.9
  54.9 0.8 copy-start.10
  54.9 0.8 copy-start.11
  66.2 27.2 %copy-start.1 = (f32[32,256,128]{2,1,0:T(8,128)}, f32[32,256,128]{2,1,0:T(8,128)S(1)}, u32[]{:S(2)}) copy-start(f32[32,256,128]{2,1,0:T(8,128)S(1)} %fusion.25) | copy-start | bytes 12582916
  69.7 4.5 %collective-permute-start.9 = (f32[128,128]{0,1:T(8,128)S(1)}, f32[128,128]{0,1:T(8,128)S(1)}, u32[]{:S(2)}, u32[]{:S(2)}) collective-permute-start(f32[128,128]{0,1:T(8,128)S(1)} %convolution_bitcast_fusion.1), channel_id=1, source_target_pairs={{0,2},{1,3},{2,0},{3,1},{4,6},{5,7},{6,4},{7,5},{8,10},{9,11},{10,... | collective-permute-start | bytes 196616 | tf_op jit(solution)/shard_map/ppermute | solution.py:110
  71.9 2.2 %collective-permute-start.8 = (f32[128,128]{0,1:T(8,128)S(1)}, f32[128,128]{0,1:T(8,128)S(1)}, u32[]{:S(2)}, u32[]{:S(2)}) collective-permute-start(f32[128,128]{0,1:T(8,128)S(1)} %convolution_bitcast_fusion.1), channel_id=1, source_target_pairs={{0,1},{1,0},{2,3},{3,2},{4,5},{5,4},{6,7},{7,6},{8,9},{9,8},{10,11... | collective-permute-start | bytes 196616 | tf_op jit(solution)/shard_map/ppermute | solution.py:110
  73.2 4.2 %collective-permute-start.10 = (f32[128,128]{0,1:T(8,128)S(1)}, f32[128,128]{0,1:T(8,128)S(1)}, u32[]{:S(2)}, u32[]{:S(2)}) collective-permute-start(f32[128,128]{0,1:T(8,128)S(1)} %convolution_bitcast_fusion.1), channel_id=1, source_target_pairs={{0,3},{1,2},{2,1},{3,0},{4,7},{5,6},{6,5},{7,4},{8,11},{9,10},{10,... | collective-permute-start | bytes 196616 | tf_op jit(solution)/shard_map/ppermute | solution.py:110
  77.4 9.4 %collective-permute-start.13 = (f32[128,128]{0,1:T(8,128)S(1)}, f32[128,128]{0,1:T(8,128)S(1)}, u32[]{:S(2)}, u32[]{:S(2)}) collective-permute-start(f32[128,128]{0,1:T(8,128)S(1)} %add_add_fusion.2), channel_id=1, source_target_pairs={{0,12},{1,13},{2,14},{3,15},{4,8},{5,9},{6,10},{7,11},{8,4},{9,5},... | collective-permute-start | bytes 196616 | tf_op jit(solution)/shard_map/ppermute | solution.py:110
  82.1 10.6 %collective-permute-start.12 = (f32[128,128]{0,1:T(8,128)S(1)}, f32[128,128]{0,1:T(8,128)S(1)}, u32[]{:S(2)}, u32[]{:S(2)}) collective-permute-start(f32[128,128]{0,1:T(8,128)S(1)} %add_add_fusion.2), channel_id=1, source_target_pairs={{0,8},{1,9},{2,10},{3,11},{4,12},{5,13},{6,14},{7,15},{8,0},{9,1},... | collective-permute-start | bytes 196616 | tf_op jit(solution)/shard_map/ppermute | solution.py:110
  86.8 6.6 %collective-permute-start.11 = (f32[128,128]{0,1:T(8,128)S(1)}, f32[128,128]{0,1:T(8,128)S(1)}, u32[]{:S(2)}, u32[]{:S(2)}) collective-permute-start(f32[128,128]{0,1:T(8,128)S(1)} %add_add_fusion.2), channel_id=1, source_target_pairs={{0,4},{1,5},{2,6},{3,7},{4,0},{5,1},{6,2},{7,3},{8,12},{9,13},{10,... | collective-permute-start | bytes 196616 | tf_op jit(solution)/shard_map/ppermute | solution.py:110
  93.4 5.0 %collective-permute-start.16 = (f32[128,128]{0,1:T(8,128)S(1)}, f32[128,128]{0,1:T(8,128)S(1)}, u32[]{:S(2)}, u32[]{:S(2)}) collective-permute-start(f32[128,128]{0,1:T(8,128)S(1)} %add_add_fusion.1), channel_id=1, source_target_pairs={{0,48},{16,32},{32,16},{48,0},{64,112},{80,96},{96,80},{112,64},{1... | collective-permute-start | bytes 196616 | tf_op jit(solution)/shard_map/ppermute | solution.py:110
  95.0 5.8 %collective-permute-start.15 = (f32[128,128]{0,1:T(8,128)S(1)}, f32[128,128]{0,1:T(8,128)S(1)}, u32[]{:S(2)}, u32[]{:S(2)}) collective-permute-start(f32[128,128]{0,1:T(8,128)S(1)} %add_add_fusion.1), channel_id=1, source_target_pairs={{0,32},{16,48},{32,0},{48,16},{64,96},{80,112},{96,64},{112,80},{1... | collective-permute-start | bytes 196616 | tf_op jit(solution)/shard_map/ppermute | solution.py:110
  97.3 4.5 %collective-permute-start.14 = (f32[128,128]{0,1:T(8,128)S(1)}, f32[128,128]{0,1:T(8,128)S(1)}, u32[]{:S(2)}, u32[]{:S(2)}) collective-permute-start(f32[128,128]{0,1:T(8,128)S(1)} %add_add_fusion.1), channel_id=1, source_target_pairs={{0,16},{16,0},{32,48},{48,32},{64,80},{80,64},{96,112},{112,96},{1... | collective-permute-start | bytes 196616 | tf_op jit(solution)/shard_map/ppermute | solution.py:110
  101.8 8.4 %collective-permute-start.19 = (f32[128,128]{0,1:T(8,128)S(1)}, f32[128,128]{0,1:T(8,128)S(1)}, u32[]{:S(2)}, u32[]{:S(2)}) collective-permute-start(f32[128,128]{0,1:T(8,128)S(1)} %add_add_fusion), channel_id=1, source_target_pairs={{0,192},{16,208},{32,224},{48,240},{64,128},{80,144},{96,160},{112... | collective-permute-start | bytes 196616 | tf_op jit(solution)/shard_map/ppermute | solution.py:110
  107.7 5.8 %collective-permute-start.18 = (f32[128,128]{0,1:T(8,128)S(1)}, f32[128,128]{0,1:T(8,128)S(1)}, u32[]{:S(2)}, u32[]{:S(2)}) collective-permute-start(f32[128,128]{0,1:T(8,128)S(1)} %add_add_fusion), channel_id=1, source_target_pairs={{0,128},{16,144},{32,160},{48,176},{64,192},{80,208},{96,224},{112... | collective-permute-start | bytes 196616 | tf_op jit(solution)/shard_map/ppermute | solution.py:110
  108.3 5.1 %collective-permute-start.17 = (f32[128,128]{0,1:T(8,128)S(1)}, f32[128,128]{0,1:T(8,128)S(1)}, u32[]{:S(2)}, u32[]{:S(2)}) collective-permute-start(f32[128,128]{0,1:T(8,128)S(1)} %add_add_fusion), channel_id=1, source_target_pairs={{0,64},{16,80},{32,96},{48,112},{64,0},{80,16},{96,32},{112,48},{1... | collective-permute-start | bytes 196616 | tf_op jit(solution)/shard_map/ppermute | solution.py:110

commit v10 on v7

--- a/solution.py
+++ b/solution.py
@@ -151,7 +151,7 @@
     pixel_total = float(total_rows * total_cols)
     gram_local = jnp.einsum(
         "rck,rcj->kj", filtered, filtered,
-        precision=lax.Precision.HIGH, preferred_element_type=jnp.float32,
+        precision=lax.Precision.HIGHEST, preferred_element_type=jnp.float32,
     )
     gram = all_sum(all_sum(gram_local, "col"), "row") / pixel_total
     factor = jnp.linalg.cholesky(gram)
@@ -160,7 +160,7 @@
     )
     ortho = jnp.einsum(
         "kj,rcj->krc", inverse, filtered,
-        precision=lax.Precision.HIGH, preferred_element_type=jnp.float32,
+        precision=lax.Precision.HIGHEST, preferred_element_type=jnp.float32,
     )
     return (ortho, factor.T)
 

time: 145 us -> 151 us (1.041)
  matrix products: 7.8 us -> 13.1 us
    dot_general x1, matrix products: 3.5 us -> 6.94 us  [per_device(): jnp.einsum('rck,rcj->kj', filtered, filtered, precision=lax.Precision.HIG...]
    dot_general x1, matrix products: 4.05 us -> 5.86 us  [per_device(): jnp.einsum('kj,rcj->krc', inverse, filtered, precision=lax.Precision.HIGH...]
  transfers between devices with their start and end apart: 20 -> 20, of which waited for: 11 -> 11; matrix products, arithmetic and copies ran while one was open for 6% -> 5% of each run, Pallas kernels for 0% -> 0%
where the time goes in v10:
time: 151 us; the launch traced here: 149 us
  other arithmetic  50.8 us (34%)
  starting transfers between devices  47.9 us (32%)
  waiting for transfers between devices  24.6 us (16%)
  matrix products  13.1 us (9%)
  local copies, waits for them, and re-layouts  11.7 us (8%)
    ppermute x12, starting transfers between devices, exchange_sum(): received.append(lax.ppermute(block, axis, route))  26.5 us
    sub x2, other arithmetic, apply_pixels(): return shifted_pixels(values_in, 0, 0) - summed  21.6 us
    ppermute x12, waiting for transfers between devices, exchange_sum(): received.append(lax.ppermute(block, axis, route))  19.1 us
    ppermute x4, starting transfers between devices, padded(): lax.ppermute(tail, axis, [(i, (i + 1) % count) for i in range(ends)])  13.5 us
    another operation x3, other arithmetic, per_device(): factor = jnp.linalg.cholesky(gram)  12.4 us
    unnamed x11, local copies, waits for them, and re-layouts  10.5 us
    another operation x1, other arithmetic, per_device(): jax.scipy.linalg.solve_triangular(factor, jnp.eye(vectors, dtype=jnp.floa...  9.81 us
    ppermute x4, starting transfers between devices, padded(): lax.ppermute(head, axis, [((i + 1) % count, i) for i in range(ends)])  7.79 us
  transfers between devices with their start and end apart: 20, of which 11 were waited for; matrix products, arithmetic and copies ran while one was open for 5% of the time, Pallas kernels for 0%

profile of v10, /device:TPU:2, one launch (start us, length us, event | category | flops | bytes accessed | tf_op | source)
XLA Modules:
  0.0 149.1 jit_solution(7097993081036285797)
XLA Ops:
  0.6 0.8 pad_add_fusion.3
  1.4 3.4 %collective-permute-start.4 = (s32[5,3,256]{2,1,0:T(4,128)S(1)}, s32[5,3,256]{2,1,0:T(4,128)S(1)}, u32[]{:S(2)}, u32[]{:S(2)}) collective-permute-start(s32[5,3,256]{2,1,0:T(4,128)S(1)} %get-tuple-element.27), channel_id=1, source_target_pairs={{0,16},{16,32},{32,48},{48,64},{64,80},{80,96},{96,112},{112,128},... | collective-permute-start | bytes 46088 | tf_op jit(solution)/shard_map/ppermute | solution.py:27
  4.8 0.0 copy-start.2
  4.8 0.0 copy-start.3
  4.9 2.6 %collective-permute-start.5 = (s32[5,3,256]{2,1,0:T(4,128)S(1)}, s32[5,3,256]{2,1,0:T(4,128)S(1)}, u32[]{:S(2)}, u32[]{:S(2)}) collective-permute-start(s32[5,3,256]{2,1,0:T(4,128)S(1)} %get-tuple-element.28), channel_id=1, source_target_pairs={{16,0},{32,16},{48,32},{64,48},{80,64},{96,80},{112,96},{128,112},... | collective-permute-start | bytes 46088 | tf_op jit(solution)/shard_map/ppermute | solution.py:29
  7.4 5.3 %copy.15 = f32[128,32,256]{0,2,1:T(8,128)} copy(f32[128,32,256]{2,1,0:T(8,128)} %param.5) | data formatting | bytes 8388608 | tf_op args[2]
  12.7 1.1 fusion.80
  13.8 3.4 %collective-permute-start = (f32[2,256,128]{2,1,0:T(8,128)S(1)}, f32[2,256,128]{2,1,0:T(8,128)S(1)}, u32[]{:S(2)}, u32[]{:S(2)}) collective-permute-start(f32[2,256,128]{2,1,0:T(8,128)S(1)} %get-tuple-element.19), channel_id=1, source_target_pairs={{0,16},{16,32},{32,48},{48,64},{64,80},{80,96},{96,112},{112,128},... | collective-permute-start | bytes 786440 | tf_op jit(solution)/shard_map/ppermute | solution.py:27
  17.2 2.5 %collective-permute-start.1 = (f32[2,256,128]{2,1,0:T(8,128)S(1)}, f32[2,256,128]{2,1,0:T(8,128)S(1)}, u32[]{:S(2)}, u32[]{:S(2)}) collective-permute-start(f32[2,256,128]{2,1,0:T(8,128)S(1)} %get-tuple-element.20), channel_id=1, source_target_pairs={{16,0},{32,16},{48,32},{64,48},{80,64},{96,80},{112,96},{128,112},... | collective-permute-start | bytes 786440 | tf_op jit(solution)/shard_map/ppermute | solution.py:29
  19.7 0.0 copy-start
  19.7 0.0 collective-permute-done.4
  19.7 0.0 collective-permute-done.5
  19.8 0.1 fusion.81
  19.9 1.6 %collective-permute-start.6 = (s32[5,38,3]{2,1,0:T(8,128)S(1)}, s32[5,38,3]{2,1,0:T(8,128)S(1)}, u32[]{:S(2)}, u32[]{:S(2)}) collective-permute-start(s32[5,38,3]{2,1,0:T(8,128)S(1)} %get-tuple-element.25), channel_id=1, source_target_pairs={{0,1},{1,2},{2,3},{3,4},{4,5},{5,6},{6,7},{7,8},{8,9},{9,10},{10,1... | collective-permute-start | bytes 6848 | tf_op jit(solution)/shard_map/ppermute | solution.py:27
  21.5 1.3 collective-permute-start.7
  22.8 0.1 broadcast_multiply_fusion
  22.8 4.0 %collective-permute-done.7 = s32[5,38,3]{2,1,0:T(8,128)S(1)} collective-permute-done((s32[5,38,3]{2,1,0:T(8,128)S(1)}, s32[5,38,3]{2,1,0:T(8,128)S(1)}, u32[]{:S(2)}, u32[]{:S(2)}) %collective-permute-start.7) | collective-permute-done | bytes 2312 | tf_op jit(solution)/shard_map/ppermute | solution.py:29
  26.8 0.2 pad_add_fusion
  27.1 0.1 fusion.65
  27.2 0.4 add_rsqrt_fusion
  27.5 0.2 slice_multiply_fusion.46
  27.7 0.1 slice_multiply_fusion.28
  27.9 0.3 slice_multiply_fusion.30
  28.2 0.0 collective-permute-done.1
  28.2 5.2 %collective-permute-start.2 = (f32[36,2,128]{2,1,0:T(2,128)S(1)}, f32[36,2,128]{2,1,0:T(2,128)S(1)}, u32[]{:S(2)}, u32[]{:S(2)}) collective-permute-start(f32[36,2,128]{2,1,0:T(2,128)S(1)} %get-tuple-element.17), channel_id=1, source_target_pairs={{0,1},{1,2},{2,3},{3,4},{4,5},{5,6},{6,7},{7,8},{8,9},{9,10},{10,1... | collective-permute-start | bytes 110600 | tf_op jit(solution)/shard_map/ppermute | solution.py:27
  33.4 1.5 collective-permute-start.3
  34.9 0.1 slice_multiply_fusion.34
  35.0 1.5 %collective-permute-done.3 = f32[36,2,128]{2,1,0:T(2,128)S(1)} collective-permute-done((f32[36,2,128]{2,1,0:T(2,128)S(1)}, f32[36,2,128]{2,1,0:T(2,128)S(1)}, u32[]{:S(2)}, u32[]{:S(2)}) %collective-permute-start.3) | collective-permute-done | bytes 36896 | tf_op jit(solution)/shard_map/ppermute | solution.py:29
  36.5 2.3 %maximum_maximum_fusion = (f32[36,258,128]{2,1,0:T(8,128)S(1)}, f32[36,258,128]{2,1,0:T(8,128)S(1)}) fusion(f32[2,256,128]{2,1,0:T(8,128)S(1)} %collective-permute-done.1, f32[32,256,128]{2,1,0:T(8,128)S(1)} %bitcast.37, f32[2,256,128]{2,1,0:T(8,128)S(1)} %collective-permute-done, f32[36,2,128]{2,1,0:T(2,128)S(1)} %collective-permute-done.2, ...), kind=kLoop, calls=%fused_computation.2 | loop fusion | flops 7133184 | bytes 14303232 | tf_op jit(solution)/shard_map/concatenate | solution.py:25
  38.8 1.6 %pad_maximum_fusion = f32[36,260,128]{2,1,0:T(8,128)S(1)} fusion(f32[36,2,128]{2,1,0:T(2,128)S(1)} %collective-permute-done.3, f32[2,256,128]{2,1,0:T(8,128)S(1)} %collective-permute-done.1, f32[32,256,128]{2,1,0:T(8,128)S(1)} %bitcast.38, f32[2,256,128]{2,1,0:T(8,128)S(1)} %collective-permute-done, f32[36,2,128]{2,1,0:T(2,128)S(1)} %collective-permute-done.2), kind=kLoop, calls=%fused_computation | loop fusion | flops 4792320 | bytes 9584640 | tf_op jit(solution)/shard_map/concatenate | solution.py:25
  40.4 11.6 %fusion.1 = f32[34,258,128]{2,1,0:T(8,128)S(1)} fusion(f32[36,258,128]{2,1,0:T(8,128)S(1)} %get-tuple-element.16, f32[36,258,128]{2,1,0:T(8,128)S(1)} %get-tuple-element.15, f32[36,260,128]{2,1,0:T(8,128)S(1)} %pad_maximum_fusion, f32[34,258]{1,0:T(8,128)S(1)} %get-tuple-element.40, f32[34,258]{1,0:T(8,128)S(1)} %get-tuple-element.41, ...), kind=kLoop, calls=%fused_computation.5 | loop fusion | flops 17965056 | bytes 45193344 | tf_op jit(solution)/shard_map/sub | solution.py:101
  52.0 10.1 %fusion.9 = f32[32,256,128]{2,1,0:T(8,128)S(1)} fusion(f32[34,258,128]{2,1,0:T(8,128)S(1)} %fusion.1, f32[32,256]{1,0:T(8,128)S(1)} %get-tuple-element.38, f32[32,256]{1,0:T(8,128)S(1)} %get-tuple-element.37, f32[32,256]{1,0:T(8,128)S(1)} %get-tuple-element.32, f32[32,256]{1,0:T(8,128)S(1)} %get-tuple-element.33, f32[32,256]{1,0:T(8,128)S(1)} %get-tuple-element.34, ...), kind=kLoop, calls=%fused_computation.21 | loop fusion | flops 16777216 | bytes 42205184 | tf_op jit(solution)/shard_map/sub | solution.py:101
  62.1 0.0 copy-start.1
  62.1 6.9 %convolution_bitcast_fusion.1 = f32[128,128]{0,1:T(8,128)S(1)} fusion(f32[32,256,128]{2,1,0:T(8,128)S(1)} %fusion.9), kind=kOutput, calls=%fused_computation.36 | convolution fusion | flops 1610612736 | bytes 4259840 | tf_op jit(solution)/shard_map/rck,rcj->kj/dot_general | solution.py:152
  69.0 4.1 %collective-permute-start.10 = (f32[128,128]{0,1:T(8,128)S(1)}, f32[128,128]{0,1:T(8,128)S(1)}, u32[]{:S(2)}, u32[]{:S(2)}) collective-permute-start(f32[128,128]{0,1:T(8,128)S(1)} %convolution_bitcast_fusion.1), channel_id=1, source_target_pairs={{0,3},{1,2},{2,1},{3,0},{4,7},{5,6},{6,5},{7,4},{8,11},{9,10},{10,... | collective-permute-start | bytes 196616 | tf_op jit(solution)/shard_map/ppermute | solution.py:110
  73.1 0.5 collective-permute-start.9
  73.6 1.8 %collective-permute-done.10 = f32[128,128]{0,1:T(8,128)S(1)} collective-permute-done((f32[128,128]{0,1:T(8,128)S(1)}, f32[128,128]{0,1:T(8,128)S(1)}, u32[]{:S(2)}, u32[]{:S(2)}) %collective-permute-start.10) | collective-permute-done | bytes 65568 | tf_op jit(solution)/shard_map/ppermute | solution.py:110
  75.4 0.0 collective-permute-done.8
  75.4 2.2 %collective-permute-done.9 = f32[128,128]{0,1:T(8,128)S(1)} collective-permute-done((f32[128,128]{0,1:T(8,128)S(1)}, f32[128,128]{0,1:T(8,128)S(1)}, u32[]{:S(2)}, u32[]{:S(2)}) %collective-permute-start.9) | collective-permute-done | bytes 65568 | tf_op jit(solution)/shard_map/ppermute | solution.py:110
  77.6 6.9 %collective-permute-start.11 = (f32[128,128]{0,1:T(8,128)S(1)}, f32[128,128]{0,1:T(8,128)S(1)}, u32[]{:S(2)}, u32[]{:S(2)}) collective-permute-start(f32[128,128]{0,1:T(8,128)S(1)} %add_add_fusion.2), channel_id=1, source_target_pairs={{0,4},{1,5},{2,6},{3,7},{4,0},{5,1},{6,2},{7,3},{8,12},{9,13},{10,... | collective-permute-start | bytes 196616 | tf_op jit(solution)/shard_map/ppermute | solution.py:110
  84.5 0.0 collective-permute-start.12
  84.6 3.7 %collective-permute-start.13 = (f32[128,128]{0,1:T(8,128)S(1)}, f32[128,128]{0,1:T(8,128)S(1)}, u32[]{:S(2)}, u32[]{:S(2)}) collective-permute-start(f32[128,128]{0,1:T(8,128)S(1)} %add_add_fusion.2), channel_id=1, source_target_pairs={{0,12},{1,13},{2,14},{3,15},{4,8},{5,9},{6,10},{7,11},{8,4},{9,5},... | collective-permute-start | bytes 196616 | tf_op jit(solution)/shard_map/ppermute | solution.py:110
  88.2 0.3 collective-permute-done.11
  88.6 5.5 %collective-permute-done.12 = f32[128,128]{0,1:T(8,128)S(1)} collective-permute-done((f32[128,128]{0,1:T(8,128)S(1)}, f32[128,128]{0,1:T(8,128)S(1)}, u32[]{:S(2)}, u32[]{:S(2)}) %collective-permute-start.12) | collective-permute-done | bytes 65568 | tf_op jit(solution)/shard_map/ppermute | solution.py:110
  94.1 0.0 collective-permute-done.13
  94.1 0.1 collective-permute-start.14
  94.2 3.8 %collective-permute-start.15 = (f32[128,128]{0,1:T(8,128)S(1)}, f32[128,128]{0,1:T(8,128)S(1)}, u32[]{:S(2)}, u32[]{:S(2)}) collective-permute-start(f32[128,128]{0,1:T(8,128)S(1)} %add_add_fusion.1), channel_id=1, source_target_pairs={{0,32},{16,48},{32,0},{48,16},{64,96},{80,112},{96,64},{112,80},{1... | collective-permute-start | bytes 196616 | tf_op jit(solution)/shard_map/ppermute | solution.py:110
  98.0 0.5 collective-permute-start.16
  98.4 0.3 collective-permute-done.14
  98.7 2.1 %collective-permute-done.15 = f32[128,128]{0,1:T(8,128)S(1)} collective-permute-done((f32[128,128]{0,1:T(8,128)S(1)}, f32[128,128]{0,1:T(8,128)S(1)}, u32[]{:S(2)}, u32[]{:S(2)}) %collective-permute-start.15) | collective-permute-done | bytes 65568 | tf_op jit(solution)/shard_map/ppermute | solution.py:110
  100.8 1.4 collective-permute-done.16
  102.3 4.1 %collective-permute-start.17 = (f32[128,128]{0,1:T(8,128)S(1)}, f32[128,128]{0,1:T(8,128)S(1)}, u32[]{:S(2)}, u32[]{:S(2)}) collective-permute-start(f32[128,128]{0,1:T(8,128)S(1)} %add_add_fusion), channel_id=1, source_target_pairs={{0,64},{16,80},{32,96},{48,112},{64,0},{80,16},{96,32},{112,48},{1... | collective-permute-start | bytes 196616 | tf_op jit(solution)/shard_map/ppermute | solution.py:110
  106.4 2.9 %collective-permute-start.18 = (f32[128,128]{0,1:T(8,128)S(1)}, f32[128,128]{0,1:T(8,128)S(1)}, u32[]{:S(2)}, u32[]{:S(2)}) collective-permute-start(f32[128,128]{0,1:T(8,128)S(1)} %add_add_fusion), channel_id=1, source_target_pairs={{0,128},{16,144},{32,160},{48,176},{64,192},{80,208},{96,224},{112... | collective-permute-start | bytes 196616 | tf_op jit(solution)/shard_map/ppermute | solution.py:110
  109.3 2.9 %collective-permute-done.18 = f32[128,128]{0,1:T(8,128)S(1)} collective-permute-done((f32[128,128]{0,1:T(8,128)S(1)}, f32[128,128]{0,1:T(8,128)S(1)}, u32[]{:S(2)}, u32[]{:S(2)}) %collective-permute-start.18) | collective-permute-done | bytes 65568 | tf_op jit(solution)/shard_map/ppermute | solution.py:110
  112.2 2.5 %collective-permute-done.19 = f32[128,128]{0,1:T(8,128)S(1)} collective-permute-done((f32[128,128]{0,1:T(8,128)S(1)}, f32[128,128]{0,1:T(8,128)S(1)}, u32[]{:S(2)}, u32[]{:S(2)}) %collective-permute-start.19) | collective-permute-done | bytes 65568 | tf_op jit(solution)/shard_map/ppermute | solution.py:110
  114.8 0.1 copy.21
  114.9 11.7 %cholesky.17 = f32[128,128]{1,0:T(8,128)S(1)} custom-call(f32[128,128]{1,0:T(8,128)S(1)} %fusion.17), custom_call_target="Cholesky" | custom-call | tf_op jit(solution)/shard_map/jit(cholesky)/cholesky | solution.py:157
  126.6 0.6 compare_reduce_fusion
  127.3 0.7 fusion.67
  128.0 9.8 %custom-call.7 = f32[1,128,128]{1,2,0:T(8,128)S(1)} custom-call(f32[1,128,128]{2,1,0:T(8,128)S(1)} %get-tuple-element.30), custom_call_target="InvertDiagBlocksLowerTriangular" | custom-call | tf_op jit(solution)/shard_map/jit(_solve_triangular)/triangular_solve | solution.py:158
  137.8 0.2 convolution_bitcast_fusion
  138.0 5.9 %fusion.82 = f32[128,32,256]{2,0,1:T(8,128)S(1)} fusion(f32[128,128,1]{1,0,2:T(8,128)S(1)} %convolution_bitcast_fusion, f32[32,256,128]{2,1,0:T(8,128)} %copy-done.1), kind=kOutput, calls=%fused_computation.179 | convolution fusion | flops 1610612736 | bytes 8454144 | tf_op jit(solution)/shard_map/kj,rcj->krc/dot_general | solution.py:161
  143.9 4.4 %copy.22 = f32[128,32,256]{2,1,0:T(8,128)} copy(f32[128,32,256]{2,0,1:T(8,128)S(1)} %fusion.82) | data formatting | bytes 8388608
  148.3 0.7 copy.23
  (22 shorter events, 0.2 us)
Async XLA Ops:
  1.4 18.3 %collective-permute-start.4 = (s32[5,3,256]{2,1,0:T(4,128)S(1)}, s32[5,3,256]{2,1,0:T(4,128)S(1)}, u32[]{:S(2)}, u32[]{:S(2)}) collective-permute-start(s32[5,3,256]{2,1,0:T(4,128)S(1)} %get-tuple-element.27), channel_id=1, source_target_pairs={{0,16},{16,32},{32,48},{48,64},{64,80},{80,96},{96,112},{112,128},... | collective-permute-start | bytes 46088 | tf_op jit(solution)/shard_map/ppermute | solution.py:27
  4.8 14.9 %copy-start.2 = (s32[4,32,256]{2,1,0:T(8,128)S(1)}, s32[4,32,256]{2,1,0:T(8,128)}, u32[]{:S(2)}) copy-start(s32[4,32,256]{2,1,0:T(8,128)} %param.4) | copy-start | bytes 393220
  4.8 14.9 %copy-start.3 = (s32[32,256]{1,0:T(8,128)S(1)}, s32[32,256]{1,0:T(8,128)}, u32[]{:S(2)}) copy-start(s32[32,256]{1,0:T(8,128)} %param.3) | copy-start | bytes 98308
  4.9 14.9 %collective-permute-start.5 = (s32[5,3,256]{2,1,0:T(4,128)S(1)}, s32[5,3,256]{2,1,0:T(4,128)S(1)}, u32[]{:S(2)}, u32[]{:S(2)}) collective-permute-start(s32[5,3,256]{2,1,0:T(4,128)S(1)} %get-tuple-element.28), channel_id=1, source_target_pairs={{16,0},{32,16},{48,32},{64,48},{80,64},{96,80},{112,96},{128,112},... | collective-permute-start | bytes 46088 | tf_op jit(solution)/shard_map/ppermute | solution.py:29
  13.8 14.3 %collective-permute-start = (f32[2,256,128]{2,1,0:T(8,128)S(1)}, f32[2,256,128]{2,1,0:T(8,128)S(1)}, u32[]{:S(2)}, u32[]{:S(2)}) collective-permute-start(f32[2,256,128]{2,1,0:T(8,128)S(1)} %get-tuple-element.19), channel_id=1, source_target_pairs={{0,16},{16,32},{32,48},{48,64},{64,80},{80,96},{96,112},{112,128},... | collective-permute-start | bytes 786440 | tf_op jit(solution)/shard_map/ppermute | solution.py:27
  17.2 10.9 %collective-permute-start.1 = (f32[2,256,128]{2,1,0:T(8,128)S(1)}, f32[2,256,128]{2,1,0:T(8,128)S(1)}, u32[]{:S(2)}, u32[]{:S(2)}) collective-permute-start(f32[2,256,128]{2,1,0:T(8,128)S(1)} %get-tuple-element.20), channel_id=1, source_target_pairs={{16,0},{32,16},{48,32},{64,48},{80,64},{96,80},{112,96},{128,112},... | collective-permute-start | bytes 786440 | tf_op jit(solution)/shard_map/ppermute | solution.py:29
  19.7 8.5 %copy-start = (f32[128,32,256]{0,2,1:T(8,128)S(1)}, f32[128,32,256]{0,2,1:T(8,128)}, u32[]{:S(2)}) copy-start(f32[128,32,256]{0,2,1:T(8,128)} %copy.15) | copy-start | bytes 12582916
  19.9 2.9 %collective-permute-start.6 = (s32[5,38,3]{2,1,0:T(8,128)S(1)}, s32[5,38,3]{2,1,0:T(8,128)S(1)}, u32[]{:S(2)}, u32[]{:S(2)}) collective-permute-start(s32[5,38,3]{2,1,0:T(8,128)S(1)} %get-tuple-element.25), channel_id=1, source_target_pairs={{0,1},{1,2},{2,3},{3,4},{4,5},{5,6},{6,7},{7,8},{8,9},{9,10},{10,1... | collective-permute-start | bytes 6848 | tf_op jit(solution)/shard_map/ppermute | solution.py:27
  21.5 5.3 %collective-permute-start.7 = (s32[5,38,3]{2,1,0:T(8,128)S(1)}, s32[5,38,3]{2,1,0:T(8,128)S(1)}, u32[]{:S(2)}, u32[]{:S(2)}) collective-permute-start(s32[5,38,3]{2,1,0:T(8,128)S(1)} %get-tuple-element.26), channel_id=1, source_target_pairs={{1,0},{2,1},{3,2},{4,3},{5,4},{6,5},{7,6},{8,7},{9,8},{10,9},{11,1... | collective-permute-start | bytes 6848 | tf_op jit(solution)/shard_map/ppermute | solution.py:29
  28.2 6.8 %collective-permute-start.2 = (f32[36,2,128]{2,1,0:T(2,128)S(1)}, f32[36,2,128]{2,1,0:T(2,128)S(1)}, u32[]{:S(2)}, u32[]{:S(2)}) collective-permute-start(f32[36,2,128]{2,1,0:T(2,128)S(1)} %get-tuple-element.17), channel_id=1, source_target_pairs={{0,1},{1,2},{2,3},{3,4},{4,5},{5,6},{6,7},{7,8},{8,9},{9,10},{10,1... | collective-permute-start | bytes 110600 | tf_op jit(solution)/shard_map/ppermute | solution.py:27
  33.4 3.1 %collective-permute-start.3 = (f32[36,2,128]{2,1,0:T(2,128)S(1)}, f32[36,2,128]{2,1,0:T(2,128)S(1)}, u32[]{:S(2)}, u32[]{:S(2)}) collective-permute-start(f32[36,2,128]{2,1,0:T(2,128)S(1)} %get-tuple-element.18), channel_id=1, source_target_pairs={{1,0},{2,1},{3,2},{4,3},{5,4},{6,5},{7,6},{8,7},{9,8},{10,9},{11,1... | collective-permute-start | bytes 110600 | tf_op jit(solution)/shard_map/ppermute | solution.py:29
  62.1 40.2 %copy-start.1 = (f32[32,256,128]{2,1,0:T(8,128)}, f32[32,256,128]{2,1,0:T(8,128)S(1)}, u32[]{:S(2)}) copy-start(f32[32,256,128]{2,1,0:T(8,128)S(1)} %fusion.9) | copy-start | bytes 12582916
  69.0 6.4 %collective-permute-start.10 = (f32[128,128]{0,1:T(8,128)S(1)}, f32[128,128]{0,1:T(8,128)S(1)}, u32[]{:S(2)}, u32[]{:S(2)}) collective-permute-start(f32[128,128]{0,1:T(8,128)S(1)} %convolution_bitcast_fusion.1), channel_id=1, source_target_pairs={{0,3},{1,2},{2,1},{3,0},{4,7},{5,6},{6,5},{7,4},{8,11},{9,10},{10,... | collective-permute-start | bytes 196616 | tf_op jit(solution)/shard_map/ppermute | solution.py:110
  73.1 2.3 %collective-permute-start.8 = (f32[128,128]{0,1:T(8,128)S(1)}, f32[128,128]{0,1:T(8,128)S(1)}, u32[]{:S(2)}, u32[]{:S(2)}) collective-permute-start(f32[128,128]{0,1:T(8,128)S(1)} %convolution_bitcast_fusion.1), channel_id=1, source_target_pairs={{0,1},{1,0},{2,3},{3,2},{4,5},{5,4},{6,7},{7,6},{8,9},{9,8},{10,11... | collective-permute-start | bytes 196616 | tf_op jit(solution)/shard_map/ppermute | solution.py:110
  73.1 4.5 %collective-permute-start.9 = (f32[128,128]{0,1:T(8,128)S(1)}, f32[128,128]{0,1:T(8,128)S(1)}, u32[]{:S(2)}, u32[]{:S(2)}) collective-permute-start(f32[128,128]{0,1:T(8,128)S(1)} %convolution_bitcast_fusion.1), channel_id=1, source_target_pairs={{0,2},{1,3},{2,0},{3,1},{4,6},{5,7},{6,4},{7,5},{8,10},{9,11},{10,... | collective-permute-start | bytes 196616 | tf_op jit(solution)/shard_map/ppermute | solution.py:110
  77.6 10.9 %collective-permute-start.11 = (f32[128,128]{0,1:T(8,128)S(1)}, f32[128,128]{0,1:T(8,128)S(1)}, u32[]{:S(2)}, u32[]{:S(2)}) collective-permute-start(f32[128,128]{0,1:T(8,128)S(1)} %add_add_fusion.2), channel_id=1, source_target_pairs={{0,4},{1,5},{2,6},{3,7},{4,0},{5,1},{6,2},{7,3},{8,12},{9,13},{10,... | collective-permute-start | bytes 196616 | tf_op jit(solution)/shard_map/ppermute | solution.py:110
  84.5 9.5 %collective-permute-start.12 = (f32[128,128]{0,1:T(8,128)S(1)}, f32[128,128]{0,1:T(8,128)S(1)}, u32[]{:S(2)}, u32[]{:S(2)}) collective-permute-start(f32[128,128]{0,1:T(8,128)S(1)} %add_add_fusion.2), channel_id=1, source_target_pairs={{0,8},{1,9},{2,10},{3,11},{4,12},{5,13},{6,14},{7,15},{8,0},{9,1},... | collective-permute-start | bytes 196616 | tf_op jit(solution)/shard_map/ppermute | solution.py:110
  84.6 9.5 %collective-permute-start.13 = (f32[128,128]{0,1:T(8,128)S(1)}, f32[128,128]{0,1:T(8,128)S(1)}, u32[]{:S(2)}, u32[]{:S(2)}) collective-permute-start(f32[128,128]{0,1:T(8,128)S(1)} %add_add_fusion.2), channel_id=1, source_target_pairs={{0,12},{1,13},{2,14},{3,15},{4,8},{5,9},{6,10},{7,11},{8,4},{9,5},... | collective-permute-start | bytes 196616 | tf_op jit(solution)/shard_map/ppermute | solution.py:110
  94.1 4.6 %collective-permute-start.14 = (f32[128,128]{0,1:T(8,128)S(1)}, f32[128,128]{0,1:T(8,128)S(1)}, u32[]{:S(2)}, u32[]{:S(2)}) collective-permute-start(f32[128,128]{0,1:T(8,128)S(1)} %add_add_fusion.1), channel_id=1, source_target_pairs={{0,16},{16,0},{32,48},{48,32},{64,80},{80,64},{96,112},{112,96},{1... | collective-permute-start | bytes 196616 | tf_op jit(solution)/shard_map/ppermute | solution.py:110
  94.2 6.6 %collective-permute-start.15 = (f32[128,128]{0,1:T(8,128)S(1)}, f32[128,128]{0,1:T(8,128)S(1)}, u32[]{:S(2)}, u32[]{:S(2)}) collective-permute-start(f32[128,128]{0,1:T(8,128)S(1)} %add_add_fusion.1), channel_id=1, source_target_pairs={{0,32},{16,48},{32,0},{48,16},{64,96},{80,112},{96,64},{112,80},{1... | collective-permute-start | bytes 196616 | tf_op jit(solution)/shard_map/ppermute | solution.py:110
  98.0 4.3 %collective-permute-start.16 = (f32[128,128]{0,1:T(8,128)S(1)}, f32[128,128]{0,1:T(8,128)S(1)}, u32[]{:S(2)}, u32[]{:S(2)}) collective-permute-start(f32[128,128]{0,1:T(8,128)S(1)} %add_add_fusion.1), channel_id=1, source_target_pairs={{0,48},{16,32},{32,16},{48,0},{64,112},{80,96},{96,80},{112,64},{1... | collective-permute-start | bytes 196616 | tf_op jit(solution)/shard_map/ppermute | solution.py:110
  102.3 7.0 %collective-permute-start.17 = (f32[128,128]{0,1:T(8,128)S(1)}, f32[128,128]{0,1:T(8,128)S(1)}, u32[]{:S(2)}, u32[]{:S(2)}) collective-permute-start(f32[128,128]{0,1:T(8,128)S(1)} %add_add_fusion), channel_id=1, source_target_pairs={{0,64},{16,80},{32,96},{48,112},{64,0},{80,16},{96,32},{112,48},{1... | collective-permute-start | bytes 196616 | tf_op jit(solution)/shard_map/ppermute | solution.py:110
  106.4 5.8 %collective-permute-start.18 = (f32[128,128]{0,1:T(8,128)S(1)}, f32[128,128]{0,1:T(8,128)S(1)}, u32[]{:S(2)}, u32[]{:S(2)}) collective-permute-start(f32[128,128]{0,1:T(8,128)S(1)} %add_add_fusion), channel_id=1, source_target_pairs={{0,128},{16,144},{32,160},{48,176},{64,192},{80,208},{96,224},{112... | collective-permute-start | bytes 196616 | tf_op jit(solution)/shard_map/ppermute | solution.py:110
  109.3 5.5 %collective-permute-start.19 = (f32[128,128]{0,1:T(8,128)S(1)}, f32[128,128]{0,1:T(8,128)S(1)}, u32[]{:S(2)}, u32[]{:S(2)}) collective-permute-start(f32[128,128]{0,1:T(8,128)S(1)} %add_add_fusion), channel_id=1, source_target_pairs={{0,192},{16,208},{32,224},{48,240},{64,128},{80,144},{96,160},{112... | collective-permute-start | bytes 196616 | tf_op jit(solution)/shard_map/ppermute | solution.py:110

commit v11 on v10

--- a/solution.py
+++ b/solution.py
@@ -153,7 +153,7 @@
         "rck,rcj->kj", filtered, filtered,
         precision=lax.Precision.HIGHEST, preferred_element_type=jnp.float32,
     )
-    gram = all_sum(all_sum(gram_local, "col"), "row") / pixel_total
+    gram = all_sum(all_sum(gram_local, "row"), "col") / pixel_total
     factor = jnp.linalg.cholesky(gram)
     inverse = jax.scipy.linalg.solve_triangular(
         factor, jnp.eye(vectors, dtype=jnp.float32), lower=True

time: 151 us -> 149 us (0.987)
  starting transfers between devices: 47.9 us -> 43.8 us
  waiting for transfers between devices: 24.6 us -> 26.4 us
    ppermute x12, starting transfers between devices: 26.5 us -> 22.4 us  [exchange_sum(): received.append(lax.ppermute(block, axis, route))]
    ppermute x12, waiting for transfers between devices: 19.1 us -> 20.9 us  [exchange_sum(): received.append(lax.ppermute(block, axis, route))]
where the time goes in v11:
time: 149 us; the launch traced here: 147 us
  other arithmetic  50.8 us (34%)
  starting transfers between devices  43.8 us (29%)
  waiting for transfers between devices  26.4 us (18%)
  matrix products  13.1 us (9%)
  local copies, waits for them, and re-layouts  11.7 us (8%)
    ppermute x12, starting transfers between devices, exchange_sum(): received.append(lax.ppermute(block, axis, route))  22.4 us
    sub x2, other arithmetic, apply_pixels(): return shifted_pixels(values_in, 0, 0) - summed  21.6 us
    ppermute x12, waiting for transfers between devices, exchange_sum(): received.append(lax.ppermute(block, axis, route))  20.9 us
    ppermute x4, starting transfers between devices, padded(): lax.ppermute(tail, axis, [(i, (i + 1) % count) for i in range(ends)])  13.5 us
    another operation x3, other arithmetic, per_device(): factor = jnp.linalg.cholesky(gram)  12.4 us
    unnamed x11, local copies, waits for them, and re-layouts  10.5 us
    another operation x1, other arithmetic, per_device(): jax.scipy.linalg.solve_triangular(factor, jnp.eye(vectors, dtype=jnp.floa...  9.81 us
    ppermute x4, starting transfers between devices, padded(): lax.ppermute(head, axis, [((i + 1) % count, i) for i in range(ends)])  7.79 us
  transfers between devices with their start and end apart: 20, of which 11 were waited for; matrix products, arithmetic and copies ran while one was open for 5% of the time, Pallas kernels for 0%

profile of v11, /device:TPU:2, one launch (start us, length us, event | category | flops | bytes accessed | tf_op | source)
XLA Modules:
  0.0 146.7 jit_solution(18131875406489942970)
XLA Ops:
  0.6 0.8 pad_add_fusion.3
  1.4 3.4 %collective-permute-start.4 = (s32[5,3,256]{2,1,0:T(4,128)S(1)}, s32[5,3,256]{2,1,0:T(4,128)S(1)}, u32[]{:S(2)}, u32[]{:S(2)}) collective-permute-start(s32[5,3,256]{2,1,0:T(4,128)S(1)} %get-tuple-element.27), channel_id=1, source_target_pairs={{0,16},{16,32},{32,48},{48,64},{64,80},{80,96},{96,112},{112,128},... | collective-permute-start | bytes 46088 | tf_op jit(solution)/shard_map/ppermute | solution.py:27
  4.8 0.0 copy-start.2
  4.8 0.0 copy-start.3
  4.9 2.6 %collective-permute-start.5 = (s32[5,3,256]{2,1,0:T(4,128)S(1)}, s32[5,3,256]{2,1,0:T(4,128)S(1)}, u32[]{:S(2)}, u32[]{:S(2)}) collective-permute-start(s32[5,3,256]{2,1,0:T(4,128)S(1)} %get-tuple-element.28), channel_id=1, source_target_pairs={{16,0},{32,16},{48,32},{64,48},{80,64},{96,80},{112,96},{128,112},... | collective-permute-start | bytes 46088 | tf_op jit(solution)/shard_map/ppermute | solution.py:29
  7.4 5.3 %copy.15 = f32[128,32,256]{0,2,1:T(8,128)} copy(f32[128,32,256]{2,1,0:T(8,128)} %param.5) | data formatting | bytes 8388608 | tf_op args[2]
  12.7 1.1 fusion.80
  13.8 3.4 %collective-permute-start = (f32[2,256,128]{2,1,0:T(8,128)S(1)}, f32[2,256,128]{2,1,0:T(8,128)S(1)}, u32[]{:S(2)}, u32[]{:S(2)}) collective-permute-start(f32[2,256,128]{2,1,0:T(8,128)S(1)} %get-tuple-element.19), channel_id=1, source_target_pairs={{0,16},{16,32},{32,48},{48,64},{64,80},{80,96},{96,112},{112,128},... | collective-permute-start | bytes 786440 | tf_op jit(solution)/shard_map/ppermute | solution.py:27
  17.2 2.5 %collective-permute-start.1 = (f32[2,256,128]{2,1,0:T(8,128)S(1)}, f32[2,256,128]{2,1,0:T(8,128)S(1)}, u32[]{:S(2)}, u32[]{:S(2)}) collective-permute-start(f32[2,256,128]{2,1,0:T(8,128)S(1)} %get-tuple-element.20), channel_id=1, source_target_pairs={{16,0},{32,16},{48,32},{64,48},{80,64},{96,80},{112,96},{128,112},... | collective-permute-start | bytes 786440 | tf_op jit(solution)/shard_map/ppermute | solution.py:29
  19.7 0.0 copy-start
  19.7 0.0 collective-permute-done.4
  19.8 0.1 fusion.81
  19.9 1.6 %collective-permute-start.6 = (s32[5,38,3]{2,1,0:T(8,128)S(1)}, s32[5,38,3]{2,1,0:T(8,128)S(1)}, u32[]{:S(2)}, u32[]{:S(2)}) collective-permute-start(s32[5,38,3]{2,1,0:T(8,128)S(1)} %get-tuple-element.25), channel_id=1, source_target_pairs={{0,1},{1,2},{2,3},{3,4},{4,5},{5,6},{6,7},{7,8},{8,9},{9,10},{10,1... | collective-permute-start | bytes 6848 | tf_op jit(solution)/shard_map/ppermute | solution.py:27
  21.5 1.3 collective-permute-start.7
  22.8 0.1 broadcast_multiply_fusion
  22.8 4.0 %collective-permute-done.7 = s32[5,38,3]{2,1,0:T(8,128)S(1)} collective-permute-done((s32[5,38,3]{2,1,0:T(8,128)S(1)}, s32[5,38,3]{2,1,0:T(8,128)S(1)}, u32[]{:S(2)}, u32[]{:S(2)}) %collective-permute-start.7) | collective-permute-done | bytes 2312 | tf_op jit(solution)/shard_map/ppermute | solution.py:29
  26.8 0.2 pad_add_fusion
  27.1 0.1 fusion.65
  27.2 0.4 add_rsqrt_fusion
  27.5 0.2 slice_multiply_fusion.46
  27.7 0.1 slice_multiply_fusion.28
  27.9 0.3 slice_multiply_fusion.30
  28.1 0.0 collective-permute-done
  28.2 0.0 collective-permute-done.1
  28.2 5.2 %collective-permute-start.2 = (f32[36,2,128]{2,1,0:T(2,128)S(1)}, f32[36,2,128]{2,1,0:T(2,128)S(1)}, u32[]{:S(2)}, u32[]{:S(2)}) collective-permute-start(f32[36,2,128]{2,1,0:T(2,128)S(1)} %get-tuple-element.17), channel_id=1, source_target_pairs={{0,1},{1,2},{2,3},{3,4},{4,5},{5,6},{6,7},{7,8},{8,9},{9,10},{10,1... | collective-permute-start | bytes 110600 | tf_op jit(solution)/shard_map/ppermute | solution.py:27
  33.4 1.5 %collective-permute-start.3 = (f32[36,2,128]{2,1,0:T(2,128)S(1)}, f32[36,2,128]{2,1,0:T(2,128)S(1)}, u32[]{:S(2)}, u32[]{:S(2)}) collective-permute-start(f32[36,2,128]{2,1,0:T(2,128)S(1)} %get-tuple-element.18), channel_id=1, source_target_pairs={{1,0},{2,1},{3,2},{4,3},{5,4},{6,5},{7,6},{8,7},{9,8},{10,9},{11,1... | collective-permute-start | bytes 110600 | tf_op jit(solution)/shard_map/ppermute | solution.py:29
  34.9 0.1 slice_multiply_fusion.34
  35.0 1.5 %collective-permute-done.3 = f32[36,2,128]{2,1,0:T(2,128)S(1)} collective-permute-done((f32[36,2,128]{2,1,0:T(2,128)S(1)}, f32[36,2,128]{2,1,0:T(2,128)S(1)}, u32[]{:S(2)}, u32[]{:S(2)}) %collective-permute-start.3) | collective-permute-done | bytes 36896 | tf_op jit(solution)/shard_map/ppermute | solution.py:29
  36.5 2.3 %maximum_maximum_fusion = (f32[36,258,128]{2,1,0:T(8,128)S(1)}, f32[36,258,128]{2,1,0:T(8,128)S(1)}) fusion(f32[2,256,128]{2,1,0:T(8,128)S(1)} %collective-permute-done.1, f32[32,256,128]{2,1,0:T(8,128)S(1)} %bitcast.37, f32[2,256,128]{2,1,0:T(8,128)S(1)} %collective-permute-done, f32[36,2,128]{2,1,0:T(2,128)S(1)} %collective-permute-done.2, ...), kind=kLoop, calls=%fused_computation.2 | loop fusion | flops 7133184 | bytes 14303232 | tf_op jit(solution)/shard_map/concatenate | solution.py:25
  38.8 1.6 %pad_maximum_fusion = f32[36,260,128]{2,1,0:T(8,128)S(1)} fusion(f32[36,2,128]{2,1,0:T(2,128)S(1)} %collective-permute-done.3, f32[2,256,128]{2,1,0:T(8,128)S(1)} %collective-permute-done.1, f32[32,256,128]{2,1,0:T(8,128)S(1)} %bitcast.38, f32[2,256,128]{2,1,0:T(8,128)S(1)} %collective-permute-done, f32[36,2,128]{2,1,0:T(2,128)S(1)} %collective-permute-done.2), kind=kLoop, calls=%fused_computation | loop fusion | flops 4792320 | bytes 9584640 | tf_op jit(solution)/shard_map/concatenate | solution.py:25
  40.4 11.6 %fusion.1 = f32[34,258,128]{2,1,0:T(8,128)S(1)} fusion(f32[36,258,128]{2,1,0:T(8,128)S(1)} %get-tuple-element.16, f32[36,258,128]{2,1,0:T(8,128)S(1)} %get-tuple-element.15, f32[36,260,128]{2,1,0:T(8,128)S(1)} %pad_maximum_fusion, f32[34,258]{1,0:T(8,128)S(1)} %get-tuple-element.40, f32[34,258]{1,0:T(8,128)S(1)} %get-tuple-element.41, ...), kind=kLoop, calls=%fused_computation.5 | loop fusion | flops 17965056 | bytes 45193344 | tf_op jit(solution)/shard_map/sub | solution.py:101
  52.0 10.1 %fusion.9 = f32[32,256,128]{2,1,0:T(8,128)S(1)} fusion(f32[34,258,128]{2,1,0:T(8,128)S(1)} %fusion.1, f32[32,256]{1,0:T(8,128)S(1)} %get-tuple-element.38, f32[32,256]{1,0:T(8,128)S(1)} %get-tuple-element.37, f32[32,256]{1,0:T(8,128)S(1)} %get-tuple-element.32, f32[32,256]{1,0:T(8,128)S(1)} %get-tuple-element.33, f32[32,256]{1,0:T(8,128)S(1)} %get-tuple-element.34, ...), kind=kLoop, calls=%fused_computation.21 | loop fusion | flops 16777216 | bytes 42205184 | tf_op jit(solution)/shard_map/sub | solution.py:101
  62.1 0.0 copy-start.1
  62.1 6.9 %convolution_bitcast_fusion.1 = f32[128,128]{0,1:T(8,128)S(1)} fusion(f32[32,256,128]{2,1,0:T(8,128)S(1)} %fusion.9), kind=kOutput, calls=%fused_computation.36 | convolution fusion | flops 1610612736 | bytes 4259840 | tf_op jit(solution)/shard_map/rck,rcj->kj/dot_general | solution.py:152
  69.0 1.6 %collective-permute-start.10 = (f32[128,128]{0,1:T(8,128)S(1)}, f32[128,128]{0,1:T(8,128)S(1)}, u32[]{:S(2)}, u32[]{:S(2)}) collective-permute-start(f32[128,128]{0,1:T(8,128)S(1)} %convolution_bitcast_fusion.1), channel_id=1, source_target_pairs={{0,48},{16,32},{32,16},{48,0},{64,112},{80,96},{96,80},{112,64},{1... | collective-permute-start | bytes 196616 | tf_op jit(solution)/shard_map/ppermute | solution.py:110
  70.6 3.4 %collective-permute-start.8 = (f32[128,128]{0,1:T(8,128)S(1)}, f32[128,128]{0,1:T(8,128)S(1)}, u32[]{:S(2)}, u32[]{:S(2)}) collective-permute-start(f32[128,128]{0,1:T(8,128)S(1)} %convolution_bitcast_fusion.1), channel_id=1, source_target_pairs={{0,16},{16,0},{32,48},{48,32},{64,80},{80,64},{96,112},{112,96},{1... | collective-permute-start | bytes 196616 | tf_op jit(solution)/shard_map/ppermute | solution.py:110
  74.0 0.0 collective-permute-start.9
  74.0 0.0 collective-permute-done.10
  74.0 2.2 %collective-permute-done.8 = f32[128,128]{0,1:T(8,128)S(1)} collective-permute-done((f32[128,128]{0,1:T(8,128)S(1)}, f32[128,128]{0,1:T(8,128)S(1)}, u32[]{:S(2)}, u32[]{:S(2)}) %collective-permute-start.8) | collective-permute-done | bytes 65568 | tf_op jit(solution)/shard_map/ppermute | solution.py:110
  76.2 3.5 %collective-permute-done.9 = f32[128,128]{0,1:T(8,128)S(1)} collective-permute-done((f32[128,128]{0,1:T(8,128)S(1)}, f32[128,128]{0,1:T(8,128)S(1)}, u32[]{:S(2)}, u32[]{:S(2)}) %collective-permute-start.9) | collective-permute-done | bytes 65568 | tf_op jit(solution)/shard_map/ppermute | solution.py:110
  79.8 2.6 %collective-permute-start.11 = (f32[128,128]{0,1:T(8,128)S(1)}, f32[128,128]{0,1:T(8,128)S(1)}, u32[]{:S(2)}, u32[]{:S(2)}) collective-permute-start(f32[128,128]{0,1:T(8,128)S(1)} %add_add_fusion.2), channel_id=1, source_target_pairs={{0,64},{16,80},{32,96},{48,112},{64,0},{80,16},{96,32},{112,48},{1... | collective-permute-start | bytes 196616 | tf_op jit(solution)/shard_map/ppermute | solution.py:110
  82.3 2.9 %collective-permute-start.12 = (f32[128,128]{0,1:T(8,128)S(1)}, f32[128,128]{0,1:T(8,128)S(1)}, u32[]{:S(2)}, u32[]{:S(2)}) collective-permute-start(f32[128,128]{0,1:T(8,128)S(1)} %add_add_fusion.2), channel_id=1, source_target_pairs={{0,128},{16,144},{32,160},{48,176},{64,192},{80,208},{96,224},{112... | collective-permute-start | bytes 196616 | tf_op jit(solution)/shard_map/ppermute | solution.py:110
  85.2 3.8 %collective-permute-done.12 = f32[128,128]{0,1:T(8,128)S(1)} collective-permute-done((f32[128,128]{0,1:T(8,128)S(1)}, f32[128,128]{0,1:T(8,128)S(1)}, u32[]{:S(2)}, u32[]{:S(2)}) %collective-permute-start.12) | collective-permute-done | bytes 65568 | tf_op jit(solution)/shard_map/ppermute | solution.py:110
  89.1 1.6 %collective-permute-done.13 = f32[128,128]{0,1:T(8,128)S(1)} collective-permute-done((f32[128,128]{0,1:T(8,128)S(1)}, f32[128,128]{0,1:T(8,128)S(1)}, u32[]{:S(2)}, u32[]{:S(2)}) %collective-permute-start.13) | collective-permute-done | bytes 65568 | tf_op jit(solution)/shard_map/ppermute | solution.py:110
  90.7 0.1 collective-permute-start.14
  90.8 2.1 %collective-permute-start.15 = (f32[128,128]{0,1:T(8,128)S(1)}, f32[128,128]{0,1:T(8,128)S(1)}, u32[]{:S(2)}, u32[]{:S(2)}) collective-permute-start(f32[128,128]{0,1:T(8,128)S(1)} %add_add_fusion.1), channel_id=1, source_target_pairs={{0,2},{1,3},{2,0},{3,1},{4,6},{5,7},{6,4},{7,5},{8,10},{9,11},{10,... | collective-permute-start | bytes 196616 | tf_op jit(solution)/shard_map/ppermute | solution.py:110
  92.9 0.0 collective-permute-start.16
  92.9 2.6 %collective-permute-done.15 = f32[128,128]{0,1:T(8,128)S(1)} collective-permute-done((f32[128,128]{0,1:T(8,128)S(1)}, f32[128,128]{0,1:T(8,128)S(1)}, u32[]{:S(2)}, u32[]{:S(2)}) %collective-permute-start.15) | collective-permute-done | bytes 65568 | tf_op jit(solution)/shard_map/ppermute | solution.py:110
  95.6 1.4 collective-permute-done.16
  97.0 6.1 %collective-permute-start.17 = (f32[128,128]{0,1:T(8,128)S(1)}, f32[128,128]{0,1:T(8,128)S(1)}, u32[]{:S(2)}, u32[]{:S(2)}) collective-permute-start(f32[128,128]{0,1:T(8,128)S(1)} %add_add_fusion), channel_id=1, source_target_pairs={{0,4},{1,5},{2,6},{3,7},{4,0},{5,1},{6,2},{7,3},{8,12},{9,13},{10,... | collective-permute-start | bytes 196616 | tf_op jit(solution)/shard_map/ppermute | solution.py:110
  103.1 2.3 %collective-permute-start.18 = (f32[128,128]{0,1:T(8,128)S(1)}, f32[128,128]{0,1:T(8,128)S(1)}, u32[]{:S(2)}, u32[]{:S(2)}) collective-permute-start(f32[128,128]{0,1:T(8,128)S(1)} %add_add_fusion), channel_id=1, source_target_pairs={{0,8},{1,9},{2,10},{3,11},{4,12},{5,13},{6,14},{7,15},{8,0},{9,1},... | collective-permute-start | bytes 196616 | tf_op jit(solution)/shard_map/ppermute | solution.py:110
  105.4 1.4 collective-permute-start.19
  106.8 0.1 collective-permute-done.17
  106.9 4.5 %collective-permute-done.18 = f32[128,128]{0,1:T(8,128)S(1)} collective-permute-done((f32[128,128]{0,1:T(8,128)S(1)}, f32[128,128]{0,1:T(8,128)S(1)}, u32[]{:S(2)}, u32[]{:S(2)}) %collective-permute-start.18) | collective-permute-done | bytes 65568 | tf_op jit(solution)/shard_map/ppermute | solution.py:110
  111.5 0.9 collective-permute-done.19
  112.4 0.1 copy.21
  112.5 11.7 %cholesky.17 = f32[128,128]{1,0:T(8,128)S(1)} custom-call(f32[128,128]{1,0:T(8,128)S(1)} %fusion.17), custom_call_target="Cholesky" | custom-call | tf_op jit(solution)/shard_map/jit(cholesky)/cholesky | solution.py:157
  124.3 0.6 compare_reduce_fusion
  124.9 0.7 fusion.67
  125.6 9.8 %custom-call.7 = f32[1,128,128]{1,2,0:T(8,128)S(1)} custom-call(f32[1,128,128]{2,1,0:T(8,128)S(1)} %get-tuple-element.30), custom_call_target="InvertDiagBlocksLowerTriangular" | custom-call | tf_op jit(solution)/shard_map/jit(_solve_triangular)/triangular_solve | solution.py:158
  135.4 0.2 convolution_bitcast_fusion
  135.7 5.9 %fusion.82 = f32[128,32,256]{2,0,1:T(8,128)S(1)} fusion(f32[128,128,1]{1,0,2:T(8,128)S(1)} %convolution_bitcast_fusion, f32[32,256,128]{2,1,0:T(8,128)} %copy-done.1), kind=kOutput, calls=%fused_computation.179 | convolution fusion | flops 1610612736 | bytes 8454144 | tf_op jit(solution)/shard_map/kj,rcj->krc/dot_general | solution.py:161
  141.5 4.4 %copy.22 = f32[128,32,256]{2,1,0:T(8,128)} copy(f32[128,32,256]{2,0,1:T(8,128)S(1)} %fusion.82) | data formatting | bytes 8388608
  146.0 0.7 copy.23
  (22 shorter events, 0.2 us)
Async XLA Ops:
  1.4 18.3 %collective-permute-start.4 = (s32[5,3,256]{2,1,0:T(4,128)S(1)}, s32[5,3,256]{2,1,0:T(4,128)S(1)}, u32[]{:S(2)}, u32[]{:S(2)}) collective-permute-start(s32[5,3,256]{2,1,0:T(4,128)S(1)} %get-tuple-element.27), channel_id=1, source_target_pairs={{0,16},{16,32},{32,48},{48,64},{64,80},{80,96},{96,112},{112,128},... | collective-permute-start | bytes 46088 | tf_op jit(solution)/shard_map/ppermute | solution.py:27
  4.8 14.9 %copy-start.2 = (s32[4,32,256]{2,1,0:T(8,128)S(1)}, s32[4,32,256]{2,1,0:T(8,128)}, u32[]{:S(2)}) copy-start(s32[4,32,256]{2,1,0:T(8,128)} %param.4) | copy-start | bytes 393220
  4.8 14.9 %copy-start.3 = (s32[32,256]{1,0:T(8,128)S(1)}, s32[32,256]{1,0:T(8,128)}, u32[]{:S(2)}) copy-start(s32[32,256]{1,0:T(8,128)} %param.3) | copy-start | bytes 98308
  4.9 14.9 %collective-permute-start.5 = (s32[5,3,256]{2,1,0:T(4,128)S(1)}, s32[5,3,256]{2,1,0:T(4,128)S(1)}, u32[]{:S(2)}, u32[]{:S(2)}) collective-permute-start(s32[5,3,256]{2,1,0:T(4,128)S(1)} %get-tuple-element.28), channel_id=1, source_target_pairs={{16,0},{32,16},{48,32},{64,48},{80,64},{96,80},{112,96},{128,112},... | collective-permute-start | bytes 46088 | tf_op jit(solution)/shard_map/ppermute | solution.py:29
  13.8 14.3 %collective-permute-start = (f32[2,256,128]{2,1,0:T(8,128)S(1)}, f32[2,256,128]{2,1,0:T(8,128)S(1)}, u32[]{:S(2)}, u32[]{:S(2)}) collective-permute-start(f32[2,256,128]{2,1,0:T(8,128)S(1)} %get-tuple-element.19), channel_id=1, source_target_pairs={{0,16},{16,32},{32,48},{48,64},{64,80},{80,96},{96,112},{112,128},... | collective-permute-start | bytes 786440 | tf_op jit(solution)/shard_map/ppermute | solution.py:27
  17.2 10.9 %collective-permute-start.1 = (f32[2,256,128]{2,1,0:T(8,128)S(1)}, f32[2,256,128]{2,1,0:T(8,128)S(1)}, u32[]{:S(2)}, u32[]{:S(2)}) collective-permute-start(f32[2,256,128]{2,1,0:T(8,128)S(1)} %get-tuple-element.20), channel_id=1, source_target_pairs={{16,0},{32,16},{48,32},{64,48},{80,64},{96,80},{112,96},{128,112},... | collective-permute-start | bytes 786440 | tf_op jit(solution)/shard_map/ppermute | solution.py:29
  19.7 8.5 %copy-start = (f32[128,32,256]{0,2,1:T(8,128)S(1)}, f32[128,32,256]{0,2,1:T(8,128)}, u32[]{:S(2)}) copy-start(f32[128,32,256]{0,2,1:T(8,128)} %copy.15) | copy-start | bytes 12582916
  19.9 2.9 %collective-permute-start.6 = (s32[5,38,3]{2,1,0:T(8,128)S(1)}, s32[5,38,3]{2,1,0:T(8,128)S(1)}, u32[]{:S(2)}, u32[]{:S(2)}) collective-permute-start(s32[5,38,3]{2,1,0:T(8,128)S(1)} %get-tuple-element.25), channel_id=1, source_target_pairs={{0,1},{1,2},{2,3},{3,4},{4,5},{5,6},{6,7},{7,8},{8,9},{9,10},{10,1... | collective-permute-start | bytes 6848 | tf_op jit(solution)/shard_map/ppermute | solution.py:27
  21.5 5.3 %collective-permute-start.7 = (s32[5,38,3]{2,1,0:T(8,128)S(1)}, s32[5,38,3]{2,1,0:T(8,128)S(1)}, u32[]{:S(2)}, u32[]{:S(2)}) collective-permute-start(s32[5,38,3]{2,1,0:T(8,128)S(1)} %get-tuple-element.26), channel_id=1, source_target_pairs={{1,0},{2,1},{3,2},{4,3},{5,4},{6,5},{7,6},{8,7},{9,8},{10,9},{11,1... | collective-permute-start | bytes 6848 | tf_op jit(solution)/shard_map/ppermute | solution.py:29
  28.2 6.8 %collective-permute-start.2 = (f32[36,2,128]{2,1,0:T(2,128)S(1)}, f32[36,2,128]{2,1,0:T(2,128)S(1)}, u32[]{:S(2)}, u32[]{:S(2)}) collective-permute-start(f32[36,2,128]{2,1,0:T(2,128)S(1)} %get-tuple-element.17), channel_id=1, source_target_pairs={{0,1},{1,2},{2,3},{3,4},{4,5},{5,6},{6,7},{7,8},{8,9},{9,10},{10,1... | collective-permute-start | bytes 110600 | tf_op jit(solution)/shard_map/ppermute | solution.py:27
  33.4 3.1 %collective-permute-start.3 = (f32[36,2,128]{2,1,0:T(2,128)S(1)}, f32[36,2,128]{2,1,0:T(2,128)S(1)}, u32[]{:S(2)}, u32[]{:S(2)}) collective-permute-start(f32[36,2,128]{2,1,0:T(2,128)S(1)} %get-tuple-element.18), channel_id=1, source_target_pairs={{1,0},{2,1},{3,2},{4,3},{5,4},{6,5},{7,6},{8,7},{9,8},{10,9},{11,1... | collective-permute-start | bytes 110600 | tf_op jit(solution)/shard_map/ppermute | solution.py:29
  62.1 34.9 %copy-start.1 = (f32[32,256,128]{2,1,0:T(8,128)}, f32[32,256,128]{2,1,0:T(8,128)S(1)}, u32[]{:S(2)}) copy-start(f32[32,256,128]{2,1,0:T(8,128)S(1)} %fusion.9) | copy-start | bytes 12582916
  69.0 5.0 %collective-permute-start.10 = (f32[128,128]{0,1:T(8,128)S(1)}, f32[128,128]{0,1:T(8,128)S(1)}, u32[]{:S(2)}, u32[]{:S(2)}) collective-permute-start(f32[128,128]{0,1:T(8,128)S(1)} %convolution_bitcast_fusion.1), channel_id=1, source_target_pairs={{0,48},{16,32},{32,16},{48,0},{64,112},{80,96},{96,80},{112,64},{1... | collective-permute-start | bytes 196616 | tf_op jit(solution)/shard_map/ppermute | solution.py:110
  70.6 5.6 %collective-permute-start.8 = (f32[128,128]{0,1:T(8,128)S(1)}, f32[128,128]{0,1:T(8,128)S(1)}, u32[]{:S(2)}, u32[]{:S(2)}) collective-permute-start(f32[128,128]{0,1:T(8,128)S(1)} %convolution_bitcast_fusion.1), channel_id=1, source_target_pairs={{0,16},{16,0},{32,48},{48,32},{64,80},{80,64},{96,112},{112,96},{1... | collective-permute-start | bytes 196616 | tf_op jit(solution)/shard_map/ppermute | solution.py:110
  74.0 5.8 %collective-permute-start.9 = (f32[128,128]{0,1:T(8,128)S(1)}, f32[128,128]{0,1:T(8,128)S(1)}, u32[]{:S(2)}, u32[]{:S(2)}) collective-permute-start(f32[128,128]{0,1:T(8,128)S(1)} %convolution_bitcast_fusion.1), channel_id=1, source_target_pairs={{0,32},{16,48},{32,0},{48,16},{64,96},{80,112},{96,64},{112,80},{1... | collective-permute-start | bytes 196616 | tf_op jit(solution)/shard_map/ppermute | solution.py:110
  79.8 5.5 %collective-permute-start.11 = (f32[128,128]{0,1:T(8,128)S(1)}, f32[128,128]{0,1:T(8,128)S(1)}, u32[]{:S(2)}, u32[]{:S(2)}) collective-permute-start(f32[128,128]{0,1:T(8,128)S(1)} %add_add_fusion.2), channel_id=1, source_target_pairs={{0,64},{16,80},{32,96},{48,112},{64,0},{80,16},{96,32},{112,48},{1... | collective-permute-start | bytes 196616 | tf_op jit(solution)/shard_map/ppermute | solution.py:110
  82.3 6.7 %collective-permute-start.12 = (f32[128,128]{0,1:T(8,128)S(1)}, f32[128,128]{0,1:T(8,128)S(1)}, u32[]{:S(2)}, u32[]{:S(2)}) collective-permute-start(f32[128,128]{0,1:T(8,128)S(1)} %add_add_fusion.2), channel_id=1, source_target_pairs={{0,128},{16,144},{32,160},{48,176},{64,192},{80,208},{96,224},{112... | collective-permute-start | bytes 196616 | tf_op jit(solution)/shard_map/ppermute | solution.py:110
  85.2 5.5 %collective-permute-start.13 = (f32[128,128]{0,1:T(8,128)S(1)}, f32[128,128]{0,1:T(8,128)S(1)}, u32[]{:S(2)}, u32[]{:S(2)}) collective-permute-start(f32[128,128]{0,1:T(8,128)S(1)} %add_add_fusion.2), channel_id=1, source_target_pairs={{0,192},{16,208},{32,224},{48,240},{64,128},{80,144},{96,160},{112... | collective-permute-start | bytes 196616 | tf_op jit(solution)/shard_map/ppermute | solution.py:110
  90.7 2.2 %collective-permute-start.14 = (f32[128,128]{0,1:T(8,128)S(1)}, f32[128,128]{0,1:T(8,128)S(1)}, u32[]{:S(2)}, u32[]{:S(2)}) collective-permute-start(f32[128,128]{0,1:T(8,128)S(1)} %add_add_fusion.1), channel_id=1, source_target_pairs={{0,1},{1,0},{2,3},{3,2},{4,5},{5,4},{6,7},{7,6},{8,9},{9,8},{10,11... | collective-permute-start | bytes 196616 | tf_op jit(solution)/shard_map/ppermute | solution.py:110
  90.8 4.7 %collective-permute-start.15 = (f32[128,128]{0,1:T(8,128)S(1)}, f32[128,128]{0,1:T(8,128)S(1)}, u32[]{:S(2)}, u32[]{:S(2)}) collective-permute-start(f32[128,128]{0,1:T(8,128)S(1)} %add_add_fusion.1), channel_id=1, source_target_pairs={{0,2},{1,3},{2,0},{3,1},{4,6},{5,7},{6,4},{7,5},{8,10},{9,11},{10,... | collective-permute-start | bytes 196616 | tf_op jit(solution)/shard_map/ppermute | solution.py:110
  92.9 4.1 %collective-permute-start.16 = (f32[128,128]{0,1:T(8,128)S(1)}, f32[128,128]{0,1:T(8,128)S(1)}, u32[]{:S(2)}, u32[]{:S(2)}) collective-permute-start(f32[128,128]{0,1:T(8,128)S(1)} %add_add_fusion.1), channel_id=1, source_target_pairs={{0,3},{1,2},{2,1},{3,0},{4,7},{5,6},{6,5},{7,4},{8,11},{9,10},{10,... | collective-permute-start | bytes 196616 | tf_op jit(solution)/shard_map/ppermute | solution.py:110
  97.0 9.9 %collective-permute-start.17 = (f32[128,128]{0,1:T(8,128)S(1)}, f32[128,128]{0,1:T(8,128)S(1)}, u32[]{:S(2)}, u32[]{:S(2)}) collective-permute-start(f32[128,128]{0,1:T(8,128)S(1)} %add_add_fusion), channel_id=1, source_target_pairs={{0,4},{1,5},{2,6},{3,7},{4,0},{5,1},{6,2},{7,3},{8,12},{9,13},{10,... | collective-permute-start | bytes 196616 | tf_op jit(solution)/shard_map/ppermute | solution.py:110
  103.1 8.3 %collective-permute-start.18 = (f32[128,128]{0,1:T(8,128)S(1)}, f32[128,128]{0,1:T(8,128)S(1)}, u32[]{:S(2)}, u32[]{:S(2)}) collective-permute-start(f32[128,128]{0,1:T(8,128)S(1)} %add_add_fusion), channel_id=1, source_target_pairs={{0,8},{1,9},{2,10},{3,11},{4,12},{5,13},{6,14},{7,15},{8,0},{9,1},... | collective-permute-start | bytes 196616 | tf_op jit(solution)/shard_map/ppermute | solution.py:110
  105.4 7.0 %collective-permute-start.19 = (f32[128,128]{0,1:T(8,128)S(1)}, f32[128,128]{0,1:T(8,128)S(1)}, u32[]{:S(2)}, u32[]{:S(2)}) collective-permute-start(f32[128,128]{0,1:T(8,128)S(1)} %add_add_fusion), channel_id=1, source_target_pairs={{0,12},{1,13},{2,14},{3,15},{4,8},{5,9},{6,10},{7,11},{8,4},{9,5},... | collective-permute-start | bytes 196616 | tf_op jit(solution)/shard_map/ppermute | solution.py:110

commit v12 on v11

--- a/solution.py
+++ b/solution.py
@@ -118,11 +118,14 @@
     levels = count.bit_length() - 1
     if (1 << levels) != count:
         return lax.psum(block, axis)
+    groups = []
     low_bit = 0
     while low_bit < levels:
         bits = min(2, levels - low_bit)
+        groups.append((low_bit, bits))
+        low_bit += bits
+    for low_bit, bits in reversed(groups):
         block = exchange_sum(block, axis, low_bit, bits)
-        low_bit += bits
     return block
 
 

time: 149 us -> 149 us (level)
  waiting for transfers between devices: 26.4 us -> 24.4 us
  starting transfers between devices: 43.8 us -> 45.3 us
    ppermute x12, waiting for transfers between devices: 20.9 us -> 18.9 us  [exchange_sum(): received.append(lax.ppermute(block, axis, route))]
    ppermute x12, starting transfers between devices: 22.4 us -> 23.9 us  [exchange_sum(): received.append(lax.ppermute(block, axis, route))]
where the time goes in v12:
time: 149 us; the launch traced here: 146 us
  other arithmetic  50.8 us (34%)
  starting transfers between devices  45.3 us (30%)
  waiting for transfers between devices  24.4 us (16%)
  matrix products  13.1 us (9%)
  local copies, waits for them, and re-layouts  11.7 us (8%)
    ppermute x12, starting transfers between devices, exchange_sum(): received.append(lax.ppermute(block, axis, route))  23.9 us
    sub x2, other arithmetic, apply_pixels(): return shifted_pixels(values_in, 0, 0) - summed  21.6 us
    ppermute x12, waiting for transfers between devices, exchange_sum(): received.append(lax.ppermute(block, axis, route))  18.9 us
    ppermute x4, starting transfers between devices, padded(): lax.ppermute(tail, axis, [(i, (i + 1) % count) for i in range(ends)])  13.5 us
    another operation x3, other arithmetic, per_device(): factor = jnp.linalg.cholesky(gram)  12.4 us
    unnamed x11, local copies, waits for them, and re-layouts  10.5 us
    another operation x1, other arithmetic, per_device(): jax.scipy.linalg.solve_triangular(factor, jnp.eye(vectors, dtype=jnp.floa...  9.81 us
    ppermute x4, starting transfers between devices, padded(): lax.ppermute(head, axis, [((i + 1) % count, i) for i in range(ends)])  7.79 us
  transfers between devices with their start and end apart: 20, of which 11 were waited for; matrix products, arithmetic and copies ran while one was open for 5% of the time, Pallas kernels for 0%

profile of v12, /device:TPU:2, one launch (start us, length us, event | category | flops | bytes accessed | tf_op | source)
XLA Modules:
  0.0 146.2 jit_solution(6821316940906625598)
XLA Ops:
  0.6 0.8 pad_add_fusion.3
  1.4 3.4 %collective-permute-start.4 = (s32[5,3,256]{2,1,0:T(4,128)S(1)}, s32[5,3,256]{2,1,0:T(4,128)S(1)}, u32[]{:S(2)}, u32[]{:S(2)}) collective-permute-start(s32[5,3,256]{2,1,0:T(4,128)S(1)} %get-tuple-element.27), channel_id=1, source_target_pairs={{0,16},{16,32},{32,48},{48,64},{64,80},{80,96},{96,112},{112,128},... | collective-permute-start | bytes 46088 | tf_op jit(solution)/shard_map/ppermute | solution.py:27
  4.8 0.0 copy-start.2
  4.8 0.0 copy-start.3
  4.9 2.6 %collective-permute-start.5 = (s32[5,3,256]{2,1,0:T(4,128)S(1)}, s32[5,3,256]{2,1,0:T(4,128)S(1)}, u32[]{:S(2)}, u32[]{:S(2)}) collective-permute-start(s32[5,3,256]{2,1,0:T(4,128)S(1)} %get-tuple-element.28), channel_id=1, source_target_pairs={{16,0},{32,16},{48,32},{64,48},{80,64},{96,80},{112,96},{128,112},... | collective-permute-start | bytes 46088 | tf_op jit(solution)/shard_map/ppermute | solution.py:29
  7.4 5.3 %copy.15 = f32[128,32,256]{0,2,1:T(8,128)} copy(f32[128,32,256]{2,1,0:T(8,128)} %param.5) | data formatting | bytes 8388608 | tf_op args[2]
  12.7 1.1 fusion.80
  13.8 3.4 %collective-permute-start = (f32[2,256,128]{2,1,0:T(8,128)S(1)}, f32[2,256,128]{2,1,0:T(8,128)S(1)}, u32[]{:S(2)}, u32[]{:S(2)}) collective-permute-start(f32[2,256,128]{2,1,0:T(8,128)S(1)} %get-tuple-element.19), channel_id=1, source_target_pairs={{0,16},{16,32},{32,48},{48,64},{64,80},{80,96},{96,112},{112,128},... | collective-permute-start | bytes 786440 | tf_op jit(solution)/shard_map/ppermute | solution.py:27
  17.2 2.5 %collective-permute-start.1 = (f32[2,256,128]{2,1,0:T(8,128)S(1)}, f32[2,256,128]{2,1,0:T(8,128)S(1)}, u32[]{:S(2)}, u32[]{:S(2)}) collective-permute-start(f32[2,256,128]{2,1,0:T(8,128)S(1)} %get-tuple-element.20), channel_id=1, source_target_pairs={{16,0},{32,16},{48,32},{64,48},{80,64},{96,80},{112,96},{128,112},... | collective-permute-start | bytes 786440 | tf_op jit(solution)/shard_map/ppermute | solution.py:29
  19.7 0.0 copy-start
  19.7 0.0 collective-permute-done.5
  19.8 0.1 fusion.81
  19.9 1.6 %collective-permute-start.6 = (s32[5,38,3]{2,1,0:T(8,128)S(1)}, s32[5,38,3]{2,1,0:T(8,128)S(1)}, u32[]{:S(2)}, u32[]{:S(2)}) collective-permute-start(s32[5,38,3]{2,1,0:T(8,128)S(1)} %get-tuple-element.25), channel_id=1, source_target_pairs={{0,1},{1,2},{2,3},{3,4},{4,5},{5,6},{6,7},{7,8},{8,9},{9,10},{10,1... | collective-permute-start | bytes 6848 | tf_op jit(solution)/shard_map/ppermute | solution.py:27
  21.5 1.3 collective-permute-start.7
  22.8 0.1 broadcast_multiply_fusion
  22.8 0.0 collective-permute-done.6
  22.8 4.0 %collective-permute-done.7 = s32[5,38,3]{2,1,0:T(8,128)S(1)} collective-permute-done((s32[5,38,3]{2,1,0:T(8,128)S(1)}, s32[5,38,3]{2,1,0:T(8,128)S(1)}, u32[]{:S(2)}, u32[]{:S(2)}) %collective-permute-start.7) | collective-permute-done | bytes 2312 | tf_op jit(solution)/shard_map/ppermute | solution.py:29
  26.8 0.2 pad_add_fusion
  27.1 0.1 fusion.65
  27.2 0.4 add_rsqrt_fusion
  27.5 0.2 slice_multiply_fusion.46
  27.7 0.1 slice_multiply_fusion.28
  27.9 0.3 slice_multiply_fusion.30
  28.1 0.0 collective-permute-done
  28.2 5.2 %collective-permute-start.2 = (f32[36,2,128]{2,1,0:T(2,128)S(1)}, f32[36,2,128]{2,1,0:T(2,128)S(1)}, u32[]{:S(2)}, u32[]{:S(2)}) collective-permute-start(f32[36,2,128]{2,1,0:T(2,128)S(1)} %get-tuple-element.17), channel_id=1, source_target_pairs={{0,1},{1,2},{2,3},{3,4},{4,5},{5,6},{6,7},{7,8},{8,9},{9,10},{10,1... | collective-permute-start | bytes 110600 | tf_op jit(solution)/shard_map/ppermute | solution.py:27
  33.4 1.5 %collective-permute-start.3 = (f32[36,2,128]{2,1,0:T(2,128)S(1)}, f32[36,2,128]{2,1,0:T(2,128)S(1)}, u32[]{:S(2)}, u32[]{:S(2)}) collective-permute-start(f32[36,2,128]{2,1,0:T(2,128)S(1)} %get-tuple-element.18), channel_id=1, source_target_pairs={{1,0},{2,1},{3,2},{4,3},{5,4},{6,5},{7,6},{8,7},{9,8},{10,9},{11,1... | collective-permute-start | bytes 110600 | tf_op jit(solution)/shard_map/ppermute | solution.py:29
  34.9 0.1 slice_multiply_fusion.34
  35.0 0.0 collective-permute-done.2
  35.0 1.5 %collective-permute-done.3 = f32[36,2,128]{2,1,0:T(2,128)S(1)} collective-permute-done((f32[36,2,128]{2,1,0:T(2,128)S(1)}, f32[36,2,128]{2,1,0:T(2,128)S(1)}, u32[]{:S(2)}, u32[]{:S(2)}) %collective-permute-start.3) | collective-permute-done | bytes 36896 | tf_op jit(solution)/shard_map/ppermute | solution.py:29
  36.5 2.3 %maximum_maximum_fusion = (f32[36,258,128]{2,1,0:T(8,128)S(1)}, f32[36,258,128]{2,1,0:T(8,128)S(1)}) fusion(f32[2,256,128]{2,1,0:T(8,128)S(1)} %collective-permute-done.1, f32[32,256,128]{2,1,0:T(8,128)S(1)} %bitcast.37, f32[2,256,128]{2,1,0:T(8,128)S(1)} %collective-permute-done, f32[36,2,128]{2,1,0:T(2,128)S(1)} %collective-permute-done.2, ...), kind=kLoop, calls=%fused_computation.2 | loop fusion | flops 7133184 | bytes 14303232 | tf_op jit(solution)/shard_map/concatenate | solution.py:25
  38.8 1.6 %pad_maximum_fusion = f32[36,260,128]{2,1,0:T(8,128)S(1)} fusion(f32[36,2,128]{2,1,0:T(2,128)S(1)} %collective-permute-done.3, f32[2,256,128]{2,1,0:T(8,128)S(1)} %collective-permute-done.1, f32[32,256,128]{2,1,0:T(8,128)S(1)} %bitcast.38, f32[2,256,128]{2,1,0:T(8,128)S(1)} %collective-permute-done, f32[36,2,128]{2,1,0:T(2,128)S(1)} %collective-permute-done.2), kind=kLoop, calls=%fused_computation | loop fusion | flops 4792320 | bytes 9584640 | tf_op jit(solution)/shard_map/concatenate | solution.py:25
  40.4 11.6 %fusion.1 = f32[34,258,128]{2,1,0:T(8,128)S(1)} fusion(f32[36,258,128]{2,1,0:T(8,128)S(1)} %get-tuple-element.16, f32[36,258,128]{2,1,0:T(8,128)S(1)} %get-tuple-element.15, f32[36,260,128]{2,1,0:T(8,128)S(1)} %pad_maximum_fusion, f32[34,258]{1,0:T(8,128)S(1)} %get-tuple-element.40, f32[34,258]{1,0:T(8,128)S(1)} %get-tuple-element.41, ...), kind=kLoop, calls=%fused_computation.5 | loop fusion | flops 17965056 | bytes 45193344 | tf_op jit(solution)/shard_map/sub | solution.py:101
  52.0 10.1 %fusion.9 = f32[32,256,128]{2,1,0:T(8,128)S(1)} fusion(f32[34,258,128]{2,1,0:T(8,128)S(1)} %fusion.1, f32[32,256]{1,0:T(8,128)S(1)} %get-tuple-element.38, f32[32,256]{1,0:T(8,128)S(1)} %get-tuple-element.37, f32[32,256]{1,0:T(8,128)S(1)} %get-tuple-element.32, f32[32,256]{1,0:T(8,128)S(1)} %get-tuple-element.33, f32[32,256]{1,0:T(8,128)S(1)} %get-tuple-element.34, ...), kind=kLoop, calls=%fused_computation.21 | loop fusion | flops 16777216 | bytes 42205184 | tf_op jit(solution)/shard_map/sub | solution.py:101
  62.1 0.0 copy-start.1
  62.1 6.9 %convolution_bitcast_fusion.1 = f32[128,128]{0,1:T(8,128)S(1)} fusion(f32[32,256,128]{2,1,0:T(8,128)S(1)} %fusion.9), kind=kOutput, calls=%fused_computation.36 | convolution fusion | flops 1610612736 | bytes 4259840 | tf_op jit(solution)/shard_map/rck,rcj->kj/dot_general | solution.py:155
  69.0 3.7 %collective-permute-start.10 = (f32[128,128]{0,1:T(8,128)S(1)}, f32[128,128]{0,1:T(8,128)S(1)}, u32[]{:S(2)}, u32[]{:S(2)}) collective-permute-start(f32[128,128]{0,1:T(8,128)S(1)} %convolution_bitcast_fusion.1), channel_id=1, source_target_pairs={{0,192},{16,208},{32,224},{48,240},{64,128},{80,144},{96,160},{112... | collective-permute-start | bytes 196616 | tf_op jit(solution)/shard_map/ppermute | solution.py:110
  72.7 0.1 collective-permute-start.8
  72.9 1.4 collective-permute-start.9
  74.3 0.7 collective-permute-done.10
  75.0 2.0 %collective-permute-done.8 = f32[128,128]{0,1:T(8,128)S(1)} collective-permute-done((f32[128,128]{0,1:T(8,128)S(1)}, f32[128,128]{0,1:T(8,128)S(1)}, u32[]{:S(2)}, u32[]{:S(2)}) %collective-permute-start.8) | collective-permute-done | bytes 65568 | tf_op jit(solution)/shard_map/ppermute | solution.py:110
  77.0 1.7 %collective-permute-done.9 = f32[128,128]{0,1:T(8,128)S(1)} collective-permute-done((f32[128,128]{0,1:T(8,128)S(1)}, f32[128,128]{0,1:T(8,128)S(1)}, u32[]{:S(2)}, u32[]{:S(2)}) %collective-permute-start.9) | collective-permute-done | bytes 65568 | tf_op jit(solution)/shard_map/ppermute | solution.py:110
  78.8 4.4 %collective-permute-start.11 = (f32[128,128]{0,1:T(8,128)S(1)}, f32[128,128]{0,1:T(8,128)S(1)}, u32[]{:S(2)}, u32[]{:S(2)}) collective-permute-start(f32[128,128]{0,1:T(8,128)S(1)} %add_add_fusion.2), channel_id=1, source_target_pairs={{0,16},{16,0},{32,48},{48,32},{64,80},{80,64},{96,112},{112,96},{1... | collective-permute-start | bytes 196616 | tf_op jit(solution)/shard_map/ppermute | solution.py:110
  83.2 1.6 %collective-permute-start.13 = (f32[128,128]{0,1:T(8,128)S(1)}, f32[128,128]{0,1:T(8,128)S(1)}, u32[]{:S(2)}, u32[]{:S(2)}) collective-permute-start(f32[128,128]{0,1:T(8,128)S(1)} %add_add_fusion.2), channel_id=1, source_target_pairs={{0,48},{16,32},{32,16},{48,0},{64,112},{80,96},{96,80},{112,64},{1... | collective-permute-start | bytes 196616 | tf_op jit(solution)/shard_map/ppermute | solution.py:110
  84.8 1.3 collective-permute-done.11
  86.0 3.2 %collective-permute-done.12 = f32[128,128]{0,1:T(8,128)S(1)} collective-permute-done((f32[128,128]{0,1:T(8,128)S(1)}, f32[128,128]{0,1:T(8,128)S(1)}, u32[]{:S(2)}, u32[]{:S(2)}) %collective-permute-start.12) | collective-permute-done | bytes 65568 | tf_op jit(solution)/shard_map/ppermute | solution.py:110
  89.3 3.6 %collective-permute-start.14 = (f32[128,128]{0,1:T(8,128)S(1)}, f32[128,128]{0,1:T(8,128)S(1)}, u32[]{:S(2)}, u32[]{:S(2)}) collective-permute-start(f32[128,128]{0,1:T(8,128)S(1)} %add_add_fusion.1), channel_id=1, source_target_pairs={{0,4},{1,5},{2,6},{3,7},{4,0},{5,1},{6,2},{7,3},{8,12},{9,13},{10,... | collective-permute-start | bytes 196616 | tf_op jit(solution)/shard_map/ppermute | solution.py:110
  92.8 6.0 %collective-permute-start.15 = (f32[128,128]{0,1:T(8,128)S(1)}, f32[128,128]{0,1:T(8,128)S(1)}, u32[]{:S(2)}, u32[]{:S(2)}) collective-permute-start(f32[128,128]{0,1:T(8,128)S(1)} %add_add_fusion.1), channel_id=1, source_target_pairs={{0,8},{1,9},{2,10},{3,11},{4,12},{5,13},{6,14},{7,15},{8,0},{9,1},... | collective-permute-start | bytes 196616 | tf_op jit(solution)/shard_map/ppermute | solution.py:110
  98.8 0.5 collective-permute-start.16
  99.3 3.8 %collective-permute-done.15 = f32[128,128]{0,1:T(8,128)S(1)} collective-permute-done((f32[128,128]{0,1:T(8,128)S(1)}, f32[128,128]{0,1:T(8,128)S(1)}, u32[]{:S(2)}, u32[]{:S(2)}) %collective-permute-start.15) | collective-permute-done | bytes 65568 | tf_op jit(solution)/shard_map/ppermute | solution.py:110
  103.2 2.1 %collective-permute-done.16 = f32[128,128]{0,1:T(8,128)S(1)} collective-permute-done((f32[128,128]{0,1:T(8,128)S(1)}, f32[128,128]{0,1:T(8,128)S(1)}, u32[]{:S(2)}, u32[]{:S(2)}) %collective-permute-start.16) | collective-permute-done | bytes 65568 | tf_op jit(solution)/shard_map/ppermute | solution.py:110
  105.3 0.1 collective-permute-start.17
  105.4 2.5 %collective-permute-start.18 = (f32[128,128]{0,1:T(8,128)S(1)}, f32[128,128]{0,1:T(8,128)S(1)}, u32[]{:S(2)}, u32[]{:S(2)}) collective-permute-start(f32[128,128]{0,1:T(8,128)S(1)} %add_add_fusion), channel_id=1, source_target_pairs={{0,2},{1,3},{2,0},{3,1},{4,6},{5,7},{6,4},{7,5},{8,10},{9,11},{10,... | collective-permute-start | bytes 196616 | tf_op jit(solution)/shard_map/ppermute | solution.py:110
  107.8 0.0 collective-permute-start.19
  107.9 2.6 %collective-permute-done.18 = f32[128,128]{0,1:T(8,128)S(1)} collective-permute-done((f32[128,128]{0,1:T(8,128)S(1)}, f32[128,128]{0,1:T(8,128)S(1)}, u32[]{:S(2)}, u32[]{:S(2)}) %collective-permute-start.18) | collective-permute-done | bytes 65568 | tf_op jit(solution)/shard_map/ppermute | solution.py:110
  110.5 1.4 collective-permute-done.19
  111.9 0.1 copy.21
  112.1 11.7 %cholesky.17 = f32[128,128]{1,0:T(8,128)S(1)} custom-call(f32[128,128]{1,0:T(8,128)S(1)} %fusion.17), custom_call_target="Cholesky" | custom-call | tf_op jit(solution)/shard_map/jit(cholesky)/cholesky | solution.py:160
  123.8 0.6 compare_reduce_fusion
  124.4 0.7 fusion.67
  125.1 9.8 %custom-call.7 = f32[1,128,128]{1,2,0:T(8,128)S(1)} custom-call(f32[1,128,128]{2,1,0:T(8,128)S(1)} %get-tuple-element.30), custom_call_target="InvertDiagBlocksLowerTriangular" | custom-call | tf_op jit(solution)/shard_map/jit(_solve_triangular)/triangular_solve | solution.py:161
  134.9 0.2 convolution_bitcast_fusion
  135.2 5.9 %fusion.82 = f32[128,32,256]{2,0,1:T(8,128)S(1)} fusion(f32[128,128,1]{1,0,2:T(8,128)S(1)} %convolution_bitcast_fusion, f32[32,256,128]{2,1,0:T(8,128)} %copy-done.1), kind=kOutput, calls=%fused_computation.179 | convolution fusion | flops 1610612736 | bytes 8454144 | tf_op jit(solution)/shard_map/kj,rcj->krc/dot_general | solution.py:164
  141.0 4.4 %copy.22 = f32[128,32,256]{2,1,0:T(8,128)} copy(f32[128,32,256]{2,0,1:T(8,128)S(1)} %fusion.82) | data formatting | bytes 8388608
  145.5 0.7 copy.23
  (22 shorter events, 0.3 us)
Async XLA Ops:
  1.4 18.3 %collective-permute-start.4 = (s32[5,3,256]{2,1,0:T(4,128)S(1)}, s32[5,3,256]{2,1,0:T(4,128)S(1)}, u32[]{:S(2)}, u32[]{:S(2)}) collective-permute-start(s32[5,3,256]{2,1,0:T(4,128)S(1)} %get-tuple-element.27), channel_id=1, source_target_pairs={{0,16},{16,32},{32,48},{48,64},{64,80},{80,96},{96,112},{112,128},... | collective-permute-start | bytes 46088 | tf_op jit(solution)/shard_map/ppermute | solution.py:27
  4.8 14.9 %copy-start.2 = (s32[4,32,256]{2,1,0:T(8,128)S(1)}, s32[4,32,256]{2,1,0:T(8,128)}, u32[]{:S(2)}) copy-start(s32[4,32,256]{2,1,0:T(8,128)} %param.4) | copy-start | bytes 393220
  4.8 14.9 %copy-start.3 = (s32[32,256]{1,0:T(8,128)S(1)}, s32[32,256]{1,0:T(8,128)}, u32[]{:S(2)}) copy-start(s32[32,256]{1,0:T(8,128)} %param.3) | copy-start | bytes 98308
  4.9 14.9 %collective-permute-start.5 = (s32[5,3,256]{2,1,0:T(4,128)S(1)}, s32[5,3,256]{2,1,0:T(4,128)S(1)}, u32[]{:S(2)}, u32[]{:S(2)}) collective-permute-start(s32[5,3,256]{2,1,0:T(4,128)S(1)} %get-tuple-element.28), channel_id=1, source_target_pairs={{16,0},{32,16},{48,32},{64,48},{80,64},{96,80},{112,96},{128,112},... | collective-permute-start | bytes 46088 | tf_op jit(solution)/shard_map/ppermute | solution.py:29
  13.8 14.3 %collective-permute-start = (f32[2,256,128]{2,1,0:T(8,128)S(1)}, f32[2,256,128]{2,1,0:T(8,128)S(1)}, u32[]{:S(2)}, u32[]{:S(2)}) collective-permute-start(f32[2,256,128]{2,1,0:T(8,128)S(1)} %get-tuple-element.19), channel_id=1, source_target_pairs={{0,16},{16,32},{32,48},{48,64},{64,80},{80,96},{96,112},{112,128},... | collective-permute-start | bytes 786440 | tf_op jit(solution)/shard_map/ppermute | solution.py:27
  17.2 10.9 %collective-permute-start.1 = (f32[2,256,128]{2,1,0:T(8,128)S(1)}, f32[2,256,128]{2,1,0:T(8,128)S(1)}, u32[]{:S(2)}, u32[]{:S(2)}) collective-permute-start(f32[2,256,128]{2,1,0:T(8,128)S(1)} %get-tuple-element.20), channel_id=1, source_target_pairs={{16,0},{32,16},{48,32},{64,48},{80,64},{96,80},{112,96},{128,112},... | collective-permute-start | bytes 786440 | tf_op jit(solution)/shard_map/ppermute | solution.py:29
  19.7 8.5 %copy-start = (f32[128,32,256]{0,2,1:T(8,128)S(1)}, f32[128,32,256]{0,2,1:T(8,128)}, u32[]{:S(2)}) copy-start(f32[128,32,256]{0,2,1:T(8,128)} %copy.15) | copy-start | bytes 12582916
  19.9 2.9 %collective-permute-start.6 = (s32[5,38,3]{2,1,0:T(8,128)S(1)}, s32[5,38,3]{2,1,0:T(8,128)S(1)}, u32[]{:S(2)}, u32[]{:S(2)}) collective-permute-start(s32[5,38,3]{2,1,0:T(8,128)S(1)} %get-tuple-element.25), channel_id=1, source_target_pairs={{0,1},{1,2},{2,3},{3,4},{4,5},{5,6},{6,7},{7,8},{8,9},{9,10},{10,1... | collective-permute-start | bytes 6848 | tf_op jit(solution)/shard_map/ppermute | solution.py:27
  21.5 5.3 %collective-permute-start.7 = (s32[5,38,3]{2,1,0:T(8,128)S(1)}, s32[5,38,3]{2,1,0:T(8,128)S(1)}, u32[]{:S(2)}, u32[]{:S(2)}) collective-permute-start(s32[5,38,3]{2,1,0:T(8,128)S(1)} %get-tuple-element.26), channel_id=1, source_target_pairs={{1,0},{2,1},{3,2},{4,3},{5,4},{6,5},{7,6},{8,7},{9,8},{10,9},{11,1... | collective-permute-start | bytes 6848 | tf_op jit(solution)/shard_map/ppermute | solution.py:29
  28.2 6.8 %collective-permute-start.2 = (f32[36,2,128]{2,1,0:T(2,128)S(1)}, f32[36,2,128]{2,1,0:T(2,128)S(1)}, u32[]{:S(2)}, u32[]{:S(2)}) collective-permute-start(f32[36,2,128]{2,1,0:T(2,128)S(1)} %get-tuple-element.17), channel_id=1, source_target_pairs={{0,1},{1,2},{2,3},{3,4},{4,5},{5,6},{6,7},{7,8},{8,9},{9,10},{10,1... | collective-permute-start | bytes 110600 | tf_op jit(solution)/shard_map/ppermute | solution.py:27
  33.4 3.1 %collective-permute-start.3 = (f32[36,2,128]{2,1,0:T(2,128)S(1)}, f32[36,2,128]{2,1,0:T(2,128)S(1)}, u32[]{:S(2)}, u32[]{:S(2)}) collective-permute-start(f32[36,2,128]{2,1,0:T(2,128)S(1)} %get-tuple-element.18), channel_id=1, source_target_pairs={{1,0},{2,1},{3,2},{4,3},{5,4},{6,5},{7,6},{8,7},{9,8},{10,9},{11,1... | collective-permute-start | bytes 110600 | tf_op jit(solution)/shard_map/ppermute | solution.py:29
  62.1 43.2 %copy-start.1 = (f32[32,256,128]{2,1,0:T(8,128)}, f32[32,256,128]{2,1,0:T(8,128)S(1)}, u32[]{:S(2)}) copy-start(f32[32,256,128]{2,1,0:T(8,128)S(1)} %fusion.9) | copy-start | bytes 12582916
  69.0 6.0 %collective-permute-start.10 = (f32[128,128]{0,1:T(8,128)S(1)}, f32[128,128]{0,1:T(8,128)S(1)}, u32[]{:S(2)}, u32[]{:S(2)}) collective-permute-start(f32[128,128]{0,1:T(8,128)S(1)} %convolution_bitcast_fusion.1), channel_id=1, source_target_pairs={{0,192},{16,208},{32,224},{48,240},{64,128},{80,144},{96,160},{112... | collective-permute-start | bytes 196616 | tf_op jit(solution)/shard_map/ppermute | solution.py:110
  72.7 4.3 %collective-permute-start.8 = (f32[128,128]{0,1:T(8,128)S(1)}, f32[128,128]{0,1:T(8,128)S(1)}, u32[]{:S(2)}, u32[]{:S(2)}) collective-permute-start(f32[128,128]{0,1:T(8,128)S(1)} %convolution_bitcast_fusion.1), channel_id=1, source_target_pairs={{0,64},{16,80},{32,96},{48,112},{64,0},{80,16},{96,32},{112,48},{1... | collective-permute-start | bytes 196616 | tf_op jit(solution)/shard_map/ppermute | solution.py:110
  72.9 5.9 %collective-permute-start.9 = (f32[128,128]{0,1:T(8,128)S(1)}, f32[128,128]{0,1:T(8,128)S(1)}, u32[]{:S(2)}, u32[]{:S(2)}) collective-permute-start(f32[128,128]{0,1:T(8,128)S(1)} %convolution_bitcast_fusion.1), channel_id=1, source_target_pairs={{0,128},{16,144},{32,160},{48,176},{64,192},{80,208},{96,224},{112... | collective-permute-start | bytes 196616 | tf_op jit(solution)/shard_map/ppermute | solution.py:110
  78.8 7.3 %collective-permute-start.11 = (f32[128,128]{0,1:T(8,128)S(1)}, f32[128,128]{0,1:T(8,128)S(1)}, u32[]{:S(2)}, u32[]{:S(2)}) collective-permute-start(f32[128,128]{0,1:T(8,128)S(1)} %add_add_fusion.2), channel_id=1, source_target_pairs={{0,16},{16,0},{32,48},{48,32},{64,80},{80,64},{96,112},{112,96},{1... | collective-permute-start | bytes 196616 | tf_op jit(solution)/shard_map/ppermute | solution.py:110
  83.2 6.0 %collective-permute-start.12 = (f32[128,128]{0,1:T(8,128)S(1)}, f32[128,128]{0,1:T(8,128)S(1)}, u32[]{:S(2)}, u32[]{:S(2)}) collective-permute-start(f32[128,128]{0,1:T(8,128)S(1)} %add_add_fusion.2), channel_id=1, source_target_pairs={{0,32},{16,48},{32,0},{48,16},{64,96},{80,112},{96,64},{112,80},{1... | collective-permute-start | bytes 196616 | tf_op jit(solution)/shard_map/ppermute | solution.py:110
  83.2 6.0 %collective-permute-start.13 = (f32[128,128]{0,1:T(8,128)S(1)}, f32[128,128]{0,1:T(8,128)S(1)}, u32[]{:S(2)}, u32[]{:S(2)}) collective-permute-start(f32[128,128]{0,1:T(8,128)S(1)} %add_add_fusion.2), channel_id=1, source_target_pairs={{0,48},{16,32},{32,16},{48,0},{64,112},{80,96},{96,80},{112,64},{1... | collective-permute-start | bytes 196616 | tf_op jit(solution)/shard_map/ppermute | solution.py:110
  89.3 10.1 %collective-permute-start.14 = (f32[128,128]{0,1:T(8,128)S(1)}, f32[128,128]{0,1:T(8,128)S(1)}, u32[]{:S(2)}, u32[]{:S(2)}) collective-permute-start(f32[128,128]{0,1:T(8,128)S(1)} %add_add_fusion.1), channel_id=1, source_target_pairs={{0,4},{1,5},{2,6},{3,7},{4,0},{5,1},{6,2},{7,3},{8,12},{9,13},{10,... | collective-permute-start | bytes 196616 | tf_op jit(solution)/shard_map/ppermute | solution.py:110
  92.8 10.3 %collective-permute-start.15 = (f32[128,128]{0,1:T(8,128)S(1)}, f32[128,128]{0,1:T(8,128)S(1)}, u32[]{:S(2)}, u32[]{:S(2)}) collective-permute-start(f32[128,128]{0,1:T(8,128)S(1)} %add_add_fusion.1), channel_id=1, source_target_pairs={{0,8},{1,9},{2,10},{3,11},{4,12},{5,13},{6,14},{7,15},{8,0},{9,1},... | collective-permute-start | bytes 196616 | tf_op jit(solution)/shard_map/ppermute | solution.py:110
  98.8 6.4 %collective-permute-start.16 = (f32[128,128]{0,1:T(8,128)S(1)}, f32[128,128]{0,1:T(8,128)S(1)}, u32[]{:S(2)}, u32[]{:S(2)}) collective-permute-start(f32[128,128]{0,1:T(8,128)S(1)} %add_add_fusion.1), channel_id=1, source_target_pairs={{0,12},{1,13},{2,14},{3,15},{4,8},{5,9},{6,10},{7,11},{8,4},{9,5},... | collective-permute-start | bytes 196616 | tf_op jit(solution)/shard_map/ppermute | solution.py:110
  105.3 2.6 %collective-permute-start.17 = (f32[128,128]{0,1:T(8,128)S(1)}, f32[128,128]{0,1:T(8,128)S(1)}, u32[]{:S(2)}, u32[]{:S(2)}) collective-permute-start(f32[128,128]{0,1:T(8,128)S(1)} %add_add_fusion), channel_id=1, source_target_pairs={{0,1},{1,0},{2,3},{3,2},{4,5},{5,4},{6,7},{7,6},{8,9},{9,8},{10,11... | collective-permute-start | bytes 196616 | tf_op jit(solution)/shard_map/ppermute | solution.py:110
  105.4 5.1 %collective-permute-start.18 = (f32[128,128]{0,1:T(8,128)S(1)}, f32[128,128]{0,1:T(8,128)S(1)}, u32[]{:S(2)}, u32[]{:S(2)}) collective-permute-start(f32[128,128]{0,1:T(8,128)S(1)} %add_add_fusion), channel_id=1, source_target_pairs={{0,2},{1,3},{2,0},{3,1},{4,6},{5,7},{6,4},{7,5},{8,10},{9,11},{10,... | collective-permute-start | bytes 196616 | tf_op jit(solution)/shard_map/ppermute | solution.py:110
  107.8 4.1 %collective-permute-start.19 = (f32[128,128]{0,1:T(8,128)S(1)}, f32[128,128]{0,1:T(8,128)S(1)}, u32[]{:S(2)}, u32[]{:S(2)}) collective-permute-start(f32[128,128]{0,1:T(8,128)S(1)} %add_add_fusion), channel_id=1, source_target_pairs={{0,3},{1,2},{2,1},{3,0},{4,7},{5,6},{6,5},{7,4},{8,11},{9,10},{10,... | collective-permute-start | bytes 196616 | tf_op jit(solution)/shard_map/ppermute | solution.py:110

commit v13 on v12

--- a/solution.py
+++ b/solution.py
@@ -146,8 +146,15 @@
     counts = labels_wide[1:].astype(jnp.float32)
     weights = neighbour_weights(levels, counts, inside)
     scales = degree_scales(weights)
-    pixels = jnp.transpose(basis_block, (1, 2, 0))
-    extended = padded(pixels, (("row", 0), ("col", 1)), 2)
+    row_ends = row_count - 1
+    head = basis_block[:, :2, :]
+    tail = basis_block[:, tile_rows - 2 :, :]
+    from_above = lax.ppermute(tail, "row", [(i, i + 1) for i in range(row_ends)])
+    from_below = lax.ppermute(head, "row", [(i + 1, i) for i in range(row_ends)])
+    pixels = jnp.concatenate(
+        [jnp.transpose(part, (1, 2, 0)) for part in (from_above, basis_block, from_below)], axis=0
+    )
+    extended = padded(pixels, (("col", 1),), 2)
     first = apply_pixels(extended, pass_coefficients([cropped(w, 1) for w in weights], scales))
     tile_scales = cropped(scales, 1)
     filtered = apply_pixels(first, pass_coefficients([cropped(w, 2) for w in weights], tile_scales))

time: 149 us -> 149 us (level)
  waiting for transfers between devices: 24.4 us -> 21.8 us
  other arithmetic: 50.8 us -> 52.8 us
    ppermute x0 -> x2, starting transfers between devices: none -> 5.85 us  [the longest x1 3.4 us: per_device(): lax.ppermute(tail, 'row', [(i, i + 1) for i in range(row_ends)])]
    ppermute x4 -> x3, starting transfers between devices: 13.5 us -> 10 us  [padded(): lax.ppermute(tail, axis, [(i, (i + 1) % count) for i in range(ends)])]
    ppermute x4 -> x3, waiting for transfers between devices: 5.48 us -> 2.74 us  [padded(): lax.ppermute(head, axis, [((i + 1) % count, i) for i in range(ends)])]
    ppermute x4 -> x3, starting transfers between devices: 7.79 us -> 5.2 us  [padded(): lax.ppermute(head, axis, [((i + 1) % count, i) for i in range(ends)])]
    slice x0 -> x1, local copies, waits for them, and re-layouts: none -> 1.74 us  [per_device(): tail = basis_block[:, tile_rows - 2:, :]]
    unnamed x11 -> x13, local copies, waits for them, and re-layouts: 10.5 us -> 10.5 us
  transfers between devices with their start and end apart: 20 -> 20, of which waited for: 11 -> 10; matrix products, arithmetic and copies ran while one was open for 5% -> 7% of each run, Pallas kernels for 0% -> 0%
where the time goes in v13:
time: 149 us; the launch traced here: 146 us
  other arithmetic  52.8 us (35%)
  starting transfers between devices  44.8 us (30%)
  waiting for transfers between devices  21.8 us (15%)
  matrix products  13.1 us (9%)
  local copies, waits for them, and re-layouts  12.7 us (9%)
    ppermute x12, starting transfers between devices, exchange_sum(): received.append(lax.ppermute(block, axis, route))  23.8 us
    sub x2, other arithmetic, apply_pixels(): return shifted_pixels(values_in, 0, 0) - summed  21.6 us
    ppermute x12, waiting for transfers between devices, exchange_sum(): received.append(lax.ppermute(block, axis, route))  19.1 us
    another operation x3, other arithmetic, per_device(): factor = jnp.linalg.cholesky(gram)  12.4 us
    unnamed x13, local copies, waits for them, and re-layouts  10.5 us
    ppermute x3, starting transfers between devices, padded(): lax.ppermute(tail, axis, [(i, (i + 1) % count) for i in range(ends)])  10 us
    another operation x1, other arithmetic, per_device(): jax.scipy.linalg.solve_triangular(factor, jnp.eye(vectors, dtype=jnp.floa...  9.81 us
    dot_general x1, matrix products, per_device(): jnp.einsum('rck,rcj->kj', filtered, filtered, precision=lax.Precision.HIG...  6.94 us
  transfers between devices with their start and end apart: 20, of which 10 were waited for; matrix products, arithmetic and copies ran while one was open for 7% of the time, Pallas kernels for 0%

profile of v13, /device:TPU:2, one launch (start us, length us, event | category | flops | bytes accessed | tf_op | source)
XLA Modules:
  0.0 146.3 jit_solution(13648329171485202336)
XLA Ops:
  0.6 0.8 pad_add_fusion.3
  1.4 3.4 %collective-permute-start.4 = (s32[5,3,256]{2,1,0:T(4,128)S(1)}, s32[5,3,256]{2,1,0:T(4,128)S(1)}, u32[]{:S(2)}, u32[]{:S(2)}) collective-permute-start(s32[5,3,256]{2,1,0:T(4,128)S(1)} %get-tuple-element.27), channel_id=1, source_target_pairs={{0,16},{16,32},{32,48},{48,64},{64,80},{80,96},{96,112},{112,128},... | collective-permute-start | bytes 46088 | tf_op jit(solution)/shard_map/ppermute | solution.py:27
  4.8 2.4 %collective-permute-start.5 = (s32[5,3,256]{2,1,0:T(4,128)S(1)}, s32[5,3,256]{2,1,0:T(4,128)S(1)}, u32[]{:S(2)}, u32[]{:S(2)}) collective-permute-start(s32[5,3,256]{2,1,0:T(4,128)S(1)} %get-tuple-element.28), channel_id=1, source_target_pairs={{16,0},{32,16},{48,32},{64,48},{80,64},{96,80},{112,96},{128,112},... | collective-permute-start | bytes 46088 | tf_op jit(solution)/shard_map/ppermute | solution.py:29
  7.3 1.7 %fusion.80 = (f32[128,2,256]{2,1,0:T(2,128)S(1)}, f32[128,2,256]{2,1,0:T(2,128)S(1)}) fusion(f32[128,32,256]{2,1,0:T(8,128)} %param.5), kind=kLoop, calls=%fused_computation.177 | loop fusion | bytes 1048576 | tf_op jit(solution)/shard_map/slice | solution.py:151
  9.0 3.4 %collective-permute-start = (f32[128,2,256]{2,0,1:T(8,128)S(1)}, f32[128,2,256]{2,0,1:T(8,128)S(1)}, u32[]{:S(2)}, u32[]{:S(2)}) collective-permute-start(f32[128,2,256]{2,0,1:T(8,128)S(1)} %copy.34), channel_id=1, source_target_pairs={{0,16},{16,32},{32,48},{48,64},{64,80},{80,96},{96,112},{112,128},... | collective-permute-start | bytes 786440 | tf_op jit(solution)/shard_map/ppermute | solution.py:152
  12.5 2.5 %collective-permute-start.1 = (f32[128,2,256]{2,0,1:T(8,128)S(1)}, f32[128,2,256]{2,0,1:T(8,128)S(1)}, u32[]{:S(2)}, u32[]{:S(2)}) collective-permute-start(f32[128,2,256]{2,0,1:T(8,128)S(1)} %copy.35), channel_id=1, source_target_pairs={{16,0},{32,16},{48,32},{64,48},{80,64},{96,80},{112,96},{128,112},... | collective-permute-start | bytes 786440 | tf_op jit(solution)/shard_map/ppermute | solution.py:153
  15.0 0.0 copy-start.2
  15.0 0.0 copy-start.3
  15.0 0.0 collective-permute-done.5
  15.0 1.0 pad_add_fusion.1
  16.0 0.1 fusion.81
  16.1 1.3 collective-permute-start.6
  17.4 1.3 collective-permute-start.7
  18.7 0.1 broadcast_multiply_fusion
  18.8 5.3 %copy.16 = f32[128,32,256]{0,2,1:T(8,128)} copy(f32[128,32,256]{2,1,0:T(8,128)} %param.5) | data formatting | bytes 8388608 | tf_op args[2]
  24.1 0.2 pad_add_fusion
  24.3 0.1 fusion.65
  24.4 0.4 add_rsqrt_fusion
  24.8 0.2 slice_multiply_fusion.46
  25.0 0.1 slice_multiply_fusion.28
  25.2 0.3 slice_multiply_fusion.30
  25.4 0.1 copy.18
  25.6 0.1 copy.19
  25.7 0.0 copy-start.1
  25.7 1.1 pad_maximum_fusion.4
  26.9 5.3 %collective-permute-start.2 = (f32[36,2,128]{2,1,0:T(2,128)S(1)}, f32[36,2,128]{2,1,0:T(2,128)S(1)}, u32[]{:S(2)}, u32[]{:S(2)}) collective-permute-start(f32[36,2,128]{2,1,0:T(2,128)S(1)} %get-tuple-element.17), channel_id=1, source_target_pairs={{0,1},{1,2},{2,3},{3,4},{4,5},{5,6},{6,7},{7,8},{8,9},{9,10},{10,1... | collective-permute-start | bytes 110600 | tf_op jit(solution)/shard_map/ppermute | solution.py:27
  32.2 1.5 %collective-permute-start.3 = (f32[36,2,128]{2,1,0:T(2,128)S(1)}, f32[36,2,128]{2,1,0:T(2,128)S(1)}, u32[]{:S(2)}, u32[]{:S(2)}) collective-permute-start(f32[36,2,128]{2,1,0:T(2,128)S(1)} %get-tuple-element.18), channel_id=1, source_target_pairs={{1,0},{2,1},{3,2},{4,3},{5,4},{6,5},{7,6},{8,7},{9,8},{10,9},{11,1... | collective-permute-start | bytes 110600 | tf_op jit(solution)/shard_map/ppermute | solution.py:29
  33.7 0.1 slice_multiply_fusion.34
  33.8 2.7 %collective-permute-done.3 = f32[36,2,128]{2,1,0:T(2,128)S(1)} collective-permute-done((f32[36,2,128]{2,1,0:T(2,128)S(1)}, f32[36,2,128]{2,1,0:T(2,128)S(1)}, u32[]{:S(2)}, u32[]{:S(2)}) %collective-permute-start.3) | collective-permute-done | bytes 36896 | tf_op jit(solution)/shard_map/ppermute | solution.py:29
  36.5 2.3 %maximum_maximum_fusion = (f32[36,258,128]{2,1,0:T(8,128)S(1)}, f32[36,258,128]{2,1,0:T(8,128)S(1)}) fusion(f32[2,256,128]{2,1,0:T(8,128)S(1)} %copy.19, f32[32,256,128]{2,1,0:T(8,128)S(1)} %bitcast.38, f32[2,256,128]{2,1,0:T(8,128)S(1)} %copy.18, f32[36,2,128]{2,1,0:T(2,128)S(1)} %collective-permute-done.2, f32[36,2,128]{2,1,0:T(2,128)S(1)} %collective-permute-done.3), kind=kLoop, calls=%fused_computation.2 | loop fusion | flops 7133184 | bytes 14303232 | tf_op jit(solution)/shard_map/concatenate | solution.py:25
  38.8 1.6 %pad_maximum_fusion = f32[36,260,128]{2,1,0:T(8,128)S(1)} fusion(f32[36,2,128]{2,1,0:T(2,128)S(1)} %collective-permute-done.3, f32[2,256,128]{2,1,0:T(8,128)S(1)} %copy.19, f32[32,256,128]{2,1,0:T(8,128)S(1)} %bitcast.39, f32[2,256,128]{2,1,0:T(8,128)S(1)} %copy.18, f32[36,2,128]{2,1,0:T(2,128)S(1)} %collective-permute-done.2), kind=kLoop, calls=%fused_computation | loop fusion | flops 4792320 | bytes 9584640 | tf_op jit(solution)/shard_map/concatenate | solution.py:25
  40.5 11.6 %fusion.1 = f32[34,258,128]{2,1,0:T(8,128)S(1)} fusion(f32[36,258,128]{2,1,0:T(8,128)S(1)} %get-tuple-element.16, f32[36,258,128]{2,1,0:T(8,128)S(1)} %get-tuple-element.15, f32[36,260,128]{2,1,0:T(8,128)S(1)} %pad_maximum_fusion, f32[34,258]{1,0:T(8,128)S(1)} %get-tuple-element.40, f32[34,258]{1,0:T(8,128)S(1)} %get-tuple-element.41, ...), kind=kLoop, calls=%fused_computation.5 | loop fusion | flops 17965056 | bytes 45193344 | tf_op jit(solution)/shard_map/sub | solution.py:101
  52.0 10.1 %fusion.9 = f32[32,256,128]{2,1,0:T(8,128)S(1)} fusion(f32[34,258,128]{2,1,0:T(8,128)S(1)} %fusion.1, f32[32,256]{1,0:T(8,128)S(1)} %get-tuple-element.38, f32[32,256]{1,0:T(8,128)S(1)} %get-tuple-element.37, f32[32,256]{1,0:T(8,128)S(1)} %get-tuple-element.32, f32[32,256]{1,0:T(8,128)S(1)} %get-tuple-element.33, f32[32,256]{1,0:T(8,128)S(1)} %get-tuple-element.34, ...), kind=kLoop, calls=%fused_computation.21 | loop fusion | flops 16777216 | bytes 42205184 | tf_op jit(solution)/shard_map/sub | solution.py:101
  62.1 0.0 copy-start
  62.1 6.9 %convolution_bitcast_fusion.1 = f32[128,128]{0,1:T(8,128)S(1)} fusion(f32[32,256,128]{2,1,0:T(8,128)S(1)} %fusion.9), kind=kOutput, calls=%fused_computation.36 | convolution fusion | flops 1610612736 | bytes 4259840 | tf_op jit(solution)/shard_map/rck,rcj->kj/dot_general | solution.py:162
  69.1 3.7 %collective-permute-start.10 = (f32[128,128]{0,1:T(8,128)S(1)}, f32[128,128]{0,1:T(8,128)S(1)}, u32[]{:S(2)}, u32[]{:S(2)}) collective-permute-start(f32[128,128]{0,1:T(8,128)S(1)} %convolution_bitcast_fusion.1), channel_id=1, source_target_pairs={{0,192},{16,208},{32,224},{48,240},{64,128},{80,144},{96,160},{112... | collective-permute-start | bytes 196616 | tf_op jit(solution)/shard_map/ppermute | solution.py:110
  72.8 0.1 collective-permute-start.8
  72.9 1.4 collective-permute-start.9
  74.3 0.7 collective-permute-done.10
  75.0 2.0 %collective-permute-done.8 = f32[128,128]{0,1:T(8,128)S(1)} collective-permute-done((f32[128,128]{0,1:T(8,128)S(1)}, f32[128,128]{0,1:T(8,128)S(1)}, u32[]{:S(2)}, u32[]{:S(2)}) %collective-permute-start.8) | collective-permute-done | bytes 65568 | tf_op jit(solution)/shard_map/ppermute | solution.py:110
  77.0 1.9 %collective-permute-done.9 = f32[128,128]{0,1:T(8,128)S(1)} collective-permute-done((f32[128,128]{0,1:T(8,128)S(1)}, f32[128,128]{0,1:T(8,128)S(1)}, u32[]{:S(2)}, u32[]{:S(2)}) %collective-permute-start.9) | collective-permute-done | bytes 65568 | tf_op jit(solution)/shard_map/ppermute | solution.py:110
  79.0 4.4 %collective-permute-start.11 = (f32[128,128]{0,1:T(8,128)S(1)}, f32[128,128]{0,1:T(8,128)S(1)}, u32[]{:S(2)}, u32[]{:S(2)}) collective-permute-start(f32[128,128]{0,1:T(8,128)S(1)} %add_add_fusion.2), channel_id=1, source_target_pairs={{0,16},{16,0},{32,48},{48,32},{64,80},{80,64},{96,112},{112,96},{1... | collective-permute-start | bytes 196616 | tf_op jit(solution)/shard_map/ppermute | solution.py:110
  83.4 1.6 %collective-permute-start.13 = (f32[128,128]{0,1:T(8,128)S(1)}, f32[128,128]{0,1:T(8,128)S(1)}, u32[]{:S(2)}, u32[]{:S(2)}) collective-permute-start(f32[128,128]{0,1:T(8,128)S(1)} %add_add_fusion.2), channel_id=1, source_target_pairs={{0,48},{16,32},{32,16},{48,0},{64,112},{80,96},{96,80},{112,64},{1... | collective-permute-start | bytes 196616 | tf_op jit(solution)/shard_map/ppermute | solution.py:110
  85.0 1.3 collective-permute-done.11
  86.3 3.2 %collective-permute-done.12 = f32[128,128]{0,1:T(8,128)S(1)} collective-permute-done((f32[128,128]{0,1:T(8,128)S(1)}, f32[128,128]{0,1:T(8,128)S(1)}, u32[]{:S(2)}, u32[]{:S(2)}) %collective-permute-start.12) | collective-permute-done | bytes 65568 | tf_op jit(solution)/shard_map/ppermute | solution.py:110
  89.5 3.5 %collective-permute-start.14 = (f32[128,128]{0,1:T(8,128)S(1)}, f32[128,128]{0,1:T(8,128)S(1)}, u32[]{:S(2)}, u32[]{:S(2)}) collective-permute-start(f32[128,128]{0,1:T(8,128)S(1)} %add_add_fusion.1), channel_id=1, source_target_pairs={{0,4},{1,5},{2,6},{3,7},{4,0},{5,1},{6,2},{7,3},{8,12},{9,13},{10,... | collective-permute-start | bytes 196616 | tf_op jit(solution)/shard_map/ppermute | solution.py:110
  93.0 6.4 %collective-permute-start.15 = (f32[128,128]{0,1:T(8,128)S(1)}, f32[128,128]{0,1:T(8,128)S(1)}, u32[]{:S(2)}, u32[]{:S(2)}) collective-permute-start(f32[128,128]{0,1:T(8,128)S(1)} %add_add_fusion.1), channel_id=1, source_target_pairs={{0,8},{1,9},{2,10},{3,11},{4,12},{5,13},{6,14},{7,15},{8,0},{9,1},... | collective-permute-start | bytes 196616 | tf_op jit(solution)/shard_map/ppermute | solution.py:110
  99.4 0.5 collective-permute-start.16
  99.8 3.2 %collective-permute-done.15 = f32[128,128]{0,1:T(8,128)S(1)} collective-permute-done((f32[128,128]{0,1:T(8,128)S(1)}, f32[128,128]{0,1:T(8,128)S(1)}, u32[]{:S(2)}, u32[]{:S(2)}) %collective-permute-start.15) | collective-permute-done | bytes 65568 | tf_op jit(solution)/shard_map/ppermute | solution.py:110
  103.0 2.7 %collective-permute-done.16 = f32[128,128]{0,1:T(8,128)S(1)} collective-permute-done((f32[128,128]{0,1:T(8,128)S(1)}, f32[128,128]{0,1:T(8,128)S(1)}, u32[]{:S(2)}, u32[]{:S(2)}) %collective-permute-start.16) | collective-permute-done | bytes 65568 | tf_op jit(solution)/shard_map/ppermute | solution.py:110
  105.8 0.1 collective-permute-start.17
  105.9 2.0 %collective-permute-start.18 = (f32[128,128]{0,1:T(8,128)S(1)}, f32[128,128]{0,1:T(8,128)S(1)}, u32[]{:S(2)}, u32[]{:S(2)}) collective-permute-start(f32[128,128]{0,1:T(8,128)S(1)} %add_add_fusion), channel_id=1, source_target_pairs={{0,2},{1,3},{2,0},{3,1},{4,6},{5,7},{6,4},{7,5},{8,10},{9,11},{10,... | collective-permute-start | bytes 196616 | tf_op jit(solution)/shard_map/ppermute | solution.py:110
  107.9 0.0 collective-permute-start.19
  107.9 2.6 %collective-permute-done.18 = f32[128,128]{0,1:T(8,128)S(1)} collective-permute-done((f32[128,128]{0,1:T(8,128)S(1)}, f32[128,128]{0,1:T(8,128)S(1)}, u32[]{:S(2)}, u32[]{:S(2)}) %collective-permute-start.18) | collective-permute-done | bytes 65568 | tf_op jit(solution)/shard_map/ppermute | solution.py:110
  110.6 1.4 collective-permute-done.19
  112.0 0.1 copy.25
  112.1 11.7 %cholesky.17 = f32[128,128]{1,0:T(8,128)S(1)} custom-call(f32[128,128]{1,0:T(8,128)S(1)} %fusion.17), custom_call_target="Cholesky" | custom-call | tf_op jit(solution)/shard_map/jit(cholesky)/cholesky | solution.py:167
  123.9 0.6 compare_reduce_fusion
  124.5 0.7 fusion.67
  125.2 9.8 %custom-call.7 = f32[1,128,128]{1,2,0:T(8,128)S(1)} custom-call(f32[1,128,128]{2,1,0:T(8,128)S(1)} %get-tuple-element.30), custom_call_target="InvertDiagBlocksLowerTriangular" | custom-call | tf_op jit(solution)/shard_map/jit(_solve_triangular)/triangular_solve | solution.py:168
  135.0 0.2 convolution_bitcast_fusion
  135.2 5.9 %fusion.82 = f32[128,32,256]{2,0,1:T(8,128)S(1)} fusion(f32[128,128,1]{1,0,2:T(8,128)S(1)} %convolution_bitcast_fusion, f32[32,256,128]{2,1,0:T(8,128)} %copy-done), kind=kOutput, calls=%fused_computation.179 | convolution fusion | flops 1610612736 | bytes 8454144 | tf_op jit(solution)/shard_map/kj,rcj->krc/dot_general | solution.py:171
  141.1 4.4 %copy.26 = f32[128,32,256]{2,1,0:T(8,128)} copy(f32[128,32,256]{2,0,1:T(8,128)S(1)} %fusion.82) | data formatting | bytes 8388608
  145.5 0.7 copy.27
  (26 shorter events, 0.2 us)
Async XLA Ops:
  1.4 13.6 %collective-permute-start.4 = (s32[5,3,256]{2,1,0:T(4,128)S(1)}, s32[5,3,256]{2,1,0:T(4,128)S(1)}, u32[]{:S(2)}, u32[]{:S(2)}) collective-permute-start(s32[5,3,256]{2,1,0:T(4,128)S(1)} %get-tuple-element.27), channel_id=1, source_target_pairs={{0,16},{16,32},{32,48},{48,64},{64,80},{80,96},{96,112},{112,128},... | collective-permute-start | bytes 46088 | tf_op jit(solution)/shard_map/ppermute | solution.py:27
  4.8 10.2 %collective-permute-start.5 = (s32[5,3,256]{2,1,0:T(4,128)S(1)}, s32[5,3,256]{2,1,0:T(4,128)S(1)}, u32[]{:S(2)}, u32[]{:S(2)}) collective-permute-start(s32[5,3,256]{2,1,0:T(4,128)S(1)} %get-tuple-element.28), channel_id=1, source_target_pairs={{16,0},{32,16},{48,32},{64,48},{80,64},{96,80},{112,96},{128,112},... | collective-permute-start | bytes 46088 | tf_op jit(solution)/shard_map/ppermute | solution.py:29
  9.0 16.4 %collective-permute-start = (f32[128,2,256]{2,0,1:T(8,128)S(1)}, f32[128,2,256]{2,0,1:T(8,128)S(1)}, u32[]{:S(2)}, u32[]{:S(2)}) collective-permute-start(f32[128,2,256]{2,0,1:T(8,128)S(1)} %copy.34), channel_id=1, source_target_pairs={{0,16},{16,32},{32,48},{48,64},{64,80},{80,96},{96,112},{112,128},... | collective-permute-start | bytes 786440 | tf_op jit(solution)/shard_map/ppermute | solution.py:152
  12.5 13.1 %collective-permute-start.1 = (f32[128,2,256]{2,0,1:T(8,128)S(1)}, f32[128,2,256]{2,0,1:T(8,128)S(1)}, u32[]{:S(2)}, u32[]{:S(2)}) collective-permute-start(f32[128,2,256]{2,0,1:T(8,128)S(1)} %copy.35), channel_id=1, source_target_pairs={{16,0},{32,16},{48,32},{64,48},{80,64},{96,80},{112,96},{128,112},... | collective-permute-start | bytes 786440 | tf_op jit(solution)/shard_map/ppermute | solution.py:153
  15.0 9.1 %copy-start.2 = (s32[4,32,256]{2,1,0:T(8,128)S(1)}, s32[4,32,256]{2,1,0:T(8,128)}, u32[]{:S(2)}) copy-start(s32[4,32,256]{2,1,0:T(8,128)} %param.4) | copy-start | bytes 393220
  15.0 9.1 %copy-start.3 = (s32[32,256]{1,0:T(8,128)S(1)}, s32[32,256]{1,0:T(8,128)}, u32[]{:S(2)}) copy-start(s32[32,256]{1,0:T(8,128)} %param.3) | copy-start | bytes 98308
  16.1 8.0 %collective-permute-start.6 = (s32[5,38,3]{2,1,0:T(8,128)S(1)}, s32[5,38,3]{2,1,0:T(8,128)S(1)}, u32[]{:S(2)}, u32[]{:S(2)}) collective-permute-start(s32[5,38,3]{2,1,0:T(8,128)S(1)} %get-tuple-element.25), channel_id=1, source_target_pairs={{0,1},{1,2},{2,3},{3,4},{4,5},{5,6},{6,7},{7,8},{8,9},{9,10},{10,1... | collective-permute-start | bytes 6848 | tf_op jit(solution)/shard_map/ppermute | solution.py:27
  17.4 6.7 %collective-permute-start.7 = (s32[5,38,3]{2,1,0:T(8,128)S(1)}, s32[5,38,3]{2,1,0:T(8,128)S(1)}, u32[]{:S(2)}, u32[]{:S(2)}) collective-permute-start(s32[5,38,3]{2,1,0:T(8,128)S(1)} %get-tuple-element.26), channel_id=1, source_target_pairs={{1,0},{2,1},{3,2},{4,3},{5,4},{6,5},{7,6},{8,7},{9,8},{10,9},{11,1... | collective-permute-start | bytes 6848 | tf_op jit(solution)/shard_map/ppermute | solution.py:29
  25.7 10.8 %copy-start.1 = (f32[128,32,256]{0,2,1:T(8,128)S(1)}, f32[128,32,256]{0,2,1:T(8,128)}, u32[]{:S(2)}) copy-start(f32[128,32,256]{0,2,1:T(8,128)} %copy.16) | copy-start | bytes 12582916
  26.9 6.9 %collective-permute-start.2 = (f32[36,2,128]{2,1,0:T(2,128)S(1)}, f32[36,2,128]{2,1,0:T(2,128)S(1)}, u32[]{:S(2)}, u32[]{:S(2)}) collective-permute-start(f32[36,2,128]{2,1,0:T(2,128)S(1)} %get-tuple-element.17), channel_id=1, source_target_pairs={{0,1},{1,2},{2,3},{3,4},{4,5},{5,6},{6,7},{7,8},{8,9},{9,10},{10,1... | collective-permute-start | bytes 110600 | tf_op jit(solution)/shard_map/ppermute | solution.py:27
  32.2 4.3 %collective-permute-start.3 = (f32[36,2,128]{2,1,0:T(2,128)S(1)}, f32[36,2,128]{2,1,0:T(2,128)S(1)}, u32[]{:S(2)}, u32[]{:S(2)}) collective-permute-start(f32[36,2,128]{2,1,0:T(2,128)S(1)} %get-tuple-element.18), channel_id=1, source_target_pairs={{1,0},{2,1},{3,2},{4,3},{5,4},{6,5},{7,6},{8,7},{9,8},{10,9},{11,1... | collective-permute-start | bytes 110600 | tf_op jit(solution)/shard_map/ppermute | solution.py:29
  62.1 43.7 %copy-start = (f32[32,256,128]{2,1,0:T(8,128)}, f32[32,256,128]{2,1,0:T(8,128)S(1)}, u32[]{:S(2)}) copy-start(f32[32,256,128]{2,1,0:T(8,128)S(1)} %fusion.9) | copy-start | bytes 12582916
  69.1 6.0 %collective-permute-start.10 = (f32[128,128]{0,1:T(8,128)S(1)}, f32[128,128]{0,1:T(8,128)S(1)}, u32[]{:S(2)}, u32[]{:S(2)}) collective-permute-start(f32[128,128]{0,1:T(8,128)S(1)} %convolution_bitcast_fusion.1), channel_id=1, source_target_pairs={{0,192},{16,208},{32,224},{48,240},{64,128},{80,144},{96,160},{112... | collective-permute-start | bytes 196616 | tf_op jit(solution)/shard_map/ppermute | solution.py:110
  72.8 4.3 %collective-permute-start.8 = (f32[128,128]{0,1:T(8,128)S(1)}, f32[128,128]{0,1:T(8,128)S(1)}, u32[]{:S(2)}, u32[]{:S(2)}) collective-permute-start(f32[128,128]{0,1:T(8,128)S(1)} %convolution_bitcast_fusion.1), channel_id=1, source_target_pairs={{0,64},{16,80},{32,96},{48,112},{64,0},{80,16},{96,32},{112,48},{1... | collective-permute-start | bytes 196616 | tf_op jit(solution)/shard_map/ppermute | solution.py:110
  72.9 6.1 %collective-permute-start.9 = (f32[128,128]{0,1:T(8,128)S(1)}, f32[128,128]{0,1:T(8,128)S(1)}, u32[]{:S(2)}, u32[]{:S(2)}) collective-permute-start(f32[128,128]{0,1:T(8,128)S(1)} %convolution_bitcast_fusion.1), channel_id=1, source_target_pairs={{0,128},{16,144},{32,160},{48,176},{64,192},{80,208},{96,224},{112... | collective-permute-start | bytes 196616 | tf_op jit(solution)/shard_map/ppermute | solution.py:110
  79.0 7.3 %collective-permute-start.11 = (f32[128,128]{0,1:T(8,128)S(1)}, f32[128,128]{0,1:T(8,128)S(1)}, u32[]{:S(2)}, u32[]{:S(2)}) collective-permute-start(f32[128,128]{0,1:T(8,128)S(1)} %add_add_fusion.2), channel_id=1, source_target_pairs={{0,16},{16,0},{32,48},{48,32},{64,80},{80,64},{96,112},{112,96},{1... | collective-permute-start | bytes 196616 | tf_op jit(solution)/shard_map/ppermute | solution.py:110
  83.4 6.0 %collective-permute-start.12 = (f32[128,128]{0,1:T(8,128)S(1)}, f32[128,128]{0,1:T(8,128)S(1)}, u32[]{:S(2)}, u32[]{:S(2)}) collective-permute-start(f32[128,128]{0,1:T(8,128)S(1)} %add_add_fusion.2), channel_id=1, source_target_pairs={{0,32},{16,48},{32,0},{48,16},{64,96},{80,112},{96,64},{112,80},{1... | collective-permute-start | bytes 196616 | tf_op jit(solution)/shard_map/ppermute | solution.py:110
  83.4 6.0 %collective-permute-start.13 = (f32[128,128]{0,1:T(8,128)S(1)}, f32[128,128]{0,1:T(8,128)S(1)}, u32[]{:S(2)}, u32[]{:S(2)}) collective-permute-start(f32[128,128]{0,1:T(8,128)S(1)} %add_add_fusion.2), channel_id=1, source_target_pairs={{0,48},{16,32},{32,16},{48,0},{64,112},{80,96},{96,80},{112,64},{1... | collective-permute-start | bytes 196616 | tf_op jit(solution)/shard_map/ppermute | solution.py:110
  89.5 10.3 %collective-permute-start.14 = (f32[128,128]{0,1:T(8,128)S(1)}, f32[128,128]{0,1:T(8,128)S(1)}, u32[]{:S(2)}, u32[]{:S(2)}) collective-permute-start(f32[128,128]{0,1:T(8,128)S(1)} %add_add_fusion.1), channel_id=1, source_target_pairs={{0,4},{1,5},{2,6},{3,7},{4,0},{5,1},{6,2},{7,3},{8,12},{9,13},{10,... | collective-permute-start | bytes 196616 | tf_op jit(solution)/shard_map/ppermute | solution.py:110
  93.0 10.0 %collective-permute-start.15 = (f32[128,128]{0,1:T(8,128)S(1)}, f32[128,128]{0,1:T(8,128)S(1)}, u32[]{:S(2)}, u32[]{:S(2)}) collective-permute-start(f32[128,128]{0,1:T(8,128)S(1)} %add_add_fusion.1), channel_id=1, source_target_pairs={{0,8},{1,9},{2,10},{3,11},{4,12},{5,13},{6,14},{7,15},{8,0},{9,1},... | collective-permute-start | bytes 196616 | tf_op jit(solution)/shard_map/ppermute | solution.py:110
  99.4 6.4 %collective-permute-start.16 = (f32[128,128]{0,1:T(8,128)S(1)}, f32[128,128]{0,1:T(8,128)S(1)}, u32[]{:S(2)}, u32[]{:S(2)}) collective-permute-start(f32[128,128]{0,1:T(8,128)S(1)} %add_add_fusion.1), channel_id=1, source_target_pairs={{0,12},{1,13},{2,14},{3,15},{4,8},{5,9},{6,10},{7,11},{8,4},{9,5},... | collective-permute-start | bytes 196616 | tf_op jit(solution)/shard_map/ppermute | solution.py:110
  105.8 2.1 %collective-permute-start.17 = (f32[128,128]{0,1:T(8,128)S(1)}, f32[128,128]{0,1:T(8,128)S(1)}, u32[]{:S(2)}, u32[]{:S(2)}) collective-permute-start(f32[128,128]{0,1:T(8,128)S(1)} %add_add_fusion), channel_id=1, source_target_pairs={{0,1},{1,0},{2,3},{3,2},{4,5},{5,4},{6,7},{7,6},{8,9},{9,8},{10,11... | collective-permute-start | bytes 196616 | tf_op jit(solution)/shard_map/ppermute | solution.py:110
  105.9 4.7 %collective-permute-start.18 = (f32[128,128]{0,1:T(8,128)S(1)}, f32[128,128]{0,1:T(8,128)S(1)}, u32[]{:S(2)}, u32[]{:S(2)}) collective-permute-start(f32[128,128]{0,1:T(8,128)S(1)} %add_add_fusion), channel_id=1, source_target_pairs={{0,2},{1,3},{2,0},{3,1},{4,6},{5,7},{6,4},{7,5},{8,10},{9,11},{10,... | collective-permute-start | bytes 196616 | tf_op jit(solution)/shard_map/ppermute | solution.py:110
  107.9 4.1 %collective-permute-start.19 = (f32[128,128]{0,1:T(8,128)S(1)}, f32[128,128]{0,1:T(8,128)S(1)}, u32[]{:S(2)}, u32[]{:S(2)}) collective-permute-start(f32[128,128]{0,1:T(8,128)S(1)} %add_add_fusion), channel_id=1, source_target_pairs={{0,3},{1,2},{2,1},{3,0},{4,7},{5,6},{6,5},{7,4},{8,11},{9,10},{10,... | collective-permute-start | bytes 196616 | tf_op jit(solution)/shard_map/ppermute | solution.py:110

commit v14 on v12

--- a/solution.py
+++ b/solution.py
@@ -113,13 +113,15 @@
     return received[0]
 
 
-def all_sum(block, axis):
+def all_sum(block, axis, alone_low=False):
     count = lax.axis_size(axis)
     levels = count.bit_length() - 1
     if (1 << levels) != count:
         return lax.psum(block, axis)
     groups = []
-    low_bit = 0
+    low_bit = 1 if alone_low and levels > 1 else 0
+    if low_bit:
+        groups.append((0, 1))
     while low_bit < levels:
         bits = min(2, levels - low_bit)
         groups.append((low_bit, bits))
@@ -156,7 +158,7 @@
         "rck,rcj->kj", filtered, filtered,
         precision=lax.Precision.HIGHEST, preferred_element_type=jnp.float32,
     )
-    gram = all_sum(all_sum(gram_local, "row"), "col") / pixel_total
+    gram = all_sum(all_sum(gram_local, "row"), "col", alone_low=True) / pixel_total
     factor = jnp.linalg.cholesky(gram)
     inverse = jax.scipy.linalg.solve_triangular(
         factor, jnp.eye(vectors, dtype=jnp.float32), lower=True

time: 149 us -> 151 us (1.013)
  starting transfers between devices: 45.3 us -> 47.5 us
    ppermute x12 -> x11, starting transfers between devices: 23.9 us -> 26.1 us  [exchange_sum(): received.append(lax.ppermute(block, axis, route))]
    ppermute x12 -> x11, waiting for transfers between devices: 18.9 us -> 18.7 us  [exchange_sum(): received.append(lax.ppermute(block, axis, route))]
  transfers between devices with their start and end apart: 20 -> 19, of which waited for: 11 -> 11; matrix products, arithmetic and copies ran while one was open for 5% -> 5% of each run, Pallas kernels for 0% -> 0%
where the time goes in v14:
time: 151 us; the launch traced here: 148 us
  other arithmetic  50.8 us (34%)
  starting transfers between devices  47.5 us (31%)
  waiting for transfers between devices  24.2 us (16%)
  matrix products  13.1 us (9%)
  local copies, waits for them, and re-layouts  11.7 us (8%)
    ppermute x11, starting transfers between devices, exchange_sum(): received.append(lax.ppermute(block, axis, route))  26.1 us
    sub x2, other arithmetic, apply_pixels(): return shifted_pixels(values_in, 0, 0) - summed  21.6 us
    ppermute x11, waiting for transfers between devices, exchange_sum(): received.append(lax.ppermute(block, axis, route))  18.7 us
    ppermute x4, starting transfers between devices, padded(): lax.ppermute(tail, axis, [(i, (i + 1) % count) for i in range(ends)])  13.5 us
    another operation x3, other arithmetic, per_device(): factor = jnp.linalg.cholesky(gram)  12.4 us
    unnamed x11, local copies, waits for them, and re-layouts  10.5 us
    another operation x1, other arithmetic, per_device(): jax.scipy.linalg.solve_triangular(factor, jnp.eye(vectors, dtype=jnp.floa...  9.81 us
    ppermute x4, starting transfers between devices, padded(): lax.ppermute(head, axis, [((i + 1) % count, i) for i in range(ends)])  7.79 us
  transfers between devices with their start and end apart: 19, of which 11 were waited for; matrix products, arithmetic and copies ran while one was open for 5% of the time, Pallas kernels for 0%

profile of v14, /device:TPU:2, one launch (start us, length us, event | category | flops | bytes accessed | tf_op | source)
XLA Modules:
  0.0 148.3 jit_solution(342747289194306794)
XLA Ops:
  0.6 0.8 pad_add_fusion.3
  1.4 3.4 %collective-permute-start.4 = (s32[5,3,256]{2,1,0:T(4,128)S(1)}, s32[5,3,256]{2,1,0:T(4,128)S(1)}, u32[]{:S(2)}, u32[]{:S(2)}) collective-permute-start(s32[5,3,256]{2,1,0:T(4,128)S(1)} %get-tuple-element.27), channel_id=1, source_target_pairs={{0,16},{16,32},{32,48},{48,64},{64,80},{80,96},{96,112},{112,128},... | collective-permute-start | bytes 46088 | tf_op jit(solution)/shard_map/ppermute | solution.py:27
  4.8 0.0 copy-start.2
  4.8 0.0 copy-start.3
  4.9 2.6 %collective-permute-start.5 = (s32[5,3,256]{2,1,0:T(4,128)S(1)}, s32[5,3,256]{2,1,0:T(4,128)S(1)}, u32[]{:S(2)}, u32[]{:S(2)}) collective-permute-start(s32[5,3,256]{2,1,0:T(4,128)S(1)} %get-tuple-element.28), channel_id=1, source_target_pairs={{16,0},{32,16},{48,32},{64,48},{80,64},{96,80},{112,96},{128,112},... | collective-permute-start | bytes 46088 | tf_op jit(solution)/shard_map/ppermute | solution.py:29
  7.4 5.3 %copy.15 = f32[128,32,256]{0,2,1:T(8,128)} copy(f32[128,32,256]{2,1,0:T(8,128)} %param.5) | data formatting | bytes 8388608 | tf_op args[2]
  12.7 1.1 fusion.80
  13.8 3.4 %collective-permute-start = (f32[2,256,128]{2,1,0:T(8,128)S(1)}, f32[2,256,128]{2,1,0:T(8,128)S(1)}, u32[]{:S(2)}, u32[]{:S(2)}) collective-permute-start(f32[2,256,128]{2,1,0:T(8,128)S(1)} %get-tuple-element.19), channel_id=1, source_target_pairs={{0,16},{16,32},{32,48},{48,64},{64,80},{80,96},{96,112},{112,128},... | collective-permute-start | bytes 786440 | tf_op jit(solution)/shard_map/ppermute | solution.py:27
  17.2 2.5 %collective-permute-start.1 = (f32[2,256,128]{2,1,0:T(8,128)S(1)}, f32[2,256,128]{2,1,0:T(8,128)S(1)}, u32[]{:S(2)}, u32[]{:S(2)}) collective-permute-start(f32[2,256,128]{2,1,0:T(8,128)S(1)} %get-tuple-element.20), channel_id=1, source_target_pairs={{16,0},{32,16},{48,32},{64,48},{80,64},{96,80},{112,96},{128,112},... | collective-permute-start | bytes 786440 | tf_op jit(solution)/shard_map/ppermute | solution.py:29
  19.7 0.0 copy-start
  19.7 0.0 collective-permute-done.4
  19.7 0.0 collective-permute-done.5
  19.8 0.1 fusion.81
  19.9 1.6 %collective-permute-start.6 = (s32[5,38,3]{2,1,0:T(8,128)S(1)}, s32[5,38,3]{2,1,0:T(8,128)S(1)}, u32[]{:S(2)}, u32[]{:S(2)}) collective-permute-start(s32[5,38,3]{2,1,0:T(8,128)S(1)} %get-tuple-element.25), channel_id=1, source_target_pairs={{0,1},{1,2},{2,3},{3,4},{4,5},{5,6},{6,7},{7,8},{8,9},{9,10},{10,1... | collective-permute-start | bytes 6848 | tf_op jit(solution)/shard_map/ppermute | solution.py:27
  21.5 1.3 collective-permute-start.7
  22.8 0.1 broadcast_multiply_fusion
  22.8 0.0 collective-permute-done.6
  22.8 4.0 %collective-permute-done.7 = s32[5,38,3]{2,1,0:T(8,128)S(1)} collective-permute-done((s32[5,38,3]{2,1,0:T(8,128)S(1)}, s32[5,38,3]{2,1,0:T(8,128)S(1)}, u32[]{:S(2)}, u32[]{:S(2)}) %collective-permute-start.7) | collective-permute-done | bytes 2312 | tf_op jit(solution)/shard_map/ppermute | solution.py:29
  26.8 0.2 pad_add_fusion
  27.1 0.1 fusion.65
  27.2 0.4 add_rsqrt_fusion
  27.5 0.2 slice_multiply_fusion.46
  27.7 0.1 slice_multiply_fusion.28
  27.9 0.3 slice_multiply_fusion.30
  28.2 5.2 %collective-permute-start.2 = (f32[36,2,128]{2,1,0:T(2,128)S(1)}, f32[36,2,128]{2,1,0:T(2,128)S(1)}, u32[]{:S(2)}, u32[]{:S(2)}) collective-permute-start(f32[36,2,128]{2,1,0:T(2,128)S(1)} %get-tuple-element.17), channel_id=1, source_target_pairs={{0,1},{1,2},{2,3},{3,4},{4,5},{5,6},{6,7},{7,8},{8,9},{9,10},{10,1... | collective-permute-start | bytes 110600 | tf_op jit(solution)/shard_map/ppermute | solution.py:27
  33.4 1.5 collective-permute-start.3
  34.9 0.1 slice_multiply_fusion.34
  35.0 0.0 collective-permute-done.2
  35.0 1.5 %collective-permute-done.3 = f32[36,2,128]{2,1,0:T(2,128)S(1)} collective-permute-done((f32[36,2,128]{2,1,0:T(2,128)S(1)}, f32[36,2,128]{2,1,0:T(2,128)S(1)}, u32[]{:S(2)}, u32[]{:S(2)}) %collective-permute-start.3) | collective-permute-done | bytes 36896 | tf_op jit(solution)/shard_map/ppermute | solution.py:29
  36.5 2.3 %maximum_maximum_fusion = (f32[36,258,128]{2,1,0:T(8,128)S(1)}, f32[36,258,128]{2,1,0:T(8,128)S(1)}) fusion(f32[2,256,128]{2,1,0:T(8,128)S(1)} %collective-permute-done.1, f32[32,256,128]{2,1,0:T(8,128)S(1)} %bitcast.37, f32[2,256,128]{2,1,0:T(8,128)S(1)} %collective-permute-done, f32[36,2,128]{2,1,0:T(2,128)S(1)} %collective-permute-done.2, ...), kind=kLoop, calls=%fused_computation.2 | loop fusion | flops 7133184 | bytes 14303232 | tf_op jit(solution)/shard_map/concatenate | solution.py:25
  38.8 1.6 %pad_maximum_fusion = f32[36,260,128]{2,1,0:T(8,128)S(1)} fusion(f32[36,2,128]{2,1,0:T(2,128)S(1)} %collective-permute-done.3, f32[2,256,128]{2,1,0:T(8,128)S(1)} %collective-permute-done.1, f32[32,256,128]{2,1,0:T(8,128)S(1)} %bitcast.38, f32[2,256,128]{2,1,0:T(8,128)S(1)} %collective-permute-done, f32[36,2,128]{2,1,0:T(2,128)S(1)} %collective-permute-done.2), kind=kLoop, calls=%fused_computation | loop fusion | flops 4792320 | bytes 9584640 | tf_op jit(solution)/shard_map/concatenate | solution.py:25
  40.4 11.6 %fusion.1 = f32[34,258,128]{2,1,0:T(8,128)S(1)} fusion(f32[36,258,128]{2,1,0:T(8,128)S(1)} %get-tuple-element.16, f32[36,258,128]{2,1,0:T(8,128)S(1)} %get-tuple-element.15, f32[36,260,128]{2,1,0:T(8,128)S(1)} %pad_maximum_fusion, f32[34,258]{1,0:T(8,128)S(1)} %get-tuple-element.40, f32[34,258]{1,0:T(8,128)S(1)} %get-tuple-element.41, ...), kind=kLoop, calls=%fused_computation.5 | loop fusion | flops 17965056 | bytes 45193344 | tf_op jit(solution)/shard_map/sub | solution.py:101
  52.0 10.1 %fusion.9 = f32[32,256,128]{2,1,0:T(8,128)S(1)} fusion(f32[34,258,128]{2,1,0:T(8,128)S(1)} %fusion.1, f32[32,256]{1,0:T(8,128)S(1)} %get-tuple-element.38, f32[32,256]{1,0:T(8,128)S(1)} %get-tuple-element.37, f32[32,256]{1,0:T(8,128)S(1)} %get-tuple-element.32, f32[32,256]{1,0:T(8,128)S(1)} %get-tuple-element.33, f32[32,256]{1,0:T(8,128)S(1)} %get-tuple-element.34, ...), kind=kLoop, calls=%fused_computation.21 | loop fusion | flops 16777216 | bytes 42205184 | tf_op jit(solution)/shard_map/sub | solution.py:101
  62.1 0.0 copy-start.1
  62.1 6.9 %convolution_bitcast_fusion.1 = f32[128,128]{0,1:T(8,128)S(1)} fusion(f32[32,256,128]{2,1,0:T(8,128)S(1)} %fusion.9), kind=kOutput, calls=%fused_computation.36 | convolution fusion | flops 1610612736 | bytes 4259840 | tf_op jit(solution)/shard_map/rck,rcj->kj/dot_general | solution.py:157
  69.0 3.7 %collective-permute-start.10 = (f32[128,128]{0,1:T(8,128)S(1)}, f32[128,128]{0,1:T(8,128)S(1)}, u32[]{:S(2)}, u32[]{:S(2)}) collective-permute-start(f32[128,128]{0,1:T(8,128)S(1)} %convolution_bitcast_fusion.1), channel_id=1, source_target_pairs={{0,192},{16,208},{32,224},{48,240},{64,128},{80,144},{96,160},{112... | collective-permute-start | bytes 196616 | tf_op jit(solution)/shard_map/ppermute | solution.py:110
  72.7 0.1 collective-permute-start.8
  72.9 1.4 collective-permute-start.9
  74.3 0.7 collective-permute-done.10
  75.0 2.0 %collective-permute-done.8 = f32[128,128]{0,1:T(8,128)S(1)} collective-permute-done((f32[128,128]{0,1:T(8,128)S(1)}, f32[128,128]{0,1:T(8,128)S(1)}, u32[]{:S(2)}, u32[]{:S(2)}) %collective-permute-start.8) | collective-permute-done | bytes 65568 | tf_op jit(solution)/shard_map/ppermute | solution.py:110
  77.0 1.7 %collective-permute-done.9 = f32[128,128]{0,1:T(8,128)S(1)} collective-permute-done((f32[128,128]{0,1:T(8,128)S(1)}, f32[128,128]{0,1:T(8,128)S(1)}, u32[]{:S(2)}, u32[]{:S(2)}) %collective-permute-start.9) | collective-permute-done | bytes 65568 | tf_op jit(solution)/shard_map/ppermute | solution.py:110
  78.8 4.4 %collective-permute-start.11 = (f32[128,128]{0,1:T(8,128)S(1)}, f32[128,128]{0,1:T(8,128)S(1)}, u32[]{:S(2)}, u32[]{:S(2)}) collective-permute-start(f32[128,128]{0,1:T(8,128)S(1)} %add_add_fusion.2), channel_id=1, source_target_pairs={{0,16},{16,0},{32,48},{48,32},{64,80},{80,64},{96,112},{112,96},{1... | collective-permute-start | bytes 196616 | tf_op jit(solution)/shard_map/ppermute | solution.py:110
  83.2 0.0 collective-permute-start.12
  83.2 1.6 %collective-permute-start.13 = (f32[128,128]{0,1:T(8,128)S(1)}, f32[128,128]{0,1:T(8,128)S(1)}, u32[]{:S(2)}, u32[]{:S(2)}) collective-permute-start(f32[128,128]{0,1:T(8,128)S(1)} %add_add_fusion.2), channel_id=1, source_target_pairs={{0,48},{16,32},{32,16},{48,0},{64,112},{80,96},{96,80},{112,64},{1... | collective-permute-start | bytes 196616 | tf_op jit(solution)/shard_map/ppermute | solution.py:110
  84.8 1.3 collective-permute-done.11
  86.0 3.2 %collective-permute-done.12 = f32[128,128]{0,1:T(8,128)S(1)} collective-permute-done((f32[128,128]{0,1:T(8,128)S(1)}, f32[128,128]{0,1:T(8,128)S(1)}, u32[]{:S(2)}, u32[]{:S(2)}) %collective-permute-start.12) | collective-permute-done | bytes 65568 | tf_op jit(solution)/shard_map/ppermute | solution.py:110
  89.2 0.0 collective-permute-done.13
  89.3 9.5 %collective-permute-start.14 = (f32[128,128]{0,1:T(8,128)S(1)}, f32[128,128]{0,1:T(8,128)S(1)}, u32[]{:S(2)}, u32[]{:S(2)}) collective-permute-start(f32[128,128]{0,1:T(8,128)S(1)} %add_add_fusion.1), channel_id=1, source_target_pairs={{0,8},{1,9},{2,10},{3,11},{4,12},{5,13},{6,14},{7,15},{8,0},{9,1},... | collective-permute-start | bytes 196616 | tf_op jit(solution)/shard_map/ppermute | solution.py:110
  98.7 2.5 %collective-permute-done.14 = f32[128,128]{0,1:T(8,128)S(1)} collective-permute-done((f32[128,128]{0,1:T(8,128)S(1)}, f32[128,128]{0,1:T(8,128)S(1)}, u32[]{:S(2)}, u32[]{:S(2)}) %collective-permute-start.14) | collective-permute-done | bytes 65568 | tf_op jit(solution)/shard_map/ppermute | solution.py:110
  101.3 0.1 collective-permute-start.15
  101.4 5.2 %collective-permute-start.16 = (f32[128,128]{0,1:T(8,128)S(1)}, f32[128,128]{0,1:T(8,128)S(1)}, u32[]{:S(2)}, u32[]{:S(2)}) collective-permute-start(f32[128,128]{0,1:T(8,128)S(1)} %add.219), channel_id=1, source_target_pairs={{0,4},{1,5},{2,6},{3,7},{4,0},{5,1},{6,2},{7,3},{8,12},{9,13},{10,... | collective-permute-start | bytes 196616 | tf_op jit(solution)/shard_map/ppermute | solution.py:110
  106.6 3.6 %collective-permute-done.16 = f32[128,128]{0,1:T(8,128)S(1)} collective-permute-done((f32[128,128]{0,1:T(8,128)S(1)}, f32[128,128]{0,1:T(8,128)S(1)}, u32[]{:S(2)}, u32[]{:S(2)}) %collective-permute-start.16) | collective-permute-done | bytes 65568 | tf_op jit(solution)/shard_map/ppermute | solution.py:110
  110.2 2.4 %collective-permute-done.17 = f32[128,128]{0,1:T(8,128)S(1)} collective-permute-done((f32[128,128]{0,1:T(8,128)S(1)}, f32[128,128]{0,1:T(8,128)S(1)}, u32[]{:S(2)}, u32[]{:S(2)}) %collective-permute-start.17) | collective-permute-done | bytes 65568 | tf_op jit(solution)/shard_map/ppermute | solution.py:110
  112.6 0.1 collective-permute-start.18
  112.7 1.2 collective-permute-done.18
  114.0 0.1 copy.21
  114.1 11.7 %cholesky.17 = f32[128,128]{1,0:T(8,128)S(1)} custom-call(f32[128,128]{1,0:T(8,128)S(1)} %fusion.17), custom_call_target="Cholesky" | custom-call | tf_op jit(solution)/shard_map/jit(cholesky)/cholesky | solution.py:162
  125.9 0.6 compare_reduce_fusion
  126.5 0.7 fusion.67
  127.2 9.8 %custom-call.7 = f32[1,128,128]{1,2,0:T(8,128)S(1)} custom-call(f32[1,128,128]{2,1,0:T(8,128)S(1)} %get-tuple-element.30), custom_call_target="InvertDiagBlocksLowerTriangular" | custom-call | tf_op jit(solution)/shard_map/jit(_solve_triangular)/triangular_solve | solution.py:163
  137.0 0.2 convolution_bitcast_fusion
  137.2 5.9 %fusion.82 = f32[128,32,256]{2,0,1:T(8,128)S(1)} fusion(f32[128,128,1]{1,0,2:T(8,128)S(1)} %convolution_bitcast_fusion, f32[32,256,128]{2,1,0:T(8,128)} %copy-done.1), kind=kOutput, calls=%fused_computation.179 | convolution fusion | flops 1610612736 | bytes 8454144 | tf_op jit(solution)/shard_map/kj,rcj->krc/dot_general | solution.py:166
  143.1 4.4 %copy.22 = f32[128,32,256]{2,1,0:T(8,128)} copy(f32[128,32,256]{2,0,1:T(8,128)S(1)} %fusion.82) | data formatting | bytes 8388608
  147.5 0.7 copy.23
  (21 shorter events, 0.2 us)
Async XLA Ops:
  1.4 18.3 %collective-permute-start.4 = (s32[5,3,256]{2,1,0:T(4,128)S(1)}, s32[5,3,256]{2,1,0:T(4,128)S(1)}, u32[]{:S(2)}, u32[]{:S(2)}) collective-permute-start(s32[5,3,256]{2,1,0:T(4,128)S(1)} %get-tuple-element.27), channel_id=1, source_target_pairs={{0,16},{16,32},{32,48},{48,64},{64,80},{80,96},{96,112},{112,128},... | collective-permute-start | bytes 46088 | tf_op jit(solution)/shard_map/ppermute | solution.py:27
  4.8 14.9 %copy-start.2 = (s32[4,32,256]{2,1,0:T(8,128)S(1)}, s32[4,32,256]{2,1,0:T(8,128)}, u32[]{:S(2)}) copy-start(s32[4,32,256]{2,1,0:T(8,128)} %param.4) | copy-start | bytes 393220
  4.8 14.9 %copy-start.3 = (s32[32,256]{1,0:T(8,128)S(1)}, s32[32,256]{1,0:T(8,128)}, u32[]{:S(2)}) copy-start(s32[32,256]{1,0:T(8,128)} %param.3) | copy-start | bytes 98308
  4.9 14.9 %collective-permute-start.5 = (s32[5,3,256]{2,1,0:T(4,128)S(1)}, s32[5,3,256]{2,1,0:T(4,128)S(1)}, u32[]{:S(2)}, u32[]{:S(2)}) collective-permute-start(s32[5,3,256]{2,1,0:T(4,128)S(1)} %get-tuple-element.28), channel_id=1, source_target_pairs={{16,0},{32,16},{48,32},{64,48},{80,64},{96,80},{112,96},{128,112},... | collective-permute-start | bytes 46088 | tf_op jit(solution)/shard_map/ppermute | solution.py:29
  13.8 14.3 %collective-permute-start = (f32[2,256,128]{2,1,0:T(8,128)S(1)}, f32[2,256,128]{2,1,0:T(8,128)S(1)}, u32[]{:S(2)}, u32[]{:S(2)}) collective-permute-start(f32[2,256,128]{2,1,0:T(8,128)S(1)} %get-tuple-element.19), channel_id=1, source_target_pairs={{0,16},{16,32},{32,48},{48,64},{64,80},{80,96},{96,112},{112,128},... | collective-permute-start | bytes 786440 | tf_op jit(solution)/shard_map/ppermute | solution.py:27
  17.2 10.9 %collective-permute-start.1 = (f32[2,256,128]{2,1,0:T(8,128)S(1)}, f32[2,256,128]{2,1,0:T(8,128)S(1)}, u32[]{:S(2)}, u32[]{:S(2)}) collective-permute-start(f32[2,256,128]{2,1,0:T(8,128)S(1)} %get-tuple-element.20), channel_id=1, source_target_pairs={{16,0},{32,16},{48,32},{64,48},{80,64},{96,80},{112,96},{128,112},... | collective-permute-start | bytes 786440 | tf_op jit(solution)/shard_map/ppermute | solution.py:29
  19.7 8.5 %copy-start = (f32[128,32,256]{0,2,1:T(8,128)S(1)}, f32[128,32,256]{0,2,1:T(8,128)}, u32[]{:S(2)}) copy-start(f32[128,32,256]{0,2,1:T(8,128)} %copy.15) | copy-start | bytes 12582916
  19.9 2.9 %collective-permute-start.6 = (s32[5,38,3]{2,1,0:T(8,128)S(1)}, s32[5,38,3]{2,1,0:T(8,128)S(1)}, u32[]{:S(2)}, u32[]{:S(2)}) collective-permute-start(s32[5,38,3]{2,1,0:T(8,128)S(1)} %get-tuple-element.25), channel_id=1, source_target_pairs={{0,1},{1,2},{2,3},{3,4},{4,5},{5,6},{6,7},{7,8},{8,9},{9,10},{10,1... | collective-permute-start | bytes 6848 | tf_op jit(solution)/shard_map/ppermute | solution.py:27
  21.5 5.3 %collective-permute-start.7 = (s32[5,38,3]{2,1,0:T(8,128)S(1)}, s32[5,38,3]{2,1,0:T(8,128)S(1)}, u32[]{:S(2)}, u32[]{:S(2)}) collective-permute-start(s32[5,38,3]{2,1,0:T(8,128)S(1)} %get-tuple-element.26), channel_id=1, source_target_pairs={{1,0},{2,1},{3,2},{4,3},{5,4},{6,5},{7,6},{8,7},{9,8},{10,9},{11,1... | collective-permute-start | bytes 6848 | tf_op jit(solution)/shard_map/ppermute | solution.py:29
  28.2 6.8 %collective-permute-start.2 = (f32[36,2,128]{2,1,0:T(2,128)S(1)}, f32[36,2,128]{2,1,0:T(2,128)S(1)}, u32[]{:S(2)}, u32[]{:S(2)}) collective-permute-start(f32[36,2,128]{2,1,0:T(2,128)S(1)} %get-tuple-element.17), channel_id=1, source_target_pairs={{0,1},{1,2},{2,3},{3,4},{4,5},{5,6},{6,7},{7,8},{8,9},{9,10},{10,1... | collective-permute-start | bytes 110600 | tf_op jit(solution)/shard_map/ppermute | solution.py:27
  33.4 3.1 %collective-permute-start.3 = (f32[36,2,128]{2,1,0:T(2,128)S(1)}, f32[36,2,128]{2,1,0:T(2,128)S(1)}, u32[]{:S(2)}, u32[]{:S(2)}) collective-permute-start(f32[36,2,128]{2,1,0:T(2,128)S(1)} %get-tuple-element.18), channel_id=1, source_target_pairs={{1,0},{2,1},{3,2},{4,3},{5,4},{6,5},{7,6},{8,7},{9,8},{10,9},{11,1... | collective-permute-start | bytes 110600 | tf_op jit(solution)/shard_map/ppermute | solution.py:29
  62.1 39.2 %copy-start.1 = (f32[32,256,128]{2,1,0:T(8,128)}, f32[32,256,128]{2,1,0:T(8,128)S(1)}, u32[]{:S(2)}) copy-start(f32[32,256,128]{2,1,0:T(8,128)S(1)} %fusion.9) | copy-start | bytes 12582916
  69.0 6.0 %collective-permute-start.10 = (f32[128,128]{0,1:T(8,128)S(1)}, f32[128,128]{0,1:T(8,128)S(1)}, u32[]{:S(2)}, u32[]{:S(2)}) collective-permute-start(f32[128,128]{0,1:T(8,128)S(1)} %convolution_bitcast_fusion.1), channel_id=1, source_target_pairs={{0,192},{16,208},{32,224},{48,240},{64,128},{80,144},{96,160},{112... | collective-permute-start | bytes 196616 | tf_op jit(solution)/shard_map/ppermute | solution.py:110
  72.7 4.3 %collective-permute-start.8 = (f32[128,128]{0,1:T(8,128)S(1)}, f32[128,128]{0,1:T(8,128)S(1)}, u32[]{:S(2)}, u32[]{:S(2)}) collective-permute-start(f32[128,128]{0,1:T(8,128)S(1)} %convolution_bitcast_fusion.1), channel_id=1, source_target_pairs={{0,64},{16,80},{32,96},{48,112},{64,0},{80,16},{96,32},{112,48},{1... | collective-permute-start | bytes 196616 | tf_op jit(solution)/shard_map/ppermute | solution.py:110
  72.9 5.9 %collective-permute-start.9 = (f32[128,128]{0,1:T(8,128)S(1)}, f32[128,128]{0,1:T(8,128)S(1)}, u32[]{:S(2)}, u32[]{:S(2)}) collective-permute-start(f32[128,128]{0,1:T(8,128)S(1)} %convolution_bitcast_fusion.1), channel_id=1, source_target_pairs={{0,128},{16,144},{32,160},{48,176},{64,192},{80,208},{96,224},{112... | collective-permute-start | bytes 196616 | tf_op jit(solution)/shard_map/ppermute | solution.py:110
  78.8 7.3 %collective-permute-start.11 = (f32[128,128]{0,1:T(8,128)S(1)}, f32[128,128]{0,1:T(8,128)S(1)}, u32[]{:S(2)}, u32[]{:S(2)}) collective-permute-start(f32[128,128]{0,1:T(8,128)S(1)} %add_add_fusion.2), channel_id=1, source_target_pairs={{0,16},{16,0},{32,48},{48,32},{64,80},{80,64},{96,112},{112,96},{1... | collective-permute-start | bytes 196616 | tf_op jit(solution)/shard_map/ppermute | solution.py:110
  83.2 6.0 %collective-permute-start.12 = (f32[128,128]{0,1:T(8,128)S(1)}, f32[128,128]{0,1:T(8,128)S(1)}, u32[]{:S(2)}, u32[]{:S(2)}) collective-permute-start(f32[128,128]{0,1:T(8,128)S(1)} %add_add_fusion.2), channel_id=1, source_target_pairs={{0,32},{16,48},{32,0},{48,16},{64,96},{80,112},{96,64},{112,80},{1... | collective-permute-start | bytes 196616 | tf_op jit(solution)/shard_map/ppermute | solution.py:110
  83.2 6.0 %collective-permute-start.13 = (f32[128,128]{0,1:T(8,128)S(1)}, f32[128,128]{0,1:T(8,128)S(1)}, u32[]{:S(2)}, u32[]{:S(2)}) collective-permute-start(f32[128,128]{0,1:T(8,128)S(1)} %add_add_fusion.2), channel_id=1, source_target_pairs={{0,48},{16,32},{32,16},{48,0},{64,112},{80,96},{96,80},{112,64},{1... | collective-permute-start | bytes 196616 | tf_op jit(solution)/shard_map/ppermute | solution.py:110
  89.3 12.0 %collective-permute-start.14 = (f32[128,128]{0,1:T(8,128)S(1)}, f32[128,128]{0,1:T(8,128)S(1)}, u32[]{:S(2)}, u32[]{:S(2)}) collective-permute-start(f32[128,128]{0,1:T(8,128)S(1)} %add_add_fusion.1), channel_id=1, source_target_pairs={{0,8},{1,9},{2,10},{3,11},{4,12},{5,13},{6,14},{7,15},{8,0},{9,1},... | collective-permute-start | bytes 196616 | tf_op jit(solution)/shard_map/ppermute | solution.py:110
  101.3 5.3 %collective-permute-start.15 = (f32[128,128]{0,1:T(8,128)S(1)}, f32[128,128]{0,1:T(8,128)S(1)}, u32[]{:S(2)}, u32[]{:S(2)}) collective-permute-start(f32[128,128]{0,1:T(8,128)S(1)} %add.219), channel_id=1, source_target_pairs={{0,2},{1,3},{2,0},{3,1},{4,6},{5,7},{6,4},{7,5},{8,10},{9,11},{10,... | collective-permute-start | bytes 196616 | tf_op jit(solution)/shard_map/ppermute | solution.py:110
  101.4 8.8 %collective-permute-start.16 = (f32[128,128]{0,1:T(8,128)S(1)}, f32[128,128]{0,1:T(8,128)S(1)}, u32[]{:S(2)}, u32[]{:S(2)}) collective-permute-start(f32[128,128]{0,1:T(8,128)S(1)} %add.219), channel_id=1, source_target_pairs={{0,4},{1,5},{2,6},{3,7},{4,0},{5,1},{6,2},{7,3},{8,12},{9,13},{10,... | collective-permute-start | bytes 196616 | tf_op jit(solution)/shard_map/ppermute | solution.py:110
  106.6 6.1 %collective-permute-start.17 = (f32[128,128]{0,1:T(8,128)S(1)}, f32[128,128]{0,1:T(8,128)S(1)}, u32[]{:S(2)}, u32[]{:S(2)}) collective-permute-start(f32[128,128]{0,1:T(8,128)S(1)} %add.219), channel_id=1, source_target_pairs={{0,6},{1,7},{2,4},{3,5},{4,2},{5,3},{6,0},{7,1},{8,14},{9,15},{10,... | collective-permute-start | bytes 196616 | tf_op jit(solution)/shard_map/ppermute | solution.py:110
  112.6 1.3 collective-permute-start.18

commit v15 on v12

--- a/solution.py
+++ b/solution.py
@@ -156,7 +156,7 @@
         "rck,rcj->kj", filtered, filtered,
         precision=lax.Precision.HIGHEST, preferred_element_type=jnp.float32,
     )
-    gram = all_sum(all_sum(gram_local, "row"), "col") / pixel_total
+    gram = all_sum(all_sum(gram_local, "col"), "row") / pixel_total
     factor = jnp.linalg.cholesky(gram)
     inverse = jax.scipy.linalg.solve_triangular(
         factor, jnp.eye(vectors, dtype=jnp.float32), lower=True

time: 149 us -> 150 us (level)
  waiting for transfers between devices: 24.4 us -> 27.3 us
    ppermute x12, waiting for transfers between devices: 18.9 us -> 21.8 us  [exchange_sum(): received.append(lax.ppermute(block, axis, route))]
  transfers between devices with their start and end apart: 20 -> 20, of which waited for: 11 -> 10; matrix products, arithmetic and copies ran while one was open for 5% -> 5% of each run, Pallas kernels for 0% -> 0%
where the time goes in v15:
time: 150 us; the launch traced here: 149 us
  other arithmetic  50.8 us (34%)
  starting transfers between devices  44.9 us (30%)
  waiting for transfers between devices  27.3 us (18%)
  matrix products  13.1 us (9%)
  local copies, waits for them, and re-layouts  11.7 us (8%)
    ppermute x12, starting transfers between devices, exchange_sum(): received.append(lax.ppermute(block, axis, route))  23.5 us
    ppermute x12, waiting for transfers between devices, exchange_sum(): received.append(lax.ppermute(block, axis, route))  21.8 us
    sub x2, other arithmetic, apply_pixels(): return shifted_pixels(values_in, 0, 0) - summed  21.6 us
    ppermute x4, starting transfers between devices, padded(): lax.ppermute(tail, axis, [(i, (i + 1) % count) for i in range(ends)])  13.5 us
    another operation x3, other arithmetic, per_device(): factor = jnp.linalg.cholesky(gram)  12.4 us
    unnamed x11, local copies, waits for them, and re-layouts  10.5 us
    another operation x1, other arithmetic, per_device(): jax.scipy.linalg.solve_triangular(factor, jnp.eye(vectors, dtype=jnp.floa...  9.81 us
    ppermute x4, starting transfers between devices, padded(): lax.ppermute(head, axis, [((i + 1) % count, i) for i in range(ends)])  7.79 us
  transfers between devices with their start and end apart: 20, of which 10 were waited for; matrix products, arithmetic and copies ran while one was open for 5% of the time, Pallas kernels for 0%

profile of v15, /device:TPU:2, one launch (start us, length us, event | category | flops | bytes accessed | tf_op | source)
XLA Modules:
  0.0 148.7 jit_solution(10017432131316838107)
XLA Ops:
  0.6 0.8 pad_add_fusion.3
  1.4 3.4 %collective-permute-start.4 = (s32[5,3,256]{2,1,0:T(4,128)S(1)}, s32[5,3,256]{2,1,0:T(4,128)S(1)}, u32[]{:S(2)}, u32[]{:S(2)}) collective-permute-start(s32[5,3,256]{2,1,0:T(4,128)S(1)} %get-tuple-element.27), channel_id=1, source_target_pairs={{0,16},{16,32},{32,48},{48,64},{64,80},{80,96},{96,112},{112,128},... | collective-permute-start | bytes 46088 | tf_op jit(solution)/shard_map/ppermute | solution.py:27
  4.8 0.0 copy-start.2
  4.8 0.0 copy-start.3
  4.9 2.6 %collective-permute-start.5 = (s32[5,3,256]{2,1,0:T(4,128)S(1)}, s32[5,3,256]{2,1,0:T(4,128)S(1)}, u32[]{:S(2)}, u32[]{:S(2)}) collective-permute-start(s32[5,3,256]{2,1,0:T(4,128)S(1)} %get-tuple-element.28), channel_id=1, source_target_pairs={{16,0},{32,16},{48,32},{64,48},{80,64},{96,80},{112,96},{128,112},... | collective-permute-start | bytes 46088 | tf_op jit(solution)/shard_map/ppermute | solution.py:29
  7.4 5.3 %copy.15 = f32[128,32,256]{0,2,1:T(8,128)} copy(f32[128,32,256]{2,1,0:T(8,128)} %param.5) | data formatting | bytes 8388608 | tf_op args[2]
  12.7 1.1 fusion.80
  13.8 3.4 %collective-permute-start = (f32[2,256,128]{2,1,0:T(8,128)S(1)}, f32[2,256,128]{2,1,0:T(8,128)S(1)}, u32[]{:S(2)}, u32[]{:S(2)}) collective-permute-start(f32[2,256,128]{2,1,0:T(8,128)S(1)} %get-tuple-element.19), channel_id=1, source_target_pairs={{0,16},{16,32},{32,48},{48,64},{64,80},{80,96},{96,112},{112,128},... | collective-permute-start | bytes 786440 | tf_op jit(solution)/shard_map/ppermute | solution.py:27
  17.2 2.5 %collective-permute-start.1 = (f32[2,256,128]{2,1,0:T(8,128)S(1)}, f32[2,256,128]{2,1,0:T(8,128)S(1)}, u32[]{:S(2)}, u32[]{:S(2)}) collective-permute-start(f32[2,256,128]{2,1,0:T(8,128)S(1)} %get-tuple-element.20), channel_id=1, source_target_pairs={{16,0},{32,16},{48,32},{64,48},{80,64},{96,80},{112,96},{128,112},... | collective-permute-start | bytes 786440 | tf_op jit(solution)/shard_map/ppermute | solution.py:29
  19.7 0.0 copy-start
  19.7 0.0 collective-permute-done.4
  19.7 0.0 collective-permute-done.5
  19.8 0.1 fusion.81
  19.9 1.6 %collective-permute-start.6 = (s32[5,38,3]{2,1,0:T(8,128)S(1)}, s32[5,38,3]{2,1,0:T(8,128)S(1)}, u32[]{:S(2)}, u32[]{:S(2)}) collective-permute-start(s32[5,38,3]{2,1,0:T(8,128)S(1)} %get-tuple-element.25), channel_id=1, source_target_pairs={{0,1},{1,2},{2,3},{3,4},{4,5},{5,6},{6,7},{7,8},{8,9},{9,10},{10,1... | collective-permute-start | bytes 6848 | tf_op jit(solution)/shard_map/ppermute | solution.py:27
  21.5 1.3 collective-permute-start.7
  22.8 0.1 broadcast_multiply_fusion
  22.8 0.0 collective-permute-done.6
  22.8 4.0 %collective-permute-done.7 = s32[5,38,3]{2,1,0:T(8,128)S(1)} collective-permute-done((s32[5,38,3]{2,1,0:T(8,128)S(1)}, s32[5,38,3]{2,1,0:T(8,128)S(1)}, u32[]{:S(2)}, u32[]{:S(2)}) %collective-permute-start.7) | collective-permute-done | bytes 2312 | tf_op jit(solution)/shard_map/ppermute | solution.py:29
  26.8 0.2 pad_add_fusion
  27.1 0.1 fusion.65
  27.2 0.4 add_rsqrt_fusion
  27.5 0.2 slice_multiply_fusion.46
  27.7 0.1 slice_multiply_fusion.28
  27.9 0.3 slice_multiply_fusion.30
  28.1 0.0 collective-permute-done
  28.2 5.2 %collective-permute-start.2 = (f32[36,2,128]{2,1,0:T(2,128)S(1)}, f32[36,2,128]{2,1,0:T(2,128)S(1)}, u32[]{:S(2)}, u32[]{:S(2)}) collective-permute-start(f32[36,2,128]{2,1,0:T(2,128)S(1)} %get-tuple-element.17), channel_id=1, source_target_pairs={{0,1},{1,2},{2,3},{3,4},{4,5},{5,6},{6,7},{7,8},{8,9},{9,10},{10,1... | collective-permute-start | bytes 110600 | tf_op jit(solution)/shard_map/ppermute | solution.py:27
  33.4 1.5 collective-permute-start.3
  34.9 0.1 slice_multiply_fusion.34
  35.0 0.0 collective-permute-done.2
  35.0 1.5 %collective-permute-done.3 = f32[36,2,128]{2,1,0:T(2,128)S(1)} collective-permute-done((f32[36,2,128]{2,1,0:T(2,128)S(1)}, f32[36,2,128]{2,1,0:T(2,128)S(1)}, u32[]{:S(2)}, u32[]{:S(2)}) %collective-permute-start.3) | collective-permute-done | bytes 36896 | tf_op jit(solution)/shard_map/ppermute | solution.py:29
  36.5 2.3 %maximum_maximum_fusion = (f32[36,258,128]{2,1,0:T(8,128)S(1)}, f32[36,258,128]{2,1,0:T(8,128)S(1)}) fusion(f32[2,256,128]{2,1,0:T(8,128)S(1)} %collective-permute-done.1, f32[32,256,128]{2,1,0:T(8,128)S(1)} %bitcast.37, f32[2,256,128]{2,1,0:T(8,128)S(1)} %collective-permute-done, f32[36,2,128]{2,1,0:T(2,128)S(1)} %collective-permute-done.2, ...), kind=kLoop, calls=%fused_computation.2 | loop fusion | flops 7133184 | bytes 14303232 | tf_op jit(solution)/shard_map/concatenate | solution.py:25
  38.8 1.6 %pad_maximum_fusion = f32[36,260,128]{2,1,0:T(8,128)S(1)} fusion(f32[36,2,128]{2,1,0:T(2,128)S(1)} %collective-permute-done.3, f32[2,256,128]{2,1,0:T(8,128)S(1)} %collective-permute-done.1, f32[32,256,128]{2,1,0:T(8,128)S(1)} %bitcast.38, f32[2,256,128]{2,1,0:T(8,128)S(1)} %collective-permute-done, f32[36,2,128]{2,1,0:T(2,128)S(1)} %collective-permute-done.2), kind=kLoop, calls=%fused_computation | loop fusion | flops 4792320 | bytes 9584640 | tf_op jit(solution)/shard_map/concatenate | solution.py:25
  40.4 11.6 %fusion.1 = f32[34,258,128]{2,1,0:T(8,128)S(1)} fusion(f32[36,258,128]{2,1,0:T(8,128)S(1)} %get-tuple-element.16, f32[36,258,128]{2,1,0:T(8,128)S(1)} %get-tuple-element.15, f32[36,260,128]{2,1,0:T(8,128)S(1)} %pad_maximum_fusion, f32[34,258]{1,0:T(8,128)S(1)} %get-tuple-element.40, f32[34,258]{1,0:T(8,128)S(1)} %get-tuple-element.41, ...), kind=kLoop, calls=%fused_computation.5 | loop fusion | flops 17965056 | bytes 45193344 | tf_op jit(solution)/shard_map/sub | solution.py:101
  52.0 10.1 %fusion.9 = f32[32,256,128]{2,1,0:T(8,128)S(1)} fusion(f32[34,258,128]{2,1,0:T(8,128)S(1)} %fusion.1, f32[32,256]{1,0:T(8,128)S(1)} %get-tuple-element.38, f32[32,256]{1,0:T(8,128)S(1)} %get-tuple-element.37, f32[32,256]{1,0:T(8,128)S(1)} %get-tuple-element.32, f32[32,256]{1,0:T(8,128)S(1)} %get-tuple-element.33, f32[32,256]{1,0:T(8,128)S(1)} %get-tuple-element.34, ...), kind=kLoop, calls=%fused_computation.21 | loop fusion | flops 16777216 | bytes 42205184 | tf_op jit(solution)/shard_map/sub | solution.py:101
  62.1 0.0 copy-start.1
  62.1 6.9 %convolution_bitcast_fusion.1 = f32[128,128]{0,1:T(8,128)S(1)} fusion(f32[32,256,128]{2,1,0:T(8,128)S(1)} %fusion.9), kind=kOutput, calls=%fused_computation.36 | convolution fusion | flops 1610612736 | bytes 4259840 | tf_op jit(solution)/shard_map/rck,rcj->kj/dot_general | solution.py:155
  69.0 6.5 %collective-permute-start.10 = (f32[128,128]{0,1:T(8,128)S(1)}, f32[128,128]{0,1:T(8,128)S(1)}, u32[]{:S(2)}, u32[]{:S(2)}) collective-permute-start(f32[128,128]{0,1:T(8,128)S(1)} %convolution_bitcast_fusion.1), channel_id=1, source_target_pairs={{0,12},{1,13},{2,14},{3,15},{4,8},{5,9},{6,10},{7,11},{8,4},{9,5},... | collective-permute-start | bytes 196616 | tf_op jit(solution)/shard_map/ppermute | solution.py:110
  75.6 3.9 %collective-permute-start.8 = (f32[128,128]{0,1:T(8,128)S(1)}, f32[128,128]{0,1:T(8,128)S(1)}, u32[]{:S(2)}, u32[]{:S(2)}) collective-permute-start(f32[128,128]{0,1:T(8,128)S(1)} %convolution_bitcast_fusion.1), channel_id=1, source_target_pairs={{0,4},{1,5},{2,6},{3,7},{4,0},{5,1},{6,2},{7,3},{8,12},{9,13},{10,... | collective-permute-start | bytes 196616 | tf_op jit(solution)/shard_map/ppermute | solution.py:110
  79.4 0.0 collective-permute-start.9
  79.4 3.3 %collective-permute-done.8 = f32[128,128]{0,1:T(8,128)S(1)} collective-permute-done((f32[128,128]{0,1:T(8,128)S(1)}, f32[128,128]{0,1:T(8,128)S(1)}, u32[]{:S(2)}, u32[]{:S(2)}) %collective-permute-start.8) | collective-permute-done | bytes 65568 | tf_op jit(solution)/shard_map/ppermute | solution.py:110
  82.7 5.3 %collective-permute-done.9 = f32[128,128]{0,1:T(8,128)S(1)} collective-permute-done((f32[128,128]{0,1:T(8,128)S(1)}, f32[128,128]{0,1:T(8,128)S(1)}, u32[]{:S(2)}, u32[]{:S(2)}) %collective-permute-start.9) | collective-permute-done | bytes 65568 | tf_op jit(solution)/shard_map/ppermute | solution.py:110
  88.1 0.3 collective-permute-start.11
  88.4 0.1 collective-permute-start.12
  88.5 1.7 %collective-permute-start.13 = (f32[128,128]{0,1:T(8,128)S(1)}, f32[128,128]{0,1:T(8,128)S(1)}, u32[]{:S(2)}, u32[]{:S(2)}) collective-permute-start(f32[128,128]{0,1:T(8,128)S(1)} %add_add_fusion.2), channel_id=1, source_target_pairs={{0,3},{1,2},{2,1},{3,0},{4,7},{5,6},{6,5},{7,4},{8,11},{9,10},{10,... | collective-permute-start | bytes 196616 | tf_op jit(solution)/shard_map/ppermute | solution.py:110
  90.2 3.2 %collective-permute-done.12 = f32[128,128]{0,1:T(8,128)S(1)} collective-permute-done((f32[128,128]{0,1:T(8,128)S(1)}, f32[128,128]{0,1:T(8,128)S(1)}, u32[]{:S(2)}, u32[]{:S(2)}) %collective-permute-start.12) | collective-permute-done | bytes 65568 | tf_op jit(solution)/shard_map/ppermute | solution.py:110
  93.4 0.3 collective-permute-done.13
  93.7 2.3 %collective-permute-start.14 = (f32[128,128]{0,1:T(8,128)S(1)}, f32[128,128]{0,1:T(8,128)S(1)}, u32[]{:S(2)}, u32[]{:S(2)}) collective-permute-start(f32[128,128]{0,1:T(8,128)S(1)} %add_add_fusion.1), channel_id=1, source_target_pairs={{0,64},{16,80},{32,96},{48,112},{64,0},{80,16},{96,32},{112,48},{1... | collective-permute-start | bytes 196616 | tf_op jit(solution)/shard_map/ppermute | solution.py:110
  96.0 2.9 %collective-permute-start.15 = (f32[128,128]{0,1:T(8,128)S(1)}, f32[128,128]{0,1:T(8,128)S(1)}, u32[]{:S(2)}, u32[]{:S(2)}) collective-permute-start(f32[128,128]{0,1:T(8,128)S(1)} %add_add_fusion.1), channel_id=1, source_target_pairs={{0,128},{16,144},{32,160},{48,176},{64,192},{80,208},{96,224},{112... | collective-permute-start | bytes 196616 | tf_op jit(solution)/shard_map/ppermute | solution.py:110
  98.9 3.8 %collective-permute-done.15 = f32[128,128]{0,1:T(8,128)S(1)} collective-permute-done((f32[128,128]{0,1:T(8,128)S(1)}, f32[128,128]{0,1:T(8,128)S(1)}, u32[]{:S(2)}, u32[]{:S(2)}) %collective-permute-start.15) | collective-permute-done | bytes 65568 | tf_op jit(solution)/shard_map/ppermute | solution.py:110
  102.7 1.7 %collective-permute-done.16 = f32[128,128]{0,1:T(8,128)S(1)} collective-permute-done((f32[128,128]{0,1:T(8,128)S(1)}, f32[128,128]{0,1:T(8,128)S(1)}, u32[]{:S(2)}, u32[]{:S(2)}) %collective-permute-start.16) | collective-permute-done | bytes 65568 | tf_op jit(solution)/shard_map/ppermute | solution.py:110
  104.4 4.2 %collective-permute-start.17 = (f32[128,128]{0,1:T(8,128)S(1)}, f32[128,128]{0,1:T(8,128)S(1)}, u32[]{:S(2)}, u32[]{:S(2)}) collective-permute-start(f32[128,128]{0,1:T(8,128)S(1)} %add_add_fusion), channel_id=1, source_target_pairs={{0,16},{16,0},{32,48},{48,32},{64,80},{80,64},{96,112},{112,96},{1... | collective-permute-start | bytes 196616 | tf_op jit(solution)/shard_map/ppermute | solution.py:110
  108.6 1.6 %collective-permute-start.19 = (f32[128,128]{0,1:T(8,128)S(1)}, f32[128,128]{0,1:T(8,128)S(1)}, u32[]{:S(2)}, u32[]{:S(2)}) collective-permute-start(f32[128,128]{0,1:T(8,128)S(1)} %add_add_fusion), channel_id=1, source_target_pairs={{0,48},{16,32},{32,16},{48,0},{64,112},{80,96},{96,80},{112,64},{1... | collective-permute-start | bytes 196616 | tf_op jit(solution)/shard_map/ppermute | solution.py:110
  110.2 0.7 collective-permute-done.17
  110.9 3.5 %collective-permute-done.18 = f32[128,128]{0,1:T(8,128)S(1)} collective-permute-done((f32[128,128]{0,1:T(8,128)S(1)}, f32[128,128]{0,1:T(8,128)S(1)}, u32[]{:S(2)}, u32[]{:S(2)}) %collective-permute-start.18) | collective-permute-done | bytes 65568 | tf_op jit(solution)/shard_map/ppermute | solution.py:110
  114.4 0.0 collective-permute-done.19
  114.4 0.1 copy.21
  114.6 11.7 %cholesky.17 = f32[128,128]{1,0:T(8,128)S(1)} custom-call(f32[128,128]{1,0:T(8,128)S(1)} %fusion.17), custom_call_target="Cholesky" | custom-call | tf_op jit(solution)/shard_map/jit(cholesky)/cholesky | solution.py:160
  126.3 0.6 compare_reduce_fusion
  126.9 0.7 fusion.67
  127.6 9.8 %custom-call.7 = f32[1,128,128]{1,2,0:T(8,128)S(1)} custom-call(f32[1,128,128]{2,1,0:T(8,128)S(1)} %get-tuple-element.30), custom_call_target="InvertDiagBlocksLowerTriangular" | custom-call | tf_op jit(solution)/shard_map/jit(_solve_triangular)/triangular_solve | solution.py:161
  137.4 0.2 convolution_bitcast_fusion
  137.7 5.9 %fusion.82 = f32[128,32,256]{2,0,1:T(8,128)S(1)} fusion(f32[128,128,1]{1,0,2:T(8,128)S(1)} %convolution_bitcast_fusion, f32[32,256,128]{2,1,0:T(8,128)} %copy-done.1), kind=kOutput, calls=%fused_computation.179 | convolution fusion | flops 1610612736 | bytes 8454144 | tf_op jit(solution)/shard_map/kj,rcj->krc/dot_general | solution.py:164
  143.5 4.4 %copy.22 = f32[128,32,256]{2,1,0:T(8,128)} copy(f32[128,32,256]{2,0,1:T(8,128)S(1)} %fusion.82) | data formatting | bytes 8388608
  148.0 0.7 copy.23
  (22 shorter events, 0.2 us)
Async XLA Ops:
  1.4 18.3 %collective-permute-start.4 = (s32[5,3,256]{2,1,0:T(4,128)S(1)}, s32[5,3,256]{2,1,0:T(4,128)S(1)}, u32[]{:S(2)}, u32[]{:S(2)}) collective-permute-start(s32[5,3,256]{2,1,0:T(4,128)S(1)} %get-tuple-element.27), channel_id=1, source_target_pairs={{0,16},{16,32},{32,48},{48,64},{64,80},{80,96},{96,112},{112,128},... | collective-permute-start | bytes 46088 | tf_op jit(solution)/shard_map/ppermute | solution.py:27
  4.8 14.9 %copy-start.2 = (s32[4,32,256]{2,1,0:T(8,128)S(1)}, s32[4,32,256]{2,1,0:T(8,128)}, u32[]{:S(2)}) copy-start(s32[4,32,256]{2,1,0:T(8,128)} %param.4) | copy-start | bytes 393220
  4.8 14.9 %copy-start.3 = (s32[32,256]{1,0:T(8,128)S(1)}, s32[32,256]{1,0:T(8,128)}, u32[]{:S(2)}) copy-start(s32[32,256]{1,0:T(8,128)} %param.3) | copy-start | bytes 98308
  4.9 14.9 %collective-permute-start.5 = (s32[5,3,256]{2,1,0:T(4,128)S(1)}, s32[5,3,256]{2,1,0:T(4,128)S(1)}, u32[]{:S(2)}, u32[]{:S(2)}) collective-permute-start(s32[5,3,256]{2,1,0:T(4,128)S(1)} %get-tuple-element.28), channel_id=1, source_target_pairs={{16,0},{32,16},{48,32},{64,48},{80,64},{96,80},{112,96},{128,112},... | collective-permute-start | bytes 46088 | tf_op jit(solution)/shard_map/ppermute | solution.py:29
  13.8 14.3 %collective-permute-start = (f32[2,256,128]{2,1,0:T(8,128)S(1)}, f32[2,256,128]{2,1,0:T(8,128)S(1)}, u32[]{:S(2)}, u32[]{:S(2)}) collective-permute-start(f32[2,256,128]{2,1,0:T(8,128)S(1)} %get-tuple-element.19), channel_id=1, source_target_pairs={{0,16},{16,32},{32,48},{48,64},{64,80},{80,96},{96,112},{112,128},... | collective-permute-start | bytes 786440 | tf_op jit(solution)/shard_map/ppermute | solution.py:27
  17.2 10.9 %collective-permute-start.1 = (f32[2,256,128]{2,1,0:T(8,128)S(1)}, f32[2,256,128]{2,1,0:T(8,128)S(1)}, u32[]{:S(2)}, u32[]{:S(2)}) collective-permute-start(f32[2,256,128]{2,1,0:T(8,128)S(1)} %get-tuple-element.20), channel_id=1, source_target_pairs={{16,0},{32,16},{48,32},{64,48},{80,64},{96,80},{112,96},{128,112},... | collective-permute-start | bytes 786440 | tf_op jit(solution)/shard_map/ppermute | solution.py:29
  19.7 8.5 %copy-start = (f32[128,32,256]{0,2,1:T(8,128)S(1)}, f32[128,32,256]{0,2,1:T(8,128)}, u32[]{:S(2)}) copy-start(f32[128,32,256]{0,2,1:T(8,128)} %copy.15) | copy-start | bytes 12582916
  19.9 2.9 %collective-permute-start.6 = (s32[5,38,3]{2,1,0:T(8,128)S(1)}, s32[5,38,3]{2,1,0:T(8,128)S(1)}, u32[]{:S(2)}, u32[]{:S(2)}) collective-permute-start(s32[5,38,3]{2,1,0:T(8,128)S(1)} %get-tuple-element.25), channel_id=1, source_target_pairs={{0,1},{1,2},{2,3},{3,4},{4,5},{5,6},{6,7},{7,8},{8,9},{9,10},{10,1... | collective-permute-start | bytes 6848 | tf_op jit(solution)/shard_map/ppermute | solution.py:27
  21.5 5.3 %collective-permute-start.7 = (s32[5,38,3]{2,1,0:T(8,128)S(1)}, s32[5,38,3]{2,1,0:T(8,128)S(1)}, u32[]{:S(2)}, u32[]{:S(2)}) collective-permute-start(s32[5,38,3]{2,1,0:T(8,128)S(1)} %get-tuple-element.26), channel_id=1, source_target_pairs={{1,0},{2,1},{3,2},{4,3},{5,4},{6,5},{7,6},{8,7},{9,8},{10,9},{11,1... | collective-permute-start | bytes 6848 | tf_op jit(solution)/shard_map/ppermute | solution.py:29
  28.2 6.8 %collective-permute-start.2 = (f32[36,2,128]{2,1,0:T(2,128)S(1)}, f32[36,2,128]{2,1,0:T(2,128)S(1)}, u32[]{:S(2)}, u32[]{:S(2)}) collective-permute-start(f32[36,2,128]{2,1,0:T(2,128)S(1)} %get-tuple-element.17), channel_id=1, source_target_pairs={{0,1},{1,2},{2,3},{3,4},{4,5},{5,6},{6,7},{7,8},{8,9},{9,10},{10,1... | collective-permute-start | bytes 110600 | tf_op jit(solution)/shard_map/ppermute | solution.py:27
  33.4 3.1 %collective-permute-start.3 = (f32[36,2,128]{2,1,0:T(2,128)S(1)}, f32[36,2,128]{2,1,0:T(2,128)S(1)}, u32[]{:S(2)}, u32[]{:S(2)}) collective-permute-start(f32[36,2,128]{2,1,0:T(2,128)S(1)} %get-tuple-element.18), channel_id=1, source_target_pairs={{1,0},{2,1},{3,2},{4,3},{5,4},{6,5},{7,6},{8,7},{9,8},{10,9},{11,1... | collective-permute-start | bytes 110600 | tf_op jit(solution)/shard_map/ppermute | solution.py:29
  62.1 42.4 %copy-start.1 = (f32[32,256,128]{2,1,0:T(8,128)}, f32[32,256,128]{2,1,0:T(8,128)S(1)}, u32[]{:S(2)}) copy-start(f32[32,256,128]{2,1,0:T(8,128)S(1)} %fusion.9) | copy-start | bytes 12582916
  69.0 10.4 %collective-permute-start.10 = (f32[128,128]{0,1:T(8,128)S(1)}, f32[128,128]{0,1:T(8,128)S(1)}, u32[]{:S(2)}, u32[]{:S(2)}) collective-permute-start(f32[128,128]{0,1:T(8,128)S(1)} %convolution_bitcast_fusion.1), channel_id=1, source_target_pairs={{0,12},{1,13},{2,14},{3,15},{4,8},{5,9},{6,10},{7,11},{8,4},{9,5},... | collective-permute-start | bytes 196616 | tf_op jit(solution)/shard_map/ppermute | solution.py:110
  75.6 7.2 %collective-permute-start.8 = (f32[128,128]{0,1:T(8,128)S(1)}, f32[128,128]{0,1:T(8,128)S(1)}, u32[]{:S(2)}, u32[]{:S(2)}) collective-permute-start(f32[128,128]{0,1:T(8,128)S(1)} %convolution_bitcast_fusion.1), channel_id=1, source_target_pairs={{0,4},{1,5},{2,6},{3,7},{4,0},{5,1},{6,2},{7,3},{8,12},{9,13},{10,... | collective-permute-start | bytes 196616 | tf_op jit(solution)/shard_map/ppermute | solution.py:110
  79.4 8.6 %collective-permute-start.9 = (f32[128,128]{0,1:T(8,128)S(1)}, f32[128,128]{0,1:T(8,128)S(1)}, u32[]{:S(2)}, u32[]{:S(2)}) collective-permute-start(f32[128,128]{0,1:T(8,128)S(1)} %convolution_bitcast_fusion.1), channel_id=1, source_target_pairs={{0,8},{1,9},{2,10},{3,11},{4,12},{5,13},{6,14},{7,15},{8,0},{9,1},... | collective-permute-start | bytes 196616 | tf_op jit(solution)/shard_map/ppermute | solution.py:110
  88.1 2.2 %collective-permute-start.11 = (f32[128,128]{0,1:T(8,128)S(1)}, f32[128,128]{0,1:T(8,128)S(1)}, u32[]{:S(2)}, u32[]{:S(2)}) collective-permute-start(f32[128,128]{0,1:T(8,128)S(1)} %add_add_fusion.2), channel_id=1, source_target_pairs={{0,1},{1,0},{2,3},{3,2},{4,5},{5,4},{6,7},{7,6},{8,9},{9,8},{10,11... | collective-permute-start | bytes 196616 | tf_op jit(solution)/shard_map/ppermute | solution.py:110
  88.4 5.1 %collective-permute-start.12 = (f32[128,128]{0,1:T(8,128)S(1)}, f32[128,128]{0,1:T(8,128)S(1)}, u32[]{:S(2)}, u32[]{:S(2)}) collective-permute-start(f32[128,128]{0,1:T(8,128)S(1)} %add_add_fusion.2), channel_id=1, source_target_pairs={{0,2},{1,3},{2,0},{3,1},{4,6},{5,7},{6,4},{7,5},{8,10},{9,11},{10,... | collective-permute-start | bytes 196616 | tf_op jit(solution)/shard_map/ppermute | solution.py:110
  88.5 5.2 %collective-permute-start.13 = (f32[128,128]{0,1:T(8,128)S(1)}, f32[128,128]{0,1:T(8,128)S(1)}, u32[]{:S(2)}, u32[]{:S(2)}) collective-permute-start(f32[128,128]{0,1:T(8,128)S(1)} %add_add_fusion.2), channel_id=1, source_target_pairs={{0,3},{1,2},{2,1},{3,0},{4,7},{5,6},{6,5},{7,4},{8,11},{9,10},{10,... | collective-permute-start | bytes 196616 | tf_op jit(solution)/shard_map/ppermute | solution.py:110
  93.7 5.2 %collective-permute-start.14 = (f32[128,128]{0,1:T(8,128)S(1)}, f32[128,128]{0,1:T(8,128)S(1)}, u32[]{:S(2)}, u32[]{:S(2)}) collective-permute-start(f32[128,128]{0,1:T(8,128)S(1)} %add_add_fusion.1), channel_id=1, source_target_pairs={{0,64},{16,80},{32,96},{48,112},{64,0},{80,16},{96,32},{112,48},{1... | collective-permute-start | bytes 196616 | tf_op jit(solution)/shard_map/ppermute | solution.py:110
  96.0 6.7 %collective-permute-start.15 = (f32[128,128]{0,1:T(8,128)S(1)}, f32[128,128]{0,1:T(8,128)S(1)}, u32[]{:S(2)}, u32[]{:S(2)}) collective-permute-start(f32[128,128]{0,1:T(8,128)S(1)} %add_add_fusion.1), channel_id=1, source_target_pairs={{0,128},{16,144},{32,160},{48,176},{64,192},{80,208},{96,224},{112... | collective-permute-start | bytes 196616 | tf_op jit(solution)/shard_map/ppermute | solution.py:110
  98.9 5.5 %collective-permute-start.16 = (f32[128,128]{0,1:T(8,128)S(1)}, f32[128,128]{0,1:T(8,128)S(1)}, u32[]{:S(2)}, u32[]{:S(2)}) collective-permute-start(f32[128,128]{0,1:T(8,128)S(1)} %add_add_fusion.1), channel_id=1, source_target_pairs={{0,192},{16,208},{32,224},{48,240},{64,128},{80,144},{96,160},{112... | collective-permute-start | bytes 196616 | tf_op jit(solution)/shard_map/ppermute | solution.py:110
  104.4 6.5 %collective-permute-start.17 = (f32[128,128]{0,1:T(8,128)S(1)}, f32[128,128]{0,1:T(8,128)S(1)}, u32[]{:S(2)}, u32[]{:S(2)}) collective-permute-start(f32[128,128]{0,1:T(8,128)S(1)} %add_add_fusion), channel_id=1, source_target_pairs={{0,16},{16,0},{32,48},{48,32},{64,80},{80,64},{96,112},{112,96},{1... | collective-permute-start | bytes 196616 | tf_op jit(solution)/shard_map/ppermute | solution.py:110
  108.6 5.8 %collective-permute-start.18 = (f32[128,128]{0,1:T(8,128)S(1)}, f32[128,128]{0,1:T(8,128)S(1)}, u32[]{:S(2)}, u32[]{:S(2)}) collective-permute-start(f32[128,128]{0,1:T(8,128)S(1)} %add_add_fusion), channel_id=1, source_target_pairs={{0,32},{16,48},{32,0},{48,16},{64,96},{80,112},{96,64},{112,80},{1... | collective-permute-start | bytes 196616 | tf_op jit(solution)/shard_map/ppermute | solution.py:110
  108.6 5.8 %collective-permute-start.19 = (f32[128,128]{0,1:T(8,128)S(1)}, f32[128,128]{0,1:T(8,128)S(1)}, u32[]{:S(2)}, u32[]{:S(2)}) collective-permute-start(f32[128,128]{0,1:T(8,128)S(1)} %add_add_fusion), channel_id=1, source_target_pairs={{0,48},{16,32},{32,16},{48,0},{64,112},{80,96},{96,80},{112,64},{1... | collective-permute-start | bytes 196616 | tf_op jit(solution)/shard_map/ppermute | solution.py:110
